TPU v7x, 32 devices: a whole 2x2x4 slice. The times are simulated.
32 devices in a mesh: groups: 2 (over y), corr: 4 (over z), filt: 2 (over x), pair: 2 (over core).
Axes of the slice: x: 2, y: 2, z: 4, core: 2. Of those that a mesh axis runs over, the one named last changes fastest.
Arguments:
- raw_rows: bfloat16 [4, 32, 3, 16384], P(('groups', 'pair'), 'filt', None, 'corr'), parts along dimension 0, may hold values from -6 to 6
- valid_counts: int32 [4, 32], P(('groups', 'pair'), 'filt'), parts along dimension 0, may hold values from 4096 to 16384
- taps: bfloat16 [64], replicated, may hold values from -0.75 to 0.75
- templates: bfloat16 [128, 225], P('corr'), may hold values from -6 to 6
- masks: int32 [128, 3, 32], replicated, may hold values 0 or 1
Outputs:
- stack: float32 [4, 128, 4096], P(('groups', 'pair'), 'corr', 'filt'), parts along dimension 0
There are 2 independent parts, one for each index of `groups`. A program takes and returns all parts, laid end to end along the dimension named above; an argument that names none is the same for every part. Nothing has to cross between parts.
All inputs are finite; a program needn't handle non-finite values.
Results may differ from a plain program's by a relative error of at most 0.0051.
Values may be sent and summed in bfloat16 or wider, within the bound.
No kernel may reach another device: no remote copies, remote signals or barrier semaphores. Data moves between devices by JAX's collectives and lax.ppermute only.
A program may use at most 192 MiB of HBM per device.

v0:
```python
import jax
import jax.numpy as jnp
from jax import lax
from jax.sharding import PartitionSpec as P

L = 75
TAPS = 64
DEC = 4


def from_behind(block, axis, distance):
    devices = range(lax.axis_size(axis))
    route = [(i - distance, i) for i in devices if i - distance in devices]
    return lax.ppermute(block, axis, route)


def scaled_rows(extended):
    station_count = extended.shape[0]
    width = extended.shape[2] - (L - 1)
    slices = jnp.stack([extended[:, :, lag : lag + width] for lag in range(L)], axis=2)
    energy = jnp.einsum("scjt,scjt->sct", slices, slices, preferred_element_type=jnp.float32)
    scaled = (slices / jnp.sqrt(jnp.maximum(energy, 1.0))[:, :, None, :]).astype(jnp.bfloat16)
    return scaled.reshape(station_count * 3 * L, width)


def template_weights(template_rows, mask_rows):
    count = template_rows.shape[0]
    stations = mask_rows.shape[2]
    shaped = template_rows.astype(jnp.float32).reshape(count, 3, L)
    norms = jnp.sqrt(jnp.sum(shaped * shaped, axis=2) + 1e-06)
    base = shaped / norms[:, :, None]
    chosen = jnp.transpose(mask_rows.astype(jnp.float32), (0, 2, 1))
    full = base[:, None, :, :] * chosen[:, :, :, None]
    return full.astype(jnp.bfloat16).reshape(count, stations * 3 * L)


def body(raw_rows, valid_counts, taps, templates, masks):
    samples = raw_rows[0]
    counts = valid_counts[0]
    local_stations = samples.shape[0]
    raw_width = samples.shape[2]
    corr_place = lax.axis_index("corr")
    corr_count = lax.axis_size("corr")
    filt_count = lax.axis_size("filt")
    template_all = masks.shape[0]
    group_size = masks.shape[2] // (corr_count * filt_count)
    sample_times = corr_place * raw_width + lax.iota(jnp.int32, raw_width)
    live = jnp.where(
        sample_times[None, None, :] < counts[:, None, None], samples, jnp.zeros_like(samples)
    )
    history = from_behind(live[:, :, raw_width - (TAPS - 1) :], "corr", 1)
    extended = jnp.concatenate([history, live], axis=2).reshape(
        local_stations * 3, 1, raw_width + TAPS - 1
    )
    kernel = taps[::-1].reshape(1, 1, TAPS)
    filtered = lax.conv_general_dilated(
        extended,
        kernel,
        (DEC,),
        "VALID",
        dimension_numbers=("NCH", "OIH", "NCH"),
        preferred_element_type=jnp.float32,
    )
    decimated = raw_width // DEC
    filtered = filtered.astype(jnp.bfloat16).reshape(local_stations, 3, decimated)
    moved = lax.all_to_all(
        lax.all_to_all(filtered, "corr", split_axis=0, concat_axis=2, tiled=True),
        "filt",
        split_axis=2,
        concat_axis=0,
        tiled=True,
    )
    following = from_behind(moved[:, :, : L - 1], "filt", -1)
    lagged = jnp.concatenate([moved, following], axis=2)
    block_width = moved.shape[2]
    split_masks = masks.reshape(template_all, 3, filt_count, corr_count, group_size)
    mine = lax.dynamic_slice_in_dim(split_masks, corr_place, 1, 3).reshape(
        template_all, 3, filt_count * group_size
    )
    scaled = scaled_rows(lagged)
    empty = jnp.zeros((template_all, block_width), jnp.float32)
    weights = template_weights(lax.all_gather(templates, "corr", axis=0, tiled=True), mine)
    partial_rows = jnp.dot(weights, scaled, preferred_element_type=jnp.float32)
    totals = lax.dynamic_update_slice_in_dim(empty, partial_rows, jnp.int32(0), 0)
    stacked = lax.psum_scatter(totals, "corr", scatter_dimension=0, tiled=True)
    return stacked[None]


def solution(mesh):
    return jax.shard_map(
        body,
        mesh=mesh,
        in_specs=(
            P(("groups", "pair"), "filt", None, "corr"),
            P(("groups", "pair"), "filt"),
            P(),
            P("corr", None),
            P(),
        ),
        out_specs=P(("groups", "pair"), "corr", "filt"),
        check_vma=False,
    )
```

profile of v0, /device:TPU:0, one launch (start us, length us, event | category | flops | bytes accessed | tf_op | source)
XLA Modules:
  0.0 146.4 jit_solution(11278841921117078168)
XLA Ops:
  6.5 0.8 broadcast_compare_fusion
  7.3 1.0 bitcast_select_fusion
  8.4 4.9 %collective-permute-start = (bf16[16,3,63]{2,0,1:T(8,128)(2,1)S(1)}, bf16[16,3,63]{2,0,1:T(8,128)(2,1)S(1)}, u32[]{:S(2)}, u32[]{:S(2)}) collective-permute-start(bf16[16,3,63]{2,0,1:T(8,128)(2,1)S(1)} %slice.304), channel_id=1, source_target_pairs={{0,4},{4,8},{8,12},{1,5},{5,9},{9,13},{2,6},{6,10},{10,14},{3,7},{... | collective-permute-start | bytes 18152 | tf_op jit(solution)/shard_map/ppermute | solution.py:14
  13.4 13.7 %all_gather.3 = bf16[128,225]{1,0:T(8,128)(2,1)S(1)} all-gather(bf16[32,225]{1,0:T(8,128)(2,1)} %param.8), channel_id=1, replica_groups=mesh['groups'=2,'corr'=4,'filt'=2,'pair'=2] {'corr'}, dimensions={0}, use_global_device_ids=true | all-gather | bytes 72000 | tf_op jit(solution)/shard_map/all_gather | solution.py:82
  27.3 0.7 rev.3
  28.9 2.8 %copy.133 = bf16[48,1,4159]{0,1,2:T(2,128)(2,1)S(1)} copy(bf16[48,1,4159]{2,0,1:T(8,128)(2,1)S(1)} %reshape.73) | data formatting | bytes 798528 | tf_op jit(solution)/shard_map/reshape | solution.py:52
  31.7 11.7 %convolution_convert_fusion = bf16[48,1,1024]{0,1,2:T(2,128)(2,1)S(1)} fusion(bf16[48,1,4159]{0,1,2:T(2,128)(2,1)S(1)} %copy.133, bf16[1,1,64]{1,0,2:T(2,128)(2,1)S(1)} %copy.134), kind=kOutput, calls=%fused_computation.6 | convolution fusion | flops 6340608 | bytes 497696 | tf_op jit(solution)/shard_map/conv_general_dilated | solution.py:56
  43.7 0.7 reshape.75
  44.5 3.3 %all-to-all-start = ((bf16[16,3,1024]{2,1,0:T(4,128)(2,1)}), bf16[16,3,1024]{2,1,0:T(4,128)(2,1)S(1)}, u32[]{:S(2)}, u32[]{:S(2)}) async-start(bf16[16,3,1024]{2,1,0:T(4,128)(2,1)} %reshape.75), calls=%async_computation | async-start | bytes 262144 | tf_op jit(solution)/shard_map/all_to_all | solution.py:67
  47.8 5.9 %all-to-all-done = bf16[16,3,1024]{2,1,0:T(4,128)(2,1)S(1)} async-done(((bf16[16,3,1024]{2,1,0:T(4,128)(2,1)}), bf16[16,3,1024]{2,1,0:T(4,128)(2,1)S(1)}, u32[]{:S(2)}, u32[]{:S(2)}) %all-to-all-start) | async-done | bytes 98336 | tf_op jit(solution)/shard_map/all_to_all | solution.py:67
  53.7 4.7 %copy.149 = bf16[4,3,4,1024]{0,1,3,2:T(4,128)(2,1)} copy(bf16[4,3,4,1024]{3,1,0,2:T(4,128)(2,1)S(1)} %bitcast.336) | data formatting | bytes 196608 | tf_op jit(solution)/shard_map/all_to_all | solution.py:67
  58.4 5.8 %reshape.81 = bf16[2,2,12288]{2,1,0:T(2,128)(2,1)} reshape(bf16[4096,3,4]{2,1,0:T(4,128)(2,1)} %bitcast.334) | data formatting | bytes 196608
  64.3 3.3 %all-to-all-start.1 = ((bf16[2,2,12288]{2,1,0:T(2,128)(2,1)}), bf16[2,2,12288]{2,1,0:T(2,128)(2,1)S(1)}, u32[]{:S(2)}, u32[]{:S(2)}) async-start(bf16[2,2,12288]{2,1,0:T(2,128)(2,1)} %reshape.81), calls=%async_computation.1 | async-start | bytes 196608 | tf_op jit(solution)/shard_map/all_to_all | solution.py:66
  67.7 0.7 dynamic-slice_convert_fusion
  68.4 3.5 %all-to-all-done.1 = bf16[2,2,12288]{2,1,0:T(2,128)(2,1)S(1)} async-done(((bf16[2,2,12288]{2,1,0:T(2,128)(2,1)}), bf16[2,2,12288]{2,1,0:T(2,128)(2,1)S(1)}, u32[]{:S(2)}, u32[]{:S(2)}) %all-to-all-start.1) | async-done | bytes 98336 | tf_op jit(solution)/shard_map/all_to_all | solution.py:66
  71.9 5.1 %reshape.82 = bf16[4096,3,4]{2,1,0:T(4,128)(2,1)} reshape(bf16[2,2,12288]{2,1,0:T(2,128)(2,1)S(1)} %all-to-all-done.1) | data formatting | bytes 196608
  77.0 5.9 %copy.150 = bf16[4,3,2,2048]{3,2,0,1:T(2,128)(2,1)S(1)} copy(bf16[4,3,2,2048]{0,1,3,2:T(4,128)(2,1)} %bitcast.335) | data formatting | bytes 196608 | tf_op jit(solution)/shard_map/all_to_all | solution.py:66
  83.0 1.5 %collective-permute-start.1 = (bf16[8,3,74]{2,0,1:T(8,128)(2,1)S(1)}, bf16[8,3,74]{2,0,1:T(8,128)(2,1)S(1)}, u32[]{:S(2)}, u32[]{:S(2)}) collective-permute-start(bf16[8,3,74]{2,0,1:T(8,128)(2,1)S(1)} %slice.305), channel_id=1, source_target_pairs={{2,0},{3,1},{6,4},{7,5},{10,8},{11,9},{14,12},{15,13},{18,16},{19,... | collective-permute-start | bytes 10664 | tf_op jit(solution)/shard_map/ppermute | solution.py:14
  84.5 4.0 %collective-permute-done.1 = bf16[8,3,74]{2,0,1:T(8,128)(2,1)S(1)} collective-permute-done((bf16[8,3,74]{2,0,1:T(8,128)(2,1)S(1)}, bf16[8,3,74]{2,0,1:T(8,128)(2,1)S(1)}, u32[]{:S(2)}, u32[]{:S(2)}) %collective-permute-start.1) | collective-permute-done | bytes 3584 | tf_op jit(solution)/shard_map/ppermute | solution.py:14
  96.0 1.6 %fusion = f32[8,3,2048]{2,0,1:T(8,128)S(1)} fusion(bf16[8,3,75,2048]{3,0,1,2:T(8,128)(2,1)S(1)} %constant_dynamic-update-slice_fusion.2), kind=kLoop, calls=%fused_computation.1 | loop fusion | flops 11010048 | bytes 7569408 | tf_op jit(solution)/shard_map/scjt,scjt->sct/dot_general | solution.py:21
  97.6 1.4 copy-done
  99.0 5.3 %divide_convert_fusion = bf16[8,3,75,2048]{3,0,1,2:T(8,128)(2,1)S(1)} fusion(bf16[8,3,75,2048]{3,0,1,2:T(8,128)(2,1)} %copy-done, f32[8,3,2048]{2,0,1:T(8,128)S(1)} %maximum_sqrt_fusion), kind=kLoop, calls=%fused_computation.2 | loop fusion | flops 11059200 | bytes 14942208 | tf_op jit(solution)/shard_map/convert_element_type | solution.py:22
  104.3 9.6 %fusion.3 = f32[128,2048]{1,0:T(8,128)} fusion(bf16[8,3,75,2048]{3,0,1,2:T(8,128)(2,1)S(1)} %divide_convert_fusion, f32[128,8,3]{0,2,1:T(4,128)S(1)} %bitcast.338, f32[128,3,75]{0,2,1:T(8,128)S(1)} %broadcast_divide_fusion), kind=kOutput, calls=%fused_computation.5 | convolution fusion | flops 944179200 | bytes 8548864 | tf_op jit(solution)/shard_map/dot_general | solution.py:83
  113.9 25.6 %reduce-scatter.2.cloned.1.call-done = f32[32,2048]{1,0:T(8,128)} async-done(((f32[128,2048]{1,0:T(8,128)}), f32[32,2048]{1,0:T(8,128)}) %reduce-scatter.2.cloned.1.call-update) | async-done | bytes 262160 | tf_op jit(solution)/shard_map/reduce_scatter | solution.py:85
  (99 shorter events, 8.7 us)
Async XLA Ops:
  8.4 19.7 %collective-permute-start = (bf16[16,3,63]{2,0,1:T(8,128)(2,1)S(1)}, bf16[16,3,63]{2,0,1:T(8,128)(2,1)S(1)}, u32[]{:S(2)}, u32[]{:S(2)}) collective-permute-start(bf16[16,3,63]{2,0,1:T(8,128)(2,1)S(1)} %slice.304), channel_id=1, source_target_pairs={{0,4},{4,8},{8,12},{1,5},{5,9},{9,13},{2,6},{6,10},{10,14},{3,7},{... | collective-permute-start | bytes 18152 | tf_op jit(solution)/shard_map/ppermute | solution.py:14
  44.5 9.2 %all-to-all-start = ((bf16[16,3,1024]{2,1,0:T(4,128)(2,1)}), bf16[16,3,1024]{2,1,0:T(4,128)(2,1)S(1)}, u32[]{:S(2)}, u32[]{:S(2)}) async-start(bf16[16,3,1024]{2,1,0:T(4,128)(2,1)} %reshape.75), calls=%async_computation | async-start | bytes 262144 | tf_op jit(solution)/shard_map/all_to_all | solution.py:67
  64.3 7.6 %all-to-all-start.1 = ((bf16[2,2,12288]{2,1,0:T(2,128)(2,1)}), bf16[2,2,12288]{2,1,0:T(2,128)(2,1)S(1)}, u32[]{:S(2)}, u32[]{:S(2)}) async-start(bf16[2,2,12288]{2,1,0:T(2,128)(2,1)} %reshape.81), calls=%async_computation.1 | async-start | bytes 196608 | tf_op jit(solution)/shard_map/all_to_all | solution.py:66
  67.6 71.9 %reduce-scatter.2.cloned.1.call-start = ((), (), s32[]{:S(2)}) async-start(), calls=%async_computation.3 | async-start | bytes 1310720 | tf_op jit(solution)/shard_map/reduce_scatter | solution.py:85
  83.0 5.5 %collective-permute-start.1 = (bf16[8,3,74]{2,0,1:T(8,128)(2,1)S(1)}, bf16[8,3,74]{2,0,1:T(8,128)(2,1)S(1)}, u32[]{:S(2)}, u32[]{:S(2)}) collective-permute-start(bf16[8,3,74]{2,0,1:T(8,128)(2,1)S(1)} %slice.305), channel_id=1, source_target_pairs={{2,0},{3,1},{6,4},{7,5},{10,8},{11,9},{14,12},{15,13},{18,16},{19,... | collective-permute-start | bytes 10664 | tf_op jit(solution)/shard_map/ppermute | solution.py:14
  96.0 3.0 %copy-start = (bf16[8,3,75,2048]{3,0,1,2:T(8,128)(2,1)}, bf16[8,3,75,2048]{3,0,1,2:T(8,128)(2,1)S(1)}, u32[]{:S(2)}) copy-start(bf16[8,3,75,2048]{3,0,1,2:T(8,128)(2,1)S(1)} %constant_dynamic-update-slice_fusion.2) | copy-start | bytes 22118404
Sparse Core Ops, SparseCore 0:
  114.0 25.4 reduce-scatter.1
where the time goes:
time: 147 us; the launch traced here: 146 us
  waiting for transfers between devices  39 us (27%)
  local copies, waits for them, and re-layouts  35.5 us (24%)
  matrix products  21.2 us (14%)
  between operations  14.1 us (10%)
  blocking collectives  13.7 us (9%)
  starting transfers between devices  13.1 us (9%)
  other arithmetic  9.66 us (7%)
    reduce_scatter x1, waiting for transfers between devices, body(): stacked = lax.psum_scatter(totals, 'corr', scatter_dimension=0, tiled=True)  25.6 us
    unnamed x79, local copies, waits for them, and re-layouts  19.2 us
    all_gather x1, blocking collectives, body(): lax.all_gather(templates, 'corr', axis=0, tiled=True)  13.7 us
    conv_general_dilated x1, matrix products, body(): lax.conv_general_dilated(extended, kernel, (DEC,), 'VALID', dimension_num...  11.7 us
    dot_general x1, matrix products, body(): partial_rows = jnp.dot(weights, scaled, preferred_element_type=jnp.float32)  9.56 us
    ppermute x2, starting transfers between devices, from_behind(): return lax.ppermute(block, axis, route)  6.42 us
    all_to_all x3, local copies, waits for them, and re-layouts, body(): lax.all_to_all(lax.all_to_all(filtered, 'corr', split_axis=0, concat_axis...  5.94 us
    all_to_all x1, waiting for transfers between devices, body(): lax.all_to_all(filtered, 'corr', split_axis=0, concat_axis=2, tiled=True)  5.86 us
  transfers between devices with their start and end apart: 5, of which 4 were waited for; matrix products, arithmetic and copies ran while one was open for 1% of the time, Pallas kernels for 0%

commit v1 on v0

v1 whole, which is shorter than its diff:
```python
import functools

import jax
import jax.numpy as jnp
from jax import lax
from jax.experimental import pallas as pl
from jax.experimental.pallas import tpu as pltpu
from jax.sharding import PartitionSpec as P

L = 75
TAPS = 64
DEC = 4
JP = 76
TT = 512
RSUB = 16


def from_behind(block, axis, distance):
    devices = range(lax.axis_size(axis))
    route = [(i - distance, i) for i in devices if i - distance in devices]
    return lax.ppermute(block, axis, route)


def window_energy(rows, width):
    p1 = rows * rows
    p2 = p1[:, :-1] + p1[:, 1:]
    p4 = p2[:, :-2] + p2[:, 2:]
    p8 = p4[:, :-4] + p4[:, 4:]
    p16 = p8[:, :-8] + p8[:, 8:]
    p32 = p16[:, :-16] + p16[:, 16:]
    p64 = p32[:, :-32] + p32[:, 32:]
    return (
        p64[:, :width]
        + p8[:, 64 : 64 + width]
        + p2[:, 72 : 72 + width]
        + p1[:, 74 : 74 + width]
    )


def corr_kernel(f_ref, inv_ref, w_ref, o_ref, s_ref, *, row_block):
    q = pl.program_id(1)
    span = TT + 128

    def fill(sub, carry):
        r0 = pl.multiple_of(sub * RSUB, RSUB)
        seg = f_ref[0, pl.ds(r0, RSUB), :].astype(jnp.float32)
        inv = inv_ref[pl.ds(r0, RSUB), :]
        for j in range(JP):
            moved = seg if j == 0 else pltpu.roll(seg, span - j, 1)
            piece = (moved[:, :TT] * inv).astype(jnp.bfloat16)
            s_ref[pl.ds(pl.multiple_of(j * row_block + r0, RSUB), RSUB), :] = piece
        return carry

    lax.fori_loop(0, row_block // RSUB, fill, 0)
    part = jnp.dot(w_ref[...], s_ref[...], preferred_element_type=jnp.float32)

    @pl.when(q == 0)
    def _():
        o_ref[...] = part

    @pl.when(q > 0)
    def _():
        o_ref[...] += part


def correlate(windows, inv, weights, row_block):
    tiles, rows, span = windows.shape
    count = weights.shape[0]
    width = inv.shape[1]
    chunks = rows // row_block
    return pl.pallas_call(
        functools.partial(corr_kernel, row_block=row_block),
        grid=(tiles, chunks),
        in_specs=[
            pl.BlockSpec((1, row_block, span), lambda i, q: (i, q, 0)),
            pl.BlockSpec((row_block, TT), lambda i, q: (q, i)),
            pl.BlockSpec((count, JP * row_block), lambda i, q: (0, q)),
        ],
        out_specs=pl.BlockSpec((count, TT), lambda i, q: (0, i)),
        out_shape=jax.ShapeDtypeStruct((count, width), jnp.float32),
        scratch_shapes=[pltpu.VMEM((JP * row_block, TT), jnp.bfloat16)],
        compiler_params=pltpu.CompilerParams(
            dimension_semantics=("parallel", "arbitrary"),
            vmem_limit_bytes=48 * 1024 * 1024,
        ),
    )(windows, inv, weights)


def body(raw_rows, valid_counts, taps, templates, masks):
    samples = raw_rows[0]
    counts = valid_counts[0]
    local_stations = samples.shape[0]
    raw_width = samples.shape[2]
    corr_place = lax.axis_index("corr")
    filt_place = lax.axis_index("filt")
    filt_count = lax.axis_size("filt")
    sample_times = corr_place * raw_width + lax.iota(jnp.int32, raw_width)
    live = jnp.where(
        sample_times[None, None, :] < counts[:, None, None], samples, jnp.zeros_like(samples)
    )
    history = from_behind(live[:, :, raw_width - (TAPS - 1) :], "corr", 1)
    extended = jnp.concatenate([history, live], axis=2).reshape(
        local_stations * 3, 1, raw_width + TAPS - 1
    )
    kernel = taps[::-1].reshape(1, 1, TAPS)
    filtered = lax.conv_general_dilated(
        extended,
        kernel,
        (DEC,),
        "VALID",
        dimension_numbers=("NCH", "OIH", "NCH"),
        preferred_element_type=jnp.float32,
    )
    decimated = raw_width // DEC
    filtered = filtered.astype(jnp.bfloat16).reshape(local_stations * 3, decimated)
    whole = lax.all_gather(filtered, "corr", axis=1, tiled=True)
    total_width = whole.shape[1]
    block = total_width // filt_count
    span = block + 128
    padded = jnp.concatenate(
        [whole, jnp.zeros((whole.shape[0], 128), whole.dtype)], axis=1
    )
    pieces = jnp.stack(
        [padded[:, g * block : g * block + span] for g in range(filt_count)], axis=0
    )
    gathered = lax.all_to_all(pieces, "filt", 0, 0, tiled=True)
    rows = gathered.reshape(filt_count * local_stations * 3, span)
    energy = window_energy(rows.astype(jnp.float32), block)
    inv = lax.rsqrt(jnp.maximum(energy, 1.0))
    tiles = block // TT
    windows = jnp.stack([rows[:, i * TT : i * TT + TT + 128] for i in range(tiles)], axis=0)

    count = templates.shape[0]
    stations = masks.shape[2]
    shaped = templates.astype(jnp.float32).reshape(count, 3, L)
    norms = jnp.sqrt(jnp.sum(shaped * shaped, axis=2) + 1e-06)
    base = shaped / norms[:, :, None]
    mine = lax.dynamic_slice_in_dim(masks, corr_place * count, count, 0).astype(jnp.float32)
    full = jnp.transpose(base, (0, 2, 1))[:, :, None, :] * jnp.transpose(mine, (0, 2, 1))[:, None, :, :]
    full = full.astype(jnp.bfloat16).reshape(count, L, stations * 3)
    full = jnp.concatenate([full, jnp.zeros((count, JP - L, stations * 3), full.dtype)], axis=1)
    total_rows = stations * 3
    row_block = 96 if total_rows % 96 == 0 else total_rows
    chunks = total_rows // row_block
    weights = (
        full.reshape(count, JP, chunks, row_block)
        .transpose(0, 2, 1, 3)
        .reshape(count, chunks * JP * row_block)
    )
    stacked = correlate(windows, inv, weights, row_block)
    return stacked[None]


def solution(mesh):
    return jax.shard_map(
        body,
        mesh=mesh,
        in_specs=(
            P(("groups", "pair"), "filt", None, "corr"),
            P(("groups", "pair"), "filt"),
            P(),
            P("corr", None),
            P(),
        ),
        out_specs=P(("groups", "pair"), "corr", "filt"),
        check_vma=False,
    )
```

time: 147 us -> 72.1 us (0.49)
  waiting for transfers between devices: 39 us -> 3.44 us
  local copies, waits for them, and re-layouts: 35.5 us -> 7.65 us
  Pallas kernels: 0 us -> 18.4 us
  between operations: 14.1 us -> 0.21 us
  matrix products: 21.2 us -> 11.7 us
  starting transfers between devices: 13.1 us -> 8.6 us
  other arithmetic: 9.66 us -> 6.6 us
  blocking collectives: 13.7 us -> 15.2 us
    reduce_scatter x1 -> x0, waiting for transfers between devices: 25.6 us -> none  [body(): stacked = lax.psum_scatter(totals, 'corr', scatter_dimension=0, tiled=True)]
    pallas_call x0 -> x1, Pallas kernels: none -> 18.4 us  [correlate(): pl.pallas_call(functools.partial(corr_kernel, row_block=row_block), grid=...]
    unnamed x79 -> x1, local copies, waits for them, and re-layouts: 19.2 us -> 0.98 us
    all_to_all x4 -> x0, local copies, waits for them, and re-layouts: 10.7 us -> none  [the longest x3 5.94 us: body(): lax.all_to_all(lax.all_to_all(filtered, 'corr', split_axis=0, concat_axis...]
    dot_general x1 -> x0, matrix products: 9.56 us -> none  [body(): partial_rows = jnp.dot(weights, scaled, preferred_element_type=jnp.float32)]
    all_to_all x2 -> x1, waiting for transfers between devices: 9.37 us -> 3.44 us  [body(): gathered = lax.all_to_all(pieces, 'filt', 0, 0, tiled=True)]
    convert_element_type x2 -> x1, other arithmetic: 6.03 us -> 0.47 us  [body(): full = full.astype(jnp.bfloat16).reshape(count, L, stations * 3)]
    ppermute x2 -> x1, waiting for transfers between devices: 4.03 us -> 0.01 us  [from_behind(): return lax.ppermute(block, axis, route)]
  transfers between devices with their start and end apart: 5 -> 2, of which waited for: 4 -> 1; matrix products, arithmetic and copies ran while one was open for 1% -> 7% of each run, Pallas kernels for 0% -> 0%
where the time goes in v1:
time: 72.1 us; the launch traced here: 71.8 us
  Pallas kernels  18.4 us (26%)
  blocking collectives  15.2 us (21%)
  matrix products  11.7 us (16%)
  starting transfers between devices  8.6 us (12%)
  local copies, waits for them, and re-layouts  7.65 us (11%)
  other arithmetic  6.6 us (9%)
  waiting for transfers between devices  3.44 us (5%)
    pallas_call x1, Pallas kernels, correlate(): pl.pallas_call(functools.partial(corr_kernel, row_block=row_block), grid=...  18.4 us
    all_gather x1, blocking collectives, body(): whole = lax.all_gather(filtered, 'corr', axis=1, tiled=True)  15.2 us
    conv_general_dilated x1, matrix products, body(): lax.conv_general_dilated(extended, kernel, (DEC,), 'VALID', dimension_num...  11.7 us
    ppermute x1, starting transfers between devices, from_behind(): return lax.ppermute(block, axis, route)  4.95 us
    all_to_all x1, starting transfers between devices, body(): gathered = lax.all_to_all(pieces, 'filt', 0, 0, tiled=True)  3.65 us
    all_to_all x1, waiting for transfers between devices, body(): gathered = lax.all_to_all(pieces, 'filt', 0, 0, tiled=True)  3.44 us
    reshape x2, local copies, waits for them, and re-layouts, body(): jnp.concatenate([history, live], axis=2)  3.19 us
  transfers between devices with their start and end apart: 2, of which 1 were waited for; matrix products, arithmetic and copies ran while one was open for 7% of the time, Pallas kernels for 0%

profile of v1, /device:TPU:0, one launch (start us, length us, event | category | flops | bytes accessed | tf_op | source)
XLA Modules:
  0.0 71.8 jit_solution(848286401747712375)
XLA Ops:
  0.0 0.8 %broadcast_compare_fusion = pred[16,4096]{1,0:T(8,128)(4,1)S(1)} fusion(s32[4096]{0:T(1024)S(1)} %iota_add_fusion, s32[16]{0:T(128)} %bitcast.34), kind=kLoop, calls=%fused_computation.22 | loop fusion | flops 65536 | bytes 81984 | tf_op jit(solution)/shard_map/lt | solution.py:99
  0.8 1.0 %bitcast_select_fusion = bf16[16,3,4096]{2,0,1:T(8,128)(2,1)S(1)} fusion(bf16[1,16,3,4096]{3,1,2,0:T(8,128)(2,1)} %param.5, pred[16,4096]{1,0:T(8,128)(4,1)S(1)} %broadcast_compare_fusion), kind=kLoop, calls=%fused_computation.19 | loop fusion | flops 196608 | bytes 851968 | tf_op jit(solution)/shard_map/jit(_where)/select_n | solution.py:98
  1.9 4.9 %collective-permute-start = (bf16[16,3,63]{2,0,1:T(8,128)(2,1)S(1)}, bf16[16,3,63]{2,0,1:T(8,128)(2,1)S(1)}, u32[]{:S(2)}, u32[]{:S(2)}) collective-permute-start(bf16[16,3,63]{2,0,1:T(8,128)(2,1)S(1)} %slice.92), channel_id=1, source_target_pairs={{0,4},{4,8},{8,12},{1,5},{5,9},{9,13},{2,6},{6,10},{10,14},{3,7},{... | collective-permute-start | bytes 18152 | tf_op jit(solution)/shard_map/ppermute | solution.py:21
  6.8 0.8 %reshape.71 = f32[32,3,75]{2,1,0:T(4,128)S(1)} reshape(bf16[32,225]{1,0:T(8,128)(2,1)} %param.8) | data formatting | bytes 43200 | tf_op jit(solution)/shard_map/reshape | solution.py:135
  7.8 0.9 %convert_bitcast_fusion = f32[32,32,3]{0,1,2:T(8,128)S(1)} fusion(s32[128,3,32]{0,2,1:T(8,128)} %param.9, s32[]{:T(128)S(6)} %select_n.8), kind=kLoop, calls=%fused_computation.29 | loop fusion | flops 3072 | bytes 24580 | tf_op jit(solution)/shard_map/transpose | solution.py:139
  8.7 0.7 %rev.3 = bf16[64]{0:T(256)(128)(2,1)S(1)} reverse(bf16[64]{0:T(256)(128)(2,1)} %param.7), dimensions={0} | reverse | bytes 256 | tf_op jit(solution)/shard_map/rev | solution.py:105
  10.0 0.3 reshape.64
  10.4 2.8 %copy.18 = bf16[48,1,4159]{0,1,2:T(2,128)(2,1)S(1)} copy(bf16[48,1,4159]{2,0,1:T(8,128)(2,1)S(1)} %reshape.64) | data formatting | bytes 798528 | tf_op jit(solution)/shard_map/reshape | solution.py:102
  13.2 11.7 %convolution_convert_fusion = bf16[48,1,1024]{0,1,2:T(2,128)(2,1)S(1)} fusion(bf16[48,1,4159]{0,1,2:T(2,128)(2,1)S(1)} %copy.18, bf16[1,1,64]{1,0,2:T(2,128)(2,1)S(1)} %copy.19), kind=kOutput, calls=%fused_computation.2 | convolution fusion | flops 6340608 | bytes 497696 | tf_op jit(solution)/shard_map/conv_general_dilated | solution.py:106
  24.9 0.3 copy.20
  25.2 15.2 %all-gather = bf16[48,1,4096]{2,0,1:T(8,128)(2,1)S(1)} all-gather(bf16[48,1,1024]{2,0,1:T(8,128)(2,1)S(1)} %copy.20), channel_id=2, replica_groups=mesh['groups'=2,'corr'=4,'filt'=2,'pair'=2] {'corr'}, dimensions={2}, use_global_device_ids=true | all-gather | bytes 491520 | tf_op jit(solution)/shard_map/all_gather | solution.py:116
  40.5 0.8 %pad_maximum_fusion.1 = bf16[2,48,2176]{2,1,0:T(8,128)(2,1)} fusion(bf16[1,48,2176]{2,1,0:T(8,128)(2,1)S(1)} %get-tuple-element.12, bf16[1,48,2176]{2,1,0:T(8,128)(2,1)S(1)} %get-tuple-element.11), kind=kLoop, calls=%fused_computation.16 | loop fusion | flops 208896 | bytes 835584 | tf_op jit(solution)/shard_map/stack | solution.py:123
  41.3 3.6 %all-to-all-start = ((bf16[2,48,2176]{2,1,0:T(8,128)(2,1)}), bf16[2,48,2176]{2,1,0:T(8,128)(2,1)S(1)}, u32[]{:S(2)}, u32[]{:S(2)}) async-start(bf16[2,48,2176]{2,1,0:T(8,128)(2,1)} %pad_maximum_fusion.1), calls=%async_computation | async-start | bytes 835584 | tf_op jit(solution)/shard_map/all_to_all | solution.py:126
  45.1 0.5 fusion
  45.5 1.0 %copy.24 = bf16[32,75,96]{2,1,0:T(8,128)(2,1)S(1)} copy(bf16[32,75,96]{1,0,2:T(8,128)(2,1)S(1)} %fusion) | data formatting | bytes 921600
  46.7 0.6 reshape_transpose_reshape.3.w_ref
  47.3 3.4 %all-to-all-done = bf16[2,48,2176]{2,1,0:T(8,128)(2,1)S(1)} async-done(((bf16[2,48,2176]{2,1,0:T(8,128)(2,1)}), bf16[2,48,2176]{2,1,0:T(8,128)(2,1)S(1)}, u32[]{:S(2)}, u32[]{:S(2)}) %all-to-all-start) | async-done | bytes 417824 | tf_op jit(solution)/shard_map/all_to_all | solution.py:126
  50.8 0.3 slice_add_fusion.4
  51.1 0.3 slice_add_fusion.3
  51.4 0.3 slice_add_fusion.2
  51.7 0.3 slice_add_fusion.1
  52.0 0.3 slice_add_fusion
  52.6 0.7 fusion.2.inv_ref
  53.4 18.4 %shard_map.55 = f32[32,2048]{1,0:T(8,128)} custom-call(bf16[4,96,640]{2,1,0:T(8,128)(2,1)S(1)} %pad_maximum_fusion.f_ref, f32[96,2048]{1,0:T(8,128)S(1)} %fusion.2.inv_ref, bf16[32,7296]{1,0:T(8,128)(2,1)S(1)} %reshape_transpose_reshape.3.w_ref), custom_call_target="tpu_custom_call" | custom-call | tf_op jit(solution)/shard_map/pallas_call | solution.py:71
  (18 shorter events, 1.5 us)
Async XLA Ops:
  1.9 7.7 %collective-permute-start = (bf16[16,3,63]{2,0,1:T(8,128)(2,1)S(1)}, bf16[16,3,63]{2,0,1:T(8,128)(2,1)S(1)}, u32[]{:S(2)}, u32[]{:S(2)}) collective-permute-start(bf16[16,3,63]{2,0,1:T(8,128)(2,1)S(1)} %slice.92), channel_id=1, source_target_pairs={{0,4},{4,8},{8,12},{1,5},{5,9},{9,13},{2,6},{6,10},{10,14},{3,7},{... | collective-permute-start | bytes 18152 | tf_op jit(solution)/shard_map/ppermute | solution.py:21
  41.3 9.5 %all-to-all-start = ((bf16[2,48,2176]{2,1,0:T(8,128)(2,1)}), bf16[2,48,2176]{2,1,0:T(8,128)(2,1)S(1)}, u32[]{:S(2)}, u32[]{:S(2)}) async-start(bf16[2,48,2176]{2,1,0:T(8,128)(2,1)} %pad_maximum_fusion.1), calls=%async_computation | async-start | bytes 835584 | tf_op jit(solution)/shard_map/all_to_all | solution.py:126

commit v2 on v1

--- a/solution.py
+++ b/solution.py
@@ -98,22 +98,25 @@
     live = jnp.where(
         sample_times[None, None, :] < counts[:, None, None], samples, jnp.zeros_like(samples)
     )
-    history = from_behind(live[:, :, raw_width - (TAPS - 1) :], "corr", 1)
-    extended = jnp.concatenate([history, live], axis=2).reshape(
-        local_stations * 3, 1, raw_width + TAPS - 1
+    history = from_behind(live[:, :, raw_width - 128 :], "corr", 1)
+    extended = jnp.concatenate([history, live], axis=2).reshape(local_stations * 3, raw_width + 128)
+    decimated = raw_width // DEC
+    blocks = decimated // 128
+    frames = jnp.stack(
+        [extended[:, 512 * a : 512 * a + 640] for a in range(blocks)], axis=1
+    ).reshape(local_stations * 3 * blocks, 640)
+    ring = jnp.concatenate(
+        [jnp.zeros((65,), taps.dtype), taps[::-1], jnp.zeros((644 - 129,), taps.dtype)]
     )
-    kernel = taps[::-1].reshape(1, 1, TAPS)
-    filtered = lax.conv_general_dilated(
-        extended,
-        kernel,
-        (DEC,),
-        "VALID",
-        dimension_numbers=("NCH", "OIH", "NCH"),
-        preferred_element_type=jnp.float32,
+    bank = jnp.tile(ring, 128)[: 128 * 640].reshape(128, 640)
+    filtered = lax.dot_general(
+        frames, bank, (((1,), (1,)), ((), ())), preferred_element_type=jnp.float32
     )
-    decimated = raw_width // DEC
     filtered = filtered.astype(jnp.bfloat16).reshape(local_stations * 3, decimated)
-    whole = lax.all_gather(filtered, "corr", axis=1, tiled=True)
+    corr_count = lax.axis_size("corr")
+    copies = jnp.broadcast_to(filtered[None], (corr_count,) + filtered.shape)
+    whole = lax.all_to_all(copies, "corr", 0, 0, tiled=True)
+    whole = jnp.transpose(whole, (1, 0, 2)).reshape(filtered.shape[0], -1)
     total_width = whole.shape[1]
     block = total_width // filt_count
     span = block + 128

time: 72.1 us -> 57.9 us (0.80)
  blocking collectives: 15.2 us -> 0 us
  matrix products: 11.7 us -> 0.3 us
  waiting for transfers between devices: 3.44 us -> 14.4 us
  starting transfers between devices: 8.6 us -> 14 us
  local copies, waits for them, and re-layouts: 7.65 us -> 4.44 us
  other arithmetic: 6.6 us -> 5.72 us
    all_gather x1 -> x0, blocking collectives: 15.2 us -> none  [body(): whole = lax.all_gather(filtered, 'corr', axis=1, tiled=True)]
    conv_general_dilated x1 -> x0, matrix products: 11.7 us -> none  [body(): lax.conv_general_dilated(extended, kernel, (DEC,), 'VALID', dimension_num...]
    all_to_all x0 -> x1, waiting for transfers between devices: none -> 10.1 us  [body(): whole = lax.all_to_all(copies, 'corr', 0, 0, tiled=True)]
    all_to_all x0 -> x1, starting transfers between devices: none -> 5.58 us  [body(): whole = lax.all_to_all(copies, 'corr', 0, 0, tiled=True)]
    reshape x2 -> x1, local copies, waits for them, and re-layouts: 3.19 us -> 0.34 us  [body(): jnp.concatenate([history, live], axis=2)]
    broadcast_in_dim x0 -> x4, local copies, waits for them, and re-layouts: none -> 0.84 us  [the longest x2 0.83 us: body(): copies = jnp.broadcast_to(filtered[None], (corr_count,) + filtered.shape)]
    transpose x1, other arithmetic: 0.88 us -> 0.08 us  [body(): jnp.transpose(mine, (0, 2, 1))[:, None, :, :]]
  transfers between devices with their start and end apart: 2 -> 3, of which waited for: 1 -> 3; matrix products, arithmetic and copies ran while one was open for 7% -> 6% of each run, Pallas kernels for 0% -> 0%
where the time goes in v2:
time: 57.9 us; the launch traced here: 57.6 us
  Pallas kernels  18.4 us (32%)
  waiting for transfers between devices  14.4 us (25%)
  starting transfers between devices  14 us (24%)
  other arithmetic  5.72 us (10%)
  local copies, waits for them, and re-layouts  4.44 us (8%)
    pallas_call x1, Pallas kernels, correlate(): pl.pallas_call(functools.partial(corr_kernel, row_block=row_block), grid=...  18.4 us
    all_to_all x1, waiting for transfers between devices, body(): whole = lax.all_to_all(copies, 'corr', 0, 0, tiled=True)  10.1 us
    all_to_all x1, starting transfers between devices, body(): whole = lax.all_to_all(copies, 'corr', 0, 0, tiled=True)  5.58 us
    ppermute x1, starting transfers between devices, from_behind(): return lax.ppermute(block, axis, route)  4.96 us
    all_to_all x1, waiting for transfers between devices, body(): gathered = lax.all_to_all(pieces, 'filt', 0, 0, tiled=True)  3.62 us
    all_to_all x1, starting transfers between devices, body(): gathered = lax.all_to_all(pieces, 'filt', 0, 0, tiled=True)  3.47 us
  transfers between devices with their start and end apart: 3, of which 3 were waited for; matrix products, arithmetic and copies ran while one was open for 6% of the time, Pallas kernels for 0%

profile of v2, /device:TPU:0, one launch (start us, length us, event | category | flops | bytes accessed | tf_op | source)
XLA Modules:
  0.0 57.6 jit_solution(7918848707066156876)
XLA Ops:
  0.0 0.8 %broadcast_compare_fusion = pred[16,4096]{1,0:T(8,128)(4,1)S(1)} fusion(s32[4096]{0:T(1024)S(1)} %iota_add_fusion, s32[16]{0:T(128)} %bitcast.70), kind=kLoop, calls=%fused_computation.24 | loop fusion | flops 65536 | bytes 81984 | tf_op jit(solution)/shard_map/lt | solution.py:99
  0.8 1.0 %bitcast_select_fusion = bf16[16,3,4096]{2,0,1:T(8,128)(2,1)S(1)} fusion(bf16[1,16,3,4096]{3,1,2,0:T(8,128)(2,1)} %param.5, pred[16,4096]{1,0:T(8,128)(4,1)S(1)} %broadcast_compare_fusion), kind=kLoop, calls=%fused_computation.21 | loop fusion | flops 196608 | bytes 851968 | tf_op jit(solution)/shard_map/jit(_where)/select_n | solution.py:98
  1.8 5.0 %collective-permute-start = (bf16[16,3,128]{2,0,1:T(8,128)(2,1)S(1)}, bf16[16,3,128]{2,0,1:T(8,128)(2,1)S(1)}, u32[]{:S(2)}, u32[]{:S(2)}) collective-permute-start(bf16[16,3,128]{2,0,1:T(8,128)(2,1)S(1)} %slice.128), channel_id=1, source_target_pairs={{0,4},{4,8},{8,12},{1,5},{5,9},{9,13},{2,6},{6,10},{10,14},{3,7},{... | collective-permute-start | bytes 36872 | tf_op jit(solution)/shard_map/ppermute | solution.py:21
  7.0 0.4 tile.10
  7.5 0.6 %collective-permute-done = bf16[16,3,128]{2,0,1:T(8,128)(2,1)S(1)} collective-permute-done((bf16[16,3,128]{2,0,1:T(8,128)(2,1)S(1)}, bf16[16,3,128]{2,0,1:T(8,128)(2,1)S(1)}, u32[]{:S(2)}, u32[]{:S(2)}) %collective-permute-start) | collective-permute-done | bytes 12320 | tf_op jit(solution)/shard_map/ppermute | solution.py:21
  8.4 0.3 reshape.69
  8.9 0.3 convolution_convert_fusion
  9.3 0.8 %broadcast_in_dim.38 = bf16[4,48,1024]{2,1,0:T(8,128)(2,1)} broadcast(bf16[48,1024]{1,0:T(8,128)(2,1)S(1)} %broadcast_in_dim.37), dimensions={1,2} | broadcast | bytes 491520 | tf_op jit(solution)/shard_map/broadcast_in_dim | solution.py:117
  10.1 5.6 %all-to-all-start = ((bf16[4,48,1024]{2,1,0:T(8,128)(2,1)}), bf16[4,48,1024]{2,1,0:T(8,128)(2,1)S(1)}, u32[]{:S(2)}, u32[]{:S(2)}) async-start(bf16[4,48,1024]{2,1,0:T(8,128)(2,1)} %broadcast_in_dim.38), calls=%async_computation | async-start | bytes 786432 | tf_op jit(solution)/shard_map/all_to_all | solution.py:118
  16.1 10.1 %all-to-all-done = bf16[4,48,1024]{2,1,0:T(8,128)(2,1)S(1)} async-done(((bf16[4,48,1024]{2,1,0:T(8,128)(2,1)}), bf16[4,48,1024]{2,1,0:T(8,128)(2,1)S(1)}, u32[]{:S(2)}, u32[]{:S(2)}) %all-to-all-start) | async-done | bytes 393248 | tf_op jit(solution)/shard_map/all_to_all | solution.py:118
  26.3 0.8 %pad_maximum_fusion.1 = bf16[2,48,2176]{2,1,0:T(8,128)(2,1)} fusion(bf16[1,48,2176]{2,1,0:T(8,128)(2,1)S(1)} %get-tuple-element.12, bf16[1,48,2176]{2,1,0:T(8,128)(2,1)S(1)} %get-tuple-element.11), kind=kLoop, calls=%fused_computation.18 | loop fusion | flops 208896 | bytes 835584 | tf_op jit(solution)/shard_map/stack | solution.py:126
  27.1 3.5 %all-to-all-start.1 = ((bf16[2,48,2176]{2,1,0:T(8,128)(2,1)}), bf16[2,48,2176]{2,1,0:T(8,128)(2,1)S(1)}, u32[]{:S(2)}, u32[]{:S(2)}) async-start(bf16[2,48,2176]{2,1,0:T(8,128)(2,1)} %pad_maximum_fusion.1), calls=%async_computation.1 | async-start | bytes 835584 | tf_op jit(solution)/shard_map/all_to_all | solution.py:129
  30.7 0.5 fusion
  31.2 1.0 %copy.23 = bf16[32,75,96]{2,1,0:T(8,128)(2,1)S(1)} copy(bf16[32,75,96]{1,0,2:T(8,128)(2,1)S(1)} %fusion) | data formatting | bytes 921600
  32.3 0.6 %reshape_transpose_reshape.3.w_ref = bf16[32,7296]{1,0:T(8,128)(2,1)S(1)} reshape(bf16[32,76,96]{2,1,0:T(8,128)(2,1)S(1)} %concatenate.15.clone) | data formatting | bytes 933888 | tf_op jit(solution)/shard_map/reshape;transpose;reshape | solution.py:151
  32.9 3.6 %all-to-all-done.1 = bf16[2,48,2176]{2,1,0:T(8,128)(2,1)S(1)} async-done(((bf16[2,48,2176]{2,1,0:T(8,128)(2,1)}), bf16[2,48,2176]{2,1,0:T(8,128)(2,1)S(1)}, u32[]{:S(2)}, u32[]{:S(2)}) %all-to-all-start.1) | async-done | bytes 417824 | tf_op jit(solution)/shard_map/all_to_all | solution.py:129
  36.6 0.3 slice_add_fusion.4
  36.9 0.3 slice_add_fusion.3
  37.2 0.3 slice_add_fusion.2
  37.5 0.3 slice_add_fusion.1
  37.8 0.3 slice_add_fusion
  38.1 0.3 fusion.14
  38.4 0.7 %fusion.2.inv_ref = f32[96,2048]{1,0:T(8,128)S(1)} fusion(f32[96,2176]{1,0:T(8,128)S(1)} %convert_multiply_fusion, f32[96,2175]{1,0:T(8,128)S(1)} %slice_add_fusion.4, f32[96,2169]{1,0:T(8,128)S(1)} %slice_add_fusion.2, f32[96,2113]{1,0:T(8,128)S(1)} %get-tuple-element.6, f32[96,2113]{1,0:T(8,128)S(1)} %get-tuple-element.5), kind=kLoop, calls=%fused_computation.11 | loop fusion | flops 983040 | bytes 4718592 | tf_op jit(solution)/shard_map/rsqrt | solution.py:132
  39.2 18.4 %shard_map.55 = f32[32,2048]{1,0:T(8,128)} custom-call(bf16[4,96,640]{2,1,0:T(8,128)(2,1)S(1)} %pad_maximum_fusion.f_ref, f32[96,2048]{1,0:T(8,128)S(1)} %fusion.2.inv_ref, bf16[32,7296]{1,0:T(8,128)(2,1)S(1)} %reshape_transpose_reshape.3.w_ref), custom_call_target="tpu_custom_call" | custom-call | tf_op jit(solution)/shard_map/pallas_call | solution.py:71
  (40 shorter events, 1.6 us)
Async XLA Ops:
  0.0 6.8 %copy-start.2 = (bf16[64]{0:T(256)(128)(2,1)S(1)}, bf16[64]{0:T(256)(128)(2,1)}, u32[]{:S(2)}) copy-start(bf16[64]{0:T(256)(128)(2,1)} %param.7) | copy-start | bytes 388
  1.8 6.4 %collective-permute-start = (bf16[16,3,128]{2,0,1:T(8,128)(2,1)S(1)}, bf16[16,3,128]{2,0,1:T(8,128)(2,1)S(1)}, u32[]{:S(2)}, u32[]{:S(2)}) collective-permute-start(bf16[16,3,128]{2,0,1:T(8,128)(2,1)S(1)} %slice.128), channel_id=1, source_target_pairs={{0,4},{4,8},{8,12},{1,5},{5,9},{9,13},{2,6},{6,10},{10,14},{3,7},{... | collective-permute-start | bytes 36872 | tf_op jit(solution)/shard_map/ppermute | solution.py:21
  9.2 6.4 %copy-start = (s32[128,3,32]{0,2,1:T(8,128)S(1)}, s32[128,3,32]{0,2,1:T(8,128)}, u32[]{:S(2)}) copy-start(s32[128,3,32]{0,2,1:T(8,128)} %param.9) | copy-start | bytes 147460
  9.3 6.5 %copy-start.1 = (bf16[32,225]{1,0:T(8,128)(2,1)S(1)}, bf16[32,225]{1,0:T(8,128)(2,1)}, u32[]{:S(2)}) copy-start(bf16[32,225]{1,0:T(8,128)(2,1)} %param.8) | copy-start | bytes 43204
  10.1 16.1 %all-to-all-start = ((bf16[4,48,1024]{2,1,0:T(8,128)(2,1)}), bf16[4,48,1024]{2,1,0:T(8,128)(2,1)S(1)}, u32[]{:S(2)}, u32[]{:S(2)}) async-start(bf16[4,48,1024]{2,1,0:T(8,128)(2,1)} %broadcast_in_dim.38), calls=%async_computation | async-start | bytes 786432 | tf_op jit(solution)/shard_map/all_to_all | solution.py:118
  27.1 9.5 %all-to-all-start.1 = ((bf16[2,48,2176]{2,1,0:T(8,128)(2,1)}), bf16[2,48,2176]{2,1,0:T(8,128)(2,1)S(1)}, u32[]{:S(2)}, u32[]{:S(2)}) async-start(bf16[2,48,2176]{2,1,0:T(8,128)(2,1)} %pad_maximum_fusion.1), calls=%async_computation.1 | async-start | bytes 835584 | tf_op jit(solution)/shard_map/all_to_all | solution.py:129

commit v3 on v2

--- a/solution.py
+++ b/solution.py
@@ -114,20 +114,20 @@
     )
     filtered = filtered.astype(jnp.bfloat16).reshape(local_stations * 3, decimated)
     corr_count = lax.axis_size("corr")
-    copies = jnp.broadcast_to(filtered[None], (corr_count,) + filtered.shape)
-    whole = lax.all_to_all(copies, "corr", 0, 0, tiled=True)
-    whole = jnp.transpose(whole, (1, 0, 2)).reshape(filtered.shape[0], -1)
-    total_width = whole.shape[1]
-    block = total_width // filt_count
+    group = corr_count * filt_count
+    copies = jnp.broadcast_to(filtered[None], (group,) + filtered.shape)
+    everything = lax.all_to_all(copies, ("corr", "filt"), 0, 0, tiled=True)
+    everything = everything.reshape(corr_count, filt_count, filtered.shape[0], decimated)
+    everything = jnp.concatenate(
+        [everything, jnp.zeros((1,) + everything.shape[1:], everything.dtype)], axis=0
+    )
+    per_block = corr_count // filt_count
+    block = per_block * decimated
     span = block + 128
-    padded = jnp.concatenate(
-        [whole, jnp.zeros((whole.shape[0], 128), whole.dtype)], axis=1
-    )
-    pieces = jnp.stack(
-        [padded[:, g * block : g * block + span] for g in range(filt_count)], axis=0
-    )
-    gathered = lax.all_to_all(pieces, "filt", 0, 0, tiled=True)
-    rows = gathered.reshape(filt_count * local_stations * 3, span)
+    mine = lax.dynamic_slice_in_dim(everything, filt_place * per_block, per_block + 1, 0)
+    rows = jnp.transpose(mine, (1, 2, 0, 3)).reshape(
+        filt_count * filtered.shape[0], (per_block + 1) * decimated
+    )[:, :span]
     energy = window_energy(rows.astype(jnp.float32), block)
     inv = lax.rsqrt(jnp.maximum(energy, 1.0))
     tiles = block // TT
@@ -138,8 +138,8 @@
     shaped = templates.astype(jnp.float32).reshape(count, 3, L)
     norms = jnp.sqrt(jnp.sum(shaped * shaped, axis=2) + 1e-06)
     base = shaped / norms[:, :, None]
-    mine = lax.dynamic_slice_in_dim(masks, corr_place * count, count, 0).astype(jnp.float32)
-    full = jnp.transpose(base, (0, 2, 1))[:, :, None, :] * jnp.transpose(mine, (0, 2, 1))[:, None, :, :]
+    chosen = lax.dynamic_slice_in_dim(masks, corr_place * count, count, 0).astype(jnp.float32)
+    full = jnp.transpose(base, (0, 2, 1))[:, :, None, :] * jnp.transpose(chosen, (0, 2, 1))[:, None, :, :]
     full = full.astype(jnp.bfloat16).reshape(count, L, stations * 3)
     full = jnp.concatenate([full, jnp.zeros((count, JP - L, stations * 3), full.dtype)], axis=1)
     total_rows = stations * 3

time: 57.9 us -> 58.2 us (level)
  waiting for transfers between devices: 14.4 us -> 16.9 us
  starting transfers between devices: 14 us -> 11.6 us
  local copies, waits for them, and re-layouts: 4.44 us -> 5.45 us
  other arithmetic: 5.72 us -> 4.91 us
    all_to_all x2 -> x1, waiting for transfers between devices: 13.8 us -> 16.3 us  [body(): everything = lax.all_to_all(copies, ('corr', 'filt'), 0, 0, tiled=True)]
    all_to_all x2 -> x1, starting transfers between devices: 9.05 us -> 6.65 us  [body(): everything = lax.all_to_all(copies, ('corr', 'filt'), 0, 0, tiled=True)]
    another operation x1 -> x0, other arithmetic: 0.79 us -> none  [body(): jnp.stack([padded[:, g * block:g * block + span] for g in range(filt_coun...]
    transpose x1 -> x3, local copies, waits for them, and re-layouts: 0.04 us -> 0.63 us  [the longest x2 0.59 us: body(): jnp.transpose(mine, (1, 2, 0, 3))]
    unnamed x14 -> x15, local copies, waits for them, and re-layouts: 1.09 us -> 1.36 us
  transfers between devices with their start and end apart: 3 -> 2, of which waited for: 3 -> 2; matrix products, arithmetic and copies ran while one was open for 6% -> 6% of each run, Pallas kernels for 0% -> 0%
where the time goes in v3:
time: 58.2 us; the launch traced here: 57.9 us
  Pallas kernels  18.4 us (32%)
  waiting for transfers between devices  16.9 us (29%)
  starting transfers between devices  11.6 us (20%)
  local copies, waits for them, and re-layouts  5.45 us (9%)
  other arithmetic  4.91 us (8%)
    pallas_call x1, Pallas kernels, correlate(): pl.pallas_call(functools.partial(corr_kernel, row_block=row_block), grid=...  18.4 us
    all_to_all x1, waiting for transfers between devices, body(): everything = lax.all_to_all(copies, ('corr', 'filt'), 0, 0, tiled=True)  16.3 us
    all_to_all x1, starting transfers between devices, body(): everything = lax.all_to_all(copies, ('corr', 'filt'), 0, 0, tiled=True)  6.65 us
    ppermute x1, starting transfers between devices, from_behind(): return lax.ppermute(block, axis, route)  4.96 us
    unnamed x15, local copies, waits for them, and re-layouts  1.36 us
  transfers between devices with their start and end apart: 2, of which 2 were waited for; matrix products, arithmetic and copies ran while one was open for 6% of the time, Pallas kernels for 0%

profile of v3, /device:TPU:0, one launch (start us, length us, event | category | flops | bytes accessed | tf_op | source)
XLA Modules:
  0.0 57.9 jit_solution(9892673573448728066)
XLA Ops:
  0.0 0.8 %broadcast_compare_fusion = pred[16,4096]{1,0:T(8,128)(4,1)S(1)} fusion(s32[4096]{0:T(1024)S(1)} %iota_add_fusion, s32[16]{0:T(128)} %bitcast.68), kind=kLoop, calls=%fused_computation.22 | loop fusion | flops 65536 | bytes 81984 | tf_op jit(solution)/shard_map/lt | solution.py:99
  0.8 1.0 %bitcast_select_fusion = bf16[16,3,4096]{2,0,1:T(8,128)(2,1)S(1)} fusion(bf16[1,16,3,4096]{3,1,2,0:T(8,128)(2,1)} %param.5, pred[16,4096]{1,0:T(8,128)(4,1)S(1)} %broadcast_compare_fusion), kind=kLoop, calls=%fused_computation.21 | loop fusion | flops 196608 | bytes 851968 | tf_op jit(solution)/shard_map/jit(_where)/select_n | solution.py:98
  1.8 5.0 %collective-permute-start = (bf16[16,3,128]{2,0,1:T(8,128)(2,1)S(1)}, bf16[16,3,128]{2,0,1:T(8,128)(2,1)S(1)}, u32[]{:S(2)}, u32[]{:S(2)}) collective-permute-start(bf16[16,3,128]{2,0,1:T(8,128)(2,1)S(1)} %slice.128), channel_id=1, source_target_pairs={{0,4},{4,8},{8,12},{1,5},{5,9},{9,13},{2,6},{6,10},{10,14},{3,7},{... | collective-permute-start | bytes 36872 | tf_op jit(solution)/shard_map/ppermute | solution.py:21
  7.0 0.4 tile.10
  7.5 0.6 %collective-permute-done = bf16[16,3,128]{2,0,1:T(8,128)(2,1)S(1)} collective-permute-done((bf16[16,3,128]{2,0,1:T(8,128)(2,1)S(1)}, bf16[16,3,128]{2,0,1:T(8,128)(2,1)S(1)}, u32[]{:S(2)}, u32[]{:S(2)}) %collective-permute-start) | collective-permute-done | bytes 12320 | tf_op jit(solution)/shard_map/ppermute | solution.py:21
  8.2 0.2 copy.7
  8.4 0.3 reshape.69
  8.9 0.3 convolution_convert_fusion
  9.3 1.0 %broadcast_in_dim.38 = bf16[8,48,1024]{2,1,0:T(8,128)(2,1)} broadcast(bf16[48,1024]{1,0:T(8,128)(2,1)S(1)} %broadcast_in_dim.37), dimensions={1,2} | broadcast | bytes 884736 | tf_op jit(solution)/shard_map/broadcast_in_dim | solution.py:118
  10.3 6.7 %all-to-all-start = ((bf16[8,48,1024]{2,1,0:T(8,128)(2,1)}), bf16[8,48,1024]{2,1,0:T(8,128)(2,1)S(1)}, u32[]{:S(2)}, u32[]{:S(2)}) async-start(bf16[8,48,1024]{2,1,0:T(8,128)(2,1)} %broadcast_in_dim.38), calls=%async_computation | async-start | bytes 1572864 | tf_op jit(solution)/shard_map/all_to_all | solution.py:119
  17.5 0.5 fusion
  17.9 1.0 %copy.13 = bf16[32,75,96]{2,1,0:T(8,128)(2,1)S(1)} copy(bf16[32,75,96]{1,0,2:T(8,128)(2,1)S(1)} %fusion) | data formatting | bytes 921600
  19.1 0.6 %reshape_transpose_reshape.3.w_ref = bf16[32,7296]{1,0:T(8,128)(2,1)S(1)} reshape(bf16[32,76,96]{2,1,0:T(8,128)(2,1)S(1)} %concatenate.15.clone) | data formatting | bytes 933888 | tf_op jit(solution)/shard_map/reshape;transpose;reshape | solution.py:151
  19.7 16.3 %all-to-all-done = bf16[8,48,1024]{2,1,0:T(8,128)(2,1)S(1)} async-done(((bf16[8,48,1024]{2,1,0:T(8,128)(2,1)}), bf16[8,48,1024]{2,1,0:T(8,128)(2,1)S(1)}, u32[]{:S(2)}, u32[]{:S(2)}) %all-to-all-start) | async-done | bytes 786464 | tf_op jit(solution)/shard_map/all_to_all | solution.py:119
  36.1 0.5 copy.9
  36.6 0.3 copy.14
  37.0 0.3 slice_add_fusion.4
  37.3 0.3 slice_add_fusion.3
  37.6 0.3 slice_add_fusion.2
  37.9 0.3 slice_add_fusion.1
  38.2 0.3 slice_add_fusion
  38.4 0.3 fusion.14
  38.7 0.7 %fusion.2.inv_ref = f32[96,2048]{1,0:T(8,128)S(1)} fusion(f32[96,2176]{1,0:T(8,128)S(1)} %convert_multiply_fusion, f32[96,2175]{1,0:T(8,128)S(1)} %slice_add_fusion.4, f32[96,2169]{1,0:T(8,128)S(1)} %slice_add_fusion.2, f32[96,2113]{1,0:T(8,128)S(1)} %get-tuple-element.6, f32[96,2113]{1,0:T(8,128)S(1)} %get-tuple-element.5), kind=kLoop, calls=%fused_computation.12 | loop fusion | flops 983040 | bytes 4718592 | tf_op jit(solution)/shard_map/rsqrt | solution.py:132
  39.5 18.4 %shard_map.55 = f32[32,2048]{1,0:T(8,128)} custom-call(bf16[4,96,640]{2,1,0:T(8,128)(2,1)S(1)} %pad_maximum_fusion.f_ref, f32[96,2048]{1,0:T(8,128)S(1)} %fusion.2.inv_ref, bf16[32,7296]{1,0:T(8,128)(2,1)S(1)} %reshape_transpose_reshape.3.w_ref), custom_call_target="tpu_custom_call" | custom-call | tf_op jit(solution)/shard_map/pallas_call | solution.py:71
  (38 shorter events, 1.4 us)
Async XLA Ops:
  0.0 6.8 %copy-start.2 = (bf16[64]{0:T(256)(128)(2,1)S(1)}, bf16[64]{0:T(256)(128)(2,1)}, u32[]{:S(2)}) copy-start(bf16[64]{0:T(256)(128)(2,1)} %param.7) | copy-start | bytes 388
  1.8 6.4 %collective-permute-start = (bf16[16,3,128]{2,0,1:T(8,128)(2,1)S(1)}, bf16[16,3,128]{2,0,1:T(8,128)(2,1)S(1)}, u32[]{:S(2)}, u32[]{:S(2)}) collective-permute-start(bf16[16,3,128]{2,0,1:T(8,128)(2,1)S(1)} %slice.128), channel_id=1, source_target_pairs={{0,4},{4,8},{8,12},{1,5},{5,9},{9,13},{2,6},{6,10},{10,14},{3,7},{... | collective-permute-start | bytes 36872 | tf_op jit(solution)/shard_map/ppermute | solution.py:21
  10.3 6.7 %copy-start = (s32[128,3,32]{0,2,1:T(8,128)S(1)}, s32[128,3,32]{0,2,1:T(8,128)}, u32[]{:S(2)}) copy-start(s32[128,3,32]{0,2,1:T(8,128)} %param.9) | copy-start | bytes 147460
  10.3 6.8 %copy-start.1 = (bf16[32,225]{1,0:T(8,128)(2,1)S(1)}, bf16[32,225]{1,0:T(8,128)(2,1)}, u32[]{:S(2)}) copy-start(bf16[32,225]{1,0:T(8,128)(2,1)} %param.8) | copy-start | bytes 43204
  10.3 25.7 %all-to-all-start = ((bf16[8,48,1024]{2,1,0:T(8,128)(2,1)}), bf16[8,48,1024]{2,1,0:T(8,128)(2,1)S(1)}, u32[]{:S(2)}, u32[]{:S(2)}) async-start(bf16[8,48,1024]{2,1,0:T(8,128)(2,1)} %broadcast_in_dim.38), calls=%async_computation | async-start | bytes 1572864 | tf_op jit(solution)/shard_map/all_to_all | solution.py:119

commit v4 on v3

--- a/solution.py
+++ b/solution.py
@@ -99,9 +99,13 @@
         sample_times[None, None, :] < counts[:, None, None], samples, jnp.zeros_like(samples)
     )
     history = from_behind(live[:, :, raw_width - 128 :], "corr", 1)
-    extended = jnp.concatenate([history, live], axis=2).reshape(local_stations * 3, raw_width + 128)
+    corr_count = lax.axis_size("corr")
+    ahead = from_behind(live[:, :, :512], "corr", -1)
+    extended = jnp.concatenate([history, live, ahead], axis=2).reshape(
+        local_stations * 3, raw_width + 640
+    )
     decimated = raw_width // DEC
-    blocks = decimated // 128
+    blocks = decimated // 128 + 1
     frames = jnp.stack(
         [extended[:, 512 * a : 512 * a + 640] for a in range(blocks)], axis=1
     ).reshape(local_stations * 3 * blocks, 640)
@@ -112,22 +116,32 @@
     filtered = lax.dot_general(
         frames, bank, (((1,), (1,)), ((), ())), preferred_element_type=jnp.float32
     )
-    filtered = filtered.astype(jnp.bfloat16).reshape(local_stations * 3, decimated)
-    corr_count = lax.axis_size("corr")
-    group = corr_count * filt_count
-    copies = jnp.broadcast_to(filtered[None], (group,) + filtered.shape)
-    everything = lax.all_to_all(copies, ("corr", "filt"), 0, 0, tiled=True)
-    everything = everything.reshape(corr_count, filt_count, filtered.shape[0], decimated)
-    everything = jnp.concatenate(
-        [everything, jnp.zeros((1,) + everything.shape[1:], everything.dtype)], axis=0
-    )
+    filtered = filtered.astype(jnp.bfloat16).reshape(local_stations * 3, decimated + 128)
+    past_end = (corr_place == corr_count - 1) & (lax.iota(jnp.int32, decimated + 128) >= decimated)
+    filtered = jnp.where(past_end[None, :], jnp.zeros_like(filtered), filtered)
     per_block = corr_count // filt_count
     block = per_block * decimated
     span = block + 128
-    mine = lax.dynamic_slice_in_dim(everything, filt_place * per_block, per_block + 1, 0)
-    rows = jnp.transpose(mine, (1, 2, 0, 3)).reshape(
-        filt_count * filtered.shape[0], (per_block + 1) * decimated
-    )[:, :span]
+    sender = (corr_place % per_block) * filt_count + filt_place
+    target_filt = corr_place // per_block
+    received = []
+    for k in range(corr_count):
+        route = []
+        for c in range(corr_count):
+            for f in range(filt_count):
+                s_id = (c % per_block) * filt_count + f
+                dest = ((s_id + k) % corr_count) * filt_count + c // per_block
+                route.append((c * filt_count + f, dest))
+        received.append(lax.ppermute(filtered, ("corr", "filt"), route))
+    received = jnp.stack(received, axis=0)
+    order = (corr_place - lax.iota(jnp.int32, corr_count)) % corr_count
+    ordered = jnp.take(received, order, axis=0)
+    ordered = ordered.reshape(per_block, filt_count, filtered.shape[0], decimated + 128)
+    heads = jnp.transpose(ordered[:, :, :, :decimated], (1, 2, 0, 3)).reshape(
+        filt_count, filtered.shape[0], block
+    )
+    tail = ordered[per_block - 1, :, :, decimated:]
+    rows = jnp.concatenate([heads, tail], axis=2).reshape(filt_count * filtered.shape[0], span)
     energy = window_energy(rows.astype(jnp.float32), block)
     inv = lax.rsqrt(jnp.maximum(energy, 1.0))
     tiles = block // TT

time: 58.2 us -> 53.9 us (0.926)
  waiting for transfers between devices: 16.9 us -> 2.27 us
  starting transfers between devices: 11.6 us -> 21.7 us
    all_to_all x1 -> x0, waiting for transfers between devices: 16.3 us -> none  [body(): everything = lax.all_to_all(copies, ('corr', 'filt'), 0, 0, tiled=True)]
    ppermute x0 -> x4, starting transfers between devices: none -> 14.8 us  [body(): received.append(lax.ppermute(filtered, ('corr', 'filt'), route))]
    all_to_all x1 -> x0, starting transfers between devices: 6.65 us -> none  [body(): everything = lax.all_to_all(copies, ('corr', 'filt'), 0, 0, tiled=True)]
    ppermute x0 -> x4, waiting for transfers between devices: none -> 2.26 us  [body(): received.append(lax.ppermute(filtered, ('corr', 'filt'), route))]
    ppermute x1 -> x2, starting transfers between devices: 4.96 us -> 6.88 us  [from_behind(): return lax.ppermute(block, axis, route)]
    broadcast_in_dim x2 -> x0, local copies, waits for them, and re-layouts: 1.04 us -> none  [body(): copies = jnp.broadcast_to(filtered[None], (group,) + filtered.shape)]
    ppermute x1 -> x2, waiting for transfers between devices: 0.65 us -> 0.01 us  [from_behind(): return lax.ppermute(block, axis, route)]
    gather x0 -> x1, local copies, waits for them, and re-layouts: none -> 0.62 us  [body(): ordered = jnp.take(received, order, axis=0)]
  transfers between devices with their start and end apart: 2 -> 6, of which waited for: 2 -> 1; matrix products, arithmetic and copies ran while one was open for 6% -> 6% of each run, Pallas kernels for 0% -> 0%
where the time goes in v4:
time: 53.9 us; the launch traced here: 53.6 us
  starting transfers between devices  21.7 us (40%)
  Pallas kernels  18.4 us (34%)
  local copies, waits for them, and re-layouts  5.28 us (10%)
  other arithmetic  5.25 us (10%)
  waiting for transfers between devices  2.27 us (4%)
    pallas_call x1, Pallas kernels, correlate(): pl.pallas_call(functools.partial(corr_kernel, row_block=row_block), grid=...  18.4 us
    ppermute x4, starting transfers between devices, body(): received.append(lax.ppermute(filtered, ('corr', 'filt'), route))  14.8 us
    ppermute x2, starting transfers between devices, from_behind(): return lax.ppermute(block, axis, route)  6.88 us
    ppermute x4, waiting for transfers between devices, body(): received.append(lax.ppermute(filtered, ('corr', 'filt'), route))  2.26 us
    unnamed x16, local copies, waits for them, and re-layouts  1.17 us
  transfers between devices with their start and end apart: 6, of which 1 were waited for; matrix products, arithmetic and copies ran while one was open for 6% of the time, Pallas kernels for 0%

profile of v4, /device:TPU:0, one launch (start us, length us, event | category | flops | bytes accessed | tf_op | source)
XLA Modules:
  0.0 53.6 jit_solution(656853218801552245)
XLA Ops:
  0.0 0.8 %broadcast_compare_fusion = pred[16,4096]{1,0:T(8,128)(4,1)S(1)} fusion(s32[4096]{0:T(1024)S(1)} %iota_add_fusion, s32[16]{0:T(128)} %bitcast.83), kind=kLoop, calls=%fused_computation.25 | loop fusion | flops 65536 | bytes 81984 | tf_op jit(solution)/shard_map/lt | solution.py:99
  0.8 1.0 %bitcast_select_fusion = bf16[16,3,4096]{2,0,1:T(8,128)(2,1)S(1)} fusion(bf16[1,16,3,4096]{3,1,2,0:T(8,128)(2,1)} %param.5, pred[16,4096]{1,0:T(8,128)(4,1)S(1)} %broadcast_compare_fusion), kind=kLoop, calls=%fused_computation.23 | loop fusion | flops 196608 | bytes 851968 | tf_op jit(solution)/shard_map/jit(_where)/select_n | solution.py:98
  1.9 1.3 %collective-permute-start.1 = (bf16[16,3,512]{2,0,1:T(8,128)(2,1)S(1)}, bf16[16,3,512]{2,0,1:T(8,128)(2,1)S(1)}, u32[]{:S(2)}, u32[]{:S(2)}) collective-permute-start(bf16[16,3,512]{2,0,1:T(8,128)(2,1)S(1)} %slice.142), channel_id=1, source_target_pairs={{4,0},{8,4},{12,8},{5,1},{9,5},{13,9},{6,2},{10,6},{14,10},{7,3},{... | collective-permute-start | bytes 147464 | tf_op jit(solution)/shard_map/ppermute | solution.py:21
  3.2 5.6 %collective-permute-start = (bf16[16,3,128]{2,0,1:T(8,128)(2,1)S(1)}, bf16[16,3,128]{2,0,1:T(8,128)(2,1)S(1)}, u32[]{:S(2)}, u32[]{:S(2)}) collective-permute-start(bf16[16,3,128]{2,0,1:T(8,128)(2,1)S(1)} %slice.141), channel_id=1, source_target_pairs={{0,4},{4,8},{8,12},{1,5},{5,9},{9,13},{2,6},{6,10},{10,14},{3,7},{... | collective-permute-start | bytes 36872 | tf_op jit(solution)/shard_map/ppermute | solution.py:21
  9.5 0.4 tile.10
  10.1 0.5 fusion
  10.6 1.0 %copy.13 = bf16[32,75,96]{2,1,0:T(8,128)(2,1)S(1)} copy(bf16[32,75,96]{1,0,2:T(8,128)(2,1)S(1)} %fusion) | data formatting | bytes 921600
  11.7 0.6 %reshape_transpose_reshape.3.w_ref = bf16[32,7296]{1,0:T(8,128)(2,1)S(1)} reshape(bf16[32,76,96]{2,1,0:T(8,128)(2,1)S(1)} %concatenate.22.clone) | data formatting | bytes 933888 | tf_op jit(solution)/shard_map/reshape;transpose;reshape | solution.py:165
  12.7 0.4 reshape.134
  13.6 0.3 convolution_convert_fusion
  14.2 0.7 %collective-permute-start.2 = (bf16[48,1152]{1,0:T(8,128)(2,1)S(1)}, bf16[48,1152]{1,0:T(8,128)(2,1)S(1)}, u32[]{:S(2)}, u32[]{:S(2)}) collective-permute-start(bf16[48,1152]{1,0:T(8,128)(2,1)S(1)} %broadcast_select_fusion.1), channel_id=1, source_target_pairs={{0,0},{2,4},{4,8},{6,12},{8,2},{10,6},{12,10},{14,14},{1,1},{3,5},... | collective-permute-start | bytes 331784 | tf_op jit(solution)/shard_map/ppermute | solution.py:135
  14.8 6.7 %collective-permute-start.3 = (bf16[48,1152]{1,0:T(8,128)(2,1)S(1)}, bf16[48,1152]{1,0:T(8,128)(2,1)S(1)}, u32[]{:S(2)}, u32[]{:S(2)}) collective-permute-start(bf16[48,1152]{1,0:T(8,128)(2,1)S(1)} %broadcast_select_fusion.1), channel_id=1, source_target_pairs={{0,4},{2,8},{4,12},{6,0},{8,6},{10,10},{12,14},{14,2},{1,5},{3,9},... | collective-permute-start | bytes 331784 | tf_op jit(solution)/shard_map/ppermute | solution.py:135
  21.6 1.9 %collective-permute-start.4 = (bf16[48,1152]{1,0:T(8,128)(2,1)S(1)}, bf16[48,1152]{1,0:T(8,128)(2,1)S(1)}, u32[]{:S(2)}, u32[]{:S(2)}) collective-permute-start(bf16[48,1152]{1,0:T(8,128)(2,1)S(1)} %broadcast_select_fusion.1), channel_id=1, source_target_pairs={{0,8},{2,12},{4,0},{6,4},{8,10},{10,14},{12,2},{14,6},{1,9},{3,13}... | collective-permute-start | bytes 331784 | tf_op jit(solution)/shard_map/ppermute | solution.py:135
  23.5 5.4 %collective-permute-start.5 = (bf16[48,1152]{1,0:T(8,128)(2,1)S(1)}, bf16[48,1152]{1,0:T(8,128)(2,1)S(1)}, u32[]{:S(2)}, u32[]{:S(2)}) collective-permute-start(bf16[48,1152]{1,0:T(8,128)(2,1)S(1)} %broadcast_select_fusion.1), channel_id=1, source_target_pairs={{0,12},{2,0},{4,4},{6,8},{8,14},{10,2},{12,6},{14,10},{1,13},{3,1}... | collective-permute-start | bytes 331784 | tf_op jit(solution)/shard_map/ppermute | solution.py:135
  29.0 2.3 %collective-permute-done.5 = bf16[48,1152]{1,0:T(8,128)(2,1)S(1)} collective-permute-done((bf16[48,1152]{1,0:T(8,128)(2,1)S(1)}, bf16[48,1152]{1,0:T(8,128)(2,1)S(1)}, u32[]{:S(2)}, u32[]{:S(2)}) %collective-permute-start.5) | collective-permute-done | bytes 110624 | tf_op jit(solution)/shard_map/ppermute | solution.py:135
  31.3 0.6 %gather_fusion = bf16[4,48,1152]{2,1,0:T(8,128)(2,1)S(1)} fusion(bf16[4,48,1152]{2,1,0:T(8,128)(2,1)S(1)} %pad_maximum_fusion.3, s32[1024]{0:T(1024)S(1)} %pad_clamp_fusion), kind=kCustom, calls=%fused_computation | custom fusion | bytes 884752 | tf_op jit(solution)/shard_map/jit(_take)/gather | solution.py:138
  32.1 0.4 copy.9
  32.7 0.3 slice_add_fusion.4
  33.0 0.3 slice_add_fusion.3
  33.3 0.3 slice_add_fusion.2
  33.6 0.3 slice_add_fusion.1
  33.9 0.3 slice_add_fusion
  34.5 0.7 %fusion.2.inv_ref = f32[96,2048]{1,0:T(8,128)S(1)} fusion(f32[96,2176]{1,0:T(8,128)S(1)} %convert_multiply_fusion, f32[96,2175]{1,0:T(8,128)S(1)} %slice_add_fusion.4, f32[96,2169]{1,0:T(8,128)S(1)} %slice_add_fusion.2, f32[96,2113]{1,0:T(8,128)S(1)} %get-tuple-element.6, f32[96,2113]{1,0:T(8,128)S(1)} %get-tuple-element.5), kind=kLoop, calls=%fused_computation.12 | loop fusion | flops 983040 | bytes 4718592 | tf_op jit(solution)/shard_map/rsqrt | solution.py:146
  35.2 18.4 %shard_map.55 = f32[32,2048]{1,0:T(8,128)} custom-call(bf16[4,96,640]{2,1,0:T(8,128)(2,1)S(1)} %pad_maximum_fusion.1.f_ref, f32[96,2048]{1,0:T(8,128)S(1)} %fusion.2.inv_ref, bf16[32,7296]{1,0:T(8,128)(2,1)S(1)} %reshape_transpose_reshape.3.w_ref), custom_call_target="tpu_custom_call" | custom-call | tf_op jit(solution)/shard_map/pallas_call | solution.py:71
  (58 shorter events, 2.8 us)
Async XLA Ops:
  0.0 8.8 %copy-start.2 = (bf16[64]{0:T(256)(128)(2,1)S(1)}, bf16[64]{0:T(256)(128)(2,1)}, u32[]{:S(2)}) copy-start(bf16[64]{0:T(256)(128)(2,1)} %param.7) | copy-start | bytes 388
  0.0 8.9 %copy-start.1 = (bf16[32,225]{1,0:T(8,128)(2,1)S(1)}, bf16[32,225]{1,0:T(8,128)(2,1)}, u32[]{:S(2)}) copy-start(bf16[32,225]{1,0:T(8,128)(2,1)} %param.8) | copy-start | bytes 43204
  0.0 9.3 %copy-start = (s32[128,3,32]{0,2,1:T(8,128)S(1)}, s32[128,3,32]{0,2,1:T(8,128)}, u32[]{:S(2)}) copy-start(s32[128,3,32]{0,2,1:T(8,128)} %param.9) | copy-start | bytes 147460
  1.9 10.5 %collective-permute-start.1 = (bf16[16,3,512]{2,0,1:T(8,128)(2,1)S(1)}, bf16[16,3,512]{2,0,1:T(8,128)(2,1)S(1)}, u32[]{:S(2)}, u32[]{:S(2)}) collective-permute-start(bf16[16,3,512]{2,0,1:T(8,128)(2,1)S(1)} %slice.142), channel_id=1, source_target_pairs={{4,0},{8,4},{12,8},{5,1},{9,5},{13,9},{6,2},{10,6},{14,10},{7,3},{... | collective-permute-start | bytes 147464 | tf_op jit(solution)/shard_map/ppermute | solution.py:21
  3.2 9.2 %collective-permute-start = (bf16[16,3,128]{2,0,1:T(8,128)(2,1)S(1)}, bf16[16,3,128]{2,0,1:T(8,128)(2,1)S(1)}, u32[]{:S(2)}, u32[]{:S(2)}) collective-permute-start(bf16[16,3,128]{2,0,1:T(8,128)(2,1)S(1)} %slice.141), channel_id=1, source_target_pairs={{0,4},{4,8},{8,12},{1,5},{5,9},{9,13},{2,6},{6,10},{10,14},{3,7},{... | collective-permute-start | bytes 36872 | tf_op jit(solution)/shard_map/ppermute | solution.py:21
  14.2 14.8 %collective-permute-start.2 = (bf16[48,1152]{1,0:T(8,128)(2,1)S(1)}, bf16[48,1152]{1,0:T(8,128)(2,1)S(1)}, u32[]{:S(2)}, u32[]{:S(2)}) collective-permute-start(bf16[48,1152]{1,0:T(8,128)(2,1)S(1)} %broadcast_select_fusion.1), channel_id=1, source_target_pairs={{0,0},{2,4},{4,8},{6,12},{8,2},{10,6},{12,10},{14,14},{1,1},{3,5},... | collective-permute-start | bytes 331784 | tf_op jit(solution)/shard_map/ppermute | solution.py:135
  14.8 14.2 %collective-permute-start.3 = (bf16[48,1152]{1,0:T(8,128)(2,1)S(1)}, bf16[48,1152]{1,0:T(8,128)(2,1)S(1)}, u32[]{:S(2)}, u32[]{:S(2)}) collective-permute-start(bf16[48,1152]{1,0:T(8,128)(2,1)S(1)} %broadcast_select_fusion.1), channel_id=1, source_target_pairs={{0,4},{2,8},{4,12},{6,0},{8,6},{10,10},{12,14},{14,2},{1,5},{3,9},... | collective-permute-start | bytes 331784 | tf_op jit(solution)/shard_map/ppermute | solution.py:135
  21.6 7.4 %collective-permute-start.4 = (bf16[48,1152]{1,0:T(8,128)(2,1)S(1)}, bf16[48,1152]{1,0:T(8,128)(2,1)S(1)}, u32[]{:S(2)}, u32[]{:S(2)}) collective-permute-start(bf16[48,1152]{1,0:T(8,128)(2,1)S(1)} %broadcast_select_fusion.1), channel_id=1, source_target_pairs={{0,8},{2,12},{4,0},{6,4},{8,10},{10,14},{12,2},{14,6},{1,9},{3,13}... | collective-permute-start | bytes 331784 | tf_op jit(solution)/shard_map/ppermute | solution.py:135
  23.5 7.8 %collective-permute-start.5 = (bf16[48,1152]{1,0:T(8,128)(2,1)S(1)}, bf16[48,1152]{1,0:T(8,128)(2,1)S(1)}, u32[]{:S(2)}, u32[]{:S(2)}) collective-permute-start(bf16[48,1152]{1,0:T(8,128)(2,1)S(1)} %broadcast_select_fusion.1), channel_id=1, source_target_pairs={{0,12},{2,0},{4,4},{6,8},{8,14},{10,2},{12,6},{14,10},{1,13},{3,1}... | collective-permute-start | bytes 331784 | tf_op jit(solution)/shard_map/ppermute | solution.py:135

commit v5 on v4

--- a/solution.py
+++ b/solution.py
@@ -37,9 +37,9 @@
     )
 
 
-def corr_kernel(f_ref, inv_ref, w_ref, o_ref, s_ref, *, row_block):
+def corr_kernel(f_ref, inv_ref, w_ref, o_ref, s_ref, *, row_block, tile):
     q = pl.program_id(1)
-    span = TT + 128
+    span = tile + 128
 
     def fill(sub, carry):
         r0 = pl.multiple_of(sub * RSUB, RSUB)
@@ -47,7 +47,7 @@
         inv = inv_ref[pl.ds(r0, RSUB), :]
         for j in range(JP):
             moved = seg if j == 0 else pltpu.roll(seg, span - j, 1)
-            piece = (moved[:, :TT] * inv).astype(jnp.bfloat16)
+            piece = (moved[:, :tile] * inv).astype(jnp.bfloat16)
             s_ref[pl.ds(pl.multiple_of(j * row_block + r0, RSUB), RSUB), :] = piece
         return carry
 
@@ -67,18 +67,19 @@
     tiles, rows, span = windows.shape
     count = weights.shape[0]
     width = inv.shape[1]
+    tile = width // tiles
     chunks = rows // row_block
     return pl.pallas_call(
-        functools.partial(corr_kernel, row_block=row_block),
+        functools.partial(corr_kernel, row_block=row_block, tile=tile),
         grid=(tiles, chunks),
         in_specs=[
             pl.BlockSpec((1, row_block, span), lambda i, q: (i, q, 0)),
-            pl.BlockSpec((row_block, TT), lambda i, q: (q, i)),
+            pl.BlockSpec((row_block, tile), lambda i, q: (q, i)),
             pl.BlockSpec((count, JP * row_block), lambda i, q: (0, q)),
         ],
-        out_specs=pl.BlockSpec((count, TT), lambda i, q: (0, i)),
+        out_specs=pl.BlockSpec((count, tile), lambda i, q: (0, i)),
         out_shape=jax.ShapeDtypeStruct((count, width), jnp.float32),
-        scratch_shapes=[pltpu.VMEM((JP * row_block, TT), jnp.bfloat16)],
+        scratch_shapes=[pltpu.VMEM((JP * row_block, tile), jnp.bfloat16)],
         compiler_params=pltpu.CompilerParams(
             dimension_semantics=("parallel", "arbitrary"),
             vmem_limit_bytes=48 * 1024 * 1024,
@@ -121,38 +122,38 @@
     filtered = jnp.where(past_end[None, :], jnp.zeros_like(filtered), filtered)
     per_block = corr_count // filt_count
     block = per_block * decimated
-    span = block + 128
-    sender = (corr_place % per_block) * filt_count + filt_place
-    target_filt = corr_place // per_block
+    width = block // corr_count
+    span = width + 128
     received = []
-    for k in range(corr_count):
+    for k in range(filt_count):
+        piece = (filt_place + k) % filt_count
+        part = lax.dynamic_slice_in_dim(filtered, piece * width, span, 1)
         route = []
         for c in range(corr_count):
             for f in range(filt_count):
-                s_id = (c % per_block) * filt_count + f
-                dest = ((s_id + k) % corr_count) * filt_count + c // per_block
+                dest = ((c % per_block) * filt_count + (f + k) % filt_count) * filt_count + c // per_block
                 route.append((c * filt_count + f, dest))
-        received.append(lax.ppermute(filtered, ("corr", "filt"), route))
+        received.append(lax.ppermute(part, ("corr", "filt"), route))
     received = jnp.stack(received, axis=0)
-    order = (corr_place - lax.iota(jnp.int32, corr_count)) % corr_count
-    ordered = jnp.take(received, order, axis=0)
-    ordered = ordered.reshape(per_block, filt_count, filtered.shape[0], decimated + 128)
-    heads = jnp.transpose(ordered[:, :, :, :decimated], (1, 2, 0, 3)).reshape(
-        filt_count, filtered.shape[0], block
+    order = (corr_place - lax.iota(jnp.int32, filt_count)) % filt_count
+    rows = jnp.take(received, order, axis=0).reshape(filt_count * filtered.shape[0], span)
+    energy = window_energy(rows.astype(jnp.float32), width)
+    inv = lax.rsqrt(jnp.maximum(energy, 1.0))
+    tile = min(TT, width)
+    tiles = width // tile
+    windows = jnp.stack([rows[:, i * tile : i * tile + tile + 128] for i in range(tiles)], axis=0)
+
+    local_count = templates.shape[0]
+    copies = jnp.broadcast_to(templates[None], (corr_count,) + templates.shape)
+    templates = lax.all_to_all(copies, "corr", 0, 0, tiled=True).reshape(
+        corr_count * local_count, templates.shape[1]
     )
-    tail = ordered[per_block - 1, :, :, decimated:]
-    rows = jnp.concatenate([heads, tail], axis=2).reshape(filt_count * filtered.shape[0], span)
-    energy = window_energy(rows.astype(jnp.float32), block)
-    inv = lax.rsqrt(jnp.maximum(energy, 1.0))
-    tiles = block // TT
-    windows = jnp.stack([rows[:, i * TT : i * TT + TT + 128] for i in range(tiles)], axis=0)
-
     count = templates.shape[0]
     stations = masks.shape[2]
     shaped = templates.astype(jnp.float32).reshape(count, 3, L)
     norms = jnp.sqrt(jnp.sum(shaped * shaped, axis=2) + 1e-06)
     base = shaped / norms[:, :, None]
-    chosen = lax.dynamic_slice_in_dim(masks, corr_place * count, count, 0).astype(jnp.float32)
+    chosen = masks.astype(jnp.float32)
     full = jnp.transpose(base, (0, 2, 1))[:, :, None, :] * jnp.transpose(chosen, (0, 2, 1))[:, None, :, :]
     full = full.astype(jnp.bfloat16).reshape(count, L, stations * 3)
     full = jnp.concatenate([full, jnp.zeros((count, JP - L, stations * 3), full.dtype)], axis=1)
@@ -165,6 +166,7 @@
         .reshape(count, chunks * JP * row_block)
     )
     stacked = correlate(windows, inv, weights, row_block)
+    stacked = lax.all_to_all(stacked, "corr", 0, 1, tiled=True)
     return stacked[None]
 
 

time: 53.9 us -> 49.9 us (0.926)
  Pallas kernels: 18.4 us -> 3.98 us
  blocking collectives: 0 us -> 10.6 us
  local copies, waits for them, and re-layouts: 5.28 us -> 10.8 us
  starting transfers between devices: 21.7 us -> 16.5 us
  other arithmetic: 5.25 us -> 4.64 us
    pallas_call x1, Pallas kernels: 18.4 us -> 3.98 us  [correlate(): pl.pallas_call(functools.partial(corr_kernel, row_block=row_block, tile=t...]
    all_to_all x0 -> x1, blocking collectives: none -> 10.6 us  [body(): stacked = lax.all_to_all(stacked, 'corr', 0, 1, tiled=True)]
    ppermute x4 -> x2, starting transfers between devices: 14.8 us -> 4.89 us  [body(): received.append(lax.ppermute(part, ('corr', 'filt'), route))]
    all_to_all x0 -> x1, starting transfers between devices: none -> 6.35 us  [body(): lax.all_to_all(copies, 'corr', 0, 0, tiled=True)]
    broadcast_in_dim x0 -> x4, local copies, waits for them, and re-layouts: none -> 2.39 us  [the longest x1 1.35 us: body(): copies = jnp.broadcast_to(templates[None], (corr_count,) + templates.shape)]
    ppermute x4 -> x2, waiting for transfers between devices: 2.26 us -> 0.01 us  [body(): received.append(lax.ppermute(part, ('corr', 'filt'), route))]
    ppermute x2, waiting for transfers between devices: 0.01 us -> 2.17 us  [from_behind(): return lax.ppermute(block, axis, route)]
    another operation x1, local copies, waits for them, and re-layouts: 0.64 us -> 2.76 us  [body(): weights = full.reshape(count, JP, chunks, row_block).transpose(0, 2, 1, 3...]
  transfers between devices with their start and end apart: 6 -> 5, of which waited for: 1 -> 1; matrix products, arithmetic and copies ran while one was open for 6% -> 24% of each run, Pallas kernels for 0% -> 0%
where the time goes in v5:
time: 49.9 us; the launch traced here: 49.4 us
  starting transfers between devices  16.5 us (33%)
  local copies, waits for them, and re-layouts  10.8 us (22%)
  blocking collectives  10.6 us (21%)
  other arithmetic  4.64 us (9%)
  Pallas kernels  3.98 us (8%)
  waiting for transfers between devices  2.17 us (4%)
    all_to_all x1, blocking collectives, body(): stacked = lax.all_to_all(stacked, 'corr', 0, 1, tiled=True)  10.6 us
    all_to_all x1, starting transfers between devices, body(): lax.all_to_all(copies, 'corr', 0, 0, tiled=True)  6.35 us
    ppermute x2, starting transfers between devices, from_behind(): return lax.ppermute(block, axis, route)  5.22 us
    ppermute x2, starting transfers between devices, body(): received.append(lax.ppermute(part, ('corr', 'filt'), route))  4.89 us
    pallas_call x1, Pallas kernels, correlate(): pl.pallas_call(functools.partial(corr_kernel, row_block=row_block, tile=t...  3.98 us
    another operation x1, local copies, waits for them, and re-layouts, body(): weights = full.reshape(count, JP, chunks, row_block).transpose(0, 2, 1, 3...  2.76 us
    ppermute x2, waiting for transfers between devices, from_behind(): return lax.ppermute(block, axis, route)  2.17 us
    concatenate x1, local copies, waits for them, and re-layouts, body(): jnp.concatenate([full, jnp.zeros((count, JP - L, stations * 3), full.dtyp...  1.37 us
  transfers between devices with their start and end apart: 5, of which 1 were waited for; matrix products, arithmetic and copies ran while one was open for 24% of the time, Pallas kernels for 0%

profile of v5, /device:TPU:0, one launch (start us, length us, event | category | flops | bytes accessed | tf_op | source)
XLA Modules:
  0.0 49.4 jit_solution(6861877091295538970)
XLA Ops:
  0.0 1.4 %broadcast_in_dim.73 = bf16[4,32,225]{2,1,0:T(8,128)(2,1)} broadcast(bf16[32,225]{1,0:T(8,128)(2,1)} %param.8), dimensions={1,2} | broadcast | bytes 72000 | tf_op jit(solution)/shard_map/broadcast_in_dim | solution.py:147
  1.4 6.3 %all-to-all-start = ((bf16[4,32,225]{2,1,0:T(8,128)(2,1)}), bf16[4,32,225]{2,1,0:T(8,128)(2,1)S(1)}, u32[]{:S(2)}, u32[]{:S(2)}) async-start(bf16[4,32,225]{2,1,0:T(8,128)(2,1)} %broadcast_in_dim.73), calls=%async_computation | async-start | bytes 131072 | tf_op jit(solution)/shard_map/all_to_all | solution.py:148
  7.7 0.8 %broadcast_compare_fusion = pred[16,4096]{1,0:T(8,128)(4,1)S(1)} fusion(s32[4096]{0:T(1024)S(1)} %iota_add_fusion, s32[16]{0:T(128)} %bitcast.71), kind=kLoop, calls=%fused_computation.20 | loop fusion | flops 65536 | bytes 81984 | tf_op jit(solution)/shard_map/lt | solution.py:100
  8.5 1.0 %bitcast_select_fusion = bf16[16,3,4096]{2,0,1:T(8,128)(2,1)S(1)} fusion(bf16[1,16,3,4096]{3,1,2,0:T(8,128)(2,1)} %param.5, pred[16,4096]{1,0:T(8,128)(4,1)S(1)} %broadcast_compare_fusion), kind=kLoop, calls=%fused_computation.5 | loop fusion | flops 196608 | bytes 851968 | tf_op jit(solution)/shard_map/jit(_where)/select_n | solution.py:99
  9.5 3.9 %collective-permute-start = (bf16[16,3,128]{2,0,1:T(8,128)(2,1)S(1)}, bf16[16,3,128]{2,0,1:T(8,128)(2,1)S(1)}, u32[]{:S(2)}, u32[]{:S(2)}) collective-permute-start(bf16[16,3,128]{2,0,1:T(8,128)(2,1)S(1)} %slice.114), channel_id=1, source_target_pairs={{0,4},{4,8},{8,12},{1,5},{5,9},{9,13},{2,6},{6,10},{10,14},{3,7},{... | collective-permute-start | bytes 36872 | tf_op jit(solution)/shard_map/ppermute | solution.py:21
  13.5 1.3 %collective-permute-start.1 = (bf16[16,3,512]{2,0,1:T(8,128)(2,1)S(1)}, bf16[16,3,512]{2,0,1:T(8,128)(2,1)S(1)}, u32[]{:S(2)}, u32[]{:S(2)}) collective-permute-start(bf16[16,3,512]{2,0,1:T(8,128)(2,1)S(1)} %slice.115), channel_id=1, source_target_pairs={{4,0},{8,4},{12,8},{5,1},{9,5},{13,9},{6,2},{10,6},{14,10},{7,3},{... | collective-permute-start | bytes 147464 | tf_op jit(solution)/shard_map/ppermute | solution.py:21
  14.8 0.7 %rev.3 = bf16[64]{0:T(256)(128)(2,1)S(1)} reverse(bf16[64]{0:T(256)(128)(2,1)} %param.7), dimensions={0} | reverse | bytes 256 | tf_op jit(solution)/shard_map/rev | solution.py:114
  15.6 0.8 %convert_bitcast_fusion = f32[128,32,3]{0,1,2:T(8,128)S(1)} fusion(s32[128,3,32]{0,2,1:T(8,128)} %param.9), kind=kLoop, calls=%fused_computation.44 | loop fusion | flops 12288 | bytes 98304 | tf_op jit(solution)/shard_map/transpose | solution.py:157
  16.7 0.4 tile.10
  17.3 2.2 %collective-permute-done.1 = bf16[16,3,512]{2,0,1:T(8,128)(2,1)S(1)} collective-permute-done((bf16[16,3,512]{2,0,1:T(8,128)(2,1)S(1)}, bf16[16,3,512]{2,0,1:T(8,128)(2,1)S(1)}, u32[]{:S(2)}, u32[]{:S(2)}) %collective-permute-start.1) | collective-permute-done | bytes 49184 | tf_op jit(solution)/shard_map/ppermute | solution.py:21
  19.5 0.2 copy.7
  19.7 0.4 reshape.163
  20.4 0.2 reshape.164
  20.7 0.3 convolution_convert_fusion
  21.3 0.7 %collective-permute-start.2 = (bf16[48,640]{1,0:T(8,128)(2,1)S(1)}, bf16[48,640]{1,0:T(8,128)(2,1)S(1)}, u32[]{:S(2)}, u32[]{:S(2)}) collective-permute-start(bf16[48,640]{1,0:T(8,128)(2,1)S(1)} %get-tuple-element.7), channel_id=1, source_target_pairs={{0,0},{2,4},{4,8},{6,12},{8,2},{10,6},{12,10},{14,14},{1,1},{3,5},... | collective-permute-start | bytes 184328 | tf_op jit(solution)/shard_map/ppermute | solution.py:136
  21.9 4.2 %collective-permute-start.3 = (bf16[48,640]{1,0:T(8,128)(2,1)S(1)}, bf16[48,640]{1,0:T(8,128)(2,1)S(1)}, u32[]{:S(2)}, u32[]{:S(2)}) collective-permute-start(bf16[48,640]{1,0:T(8,128)(2,1)S(1)} %get-tuple-element.8), channel_id=1, source_target_pairs={{0,4},{2,0},{4,12},{6,8},{8,6},{10,2},{12,14},{14,10},{1,5},{3,1},... | collective-permute-start | bytes 184328 | tf_op jit(solution)/shard_map/ppermute | solution.py:136
  26.9 0.4 fusion
  27.3 0.5 copy.14
  27.8 1.4 %concatenate.11.clone = bf16[128,76,96]{0,2,1:T(8,128)(2,1)} pad(bf16[128,75,96]{0,2,1:T(8,128)(2,1)S(1)} %copy.14, bf16[]{:T(256)} %constant.64.clone.1), padding=0_0x0_1x0_0 | pad | bytes 3710978 | tf_op jit(solution)/shard_map/concatenate | solution.py:159
  29.1 2.8 %copy.12.w_ref = bf16[128,7296]{1,0:T(8,128)(2,1)S(1)} copy(bf16[128,7296]{0,1:T(8,128)(2,1)} %bitcast.66) | data formatting | bytes 3735552 | tf_op jit(solution)/shard_map/reshape;transpose;reshape | solution.py:166
  32.0 0.6 %gather_fusion = bf16[2,48,640]{2,1,0:T(8,128)(2,1)S(1)} fusion(bf16[2,48,640]{2,1,0:T(8,128)(2,1)S(1)} %pad_maximum_fusion.1, s32[1024]{0:T(1024)S(1)} %pad_clamp_fusion), kind=kCustom, calls=%fused_computation | custom fusion | bytes 245768 | tf_op jit(solution)/shard_map/jit(_take)/gather | solution.py:139
  33.8 4.0 %shard_map.55 = f32[128,512]{1,0:T(8,128)S(1)} custom-call(bf16[1,96,640]{2,1,0:T(8,128)(2,1)S(1)} %bitcast_select_fusion.2.f_ref, f32[96,512]{1,0:T(8,128)S(1)} %fusion.2.inv_ref, bf16[128,7296]{1,0:T(8,128)(2,1)S(1)} %copy.12.w_ref), custom_call_target="tpu_custom_call" | custom-call | tf_op jit(solution)/shard_map/pallas_call | solution.py:72
  37.8 10.6 %all_to_all.21 = f32[4,32,512]{2,1,0:T(8,128)S(1)} all-to-all(f32[4,32,512]{2,1,0:T(8,128)S(1)} %bitcast.65), channel_id=1, replica_groups=mesh['groups'=2,'corr'=4,'filt'=2,'pair'=2] {'corr'}, dimensions={0} | all-to-all | bytes 524288 | tf_op jit(solution)/shard_map/all_to_all | solution.py:169
  48.5 0.9 %broadcast_in_dim.74 = f32[1,32,2048]{2,1,0:T(8,128)} reshape(f32[32,4,512]{2,1,0:T(4,128)S(1)} %copy.13) | data formatting | bytes 524288 | tf_op jit(solution)/shard_map/broadcast_in_dim | solution.py:170
  (51 shorter events, 3.1 us)
Async XLA Ops:
  1.4 24.8 %all-to-all-start = ((bf16[4,32,225]{2,1,0:T(8,128)(2,1)}), bf16[4,32,225]{2,1,0:T(8,128)(2,1)S(1)}, u32[]{:S(2)}, u32[]{:S(2)}) async-start(bf16[4,32,225]{2,1,0:T(8,128)(2,1)} %broadcast_in_dim.73), calls=%async_computation | async-start | bytes 131072 | tf_op jit(solution)/shard_map/all_to_all | solution.py:148
  9.5 7.8 %collective-permute-start = (bf16[16,3,128]{2,0,1:T(8,128)(2,1)S(1)}, bf16[16,3,128]{2,0,1:T(8,128)(2,1)S(1)}, u32[]{:S(2)}, u32[]{:S(2)}) collective-permute-start(bf16[16,3,128]{2,0,1:T(8,128)(2,1)S(1)} %slice.114), channel_id=1, source_target_pairs={{0,4},{4,8},{8,12},{1,5},{5,9},{9,13},{2,6},{6,10},{10,14},{3,7},{... | collective-permute-start | bytes 36872 | tf_op jit(solution)/shard_map/ppermute | solution.py:21
  13.5 6.0 %collective-permute-start.1 = (bf16[16,3,512]{2,0,1:T(8,128)(2,1)S(1)}, bf16[16,3,512]{2,0,1:T(8,128)(2,1)S(1)}, u32[]{:S(2)}, u32[]{:S(2)}) collective-permute-start(bf16[16,3,512]{2,0,1:T(8,128)(2,1)S(1)} %slice.115), channel_id=1, source_target_pairs={{4,0},{8,4},{12,8},{5,1},{9,5},{13,9},{6,2},{10,6},{14,10},{7,3},{... | collective-permute-start | bytes 147464 | tf_op jit(solution)/shard_map/ppermute | solution.py:21
  21.3 10.7 %collective-permute-start.2 = (bf16[48,640]{1,0:T(8,128)(2,1)S(1)}, bf16[48,640]{1,0:T(8,128)(2,1)S(1)}, u32[]{:S(2)}, u32[]{:S(2)}) collective-permute-start(bf16[48,640]{1,0:T(8,128)(2,1)S(1)} %get-tuple-element.7), channel_id=1, source_target_pairs={{0,0},{2,4},{4,8},{6,12},{8,2},{10,6},{12,10},{14,14},{1,1},{3,5},... | collective-permute-start | bytes 184328 | tf_op jit(solution)/shard_map/ppermute | solution.py:136
  21.9 10.0 %collective-permute-start.3 = (bf16[48,640]{1,0:T(8,128)(2,1)S(1)}, bf16[48,640]{1,0:T(8,128)(2,1)S(1)}, u32[]{:S(2)}, u32[]{:S(2)}) collective-permute-start(bf16[48,640]{1,0:T(8,128)(2,1)S(1)} %get-tuple-element.8), channel_id=1, source_target_pairs={{0,4},{2,0},{4,12},{6,8},{8,6},{10,2},{12,14},{14,10},{1,5},{3,1},... | collective-permute-start | bytes 184328 | tf_op jit(solution)/shard_map/ppermute | solution.py:136

commit v6 on v5

--- a/solution.py
+++ b/solution.py
@@ -166,7 +166,16 @@
         .reshape(count, chunks * JP * row_block)
     )
     stacked = correlate(windows, inv, weights, row_block)
-    stacked = lax.all_to_all(stacked, "corr", 0, 1, tiled=True)
+    pieces = [lax.dynamic_slice_in_dim(stacked, corr_place * local_count, local_count, 0)]
+    for d in range(1, corr_count):
+        target = (corr_place + d) % corr_count
+        part = lax.dynamic_slice_in_dim(stacked, target * local_count, local_count, 0)
+        route = [(i, (i + d) % corr_count) for i in range(corr_count)]
+        pieces.append(lax.ppermute(part, "corr", route))
+    pieces = jnp.stack(pieces, axis=0)
+    order = (corr_place - lax.iota(jnp.int32, corr_count)) % corr_count
+    stacked = jnp.take(pieces, order, axis=0)
+    stacked = jnp.transpose(stacked, (1, 0, 2)).reshape(local_count, corr_count * width)
     return stacked[None]
 
 

time: 49.9 us -> 46.5 us (0.932)
  blocking collectives: 10.6 us -> 0 us
  starting transfers between devices: 16.5 us -> 22.9 us
  local copies, waits for them, and re-layouts: 10.8 us -> 11.5 us
    all_to_all x1 -> x0, blocking collectives: 10.6 us -> none  [body(): stacked = lax.all_to_all(stacked, 'corr', 0, 1, tiled=True)]
    ppermute x0 -> x3, starting transfers between devices: none -> 6.24 us  [body(): pieces.append(lax.ppermute(part, 'corr', route))]
    ppermute x2, waiting for transfers between devices: 2.17 us -> 0.01 us  [from_behind(): return lax.ppermute(block, axis, route)]
    ppermute x0 -> x3, waiting for transfers between devices: none -> 2.06 us  [body(): pieces.append(lax.ppermute(part, 'corr', route))]
    all_to_all x1, starting transfers between devices: 6.35 us -> 4.3 us  [body(): lax.all_to_all(copies, 'corr', 0, 0, tiled=True)]
    ppermute x2, starting transfers between devices: 5.22 us -> 6.88 us  [from_behind(): return lax.ppermute(block, axis, route)]
    another operation x0 -> x2, local copies, waits for them, and re-layouts: none -> 0.92 us  [the longest x1 0.88 us: body(): return stacked[None]]
    broadcast_in_dim x1 -> x0, local copies, waits for them, and re-layouts: 0.88 us -> none  [body(): return stacked[None]]
  transfers between devices with their start and end apart: 5 -> 8, of which waited for: 1 -> 3; matrix products, arithmetic and copies ran while one was open for 24% -> 24% of each run, Pallas kernels for 0% -> 0%
where the time goes in v6:
time: 46.5 us; the launch traced here: 46 us
  starting transfers between devices  22.9 us (49%)
  local copies, waits for them, and re-layouts  11.5 us (25%)
  other arithmetic  4.79 us (10%)
  Pallas kernels  3.97 us (9%)
  waiting for transfers between devices  2.07 us (4%)
  between operations  0.52 us (1%)
    ppermute x2, starting transfers between devices, from_behind(): return lax.ppermute(block, axis, route)  6.88 us
    ppermute x3, starting transfers between devices, body(): pieces.append(lax.ppermute(part, 'corr', route))  6.24 us
    ppermute x2, starting transfers between devices, body(): received.append(lax.ppermute(part, ('corr', 'filt'), route))  5.45 us
    all_to_all x1, starting transfers between devices, body(): lax.all_to_all(copies, 'corr', 0, 0, tiled=True)  4.3 us
    pallas_call x1, Pallas kernels, correlate(): pl.pallas_call(functools.partial(corr_kernel, row_block=row_block, tile=t...  3.97 us
    another operation x1, local copies, waits for them, and re-layouts, body(): weights = full.reshape(count, JP, chunks, row_block).transpose(0, 2, 1, 3...  2.76 us
    ppermute x3, waiting for transfers between devices, body(): pieces.append(lax.ppermute(part, 'corr', route))  2.06 us
    concatenate x1, local copies, waits for them, and re-layouts, body(): jnp.concatenate([full, jnp.zeros((count, JP - L, stations * 3), full.dtyp...  1.39 us
  transfers between devices with their start and end apart: 8, of which 3 were waited for; matrix products, arithmetic and copies ran while one was open for 24% of the time, Pallas kernels for 0%

profile of v6, /device:TPU:0, one launch (start us, length us, event | category | flops | bytes accessed | tf_op | source)
XLA Modules:
  0.0 46.0 jit_solution(2662255074495272769)
XLA Ops:
  0.0 0.8 %broadcast_compare_fusion = pred[16,4096]{1,0:T(8,128)(4,1)S(1)} fusion(s32[4096]{0:T(1024)S(1)} %iota_add_fusion, s32[16]{0:T(128)} %bitcast.79), kind=kLoop, calls=%fused_computation.23 | loop fusion | flops 65536 | bytes 81984 | tf_op jit(solution)/shard_map/lt | solution.py:100
  0.8 1.0 %bitcast_select_fusion = bf16[16,3,4096]{2,0,1:T(8,128)(2,1)S(1)} fusion(bf16[1,16,3,4096]{3,1,2,0:T(8,128)(2,1)} %param.5, pred[16,4096]{1,0:T(8,128)(4,1)S(1)} %broadcast_compare_fusion), kind=kLoop, calls=%fused_computation.6 | loop fusion | flops 196608 | bytes 851968 | tf_op jit(solution)/shard_map/jit(_where)/select_n | solution.py:99
  1.8 1.3 %collective-permute-start.1 = (bf16[16,3,512]{2,0,1:T(8,128)(2,1)S(1)}, bf16[16,3,512]{2,0,1:T(8,128)(2,1)S(1)}, u32[]{:S(2)}, u32[]{:S(2)}) collective-permute-start(bf16[16,3,512]{2,0,1:T(8,128)(2,1)S(1)} %slice.117), channel_id=1, source_target_pairs={{4,0},{8,4},{12,8},{5,1},{9,5},{13,9},{6,2},{10,6},{14,10},{7,3},{... | collective-permute-start | bytes 147464 | tf_op jit(solution)/shard_map/ppermute | solution.py:21
  3.1 5.6 %collective-permute-start = (bf16[16,3,128]{2,0,1:T(8,128)(2,1)S(1)}, bf16[16,3,128]{2,0,1:T(8,128)(2,1)S(1)}, u32[]{:S(2)}, u32[]{:S(2)}) collective-permute-start(bf16[16,3,128]{2,0,1:T(8,128)(2,1)S(1)} %slice.116), channel_id=1, source_target_pairs={{0,4},{4,8},{8,12},{1,5},{5,9},{9,13},{2,6},{6,10},{10,14},{3,7},{... | collective-permute-start | bytes 36872 | tf_op jit(solution)/shard_map/ppermute | solution.py:21
  8.7 1.4 %broadcast_in_dim.81 = bf16[4,32,225]{2,1,0:T(8,128)(2,1)} broadcast(bf16[32,225]{1,0:T(8,128)(2,1)} %param.8), dimensions={1,2} | broadcast | bytes 72000 | tf_op jit(solution)/shard_map/broadcast_in_dim | solution.py:147
  10.1 4.3 %all-to-all-start = ((bf16[4,32,225]{2,1,0:T(8,128)(2,1)}), bf16[4,32,225]{2,1,0:T(8,128)(2,1)S(1)}, u32[]{:S(2)}, u32[]{:S(2)}) async-start(bf16[4,32,225]{2,1,0:T(8,128)(2,1)} %broadcast_in_dim.81), calls=%async_computation | async-start | bytes 131072 | tf_op jit(solution)/shard_map/all_to_all | solution.py:148
  14.4 0.7 %rev.3 = bf16[64]{0:T(256)(128)(2,1)S(1)} reverse(bf16[64]{0:T(256)(128)(2,1)} %param.7), dimensions={0} | reverse | bytes 256 | tf_op jit(solution)/shard_map/rev | solution.py:114
  15.2 0.8 %convert_bitcast_fusion = f32[128,32,3]{0,1,2:T(8,128)S(1)} fusion(s32[128,3,32]{0,2,1:T(8,128)} %param.9), kind=kLoop, calls=%fused_computation.48 | loop fusion | flops 12288 | bytes 98304 | tf_op jit(solution)/shard_map/transpose | solution.py:157
  17.3 0.4 reshape.213
  18.8 0.7 %collective-permute-start.2 = (bf16[48,640]{1,0:T(8,128)(2,1)S(1)}, bf16[48,640]{1,0:T(8,128)(2,1)S(1)}, u32[]{:S(2)}, u32[]{:S(2)}) collective-permute-start(bf16[48,640]{1,0:T(8,128)(2,1)S(1)} %get-tuple-element.11), channel_id=1, source_target_pairs={{0,0},{2,4},{4,8},{6,12},{8,2},{10,6},{12,10},{14,14},{1,1},{3,5},... | collective-permute-start | bytes 184328 | tf_op jit(solution)/shard_map/ppermute | solution.py:136
  19.5 4.8 %collective-permute-start.3 = (bf16[48,640]{1,0:T(8,128)(2,1)S(1)}, bf16[48,640]{1,0:T(8,128)(2,1)S(1)}, u32[]{:S(2)}, u32[]{:S(2)}) collective-permute-start(bf16[48,640]{1,0:T(8,128)(2,1)S(1)} %get-tuple-element.12), channel_id=1, source_target_pairs={{0,4},{2,0},{4,12},{6,8},{8,6},{10,2},{12,14},{14,10},{1,5},{3,1},... | collective-permute-start | bytes 184328 | tf_op jit(solution)/shard_map/ppermute | solution.py:136
  25.4 0.5 %copy.13 = bf16[128,75,96]{0,2,1:T(8,128)(2,1)S(1)} copy(bf16[128,75,96]{0,1,2:T(8,128)(2,1)S(1)} %fusion) | data formatting | bytes 3686400
  25.9 1.4 %concatenate.11.clone = bf16[128,76,96]{0,2,1:T(8,128)(2,1)} pad(bf16[128,75,96]{0,2,1:T(8,128)(2,1)S(1)} %copy.13, bf16[]{:T(256)} %constant.105.clone.1), padding=0_0x0_1x0_0 | pad | bytes 3710978 | tf_op jit(solution)/shard_map/concatenate | solution.py:159
  27.3 2.8 %copy.11.w_ref = bf16[128,7296]{1,0:T(8,128)(2,1)S(1)} copy(bf16[128,7296]{0,1:T(8,128)(2,1)} %bitcast.72) | data formatting | bytes 3735552 | tf_op jit(solution)/shard_map/reshape;transpose;reshape | solution.py:166
  30.1 0.6 %gather_fusion = bf16[2,48,640]{2,1,0:T(8,128)(2,1)S(1)} fusion(bf16[2,48,640]{2,1,0:T(8,128)(2,1)S(1)} %pad_maximum_fusion.2, s32[1024]{0:T(1024)S(1)} %pad_clamp_fusion.1), kind=kCustom, calls=%fused_computation | custom fusion | bytes 245768 | tf_op jit(solution)/shard_map/jit(_take)/gather | solution.py:139
  31.9 4.0 %shard_map.55 = f32[128,512]{1,0:T(8,128)S(1)} custom-call(bf16[1,96,640]{2,1,0:T(8,128)(2,1)S(1)} %bitcast_select_fusion.2.f_ref, f32[96,512]{1,0:T(8,128)S(1)} %fusion.2.inv_ref, bf16[128,7296]{1,0:T(8,128)(2,1)S(1)} %copy.11.w_ref), custom_call_target="tpu_custom_call" | custom-call | tf_op jit(solution)/shard_map/pallas_call | solution.py:72
  35.9 2.4 %collective-permute-start.4 = (f32[32,512]{1,0:T(8,128)S(1)}, f32[32,512]{1,0:T(8,128)S(1)}, u32[]{:S(2)}, u32[]{:S(2)}) collective-permute-start(f32[32,512]{1,0:T(8,128)S(1)} %get-tuple-element.8), channel_id=1, source_target_pairs={{0,4},{4,8},{8,12},{12,0},{1,5},{5,9},{9,13},{13,1},{2,6},{6,10},{... | collective-permute-start | bytes 196616 | tf_op jit(solution)/shard_map/ppermute | solution.py:174
  38.4 0.9 %collective-permute-start.5 = (f32[32,512]{1,0:T(8,128)S(1)}, f32[32,512]{1,0:T(8,128)S(1)}, u32[]{:S(2)}, u32[]{:S(2)}) collective-permute-start(f32[32,512]{1,0:T(8,128)S(1)} %get-tuple-element.7), channel_id=1, source_target_pairs={{0,8},{4,12},{8,0},{12,4},{1,9},{5,13},{9,1},{13,5},{2,10},{6,14},... | collective-permute-start | bytes 196616 | tf_op jit(solution)/shard_map/ppermute | solution.py:174
  39.3 2.8 %collective-permute-start.6 = (f32[32,512]{1,0:T(8,128)S(1)}, f32[32,512]{1,0:T(8,128)S(1)}, u32[]{:S(2)}, u32[]{:S(2)}) collective-permute-start(f32[32,512]{1,0:T(8,128)S(1)} %get-tuple-element.6), channel_id=1, source_target_pairs={{0,12},{4,0},{8,4},{12,8},{1,13},{5,1},{9,5},{13,9},{2,14},{6,2},{... | collective-permute-start | bytes 196616 | tf_op jit(solution)/shard_map/ppermute | solution.py:174
  42.2 0.5 %collective-permute-done.4 = f32[32,512]{1,0:T(8,128)S(1)} collective-permute-done((f32[32,512]{1,0:T(8,128)S(1)}, f32[32,512]{1,0:T(8,128)S(1)}, u32[]{:S(2)}, u32[]{:S(2)}) %collective-permute-start.4) | collective-permute-done | bytes 65568 | tf_op jit(solution)/shard_map/ppermute | solution.py:174
  42.7 0.9 %collective-permute-done.5 = f32[32,512]{1,0:T(8,128)S(1)} collective-permute-done((f32[32,512]{1,0:T(8,128)S(1)}, f32[32,512]{1,0:T(8,128)S(1)}, u32[]{:S(2)}, u32[]{:S(2)}) %collective-permute-start.5) | collective-permute-done | bytes 65568 | tf_op jit(solution)/shard_map/ppermute | solution.py:174
  43.6 0.6 %collective-permute-done.6 = f32[32,512]{1,0:T(8,128)S(1)} collective-permute-done((f32[32,512]{1,0:T(8,128)S(1)}, f32[32,512]{1,0:T(8,128)S(1)}, u32[]{:S(2)}, u32[]{:S(2)}) %collective-permute-start.6) | collective-permute-done | bytes 65568 | tf_op jit(solution)/shard_map/ppermute | solution.py:174
  44.3 0.6 %gather_fusion.1 = f32[4,32,512]{2,1,0:T(8,128)S(1)} fusion(f32[4,32,512]{2,1,0:T(8,128)S(1)} %pad_maximum_fusion.1, s32[1024]{0:T(1024)S(1)} %pad_clamp_fusion), kind=kCustom, calls=%fused_computation.1 | custom fusion | bytes 524304 | tf_op jit(solution)/shard_map/jit(_take)/gather | solution.py:177
  45.1 0.9 %broadcast_in_dim_reshape.3 = f32[1,32,2048]{2,1,0:T(8,128)} reshape(f32[32,4,512]{2,1,0:T(4,128)S(1)} %copy.12) | data formatting | bytes 524288 | tf_op jit(solution)/shard_map/broadcast_in_dim;reshape | solution.py:179
  (63 shorter events, 4.8 us)
Async XLA Ops:
  1.8 15.2 %collective-permute-start.1 = (bf16[16,3,512]{2,0,1:T(8,128)(2,1)S(1)}, bf16[16,3,512]{2,0,1:T(8,128)(2,1)S(1)}, u32[]{:S(2)}, u32[]{:S(2)}) collective-permute-start(bf16[16,3,512]{2,0,1:T(8,128)(2,1)S(1)} %slice.117), channel_id=1, source_target_pairs={{4,0},{8,4},{12,8},{5,1},{9,5},{13,9},{6,2},{10,6},{14,10},{7,3},{... | collective-permute-start | bytes 147464 | tf_op jit(solution)/shard_map/ppermute | solution.py:21
  3.1 13.8 %collective-permute-start = (bf16[16,3,128]{2,0,1:T(8,128)(2,1)S(1)}, bf16[16,3,128]{2,0,1:T(8,128)(2,1)S(1)}, u32[]{:S(2)}, u32[]{:S(2)}) collective-permute-start(bf16[16,3,128]{2,0,1:T(8,128)(2,1)S(1)} %slice.116), channel_id=1, source_target_pairs={{0,4},{4,8},{8,12},{1,5},{5,9},{9,13},{2,6},{6,10},{10,14},{3,7},{... | collective-permute-start | bytes 36872 | tf_op jit(solution)/shard_map/ppermute | solution.py:21
  10.1 14.2 %all-to-all-start = ((bf16[4,32,225]{2,1,0:T(8,128)(2,1)}), bf16[4,32,225]{2,1,0:T(8,128)(2,1)S(1)}, u32[]{:S(2)}, u32[]{:S(2)}) async-start(bf16[4,32,225]{2,1,0:T(8,128)(2,1)} %broadcast_in_dim.81), calls=%async_computation | async-start | bytes 131072 | tf_op jit(solution)/shard_map/all_to_all | solution.py:148
  18.8 11.2 %collective-permute-start.2 = (bf16[48,640]{1,0:T(8,128)(2,1)S(1)}, bf16[48,640]{1,0:T(8,128)(2,1)S(1)}, u32[]{:S(2)}, u32[]{:S(2)}) collective-permute-start(bf16[48,640]{1,0:T(8,128)(2,1)S(1)} %get-tuple-element.11), channel_id=1, source_target_pairs={{0,0},{2,4},{4,8},{6,12},{8,2},{10,6},{12,10},{14,14},{1,1},{3,5},... | collective-permute-start | bytes 184328 | tf_op jit(solution)/shard_map/ppermute | solution.py:136
  19.5 10.6 %collective-permute-start.3 = (bf16[48,640]{1,0:T(8,128)(2,1)S(1)}, bf16[48,640]{1,0:T(8,128)(2,1)S(1)}, u32[]{:S(2)}, u32[]{:S(2)}) collective-permute-start(bf16[48,640]{1,0:T(8,128)(2,1)S(1)} %get-tuple-element.12), channel_id=1, source_target_pairs={{0,4},{2,0},{4,12},{6,8},{8,6},{10,2},{12,14},{14,10},{1,5},{3,1},... | collective-permute-start | bytes 184328 | tf_op jit(solution)/shard_map/ppermute | solution.py:136
  35.9 6.8 %collective-permute-start.4 = (f32[32,512]{1,0:T(8,128)S(1)}, f32[32,512]{1,0:T(8,128)S(1)}, u32[]{:S(2)}, u32[]{:S(2)}) collective-permute-start(f32[32,512]{1,0:T(8,128)S(1)} %get-tuple-element.8), channel_id=1, source_target_pairs={{0,4},{4,8},{8,12},{12,0},{1,5},{5,9},{9,13},{13,1},{2,6},{6,10},{... | collective-permute-start | bytes 196616 | tf_op jit(solution)/shard_map/ppermute | solution.py:174
  38.4 5.2 %collective-permute-start.5 = (f32[32,512]{1,0:T(8,128)S(1)}, f32[32,512]{1,0:T(8,128)S(1)}, u32[]{:S(2)}, u32[]{:S(2)}) collective-permute-start(f32[32,512]{1,0:T(8,128)S(1)} %get-tuple-element.7), channel_id=1, source_target_pairs={{0,8},{4,12},{8,0},{12,4},{1,9},{5,13},{9,1},{13,5},{2,10},{6,14},... | collective-permute-start | bytes 196616 | tf_op jit(solution)/shard_map/ppermute | solution.py:174
  39.3 4.9 %collective-permute-start.6 = (f32[32,512]{1,0:T(8,128)S(1)}, f32[32,512]{1,0:T(8,128)S(1)}, u32[]{:S(2)}, u32[]{:S(2)}) collective-permute-start(f32[32,512]{1,0:T(8,128)S(1)} %get-tuple-element.6), channel_id=1, source_target_pairs={{0,12},{4,0},{8,4},{12,8},{1,13},{5,1},{9,5},{13,9},{2,14},{6,2},{... | collective-permute-start | bytes 196616 | tf_op jit(solution)/shard_map/ppermute | solution.py:174

commit v7 on v6

--- a/solution.py
+++ b/solution.py
@@ -95,13 +95,37 @@
     corr_place = lax.axis_index("corr")
     filt_place = lax.axis_index("filt")
     filt_count = lax.axis_size("filt")
+    corr_place = lax.axis_index("corr")
     sample_times = corr_place * raw_width + lax.iota(jnp.int32, raw_width)
     live = jnp.where(
         sample_times[None, None, :] < counts[:, None, None], samples, jnp.zeros_like(samples)
     )
-    history = from_behind(live[:, :, raw_width - 128 :], "corr", 1)
     corr_count = lax.axis_size("corr")
-    ahead = from_behind(live[:, :, :512], "corr", -1)
+    head = live[:, :, :512].reshape(-1)
+    tail = live[:, :, raw_width - 128 :].reshape(-1)
+    tail = jnp.concatenate([tail, jnp.zeros((head.shape[0] - tail.shape[0],), tail.dtype)])
+    own_templates = templates.reshape(-1)
+    peers = lax.iota(jnp.int32, corr_count)
+    lead = jnp.where(
+        (peers == corr_place - 1)[:, None],
+        head[None, :],
+        jnp.where((peers == corr_place + 1)[:, None], tail[None, :], jnp.zeros_like(head)[None, :]),
+    )
+    parcels = jnp.concatenate(
+        [lead, jnp.broadcast_to(own_templates[None, :], (corr_count, own_templates.shape[0]))], axis=1
+    )
+    arrived = lax.all_to_all(parcels, "corr", 0, 0, tiled=True)
+    previous = lax.dynamic_index_in_dim(arrived, jnp.maximum(corr_place - 1, 0), 0, keepdims=False)
+    following = lax.dynamic_index_in_dim(
+        arrived, jnp.minimum(corr_place + 1, corr_count - 1), 0, keepdims=False
+    )
+    history = previous[: tail.shape[0]][: local_stations * 3 * 128].reshape(local_stations, 3, 128)
+    history = jnp.where(corr_place > 0, history, jnp.zeros_like(history))
+    ahead = following[: head.shape[0]].reshape(local_stations, 3, 512)
+    ahead = jnp.where(corr_place < corr_count - 1, ahead, jnp.zeros_like(ahead))
+    gathered_templates = arrived[:, head.shape[0] :].reshape(
+        corr_count * templates.shape[0], templates.shape[1]
+    )
     extended = jnp.concatenate([history, live, ahead], axis=2).reshape(
         local_stations * 3, raw_width + 640
     )
@@ -144,10 +168,7 @@
     windows = jnp.stack([rows[:, i * tile : i * tile + tile + 128] for i in range(tiles)], axis=0)
 
     local_count = templates.shape[0]
-    copies = jnp.broadcast_to(templates[None], (corr_count,) + templates.shape)
-    templates = lax.all_to_all(copies, "corr", 0, 0, tiled=True).reshape(
-        corr_count * local_count, templates.shape[1]
-    )
+    templates = gathered_templates
     count = templates.shape[0]
     stations = masks.shape[2]
     shaped = templates.astype(jnp.float32).reshape(count, 3, L)

time: 46.5 us -> 49 us (1.054)
  starting transfers between devices: 22.9 us -> 15.6 us
  waiting for transfers between devices: 2.07 us -> 8.07 us
  local copies, waits for them, and re-layouts: 11.5 us -> 14.2 us
  other arithmetic: 4.79 us -> 5.75 us
    ppermute x2 -> x0, starting transfers between devices: 6.88 us -> none  [from_behind(): return lax.ppermute(block, axis, route)]
    all_to_all x1, waiting for transfers between devices: 0.01 us -> 6.19 us  [body(): arrived = lax.all_to_all(parcels, 'corr', 0, 0, tiled=True)]
    ppermute x2, starting transfers between devices: 5.45 us -> 2.35 us  [body(): received.append(lax.ppermute(part, ('corr', 'filt'), route))]
    unnamed x9 -> x18, local copies, waits for them, and re-layouts: 0.58 us -> 3.01 us
    all_to_all x1, starting transfers between devices: 4.3 us -> 6.35 us  [body(): arrived = lax.all_to_all(parcels, 'corr', 0, 0, tiled=True)]
    all_to_all x0 -> x2, other arithmetic: none -> 1.11 us  [body(): arrived = lax.all_to_all(parcels, 'corr', 0, 0, tiled=True)]
    transpose x1, other arithmetic: 0.81 us -> 0.01 us  [body(): jnp.transpose(chosen, (0, 2, 1))[:, None, :, :]]
    ppermute x3, starting transfers between devices: 6.24 us -> 6.93 us  [body(): pieces.append(lax.ppermute(part, 'corr', route))]
  transfers between devices with their start and end apart: 8 -> 6, of which waited for: 3 -> 3; matrix products, arithmetic and copies ran while one was open for 24% -> 17% of each run, Pallas kernels for 0% -> 0%
where the time goes in v7:
time: 49 us; the launch traced here: 48.6 us
  starting transfers between devices  15.6 us (32%)
  local copies, waits for them, and re-layouts  14.2 us (29%)
  waiting for transfers between devices  8.07 us (16%)
  other arithmetic  5.75 us (12%)
  Pallas kernels  3.97 us (8%)
  between operations  0.65 us (1%)
    ppermute x3, starting transfers between devices, body(): pieces.append(lax.ppermute(part, 'corr', route))  6.93 us
    all_to_all x1, starting transfers between devices, body(): arrived = lax.all_to_all(parcels, 'corr', 0, 0, tiled=True)  6.35 us
    all_to_all x1, waiting for transfers between devices, body(): arrived = lax.all_to_all(parcels, 'corr', 0, 0, tiled=True)  6.19 us
    pallas_call x1, Pallas kernels, correlate(): pl.pallas_call(functools.partial(corr_kernel, row_block=row_block, tile=t...  3.97 us
    unnamed x18, local copies, waits for them, and re-layouts  3.01 us
    another operation x1, local copies, waits for them, and re-layouts, body(): weights = full.reshape(count, JP, chunks, row_block).transpose(0, 2, 1, 3...  2.76 us
    ppermute x2, starting transfers between devices, body(): received.append(lax.ppermute(part, ('corr', 'filt'), route))  2.35 us
    ppermute x3, waiting for transfers between devices, body(): pieces.append(lax.ppermute(part, 'corr', route))  1.88 us
  transfers between devices with their start and end apart: 6, of which 3 were waited for; matrix products, arithmetic and copies ran while one was open for 17% of the time, Pallas kernels for 0%

profile of v7, /device:TPU:0, one launch (start us, length us, event | category | flops | bytes accessed | tf_op | source)
XLA Modules:
  0.0 48.6 jit_solution(3859473433748272409)
XLA Ops:
  0.0 0.8 %broadcast_compare_fusion = pred[16,4096]{1,0:T(8,128)(4,1)S(1)} fusion(s32[4096]{0:T(1024)S(1)} %iota_add_fusion, s32[16]{0:T(128)} %bitcast.91), kind=kLoop, calls=%fused_computation.27 | loop fusion | flops 65536 | bytes 81984 | tf_op jit(solution)/shard_map/lt | solution.py:101
  0.8 1.0 %bitcast_select_fusion = bf16[16,3,4096]{2,0,1:T(8,128)(2,1)S(1)} fusion(bf16[1,16,3,4096]{3,1,2,0:T(8,128)(2,1)} %param.5, pred[16,4096]{1,0:T(8,128)(4,1)S(1)} %broadcast_compare_fusion), kind=kLoop, calls=%fused_computation.5 | loop fusion | flops 196608 | bytes 851968 | tf_op jit(solution)/shard_map/jit(_where)/select_n | solution.py:100
  2.0 0.9 %reshape.271 = bf16[7200]{0:T(1024)(128)(2,1)S(1)} reshape(bf16[32,225]{1,0:T(8,128)(2,1)} %param.8) | data formatting | bytes 28800 | tf_op jit(solution)/shard_map/broadcast_in_dim | solution.py:115
  3.3 0.5 %broadcast.307 = bf16[]{:T(256)} broadcast(bf16[]{:T(256)} %constant.233), dimensions={} | broadcast | bytes 4 | tf_op jit(solution)/shard_map/all_to_all | solution.py:117
  3.8 1.0 %reduce.4 = bf16[4,31776]{1,0:T(4,128)(2,1)S(1)} reduce(bf16[4,1,31776]{2,0,1:T(4,128)(2,1)S(1)} %maximum_bitcast_fusion, bf16[]{:T(256)} %broadcast.307), dimensions={1}, to_apply=%copy.28.reduce_sub_computation | reduce | bytes 508418 | tf_op jit(solution)/shard_map/all_to_all | solution.py:117
  4.8 1.0 %reshape.272 = bf16[4,2,15888]{2,1,0:T(2,128)(2,1)} reshape(bf16[4,31776]{1,0:T(4,128)(2,1)S(1)} %reduce.4) | data formatting | bytes 508416
  5.8 6.4 %all-to-all-start = ((bf16[4,2,15888]{2,1,0:T(2,128)(2,1)}), bf16[4,2,15888]{2,1,0:T(2,128)(2,1)S(1)}, u32[]{:S(2)}, u32[]{:S(2)}) async-start(bf16[4,2,15888]{2,1,0:T(2,128)(2,1)} %reshape.272), calls=%async_computation | async-start | bytes 512000 | tf_op jit(solution)/shard_map/all_to_all | solution.py:117
  12.8 0.4 broadcast_in_dim.142
  14.7 6.2 %all-to-all-done = bf16[4,2,15888]{2,1,0:T(2,128)(2,1)S(1)} async-done(((bf16[4,2,15888]{2,1,0:T(2,128)(2,1)}), bf16[4,2,15888]{2,1,0:T(2,128)(2,1)S(1)}, u32[]{:S(2)}, u32[]{:S(2)}) %all-to-all-start) | async-done | bytes 254240 | tf_op jit(solution)/shard_map/all_to_all | solution.py:117
  20.9 0.9 %reshape.273 = bf16[4,1,31776]{2,1,0:T(2,128)(2,1)S(1)} reshape(bf16[4,2,15888]{2,1,0:T(2,128)(2,1)S(1)} %all-to-all-done) | data formatting | bytes 508416
  23.8 0.7 %collective-permute-start = (bf16[48,640]{1,0:T(8,128)(2,1)S(1)}, bf16[48,640]{1,0:T(8,128)(2,1)S(1)}, u32[]{:S(2)}, u32[]{:S(2)}) collective-permute-start(bf16[48,640]{1,0:T(8,128)(2,1)S(1)} %get-tuple-element.13), channel_id=1, source_target_pairs={{0,0},{2,4},{4,8},{6,12},{8,2},{10,6},{12,10},{14,14},{1,1},{3,5},... | collective-permute-start | bytes 184328 | tf_op jit(solution)/shard_map/ppermute | solution.py:160
  24.5 1.7 %collective-permute-start.1 = (bf16[48,640]{1,0:T(8,128)(2,1)S(1)}, bf16[48,640]{1,0:T(8,128)(2,1)S(1)}, u32[]{:S(2)}, u32[]{:S(2)}) collective-permute-start(bf16[48,640]{1,0:T(8,128)(2,1)S(1)} %get-tuple-element.14), channel_id=1, source_target_pairs={{0,4},{2,0},{4,12},{6,8},{8,6},{10,2},{12,14},{14,10},{1,5},{3,1},... | collective-permute-start | bytes 184328 | tf_op jit(solution)/shard_map/ppermute | solution.py:160
  27.5 0.5 copy.39
  28.0 1.4 %concatenate.25.clone = bf16[128,76,96]{0,2,1:T(8,128)(2,1)} pad(bf16[128,75,96]{0,2,1:T(8,128)(2,1)S(1)} %copy.39, bf16[]{:T(256)} %constant.119.clone.1), padding=0_0x0_1x0_0 | pad | bytes 3710978 | tf_op jit(solution)/shard_map/concatenate | solution.py:180
  29.4 2.8 %copy.35.w_ref = bf16[128,7296]{1,0:T(8,128)(2,1)S(1)} copy(bf16[128,7296]{0,1:T(8,128)(2,1)} %bitcast.82) | data formatting | bytes 3735552 | tf_op jit(solution)/shard_map/reshape;transpose;reshape | solution.py:187
  32.2 0.6 %gather_fusion = bf16[2,48,640]{2,1,0:T(8,128)(2,1)S(1)} fusion(bf16[2,48,640]{2,1,0:T(8,128)(2,1)S(1)} %pad_maximum_fusion.1, s32[1024]{0:T(1024)S(1)} %pad_clamp_fusion.1), kind=kCustom, calls=%fused_computation | custom fusion | bytes 245768 | tf_op jit(solution)/shard_map/jit(_take)/gather | solution.py:163
  34.0 4.0 %shard_map.55 = f32[128,512]{1,0:T(8,128)S(1)} custom-call(bf16[1,96,640]{2,1,0:T(8,128)(2,1)S(1)} %bitcast_select_fusion.2.f_ref, f32[96,512]{1,0:T(8,128)S(1)} %fusion.2.inv_ref, bf16[128,7296]{1,0:T(8,128)(2,1)S(1)} %copy.35.w_ref), custom_call_target="tpu_custom_call" | custom-call | tf_op jit(solution)/shard_map/pallas_call | solution.py:72
  38.1 2.4 %collective-permute-start.2 = (f32[32,512]{1,0:T(8,128)S(1)}, f32[32,512]{1,0:T(8,128)S(1)}, u32[]{:S(2)}, u32[]{:S(2)}) collective-permute-start(f32[32,512]{1,0:T(8,128)S(1)} %get-tuple-element.10), channel_id=1, source_target_pairs={{0,4},{4,8},{8,12},{12,0},{1,5},{5,9},{9,13},{13,1},{2,6},{6,10},{... | collective-permute-start | bytes 196616 | tf_op jit(solution)/shard_map/ppermute | solution.py:195
  40.5 1.6 %collective-permute-start.3 = (f32[32,512]{1,0:T(8,128)S(1)}, f32[32,512]{1,0:T(8,128)S(1)}, u32[]{:S(2)}, u32[]{:S(2)}) collective-permute-start(f32[32,512]{1,0:T(8,128)S(1)} %get-tuple-element.9), channel_id=1, source_target_pairs={{0,8},{4,12},{8,0},{12,4},{1,9},{5,13},{9,1},{13,5},{2,10},{6,14},... | collective-permute-start | bytes 196616 | tf_op jit(solution)/shard_map/ppermute | solution.py:195
  42.1 2.8 %collective-permute-start.4 = (f32[32,512]{1,0:T(8,128)S(1)}, f32[32,512]{1,0:T(8,128)S(1)}, u32[]{:S(2)}, u32[]{:S(2)}) collective-permute-start(f32[32,512]{1,0:T(8,128)S(1)} %get-tuple-element.8), channel_id=1, source_target_pairs={{0,12},{4,0},{8,4},{12,8},{1,13},{5,1},{9,5},{13,9},{2,14},{6,2},{... | collective-permute-start | bytes 196616 | tf_op jit(solution)/shard_map/ppermute | solution.py:195
  45.0 0.7 %collective-permute-done.3 = f32[32,512]{1,0:T(8,128)S(1)} collective-permute-done((f32[32,512]{1,0:T(8,128)S(1)}, f32[32,512]{1,0:T(8,128)S(1)}, u32[]{:S(2)}, u32[]{:S(2)}) %collective-permute-start.3) | collective-permute-done | bytes 65568 | tf_op jit(solution)/shard_map/ppermute | solution.py:195
  45.8 1.1 %collective-permute-done.4 = f32[32,512]{1,0:T(8,128)S(1)} collective-permute-done((f32[32,512]{1,0:T(8,128)S(1)}, f32[32,512]{1,0:T(8,128)S(1)}, u32[]{:S(2)}, u32[]{:S(2)}) %collective-permute-start.4) | collective-permute-done | bytes 65568 | tf_op jit(solution)/shard_map/ppermute | solution.py:195
  46.9 0.6 %gather_fusion.1 = f32[4,32,512]{2,1,0:T(8,128)S(1)} fusion(f32[4,32,512]{2,1,0:T(8,128)S(1)} %pad_maximum_fusion, s32[1024]{0:T(1024)S(1)} %pad_clamp_fusion), kind=kCustom, calls=%fused_computation.1 | custom fusion | bytes 524304 | tf_op jit(solution)/shard_map/jit(_take)/gather | solution.py:198
  47.8 0.9 %broadcast_in_dim_reshape.2 = f32[1,32,2048]{2,1,0:T(8,128)} reshape(f32[32,4,512]{2,1,0:T(4,128)S(1)} %copy.36) | data formatting | bytes 524288 | tf_op jit(solution)/shard_map/broadcast_in_dim;reshape | solution.py:200
  (86 shorter events, 7.2 us)
Async XLA Ops:
  0.0 12.1 %copy-start = (bf16[1,16,3,4096]{3,1,2,0:T(8,128)(2,1)S(1)}, bf16[1,16,3,4096]{3,1,2,0:T(8,128)(2,1)}, u32[]{:S(2)}) copy-start(bf16[1,16,3,4096]{3,1,2,0:T(8,128)(2,1)} %param.5) | copy-start | bytes 1179652
  3.8 9.7 %copy-start.2 = (bf16[64]{0:T(256)(128)(2,1)S(1)}, bf16[64]{0:T(256)(128)(2,1)}, u32[]{:S(2)}) copy-start(bf16[64]{0:T(256)(128)(2,1)} %param.7) | copy-start | bytes 388
  3.8 9.8 %copy-start.1 = (s32[128,3,32]{0,2,1:T(8,128)S(1)}, s32[128,3,32]{0,2,1:T(8,128)}, u32[]{:S(2)}) copy-start(s32[128,3,32]{0,2,1:T(8,128)} %param.9) | copy-start | bytes 147460
  5.8 15.1 %all-to-all-start = ((bf16[4,2,15888]{2,1,0:T(2,128)(2,1)}), bf16[4,2,15888]{2,1,0:T(2,128)(2,1)S(1)}, u32[]{:S(2)}, u32[]{:S(2)}) async-start(bf16[4,2,15888]{2,1,0:T(2,128)(2,1)} %reshape.272), calls=%async_computation | async-start | bytes 512000 | tf_op jit(solution)/shard_map/all_to_all | solution.py:117
  23.8 8.3 %collective-permute-start = (bf16[48,640]{1,0:T(8,128)(2,1)S(1)}, bf16[48,640]{1,0:T(8,128)(2,1)S(1)}, u32[]{:S(2)}, u32[]{:S(2)}) collective-permute-start(bf16[48,640]{1,0:T(8,128)(2,1)S(1)} %get-tuple-element.13), channel_id=1, source_target_pairs={{0,0},{2,4},{4,8},{6,12},{8,2},{10,6},{12,10},{14,14},{1,1},{3,5},... | collective-permute-start | bytes 184328 | tf_op jit(solution)/shard_map/ppermute | solution.py:160
  24.5 7.7 %collective-permute-start.1 = (bf16[48,640]{1,0:T(8,128)(2,1)S(1)}, bf16[48,640]{1,0:T(8,128)(2,1)S(1)}, u32[]{:S(2)}, u32[]{:S(2)}) collective-permute-start(bf16[48,640]{1,0:T(8,128)(2,1)S(1)} %get-tuple-element.14), channel_id=1, source_target_pairs={{0,4},{2,0},{4,12},{6,8},{8,6},{10,2},{12,14},{14,10},{1,5},{3,1},... | collective-permute-start | bytes 184328 | tf_op jit(solution)/shard_map/ppermute | solution.py:160
  38.1 7.0 %collective-permute-start.2 = (f32[32,512]{1,0:T(8,128)S(1)}, f32[32,512]{1,0:T(8,128)S(1)}, u32[]{:S(2)}, u32[]{:S(2)}) collective-permute-start(f32[32,512]{1,0:T(8,128)S(1)} %get-tuple-element.10), channel_id=1, source_target_pairs={{0,4},{4,8},{8,12},{12,0},{1,5},{5,9},{9,13},{13,1},{2,6},{6,10},{... | collective-permute-start | bytes 196616 | tf_op jit(solution)/shard_map/ppermute | solution.py:195
  40.5 5.3 %collective-permute-start.3 = (f32[32,512]{1,0:T(8,128)S(1)}, f32[32,512]{1,0:T(8,128)S(1)}, u32[]{:S(2)}, u32[]{:S(2)}) collective-permute-start(f32[32,512]{1,0:T(8,128)S(1)} %get-tuple-element.9), channel_id=1, source_target_pairs={{0,8},{4,12},{8,0},{12,4},{1,9},{5,13},{9,1},{13,5},{2,10},{6,14},... | collective-permute-start | bytes 196616 | tf_op jit(solution)/shard_map/ppermute | solution.py:195
  42.1 4.8 %collective-permute-start.4 = (f32[32,512]{1,0:T(8,128)S(1)}, f32[32,512]{1,0:T(8,128)S(1)}, u32[]{:S(2)}, u32[]{:S(2)}) collective-permute-start(f32[32,512]{1,0:T(8,128)S(1)} %get-tuple-element.8), channel_id=1, source_target_pairs={{0,12},{4,0},{8,4},{12,8},{1,13},{5,1},{9,5},{13,9},{2,14},{6,2},{... | collective-permute-start | bytes 196616 | tf_op jit(solution)/shard_map/ppermute | solution.py:195

commit v8 on v6

--- a/solution.py
+++ b/solution.py
@@ -96,22 +96,24 @@
     filt_place = lax.axis_index("filt")
     filt_count = lax.axis_size("filt")
     sample_times = corr_place * raw_width + lax.iota(jnp.int32, raw_width)
-    live = jnp.where(
-        sample_times[None, None, :] < counts[:, None, None], samples, jnp.zeros_like(samples)
-    )
-    history = from_behind(live[:, :, raw_width - 128 :], "corr", 1)
+    dense = samples.reshape(local_stations * 3, raw_width)
+    row_counts = jnp.repeat(counts, 3)
+    live = jnp.where(sample_times[None, :] < row_counts[:, None], dense, jnp.zeros_like(dense))
+    history = from_behind(live[:, raw_width - 128 :], "corr", 1)
     corr_count = lax.axis_size("corr")
-    ahead = from_behind(live[:, :, :512], "corr", -1)
-    extended = jnp.concatenate([history, live, ahead], axis=2).reshape(
-        local_stations * 3, raw_width + 640
-    )
+    ahead = from_behind(live[:, :512], "corr", -1)
+    extended = jnp.concatenate([history, live, ahead], axis=1)
     decimated = raw_width // DEC
     blocks = decimated // 128 + 1
     frames = jnp.stack(
         [extended[:, 512 * a : 512 * a + 640] for a in range(blocks)], axis=1
     ).reshape(local_stations * 3 * blocks, 640)
+    flip = (lax.iota(jnp.int32, TAPS)[:, None] + lax.iota(jnp.int32, TAPS)[None, :] == TAPS - 1)
+    reversed_taps = jnp.dot(
+        taps[None, :], flip.astype(taps.dtype), preferred_element_type=jnp.float32
+    )[0].astype(taps.dtype)
     ring = jnp.concatenate(
-        [jnp.zeros((65,), taps.dtype), taps[::-1], jnp.zeros((644 - 129,), taps.dtype)]
+        [jnp.zeros((65,), taps.dtype), reversed_taps, jnp.zeros((644 - 129,), taps.dtype)]
     )
     bank = jnp.tile(ring, 128)[: 128 * 640].reshape(128, 640)
     filtered = lax.dot_general(
@@ -134,9 +136,7 @@
                 dest = ((c % per_block) * filt_count + (f + k) % filt_count) * filt_count + c // per_block
                 route.append((c * filt_count + f, dest))
         received.append(lax.ppermute(part, ("corr", "filt"), route))
-    received = jnp.stack(received, axis=0)
-    order = (corr_place - lax.iota(jnp.int32, filt_count)) % filt_count
-    rows = jnp.take(received, order, axis=0).reshape(filt_count * filtered.shape[0], span)
+    rows = jnp.concatenate(received, axis=0)
     energy = window_energy(rows.astype(jnp.float32), width)
     inv = lax.rsqrt(jnp.maximum(energy, 1.0))
     tile = min(TT, width)
@@ -144,16 +144,23 @@
     windows = jnp.stack([rows[:, i * tile : i * tile + tile + 128] for i in range(tiles)], axis=0)
 
     local_count = templates.shape[0]
-    copies = jnp.broadcast_to(templates[None], (corr_count,) + templates.shape)
+    template_width = templates.shape[1]
+    lanes = -(-template_width // 128) * 128
+    wide = jnp.concatenate(
+        [templates, jnp.zeros((local_count, lanes - template_width), templates.dtype)], axis=1
+    )
+    copies = jnp.broadcast_to(wide[None], (corr_count,) + wide.shape)
     templates = lax.all_to_all(copies, "corr", 0, 0, tiled=True).reshape(
-        corr_count * local_count, templates.shape[1]
-    )
+        corr_count * local_count, lanes
+    )[:, :template_width]
     count = templates.shape[0]
     stations = masks.shape[2]
     shaped = templates.astype(jnp.float32).reshape(count, 3, L)
     norms = jnp.sqrt(jnp.sum(shaped * shaped, axis=2) + 1e-06)
     base = shaped / norms[:, :, None]
-    chosen = masks.astype(jnp.float32)
+    arrival = (corr_place - lax.iota(jnp.int32, filt_count)) % filt_count
+    chosen = jnp.take(masks.reshape(count, 3, filt_count, stations // filt_count), arrival, axis=2)
+    chosen = chosen.reshape(count, 3, stations).astype(jnp.float32)
     full = jnp.transpose(base, (0, 2, 1))[:, :, None, :] * jnp.transpose(chosen, (0, 2, 1))[:, None, :, :]
     full = full.astype(jnp.bfloat16).reshape(count, L, stations * 3)
     full = jnp.concatenate([full, jnp.zeros((count, JP - L, stations * 3), full.dtype)], axis=1)
@@ -172,10 +179,10 @@
         part = lax.dynamic_slice_in_dim(stacked, target * local_count, local_count, 0)
         route = [(i, (i + d) % corr_count) for i in range(corr_count)]
         pieces.append(lax.ppermute(part, "corr", route))
-    pieces = jnp.stack(pieces, axis=0)
-    order = (corr_place - lax.iota(jnp.int32, corr_count)) % corr_count
-    stacked = jnp.take(pieces, order, axis=0)
-    stacked = jnp.transpose(stacked, (1, 0, 2)).reshape(local_count, corr_count * width)
+    stacked = jnp.zeros((local_count, corr_count * width), jnp.float32)
+    for d, part in enumerate(pieces):
+        place = ((corr_place - d) % corr_count) * width
+        stacked = lax.dynamic_update_slice_in_dim(stacked, part, place, 1)
     return stacked[None]
 
 

time: 46.5 us -> 43.8 us (0.942)
  other arithmetic: 4.79 us -> 1.7 us
  starting transfers between devices: 22.9 us -> 23.9 us
  local copies, waits for them, and re-layouts: 11.5 us -> 10.9 us
    all_to_all x1, starting transfers between devices: 4.3 us -> 5.94 us  [body(): lax.all_to_all(copies, 'corr', 0, 0, tiled=True)]
    unnamed x9 -> x19, local copies, waits for them, and re-layouts: 0.58 us -> 2.15 us
    select_n x5 -> x2, other arithmetic: 1.24 us -> 0.18 us  [the longest x1 0.16 us: body(): jnp.where(sample_times[None, :] < row_counts[:, None], dense, jnp.zeros_l...]
    transpose x1 -> x0, other arithmetic: 0.81 us -> none  [body(): jnp.transpose(chosen, (0, 2, 1))[:, None, :, :]]
    lt x1 -> x0, other arithmetic: 0.76 us -> none  [body(): sample_times[None, None, :] < counts[:, None, None]]
    rev x1 -> x0, local copies, waits for them, and re-layouts: 0.75 us -> none  [body(): taps[::-1]]
    dynamic_update_slice x0 -> x4, local copies, waits for them, and re-layouts: none -> 0.67 us  [body(): stacked = lax.dynamic_update_slice_in_dim(stacked, part, place, 1)]
    ppermute x2, starting transfers between devices: 6.88 us -> 6.25 us  [from_behind(): return lax.ppermute(block, axis, route)]
  transfers between devices with their start and end apart: 8 -> 8, of which waited for: 3 -> 3; matrix products, arithmetic and copies ran while one was open for 24% -> 20% of each run, Pallas kernels for 0% -> 0%
where the time goes in v8:
time: 43.8 us; the launch traced here: 43.5 us
  starting transfers between devices  23.9 us (55%)
  local copies, waits for them, and re-layouts  10.9 us (25%)
  Pallas kernels  3.97 us (9%)
  waiting for transfers between devices  1.99 us (5%)
  other arithmetic  1.7 us (4%)
  between operations  0.59 us (1%)
  matrix products  0.46 us (1%)
    ppermute x2, starting transfers between devices, from_behind(): return lax.ppermute(block, axis, route)  6.25 us
    ppermute x3, starting transfers between devices, body(): pieces.append(lax.ppermute(part, 'corr', route))  6.25 us
    all_to_all x1, starting transfers between devices, body(): lax.all_to_all(copies, 'corr', 0, 0, tiled=True)  5.94 us
    ppermute x2, starting transfers between devices, body(): received.append(lax.ppermute(part, ('corr', 'filt'), route))  5.45 us
    pallas_call x1, Pallas kernels, correlate(): pl.pallas_call(functools.partial(corr_kernel, row_block=row_block, tile=t...  3.97 us
    another operation x1, local copies, waits for them, and re-layouts, body(): weights = full.reshape(count, JP, chunks, row_block).transpose(0, 2, 1, 3...  2.76 us
    unnamed x19, local copies, waits for them, and re-layouts  2.15 us
    ppermute x3, waiting for transfers between devices, body(): pieces.append(lax.ppermute(part, 'corr', route))  1.98 us
  transfers between devices with their start and end apart: 8, of which 3 were waited for; matrix products, arithmetic and copies ran while one was open for 20% of the time, Pallas kernels for 0%

profile of v8, /device:TPU:0, one launch (start us, length us, event | category | flops | bytes accessed | tf_op | source)
XLA Modules:
  0.0 43.5 jit_solution(8537380593276669033)
XLA Ops:
  0.0 1.4 %copy.19 = bf16[1,16,3,4096]{3,2,1,0:T(4,128)(2,1)S(1)} copy(bf16[1,16,3,4096]{3,1,2,0:T(8,128)(2,1)} %param.5) | data formatting | bytes 786432 | tf_op args[0]
  1.4 0.3 reshape_squeeze.3
  1.7 0.7 %broadcast_in_dim.68 = s32[16,3]{1,0:T(8,128)S(1)} broadcast(s32[16]{0:T(128)} %bitcast.83), dimensions={0} | broadcast | bytes 256 | tf_op jit(solution)/shard_map/broadcast_in_dim | solution.py:100
  2.7 5.0 %collective-permute-start = (bf16[48,128]{1,0:T(8,128)(2,1)S(1)}, bf16[48,128]{1,0:T(8,128)(2,1)S(1)}, u32[]{:S(2)}, u32[]{:S(2)}) collective-permute-start(bf16[48,128]{1,0:T(8,128)(2,1)S(1)} %slice.120), channel_id=1, source_target_pairs={{0,4},{4,8},{8,12},{1,5},{5,9},{9,13},{2,6},{6,10},{10,14},{3,7},{... | collective-permute-start | bytes 36872 | tf_op jit(solution)/shard_map/ppermute | solution.py:21
  7.7 1.3 %collective-permute-start.1 = (bf16[48,512]{1,0:T(8,128)(2,1)S(1)}, bf16[48,512]{1,0:T(8,128)(2,1)S(1)}, u32[]{:S(2)}, u32[]{:S(2)}) collective-permute-start(bf16[48,512]{1,0:T(8,128)(2,1)S(1)} %slice.128), channel_id=1, source_target_pairs={{4,0},{8,4},{12,8},{5,1},{9,5},{13,9},{6,2},{10,6},{14,10},{7,3},{... | collective-permute-start | bytes 147464 | tf_op jit(solution)/shard_map/ppermute | solution.py:21
  9.0 0.6 %broadcast_in_dim.72 = bf16[4,32,256]{2,1,0:T(8,128)(2,1)} broadcast(bf16[32,256]{1,0:T(8,128)(2,1)S(1)} %concatenate.23), dimensions={1,2} | broadcast | bytes 81920 | tf_op jit(solution)/shard_map/broadcast_in_dim | solution.py:152
  9.7 5.9 %all-to-all-start = ((bf16[4,32,256]{2,1,0:T(8,128)(2,1)}), bf16[4,32,256]{2,1,0:T(8,128)(2,1)S(1)}, u32[]{:S(2)}, u32[]{:S(2)}) async-start(bf16[4,32,256]{2,1,0:T(8,128)(2,1)} %broadcast_in_dim.72), calls=%async_computation | async-start | bytes 131072 | tf_op jit(solution)/shard_map/all_to_all | solution.py:153
  15.8 0.5 %gather_fusion = s32[2,128,3,16]{1,3,2,0:T(8,128)S(1)} fusion(s32[128,3,2,16]{0,3,2,1:T(8,128)S(1)} %bitcast.77, s32[1024]{0:T(1024)S(1)} %pad_clamp_fusion), kind=kCustom, calls=%fused_computation | custom fusion | bytes 98312 | tf_op jit(solution)/shard_map/jit(_take)/gather | solution.py:162
  16.8 0.4 tile.10
  18.0 0.3 convolution_convert_fusion
  18.6 0.7 %collective-permute-start.2 = (bf16[48,640]{1,0:T(8,128)(2,1)S(1)}, bf16[48,640]{1,0:T(8,128)(2,1)S(1)}, u32[]{:S(2)}, u32[]{:S(2)}) collective-permute-start(bf16[48,640]{1,0:T(8,128)(2,1)S(1)} %get-tuple-element.11), channel_id=1, source_target_pairs={{0,0},{2,4},{4,8},{6,12},{8,2},{10,6},{12,10},{14,14},{1,1},{3,5},... | collective-permute-start | bytes 184328 | tf_op jit(solution)/shard_map/ppermute | solution.py:138
  19.3 4.8 %collective-permute-start.3 = (bf16[48,640]{1,0:T(8,128)(2,1)S(1)}, bf16[48,640]{1,0:T(8,128)(2,1)S(1)}, u32[]{:S(2)}, u32[]{:S(2)}) collective-permute-start(bf16[48,640]{1,0:T(8,128)(2,1)S(1)} %get-tuple-element.10), channel_id=1, source_target_pairs={{0,4},{2,0},{4,12},{6,8},{8,6},{10,2},{12,14},{14,10},{1,5},{3,1},... | collective-permute-start | bytes 184328 | tf_op jit(solution)/shard_map/ppermute | solution.py:138
  24.3 0.4 fusion
  24.6 0.5 %copy.27 = bf16[128,75,96]{0,2,1:T(8,128)(2,1)S(1)} copy(bf16[128,75,96]{0,1,2:T(8,128)(2,1)S(1)} %fusion) | data formatting | bytes 3686400
  25.1 1.4 %concatenate.24.clone = bf16[128,76,96]{0,2,1:T(8,128)(2,1)} pad(bf16[128,75,96]{0,2,1:T(8,128)(2,1)S(1)} %copy.27, bf16[]{:T(256)} %constant.107.clone.1), padding=0_0x0_1x0_0 | pad | bytes 3710978 | tf_op jit(solution)/shard_map/concatenate | solution.py:166
  26.5 2.8 %copy.25.w_ref = bf16[128,7296]{1,0:T(8,128)(2,1)S(1)} copy(bf16[128,7296]{0,1:T(8,128)(2,1)} %bitcast.79) | data formatting | bytes 3735552 | tf_op jit(solution)/shard_map/reshape;transpose;reshape | solution.py:173
  30.4 4.0 %shard_map.55 = f32[128,512]{1,0:T(8,128)S(1)} custom-call(bf16[1,96,640]{2,1,0:T(8,128)(2,1)S(1)} %bitcast.78, f32[96,512]{1,0:T(8,128)S(1)} %fusion.3.inv_ref, bf16[128,7296]{1,0:T(8,128)(2,1)S(1)} %copy.25.w_ref), custom_call_target="tpu_custom_call" | custom-call | tf_op jit(solution)/shard_map/pallas_call | solution.py:72
  34.4 2.4 %collective-permute-start.4 = (f32[32,512]{1,0:T(8,128)S(1)}, f32[32,512]{1,0:T(8,128)S(1)}, u32[]{:S(2)}, u32[]{:S(2)}) collective-permute-start(f32[32,512]{1,0:T(8,128)S(1)} %get-tuple-element.7), channel_id=1, source_target_pairs={{0,4},{4,8},{8,12},{12,0},{1,5},{5,9},{9,13},{13,1},{2,6},{6,10},{... | collective-permute-start | bytes 196616 | tf_op jit(solution)/shard_map/ppermute | solution.py:181
  36.9 1.0 %collective-permute-start.5 = (f32[32,512]{1,0:T(8,128)S(1)}, f32[32,512]{1,0:T(8,128)S(1)}, u32[]{:S(2)}, u32[]{:S(2)}) collective-permute-start(f32[32,512]{1,0:T(8,128)S(1)} %get-tuple-element.6), channel_id=1, source_target_pairs={{0,8},{4,12},{8,0},{12,4},{1,9},{5,13},{9,1},{13,5},{2,10},{6,14},... | collective-permute-start | bytes 196616 | tf_op jit(solution)/shard_map/ppermute | solution.py:181
  37.8 2.8 %collective-permute-start.6 = (f32[32,512]{1,0:T(8,128)S(1)}, f32[32,512]{1,0:T(8,128)S(1)}, u32[]{:S(2)}, u32[]{:S(2)}) collective-permute-start(f32[32,512]{1,0:T(8,128)S(1)} %get-tuple-element.5), channel_id=1, source_target_pairs={{0,12},{4,0},{8,4},{12,8},{1,13},{5,1},{9,5},{13,9},{2,14},{6,2},{... | collective-permute-start | bytes 196616 | tf_op jit(solution)/shard_map/ppermute | solution.py:181
  40.7 0.5 %collective-permute-done.4 = f32[32,512]{1,0:T(8,128)S(1)} collective-permute-done((f32[32,512]{1,0:T(8,128)S(1)}, f32[32,512]{1,0:T(8,128)S(1)}, u32[]{:S(2)}, u32[]{:S(2)}) %collective-permute-start.4) | collective-permute-done | bytes 65568 | tf_op jit(solution)/shard_map/ppermute | solution.py:181
  41.2 0.9 %collective-permute-done.5 = f32[32,512]{1,0:T(8,128)S(1)} collective-permute-done((f32[32,512]{1,0:T(8,128)S(1)}, f32[32,512]{1,0:T(8,128)S(1)}, u32[]{:S(2)}, u32[]{:S(2)}) %collective-permute-start.5) | collective-permute-done | bytes 65568 | tf_op jit(solution)/shard_map/ppermute | solution.py:181
  42.1 0.6 %collective-permute-done.6 = f32[32,512]{1,0:T(8,128)S(1)} collective-permute-done((f32[32,512]{1,0:T(8,128)S(1)}, f32[32,512]{1,0:T(8,128)S(1)}, u32[]{:S(2)}, u32[]{:S(2)}) %collective-permute-start.6) | collective-permute-done | bytes 65568 | tf_op jit(solution)/shard_map/ppermute | solution.py:181
  42.8 0.6 %bitcast_dynamic-update-slice_fusion = f32[1,32,2048]{2,1,0:T(8,128)} fusion(f32[1,32,2048]{2,1,0:T(8,128)} %copy-done.1, s32[]{:T(128)S(6)} %select_n.140, f32[32,512]{1,0:T(8,128)S(1)} %collective-permute-done.6), kind=kLoop, calls=%fused_computation.22 | loop fusion | bytes 131076 | tf_op jit(solution)/shard_map/dynamic_update_slice | solution.py:185
  (70 shorter events, 3.1 us)
Async XLA Ops:
  0.0 15.8 %copy-start = (s32[128,3,32]{0,2,1:T(8,128)S(1)}, s32[128,3,32]{0,2,1:T(8,128)}, u32[]{:S(2)}) copy-start(s32[128,3,32]{0,2,1:T(8,128)} %param.9) | copy-start | bytes 147460
  0.0 9.0 %copy-start.2 = (bf16[32,225]{1,0:T(8,128)(2,1)S(1)}, bf16[32,225]{1,0:T(8,128)(2,1)}, u32[]{:S(2)}) copy-start(bf16[32,225]{1,0:T(8,128)(2,1)} %param.8) | copy-start | bytes 43204
  0.0 15.6 %copy-start.3 = (bf16[64]{0:T(256)(128)(2,1)S(1)}, bf16[64]{0:T(256)(128)(2,1)}, u32[]{:S(2)}) copy-start(bf16[64]{0:T(256)(128)(2,1)} %param.7) | copy-start | bytes 388
  2.7 14.7 %collective-permute-start = (bf16[48,128]{1,0:T(8,128)(2,1)S(1)}, bf16[48,128]{1,0:T(8,128)(2,1)S(1)}, u32[]{:S(2)}, u32[]{:S(2)}) collective-permute-start(bf16[48,128]{1,0:T(8,128)(2,1)S(1)} %slice.120), channel_id=1, source_target_pairs={{0,4},{4,8},{8,12},{1,5},{5,9},{9,13},{2,6},{6,10},{10,14},{3,7},{... | collective-permute-start | bytes 36872 | tf_op jit(solution)/shard_map/ppermute | solution.py:21
  7.7 9.9 %collective-permute-start.1 = (bf16[48,512]{1,0:T(8,128)(2,1)S(1)}, bf16[48,512]{1,0:T(8,128)(2,1)S(1)}, u32[]{:S(2)}, u32[]{:S(2)}) collective-permute-start(bf16[48,512]{1,0:T(8,128)(2,1)S(1)} %slice.128), channel_id=1, source_target_pairs={{4,0},{8,4},{12,8},{5,1},{9,5},{13,9},{6,2},{10,6},{14,10},{7,3},{... | collective-permute-start | bytes 147464 | tf_op jit(solution)/shard_map/ppermute | solution.py:21
  9.7 14.4 %all-to-all-start = ((bf16[4,32,256]{2,1,0:T(8,128)(2,1)}), bf16[4,32,256]{2,1,0:T(8,128)(2,1)S(1)}, u32[]{:S(2)}, u32[]{:S(2)}) async-start(bf16[4,32,256]{2,1,0:T(8,128)(2,1)} %broadcast_in_dim.72), calls=%async_computation | async-start | bytes 131072 | tf_op jit(solution)/shard_map/all_to_all | solution.py:153
  18.6 10.7 %collective-permute-start.2 = (bf16[48,640]{1,0:T(8,128)(2,1)S(1)}, bf16[48,640]{1,0:T(8,128)(2,1)S(1)}, u32[]{:S(2)}, u32[]{:S(2)}) collective-permute-start(bf16[48,640]{1,0:T(8,128)(2,1)S(1)} %get-tuple-element.11), channel_id=1, source_target_pairs={{0,0},{2,4},{4,8},{6,12},{8,2},{10,6},{12,10},{14,14},{1,1},{3,5},... | collective-permute-start | bytes 184328 | tf_op jit(solution)/shard_map/ppermute | solution.py:138
  19.3 10.1 %collective-permute-start.3 = (bf16[48,640]{1,0:T(8,128)(2,1)S(1)}, bf16[48,640]{1,0:T(8,128)(2,1)S(1)}, u32[]{:S(2)}, u32[]{:S(2)}) collective-permute-start(bf16[48,640]{1,0:T(8,128)(2,1)S(1)} %get-tuple-element.10), channel_id=1, source_target_pairs={{0,4},{2,0},{4,12},{6,8},{8,6},{10,2},{12,14},{14,10},{1,5},{3,1},... | collective-permute-start | bytes 184328 | tf_op jit(solution)/shard_map/ppermute | solution.py:138
  34.4 6.8 %collective-permute-start.4 = (f32[32,512]{1,0:T(8,128)S(1)}, f32[32,512]{1,0:T(8,128)S(1)}, u32[]{:S(2)}, u32[]{:S(2)}) collective-permute-start(f32[32,512]{1,0:T(8,128)S(1)} %get-tuple-element.7), channel_id=1, source_target_pairs={{0,4},{4,8},{8,12},{12,0},{1,5},{5,9},{9,13},{13,1},{2,6},{6,10},{... | collective-permute-start | bytes 196616 | tf_op jit(solution)/shard_map/ppermute | solution.py:181
  36.9 5.2 %collective-permute-start.5 = (f32[32,512]{1,0:T(8,128)S(1)}, f32[32,512]{1,0:T(8,128)S(1)}, u32[]{:S(2)}, u32[]{:S(2)}) collective-permute-start(f32[32,512]{1,0:T(8,128)S(1)} %get-tuple-element.6), channel_id=1, source_target_pairs={{0,8},{4,12},{8,0},{12,4},{1,9},{5,13},{9,1},{13,5},{2,10},{6,14},... | collective-permute-start | bytes 196616 | tf_op jit(solution)/shard_map/ppermute | solution.py:181
  37.8 4.9 %collective-permute-start.6 = (f32[32,512]{1,0:T(8,128)S(1)}, f32[32,512]{1,0:T(8,128)S(1)}, u32[]{:S(2)}, u32[]{:S(2)}) collective-permute-start(f32[32,512]{1,0:T(8,128)S(1)} %get-tuple-element.5), channel_id=1, source_target_pairs={{0,12},{4,0},{8,4},{12,8},{1,13},{5,1},{9,5},{13,9},{2,14},{6,2},{... | collective-permute-start | bytes 196616 | tf_op jit(solution)/shard_map/ppermute | solution.py:181
  42.1 0.7 %copy-start.1 = (f32[1,32,2048]{2,1,0:T(8,128)}, f32[1,32,2048]{2,1,0:T(8,128)S(1)}, u32[]{:S(2)}) copy-start(f32[1,32,2048]{2,1,0:T(8,128)S(1)} %bitcast_dynamic-update-slice_fusion.1) | copy-start | bytes 786436

commit v9 on v8

--- a/solution.py
+++ b/solution.py
@@ -96,17 +96,19 @@
     filt_place = lax.axis_index("filt")
     filt_count = lax.axis_size("filt")
     sample_times = corr_place * raw_width + lax.iota(jnp.int32, raw_width)
-    dense = samples.reshape(local_stations * 3, raw_width)
-    row_counts = jnp.repeat(counts, 3)
-    live = jnp.where(sample_times[None, :] < row_counts[:, None], dense, jnp.zeros_like(dense))
-    history = from_behind(live[:, raw_width - 128 :], "corr", 1)
+    keep = sample_times[None, None, :] < counts[:, None, None]
+    zero = jnp.zeros((), samples.dtype)
+    own_tail = jnp.where(keep[:, :, raw_width - 128 :], samples[:, :, raw_width - 128 :], zero)
+    own_head = jnp.where(keep[:, :, :512], samples[:, :, :512], zero)
+    history = from_behind(own_tail, "corr", 1)
     corr_count = lax.axis_size("corr")
-    ahead = from_behind(live[:, :512], "corr", -1)
-    extended = jnp.concatenate([history, live, ahead], axis=1)
+    ahead = from_behind(own_head, "corr", -1)
+    live = jnp.where(keep, samples, zero)
+    extended = jnp.concatenate([history, live, ahead], axis=2)
     decimated = raw_width // DEC
     blocks = decimated // 128 + 1
     frames = jnp.stack(
-        [extended[:, 512 * a : 512 * a + 640] for a in range(blocks)], axis=1
+        [extended[:, :, 512 * a : 512 * a + 640] for a in range(blocks)], axis=2
     ).reshape(local_stations * 3 * blocks, 640)
     flip = (lax.iota(jnp.int32, TAPS)[:, None] + lax.iota(jnp.int32, TAPS)[None, :] == TAPS - 1)
     reversed_taps = jnp.dot(
@@ -159,7 +161,11 @@
     norms = jnp.sqrt(jnp.sum(shaped * shaped, axis=2) + 1e-06)
     base = shaped / norms[:, :, None]
     arrival = (corr_place - lax.iota(jnp.int32, filt_count)) % filt_count
-    chosen = jnp.take(masks.reshape(count, 3, filt_count, stations // filt_count), arrival, axis=2)
+    blocked = masks.reshape(count, 3, filt_count, stations // filt_count)
+    chosen = jnp.zeros_like(blocked)
+    for k in range(filt_count):
+        for g in range(filt_count):
+            chosen = chosen.at[:, :, k].add(jnp.where(arrival[k] == g, blocked[:, :, g], 0))
     chosen = chosen.reshape(count, 3, stations).astype(jnp.float32)
     full = jnp.transpose(base, (0, 2, 1))[:, :, None, :] * jnp.transpose(chosen, (0, 2, 1))[:, None, :, :]
     full = full.astype(jnp.bfloat16).reshape(count, L, stations * 3)

time: 43.8 us -> 51.7 us (1.18)
  other arithmetic: 1.7 us -> 8.55 us
  between operations: 0.59 us -> 3.08 us
  local copies, waits for them, and re-layouts: 10.9 us -> 8.98 us
    select_n x2 -> x5, other arithmetic: 0.18 us -> 3.32 us  [the longest x1 1.04 us: body(): live = jnp.where(keep, samples, zero)]
    scatter-add x0 -> x3, other arithmetic: none -> 2.28 us  [body(): chosen.at[:, :, k].add(jnp.where(arrival[k] == g, blocked[:, :, g], 0))]
    lt x0 -> x2, other arithmetic: none -> 1.53 us  [body(): keep = sample_times[None, None, :] < counts[:, None, None]]
    unnamed x19 -> x15, local copies, waits for them, and re-layouts: 2.15 us -> 0.79 us
    broadcast_in_dim x3 -> x2, local copies, waits for them, and re-layouts: 0.89 us -> 0.01 us  [the longest x1 0.01 us: body(): own_head = jnp.where(keep[:, :, :512], samples[:, :, :512], zero)]
    concatenate x1, local copies, waits for them, and re-layouts: 0.01 us -> 0.73 us  [body(): jnp.concatenate([templates, jnp.zeros((local_count, lanes - template_widt...]
    slice x2 -> x1, local copies, waits for them, and re-layouts: 0.01 us -> 0.61 us  [body(): arrival[k] == g]
    gather x2 -> x0, local copies, waits for them, and re-layouts: 0.55 us -> none  [body(): jnp.take(masks.reshape(count, 3, filt_count, stations // filt_count), arr...]
  transfers between devices with their start and end apart: 8 -> 8, of which waited for: 3 -> 3; matrix products, arithmetic and copies ran while one was open for 20% -> 29% of each run, Pallas kernels for 0% -> 0%
where the time goes in v9:
time: 51.7 us; the launch traced here: 50.9 us
  starting transfers between devices  23.8 us (46%)
  local copies, waits for them, and re-layouts  8.98 us (17%)
  other arithmetic  8.55 us (17%)
  Pallas kernels  3.98 us (8%)
  between operations  3.08 us (6%)
  waiting for transfers between devices  2 us (4%)
    ppermute x3, starting transfers between devices, body(): pieces.append(lax.ppermute(part, 'corr', route))  6.23 us
    ppermute x2, starting transfers between devices, from_behind(): return lax.ppermute(block, axis, route)  6.22 us
    all_to_all x1, starting transfers between devices, body(): lax.all_to_all(copies, 'corr', 0, 0, tiled=True)  5.94 us
    ppermute x2, starting transfers between devices, body(): received.append(lax.ppermute(part, ('corr', 'filt'), route))  5.45 us
    pallas_call x1, Pallas kernels, correlate(): pl.pallas_call(functools.partial(corr_kernel, row_block=row_block, tile=t...  3.98 us
    another operation x1, local copies, waits for them, and re-layouts, body(): weights = full.reshape(count, JP, chunks, row_block).transpose(0, 2, 1, 3...  2.76 us
    scatter-add x3, other arithmetic, body(): chosen.at[:, :, k].add(jnp.where(arrival[k] == g, blocked[:, :, g], 0))  2.28 us
    ppermute x3, waiting for transfers between devices, body(): pieces.append(lax.ppermute(part, 'corr', route))  1.99 us
  transfers between devices with their start and end apart: 8, of which 3 were waited for; matrix products, arithmetic and copies ran while one was open for 29% of the time, Pallas kernels for 0%

profile of v9, /device:TPU:0, one launch (start us, length us, event | category | flops | bytes accessed | tf_op | source)
XLA Modules:
  0.0 50.9 jit_solution(3841087419877867458)
XLA Ops:
  0.0 0.8 %broadcast_compare_fusion.1 = pred[16,1,4096]{2,0,1:T(8,128)(4,1)S(1)} fusion(s32[4096]{0:T(1024)S(1)} %iota_add_fusion, s32[16]{0:T(128)} %bitcast.92), kind=kLoop, calls=%fused_computation.19 | loop fusion | flops 65536 | bytes 81984 | tf_op jit(solution)/shard_map/lt | solution.py:99
  0.8 0.7 %slice_select_fusion.2 = bf16[16,3,128]{2,0,1:T(8,128)(2,1)S(1)} fusion(bf16[16,3,4096]{2,0,1:T(8,128)(2,1)} %bitcast.84, pred[16,128]{1,0:T(8,128)(4,1)S(1)} %slice_bitcast_fusion.8), kind=kLoop, calls=%fused_computation.58 | loop fusion | flops 6144 | bytes 26624 | tf_op jit(solution)/shard_map/jit(_where)/select_n | solution.py:101
  1.5 4.9 %collective-permute-start = (bf16[16,3,128]{2,0,1:T(8,128)(2,1)S(1)}, bf16[16,3,128]{2,0,1:T(8,128)(2,1)S(1)}, u32[]{:S(2)}, u32[]{:S(2)}) collective-permute-start(bf16[16,3,128]{2,0,1:T(8,128)(2,1)S(1)} %slice_select_fusion.2), channel_id=1, source_target_pairs={{0,4},{4,8},{8,12},{1,5},{5,9},{9,13},{2,6},{6,10},{10,14},{3,7},{... | collective-permute-start | bytes 36872 | tf_op jit(solution)/shard_map/ppermute | solution.py:21
  6.5 0.8 %slice_select_fusion = bf16[16,3,512]{2,0,1:T(8,128)(2,1)S(1)} fusion(bf16[16,3,4096]{2,0,1:T(8,128)(2,1)} %bitcast.85, pred[16,512]{1,0:T(8,128)(4,1)S(1)} %slice_bitcast_fusion.7), kind=kLoop, calls=%fused_computation.47 | loop fusion | flops 24576 | bytes 106496 | tf_op jit(solution)/shard_map/jit(_where)/select_n | solution.py:102
  7.3 1.3 %collective-permute-start.1 = (bf16[16,3,512]{2,0,1:T(8,128)(2,1)S(1)}, bf16[16,3,512]{2,0,1:T(8,128)(2,1)S(1)}, u32[]{:S(2)}, u32[]{:S(2)}) collective-permute-start(bf16[16,3,512]{2,0,1:T(8,128)(2,1)S(1)} %slice_select_fusion), channel_id=1, source_target_pairs={{4,0},{8,4},{12,8},{5,1},{9,5},{13,9},{6,2},{10,6},{14,10},{7,3},{... | collective-permute-start | bytes 147464 | tf_op jit(solution)/shard_map/ppermute | solution.py:21
  8.6 0.7 %concatenate.31 = bf16[32,256]{1,0:T(8,128)(2,1)S(1)} pad(bf16[32,225]{1,0:T(8,128)(2,1)} %param.16, bf16[]{:T(256)} %constant.190.clone.1), padding=0_0x0_31 | pad | bytes 30786 | tf_op jit(solution)/shard_map/concatenate | solution.py:151
  9.3 0.6 %broadcast_in_dim.106 = bf16[4,32,256]{2,1,0:T(8,128)(2,1)} broadcast(bf16[32,256]{1,0:T(8,128)(2,1)S(1)} %concatenate.31), dimensions={1,2} | broadcast | bytes 81920 | tf_op jit(solution)/shard_map/broadcast_in_dim | solution.py:154
  9.9 5.9 %all-to-all-start = ((bf16[4,32,256]{2,1,0:T(8,128)(2,1)}), bf16[4,32,256]{2,1,0:T(8,128)(2,1)S(1)}, u32[]{:S(2)}, u32[]{:S(2)}) async-start(bf16[4,32,256]{2,1,0:T(8,128)(2,1)} %broadcast_in_dim.106), calls=%async_computation | async-start | bytes 131072 | tf_op jit(solution)/shard_map/all_to_all | solution.py:155
  15.9 0.8 %broadcast_compare_fusion = pred[16,4096]{1,0:T(8,128)(4,1)S(1)} fusion(s32[4096]{0:T(1024)S(1)} %iota_add_fusion, s32[16]{0:T(128)} %bitcast.93), kind=kLoop, calls=%fused_computation.18 | loop fusion | flops 65536 | bytes 81984 | tf_op jit(solution)/shard_map/lt | solution.py:99
  19.8 1.0 %broadcast_select_fusion = bf16[16,3,4096]{2,0,1:T(8,128)(2,1)S(1)} fusion(pred[16,4096]{1,0:T(8,128)(4,1)S(1)} %broadcast_compare_fusion, bf16[1,16,3,4096]{3,1,2,0:T(8,128)(2,1)} %param.13), kind=kLoop, calls=%fused_computation.5 | loop fusion | flops 196608 | bytes 851968 | tf_op jit(solution)/shard_map/jit(_where)/select_n | solution.py:106
  21.0 0.7 %slice_select_fusion.1 = s32[128,3,1,16]{0,3,2,1:T(8,128)S(1)} fusion(s32[128,3,2,16]{0,3,2,1:T(8,128)} %bitcast.86, pred[]{:T(512)} %bitcast.19), kind=kLoop, calls=%fused_computation.55 | loop fusion | flops 6144 | bytes 49153 | tf_op jit(solution)/shard_map/jit(_where)/select_n | solution.py:168
  21.7 0.8 %add_dynamic-update-slice_fusion.1 = s32[128,3,2,16]{0,3,2,1:T(8,128)S(1)} fusion(s32[128,3,2,16]{0,3,2,1:T(8,128)S(1)} %scatter-add.14, s32[128,3,2,16]{0,3,2,1:T(8,128)} %bitcast.87, pred[]{:T(512)} %bitcast.21, pred[]{:T(512)} %bitcast.19), kind=kLoop, calls=%fused_computation.52 | loop fusion | flops 18432 | bytes 73730 | tf_op jit(solution)/shard_map/scatter-add | solution.py:168
  22.5 0.8 %fusion.17 = s32[128,3,2,16]{0,3,2,1:T(8,128)S(1)} fusion(s32[128,3,2,16]{0,3,2,1:T(8,128)S(1)} %copy.34, s32[128,3,2,16]{0,3,2,1:T(8,128)} %bitcast.88, pred[]{:T(512)} %bitcast.22), kind=kLoop, calls=%fused_computation.62 | loop fusion | flops 12288 | bytes 73729 | tf_op jit(solution)/shard_map/scatter-add | solution.py:168
  23.2 0.8 %add_dynamic-update-slice_fusion = s32[128,3,2,16]{0,3,2,1:T(8,128)S(1)} fusion(s32[128,3,2,16]{0,3,2,1:T(8,128)S(1)} %fusion.17, s32[128,3,2,16]{0,3,2,1:T(8,128)} %bitcast.89, pred[]{:T(512)} %bitcast.23, pred[]{:T(512)} %bitcast.22, s32[128,3,2,16]{0,3,2,1:T(8,128)S(1)} %add_dynamic-update-slice_fusion.1), kind=kLoop, calls=%fused_computation.51 | loop fusion | flops 24576 | bytes 98306 | tf_op jit(solution)/shard_map/scatter-add | solution.py:168
  26.0 0.7 %collective-permute-start.2 = (bf16[48,640]{1,0:T(8,128)(2,1)S(1)}, bf16[48,640]{1,0:T(8,128)(2,1)S(1)}, u32[]{:S(2)}, u32[]{:S(2)}) collective-permute-start(bf16[48,640]{1,0:T(8,128)(2,1)S(1)} %get-tuple-element.59), channel_id=1, source_target_pairs={{0,0},{2,4},{4,8},{6,12},{8,2},{10,6},{12,10},{14,14},{1,1},{3,5},... | collective-permute-start | bytes 184328 | tf_op jit(solution)/shard_map/ppermute | solution.py:140
  26.7 4.8 %collective-permute-start.3 = (bf16[48,640]{1,0:T(8,128)(2,1)S(1)}, bf16[48,640]{1,0:T(8,128)(2,1)S(1)}, u32[]{:S(2)}, u32[]{:S(2)}) collective-permute-start(bf16[48,640]{1,0:T(8,128)(2,1)S(1)} %get-tuple-element.58), channel_id=1, source_target_pairs={{0,4},{2,0},{4,12},{6,8},{8,6},{10,2},{12,14},{14,10},{1,5},{3,1},... | collective-permute-start | bytes 184328 | tf_op jit(solution)/shard_map/ppermute | solution.py:140
  32.5 1.4 %concatenate.32.clone = bf16[128,76,96]{0,2,1:T(8,128)(2,1)} pad(bf16[128,75,96]{0,2,1:T(8,128)(2,1)S(1)} %copy.23, bf16[]{:T(256)} %constant.190.clone.1), padding=0_0x0_1x0_0 | pad | bytes 3710978 | tf_op jit(solution)/shard_map/concatenate | solution.py:172
  34.0 2.8 %copy.21.w_ref = bf16[128,7296]{1,0:T(8,128)(2,1)S(1)} copy(bf16[128,7296]{0,1:T(8,128)(2,1)} %bitcast.83) | data formatting | bytes 3735552 | tf_op jit(solution)/shard_map/reshape;transpose;reshape | solution.py:179
  37.8 4.0 %shard_map.55 = f32[128,512]{1,0:T(8,128)S(1)} custom-call(bf16[1,96,640]{2,1,0:T(8,128)(2,1)S(1)} %bitcast.82, f32[96,512]{1,0:T(8,128)S(1)} %fusion.3.inv_ref, bf16[128,7296]{1,0:T(8,128)(2,1)S(1)} %copy.21.w_ref), custom_call_target="tpu_custom_call" | custom-call | tf_op jit(solution)/shard_map/pallas_call | solution.py:72
  41.9 2.4 %collective-permute-start.4 = (f32[32,512]{1,0:T(8,128)S(1)}, f32[32,512]{1,0:T(8,128)S(1)}, u32[]{:S(2)}, u32[]{:S(2)}) collective-permute-start(f32[32,512]{1,0:T(8,128)S(1)} %get-tuple-element.55), channel_id=1, source_target_pairs={{0,4},{4,8},{8,12},{12,0},{1,5},{5,9},{9,13},{13,1},{2,6},{6,10},{... | collective-permute-start | bytes 196616 | tf_op jit(solution)/shard_map/ppermute | solution.py:187
  44.3 0.9 %collective-permute-start.5 = (f32[32,512]{1,0:T(8,128)S(1)}, f32[32,512]{1,0:T(8,128)S(1)}, u32[]{:S(2)}, u32[]{:S(2)}) collective-permute-start(f32[32,512]{1,0:T(8,128)S(1)} %get-tuple-element.54), channel_id=1, source_target_pairs={{0,8},{4,12},{8,0},{12,4},{1,9},{5,13},{9,1},{13,5},{2,10},{6,14},... | collective-permute-start | bytes 196616 | tf_op jit(solution)/shard_map/ppermute | solution.py:187
  45.3 2.8 %collective-permute-start.6 = (f32[32,512]{1,0:T(8,128)S(1)}, f32[32,512]{1,0:T(8,128)S(1)}, u32[]{:S(2)}, u32[]{:S(2)}) collective-permute-start(f32[32,512]{1,0:T(8,128)S(1)} %get-tuple-element.53), channel_id=1, source_target_pairs={{0,12},{4,0},{8,4},{12,8},{1,13},{5,1},{9,5},{13,9},{2,14},{6,2},{... | collective-permute-start | bytes 196616 | tf_op jit(solution)/shard_map/ppermute | solution.py:187
  48.7 0.9 %collective-permute-done.5 = f32[32,512]{1,0:T(8,128)S(1)} collective-permute-done((f32[32,512]{1,0:T(8,128)S(1)}, f32[32,512]{1,0:T(8,128)S(1)}, u32[]{:S(2)}, u32[]{:S(2)}) %collective-permute-start.5) | collective-permute-done | bytes 65568 | tf_op jit(solution)/shard_map/ppermute | solution.py:187
  50.3 0.6 %bitcast_dynamic-update-slice_fusion = f32[1,32,2048]{2,1,0:T(8,128)} fusion(f32[1,32,2048]{2,1,0:T(8,128)} %copy-done.1, s32[]{:T(128)S(6)} %select_n.151, f32[32,512]{1,0:T(8,128)S(1)} %collective-permute-done.6), kind=kLoop, calls=%fused_computation.23 | loop fusion | bytes 131076 | tf_op jit(solution)/shard_map/dynamic_update_slice | solution.py:191
  (67 shorter events, 5.8 us)
Async XLA Ops:
  0.0 20.8 %copy-start = (bf16[64]{0:T(256)(128)(2,1)S(1)}, bf16[64]{0:T(256)(128)(2,1)}, u32[]{:S(2)}) copy-start(bf16[64]{0:T(256)(128)(2,1)} %param.15) | copy-start | bytes 388
  1.5 23.4 %collective-permute-start = (bf16[16,3,128]{2,0,1:T(8,128)(2,1)S(1)}, bf16[16,3,128]{2,0,1:T(8,128)(2,1)S(1)}, u32[]{:S(2)}, u32[]{:S(2)}) collective-permute-start(bf16[16,3,128]{2,0,1:T(8,128)(2,1)S(1)} %slice_select_fusion.2), channel_id=1, source_target_pairs={{0,4},{4,8},{8,12},{1,5},{5,9},{9,13},{2,6},{6,10},{10,14},{3,7},{... | collective-permute-start | bytes 36872 | tf_op jit(solution)/shard_map/ppermute | solution.py:21
  7.3 17.7 %collective-permute-start.1 = (bf16[16,3,512]{2,0,1:T(8,128)(2,1)S(1)}, bf16[16,3,512]{2,0,1:T(8,128)(2,1)S(1)}, u32[]{:S(2)}, u32[]{:S(2)}) collective-permute-start(bf16[16,3,512]{2,0,1:T(8,128)(2,1)S(1)} %slice_select_fusion), channel_id=1, source_target_pairs={{4,0},{8,4},{12,8},{5,1},{9,5},{13,9},{6,2},{10,6},{14,10},{7,3},{... | collective-permute-start | bytes 147464 | tf_op jit(solution)/shard_map/ppermute | solution.py:21
  9.9 21.5 %all-to-all-start = ((bf16[4,32,256]{2,1,0:T(8,128)(2,1)}), bf16[4,32,256]{2,1,0:T(8,128)(2,1)S(1)}, u32[]{:S(2)}, u32[]{:S(2)}) async-start(bf16[4,32,256]{2,1,0:T(8,128)(2,1)} %broadcast_in_dim.106), calls=%async_computation | async-start | bytes 131072 | tf_op jit(solution)/shard_map/all_to_all | solution.py:155
  26.0 10.7 %collective-permute-start.2 = (bf16[48,640]{1,0:T(8,128)(2,1)S(1)}, bf16[48,640]{1,0:T(8,128)(2,1)S(1)}, u32[]{:S(2)}, u32[]{:S(2)}) collective-permute-start(bf16[48,640]{1,0:T(8,128)(2,1)S(1)} %get-tuple-element.59), channel_id=1, source_target_pairs={{0,0},{2,4},{4,8},{6,12},{8,2},{10,6},{12,10},{14,14},{1,1},{3,5},... | collective-permute-start | bytes 184328 | tf_op jit(solution)/shard_map/ppermute | solution.py:140
  26.7 10.1 %collective-permute-start.3 = (bf16[48,640]{1,0:T(8,128)(2,1)S(1)}, bf16[48,640]{1,0:T(8,128)(2,1)S(1)}, u32[]{:S(2)}, u32[]{:S(2)}) collective-permute-start(bf16[48,640]{1,0:T(8,128)(2,1)S(1)} %get-tuple-element.58), channel_id=1, source_target_pairs={{0,4},{2,0},{4,12},{6,8},{8,6},{10,2},{12,14},{14,10},{1,5},{3,1},... | collective-permute-start | bytes 184328 | tf_op jit(solution)/shard_map/ppermute | solution.py:140
  41.9 6.8 %collective-permute-start.4 = (f32[32,512]{1,0:T(8,128)S(1)}, f32[32,512]{1,0:T(8,128)S(1)}, u32[]{:S(2)}, u32[]{:S(2)}) collective-permute-start(f32[32,512]{1,0:T(8,128)S(1)} %get-tuple-element.55), channel_id=1, source_target_pairs={{0,4},{4,8},{8,12},{12,0},{1,5},{5,9},{9,13},{13,1},{2,6},{6,10},{... | collective-permute-start | bytes 196616 | tf_op jit(solution)/shard_map/ppermute | solution.py:187
  44.3 5.2 %collective-permute-start.5 = (f32[32,512]{1,0:T(8,128)S(1)}, f32[32,512]{1,0:T(8,128)S(1)}, u32[]{:S(2)}, u32[]{:S(2)}) collective-permute-start(f32[32,512]{1,0:T(8,128)S(1)} %get-tuple-element.54), channel_id=1, source_target_pairs={{0,8},{4,12},{8,0},{12,4},{1,9},{5,13},{9,1},{13,5},{2,10},{6,14},... | collective-permute-start | bytes 196616 | tf_op jit(solution)/shard_map/ppermute | solution.py:187
  45.3 4.9 %collective-permute-start.6 = (f32[32,512]{1,0:T(8,128)S(1)}, f32[32,512]{1,0:T(8,128)S(1)}, u32[]{:S(2)}, u32[]{:S(2)}) collective-permute-start(f32[32,512]{1,0:T(8,128)S(1)} %get-tuple-element.53), channel_id=1, source_target_pairs={{0,12},{4,0},{8,4},{12,8},{1,13},{5,1},{9,5},{13,9},{2,14},{6,2},{... | collective-permute-start | bytes 196616 | tf_op jit(solution)/shard_map/ppermute | solution.py:187
  49.6 0.7 %copy-start.1 = (f32[1,32,2048]{2,1,0:T(8,128)}, f32[1,32,2048]{2,1,0:T(8,128)S(1)}, u32[]{:S(2)}) copy-start(f32[1,32,2048]{2,1,0:T(8,128)S(1)} %bitcast_dynamic-update-slice_fusion.1) | copy-start | bytes 786436

commit v10 on v8

--- a/solution.py
+++ b/solution.py
@@ -149,10 +149,15 @@
     wide = jnp.concatenate(
         [templates, jnp.zeros((local_count, lanes - template_width), templates.dtype)], axis=1
     )
-    copies = jnp.broadcast_to(wide[None], (corr_count,) + wide.shape)
-    templates = lax.all_to_all(copies, "corr", 0, 0, tiled=True).reshape(
-        corr_count * local_count, lanes
-    )[:, :template_width]
+    arrived = [wide]
+    for d in range(1, corr_count):
+        route = [(i, (i + d) % corr_count) for i in range(corr_count)]
+        arrived.append(lax.ppermute(wide, "corr", route))
+    arrived = jnp.stack(arrived, axis=0)
+    order = (corr_place - lax.iota(jnp.int32, corr_count)) % corr_count
+    templates = jnp.take(arrived, order, axis=0).reshape(corr_count * local_count, lanes)[
+        :, :template_width
+    ]
     count = templates.shape[0]
     stations = masks.shape[2]
     shaped = templates.astype(jnp.float32).reshape(count, 3, L)

time: 43.8 us -> 46.9 us (1.071)
  waiting for transfers between devices: 1.99 us -> 6.99 us
  starting transfers between devices: 23.9 us -> 21.2 us
  local copies, waits for them, and re-layouts: 10.9 us -> 11.6 us
    ppermute x0 -> x3, starting transfers between devices: none -> 6.99 us  [body(): arrived.append(lax.ppermute(wide, 'corr', route))]
    all_to_all x1 -> x0, starting transfers between devices: 5.94 us -> none  [body(): lax.all_to_all(copies, 'corr', 0, 0, tiled=True)]
    ppermute x2, waiting for transfers between devices: 0.01 us -> 3.58 us  [body(): received.append(lax.ppermute(part, ('corr', 'filt'), route))]
    ppermute x2, starting transfers between devices: 6.25 us -> 3.87 us  [from_behind(): return lax.ppermute(block, axis, route)]
    ppermute x2, starting transfers between devices: 5.45 us -> 3.09 us  [body(): received.append(lax.ppermute(part, ('corr', 'filt'), route))]
    ppermute x2, waiting for transfers between devices: 0.01 us -> 1.61 us  [from_behind(): return lax.ppermute(block, axis, route)]
    ppermute x3, starting transfers between devices: 6.25 us -> 7.24 us  [body(): pieces.append(lax.ppermute(part, 'corr', route))]
    another operation x0 -> x1, local copies, waits for them, and re-layouts: none -> 0.75 us  [body(): arrived = jnp.stack(arrived, axis=0)]
  transfers between devices with their start and end apart: 8 -> 10, of which waited for: 3 -> 3; matrix products, arithmetic and copies ran while one was open for 20% -> 22% of each run, Pallas kernels for 0% -> 0%
where the time goes in v10:
time: 46.9 us; the launch traced here: 46.6 us
  starting transfers between devices  21.2 us (45%)
  local copies, waits for them, and re-layouts  11.6 us (25%)
  waiting for transfers between devices  6.99 us (15%)
  Pallas kernels  3.97 us (8%)
  other arithmetic  1.76 us (4%)
  between operations  0.68 us (1%)
    ppermute x3, starting transfers between devices, body(): pieces.append(lax.ppermute(part, 'corr', route))  7.24 us
    ppermute x3, starting transfers between devices, body(): arrived.append(lax.ppermute(wide, 'corr', route))  6.99 us
    pallas_call x1, Pallas kernels, correlate(): pl.pallas_call(functools.partial(corr_kernel, row_block=row_block, tile=t...  3.97 us
    ppermute x2, starting transfers between devices, from_behind(): return lax.ppermute(block, axis, route)  3.87 us
    ppermute x2, waiting for transfers between devices, body(): received.append(lax.ppermute(part, ('corr', 'filt'), route))  3.58 us
    ppermute x2, starting transfers between devices, body(): received.append(lax.ppermute(part, ('corr', 'filt'), route))  3.09 us
    another operation x1, local copies, waits for them, and re-layouts, body(): weights = full.reshape(count, JP, chunks, row_block).transpose(0, 2, 1, 3...  2.76 us
    unnamed x17, local copies, waits for them, and re-layouts  2.04 us
  transfers between devices with their start and end apart: 10, of which 3 were waited for; matrix products, arithmetic and copies ran while one was open for 22% of the time, Pallas kernels for 0%

profile of v10, /device:TPU:0, one launch (start us, length us, event | category | flops | bytes accessed | tf_op | source)
XLA Modules:
  0.0 46.6 jit_solution(15203136993383076026)
XLA Ops:
  0.0 0.7 %pad_bitcast_fusion = (bf16[1,32,256]{2,1,0:T(8,128)(2,1)S(1)}, bf16[32,256]{1,0:T(8,128)(2,1)S(1)}) fusion(bf16[32,225]{1,0:T(8,128)(2,1)} %param.8), kind=kLoop, calls=%fused_computation.93 | loop fusion | bytes 47168 | tf_op jit(solution)/shard_map/stack | solution.py:156
  0.8 3.1 %collective-permute-start.4 = (bf16[32,256]{1,0:T(8,128)(2,1)S(1)}, bf16[32,256]{1,0:T(8,128)(2,1)S(1)}, u32[]{:S(2)}, u32[]{:S(2)}) collective-permute-start(bf16[32,256]{1,0:T(8,128)(2,1)S(1)} %get-tuple-element.13), channel_id=1, source_target_pairs={{0,4},{4,8},{8,12},{12,0},{1,5},{5,9},{9,13},{13,1},{2,6},{6,10},{... | collective-permute-start | bytes 49160 | tf_op jit(solution)/shard_map/ppermute | solution.py:155
  3.8 2.6 %collective-permute-start.5 = (bf16[32,256]{1,0:T(8,128)(2,1)S(1)}, bf16[32,256]{1,0:T(8,128)(2,1)S(1)}, u32[]{:S(2)}, u32[]{:S(2)}) collective-permute-start(bf16[32,256]{1,0:T(8,128)(2,1)S(1)} %get-tuple-element.13), channel_id=1, source_target_pairs={{0,8},{4,12},{8,0},{12,4},{1,9},{5,13},{9,1},{13,5},{2,10},{6,14},... | collective-permute-start | bytes 49160 | tf_op jit(solution)/shard_map/ppermute | solution.py:155
  6.4 1.3 %collective-permute-start.6 = (bf16[32,256]{1,0:T(8,128)(2,1)S(1)}, bf16[32,256]{1,0:T(8,128)(2,1)S(1)}, u32[]{:S(2)}, u32[]{:S(2)}) collective-permute-start(bf16[32,256]{1,0:T(8,128)(2,1)S(1)} %get-tuple-element.13), channel_id=1, source_target_pairs={{0,12},{4,0},{8,4},{12,8},{1,13},{5,1},{9,5},{13,9},{2,14},{6,2},{... | collective-permute-start | bytes 49160 | tf_op jit(solution)/shard_map/ppermute | solution.py:155
  7.7 1.3 %copy.13 = bf16[1,16,3,4096]{3,2,1,0:T(4,128)(2,1)S(1)} copy(bf16[1,16,3,4096]{3,1,2,0:T(8,128)(2,1)} %param.5) | data formatting | bytes 786432 | tf_op args[0]
  9.4 0.7 %broadcast_in_dim.76 = s32[16,3]{1,0:T(8,128)S(1)} broadcast(s32[16]{0:T(128)} %bitcast.93), dimensions={0} | broadcast | bytes 256 | tf_op jit(solution)/shard_map/broadcast_in_dim | solution.py:100
  10.4 2.6 %collective-permute-start = (bf16[48,128]{1,0:T(8,128)(2,1)S(1)}, bf16[48,128]{1,0:T(8,128)(2,1)S(1)}, u32[]{:S(2)}, u32[]{:S(2)}) collective-permute-start(bf16[48,128]{1,0:T(8,128)(2,1)S(1)} %slice.122), channel_id=1, source_target_pairs={{0,4},{4,8},{8,12},{1,5},{5,9},{9,13},{2,6},{6,10},{10,14},{3,7},{... | collective-permute-start | bytes 36872 | tf_op jit(solution)/shard_map/ppermute | solution.py:21
  13.0 1.3 %collective-permute-start.1 = (bf16[48,512]{1,0:T(8,128)(2,1)S(1)}, bf16[48,512]{1,0:T(8,128)(2,1)S(1)}, u32[]{:S(2)}, u32[]{:S(2)}) collective-permute-start(bf16[48,512]{1,0:T(8,128)(2,1)S(1)} %slice.130), channel_id=1, source_target_pairs={{4,0},{8,4},{12,8},{5,1},{9,5},{13,9},{6,2},{10,6},{14,10},{7,3},{... | collective-permute-start | bytes 147464 | tf_op jit(solution)/shard_map/ppermute | solution.py:21
  14.6 0.5 %gather_fusion.1 = s32[2,128,3,16]{1,3,2,0:T(8,128)S(1)} fusion(s32[128,3,2,16]{0,3,2,1:T(8,128)S(1)} %bitcast.84, s32[1024]{0:T(1024)S(1)} %pad_clamp_fusion), kind=kCustom, calls=%fused_computation.1 | custom fusion | bytes 98312 | tf_op jit(solution)/shard_map/jit(_take)/gather | solution.py:167
  15.6 0.4 tile.10
  16.6 0.6 %gather_fusion = bf16[4,32,256]{2,1,0:T(8,128)(2,1)S(1)} fusion(bf16[4,32,256]{2,1,0:T(8,128)(2,1)S(1)} %pad_maximum_fusion, s32[1024]{0:T(1024)S(1)} %pad_clamp_fusion.1), kind=kCustom, calls=%fused_computation | custom fusion | bytes 131088 | tf_op jit(solution)/shard_map/jit(_take)/gather | solution.py:158
  17.4 1.6 %collective-permute-done.1 = bf16[48,512]{1,0:T(8,128)(2,1)S(1)} collective-permute-done((bf16[48,512]{1,0:T(8,128)(2,1)S(1)}, bf16[48,512]{1,0:T(8,128)(2,1)S(1)}, u32[]{:S(2)}, u32[]{:S(2)}) %collective-permute-start.1) | collective-permute-done | bytes 49184 | tf_op jit(solution)/shard_map/ppermute | solution.py:21
  20.0 0.7 %collective-permute-start.2 = (bf16[48,640]{1,0:T(8,128)(2,1)S(1)}, bf16[48,640]{1,0:T(8,128)(2,1)S(1)}, u32[]{:S(2)}, u32[]{:S(2)}) collective-permute-start(bf16[48,640]{1,0:T(8,128)(2,1)S(1)} %get-tuple-element.11), channel_id=1, source_target_pairs={{0,0},{2,4},{4,8},{6,12},{8,2},{10,6},{12,10},{14,14},{1,1},{3,5},... | collective-permute-start | bytes 184328 | tf_op jit(solution)/shard_map/ppermute | solution.py:138
  21.1 0.5 %copy.20 = bf16[128,75,96]{0,2,1:T(8,128)(2,1)S(1)} copy(bf16[128,75,96]{0,1,2:T(8,128)(2,1)S(1)} %fusion) | data formatting | bytes 3686400
  21.5 1.4 %concatenate.24.clone = bf16[128,76,96]{0,2,1:T(8,128)(2,1)} pad(bf16[128,75,96]{0,2,1:T(8,128)(2,1)S(1)} %copy.20, bf16[]{:T(256)} %constant.129.clone.1), padding=0_0x0_1x0_0 | pad | bytes 3710978 | tf_op jit(solution)/shard_map/concatenate | solution.py:171
  22.9 2.8 %copy.19.w_ref = bf16[128,7296]{1,0:T(8,128)(2,1)S(1)} copy(bf16[128,7296]{0,1:T(8,128)(2,1)} %bitcast.86) | data formatting | bytes 3735552 | tf_op jit(solution)/shard_map/reshape;transpose;reshape | solution.py:178
  25.7 2.4 %collective-permute-start.3 = (bf16[48,640]{1,0:T(8,128)(2,1)S(1)}, bf16[48,640]{1,0:T(8,128)(2,1)S(1)}, u32[]{:S(2)}, u32[]{:S(2)}) collective-permute-start(bf16[48,640]{1,0:T(8,128)(2,1)S(1)} %get-tuple-element.10), channel_id=1, source_target_pairs={{0,4},{2,0},{4,12},{6,8},{8,6},{10,2},{12,14},{14,10},{1,5},{3,1},... | collective-permute-start | bytes 184328 | tf_op jit(solution)/shard_map/ppermute | solution.py:138
  28.2 3.6 %collective-permute-done.3 = bf16[48,640]{1,0:T(8,128)(2,1)S(1)} collective-permute-done((bf16[48,640]{1,0:T(8,128)(2,1)S(1)}, bf16[48,640]{1,0:T(8,128)(2,1)S(1)}, u32[]{:S(2)}, u32[]{:S(2)}) %collective-permute-start.3) | collective-permute-done | bytes 61472 | tf_op jit(solution)/shard_map/ppermute | solution.py:138
  32.8 4.0 %shard_map.55 = f32[128,512]{1,0:T(8,128)S(1)} custom-call(bf16[1,96,640]{2,1,0:T(8,128)(2,1)S(1)} %bitcast.85, f32[96,512]{1,0:T(8,128)S(1)} %fusion.3.inv_ref, bf16[128,7296]{1,0:T(8,128)(2,1)S(1)} %copy.19.w_ref), custom_call_target="tpu_custom_call" | custom-call | tf_op jit(solution)/shard_map/pallas_call | solution.py:72
  36.8 0.9 %collective-permute-start.7 = (f32[32,512]{1,0:T(8,128)S(1)}, f32[32,512]{1,0:T(8,128)S(1)}, u32[]{:S(2)}, u32[]{:S(2)}) collective-permute-start(f32[32,512]{1,0:T(8,128)S(1)} %get-tuple-element.7), channel_id=1, source_target_pairs={{0,4},{4,8},{8,12},{12,0},{1,5},{5,9},{9,13},{13,1},{2,6},{6,10},{... | collective-permute-start | bytes 196616 | tf_op jit(solution)/shard_map/ppermute | solution.py:186
  37.7 3.5 %collective-permute-start.8 = (f32[32,512]{1,0:T(8,128)S(1)}, f32[32,512]{1,0:T(8,128)S(1)}, u32[]{:S(2)}, u32[]{:S(2)}) collective-permute-start(f32[32,512]{1,0:T(8,128)S(1)} %get-tuple-element.6), channel_id=1, source_target_pairs={{0,8},{4,12},{8,0},{12,4},{1,9},{5,13},{9,1},{13,5},{2,10},{6,14},... | collective-permute-start | bytes 196616 | tf_op jit(solution)/shard_map/ppermute | solution.py:186
  41.2 2.8 %collective-permute-start.9 = (f32[32,512]{1,0:T(8,128)S(1)}, f32[32,512]{1,0:T(8,128)S(1)}, u32[]{:S(2)}, u32[]{:S(2)}) collective-permute-start(f32[32,512]{1,0:T(8,128)S(1)} %get-tuple-element.5), channel_id=1, source_target_pairs={{0,12},{4,0},{8,4},{12,8},{1,13},{5,1},{9,5},{13,9},{2,14},{6,2},{... | collective-permute-start | bytes 196616 | tf_op jit(solution)/shard_map/ppermute | solution.py:186
  44.2 1.8 %collective-permute-done.9 = f32[32,512]{1,0:T(8,128)S(1)} collective-permute-done((f32[32,512]{1,0:T(8,128)S(1)}, f32[32,512]{1,0:T(8,128)S(1)}, u32[]{:S(2)}, u32[]{:S(2)}) %collective-permute-start.9) | collective-permute-done | bytes 65568 | tf_op jit(solution)/shard_map/ppermute | solution.py:186
  46.0 0.6 %bitcast_dynamic-update-slice_fusion = f32[1,32,2048]{2,1,0:T(8,128)} fusion(f32[1,32,2048]{2,1,0:T(8,128)} %copy-done.1, s32[]{:T(128)S(6)} %select_n.183, f32[32,512]{1,0:T(8,128)S(1)} %collective-permute-done.9), kind=kLoop, calls=%fused_computation.24 | loop fusion | bytes 131076 | tf_op jit(solution)/shard_map/dynamic_update_slice | solution.py:190
  (79 shorter events, 4.3 us)
Async XLA Ops:
  0.0 14.5 %copy-start = (s32[128,3,32]{0,2,1:T(8,128)S(1)}, s32[128,3,32]{0,2,1:T(8,128)}, u32[]{:S(2)}) copy-start(s32[128,3,32]{0,2,1:T(8,128)} %param.9) | copy-start | bytes 147460
  0.0 14.4 %copy-start.2 = (bf16[64]{0:T(256)(128)(2,1)S(1)}, bf16[64]{0:T(256)(128)(2,1)}, u32[]{:S(2)}) copy-start(bf16[64]{0:T(256)(128)(2,1)} %param.7) | copy-start | bytes 388
  0.8 15.8 %collective-permute-start.4 = (bf16[32,256]{1,0:T(8,128)(2,1)S(1)}, bf16[32,256]{1,0:T(8,128)(2,1)S(1)}, u32[]{:S(2)}, u32[]{:S(2)}) collective-permute-start(bf16[32,256]{1,0:T(8,128)(2,1)S(1)} %get-tuple-element.13), channel_id=1, source_target_pairs={{0,4},{4,8},{8,12},{12,0},{1,5},{5,9},{9,13},{13,1},{2,6},{6,10},{... | collective-permute-start | bytes 49160 | tf_op jit(solution)/shard_map/ppermute | solution.py:155
  3.8 12.8 %collective-permute-start.5 = (bf16[32,256]{1,0:T(8,128)(2,1)S(1)}, bf16[32,256]{1,0:T(8,128)(2,1)S(1)}, u32[]{:S(2)}, u32[]{:S(2)}) collective-permute-start(bf16[32,256]{1,0:T(8,128)(2,1)S(1)} %get-tuple-element.13), channel_id=1, source_target_pairs={{0,8},{4,12},{8,0},{12,4},{1,9},{5,13},{9,1},{13,5},{2,10},{6,14},... | collective-permute-start | bytes 49160 | tf_op jit(solution)/shard_map/ppermute | solution.py:155
  6.4 10.2 %collective-permute-start.6 = (bf16[32,256]{1,0:T(8,128)(2,1)S(1)}, bf16[32,256]{1,0:T(8,128)(2,1)S(1)}, u32[]{:S(2)}, u32[]{:S(2)}) collective-permute-start(bf16[32,256]{1,0:T(8,128)(2,1)S(1)} %get-tuple-element.13), channel_id=1, source_target_pairs={{0,12},{4,0},{8,4},{12,8},{1,13},{5,1},{9,5},{13,9},{2,14},{6,2},{... | collective-permute-start | bytes 49160 | tf_op jit(solution)/shard_map/ppermute | solution.py:155
  10.4 6.0 %collective-permute-start = (bf16[48,128]{1,0:T(8,128)(2,1)S(1)}, bf16[48,128]{1,0:T(8,128)(2,1)S(1)}, u32[]{:S(2)}, u32[]{:S(2)}) collective-permute-start(bf16[48,128]{1,0:T(8,128)(2,1)S(1)} %slice.122), channel_id=1, source_target_pairs={{0,4},{4,8},{8,12},{1,5},{5,9},{9,13},{2,6},{6,10},{10,14},{3,7},{... | collective-permute-start | bytes 36872 | tf_op jit(solution)/shard_map/ppermute | solution.py:21
  13.0 6.0 %collective-permute-start.1 = (bf16[48,512]{1,0:T(8,128)(2,1)S(1)}, bf16[48,512]{1,0:T(8,128)(2,1)S(1)}, u32[]{:S(2)}, u32[]{:S(2)}) collective-permute-start(bf16[48,512]{1,0:T(8,128)(2,1)S(1)} %slice.130), channel_id=1, source_target_pairs={{4,0},{8,4},{12,8},{5,1},{9,5},{13,9},{6,2},{10,6},{14,10},{7,3},{... | collective-permute-start | bytes 147464 | tf_op jit(solution)/shard_map/ppermute | solution.py:21
  20.0 8.1 %collective-permute-start.2 = (bf16[48,640]{1,0:T(8,128)(2,1)S(1)}, bf16[48,640]{1,0:T(8,128)(2,1)S(1)}, u32[]{:S(2)}, u32[]{:S(2)}) collective-permute-start(bf16[48,640]{1,0:T(8,128)(2,1)S(1)} %get-tuple-element.11), channel_id=1, source_target_pairs={{0,0},{2,4},{4,8},{6,12},{8,2},{10,6},{12,10},{14,14},{1,1},{3,5},... | collective-permute-start | bytes 184328 | tf_op jit(solution)/shard_map/ppermute | solution.py:138
  25.7 6.0 %collective-permute-start.3 = (bf16[48,640]{1,0:T(8,128)(2,1)S(1)}, bf16[48,640]{1,0:T(8,128)(2,1)S(1)}, u32[]{:S(2)}, u32[]{:S(2)}) collective-permute-start(bf16[48,640]{1,0:T(8,128)(2,1)S(1)} %get-tuple-element.10), channel_id=1, source_target_pairs={{0,4},{2,0},{4,12},{6,8},{8,6},{10,2},{12,14},{14,10},{1,5},{3,1},... | collective-permute-start | bytes 184328 | tf_op jit(solution)/shard_map/ppermute | solution.py:138
  36.8 7.3 %collective-permute-start.7 = (f32[32,512]{1,0:T(8,128)S(1)}, f32[32,512]{1,0:T(8,128)S(1)}, u32[]{:S(2)}, u32[]{:S(2)}) collective-permute-start(f32[32,512]{1,0:T(8,128)S(1)} %get-tuple-element.7), channel_id=1, source_target_pairs={{0,4},{4,8},{8,12},{12,0},{1,5},{5,9},{9,13},{13,1},{2,6},{6,10},{... | collective-permute-start | bytes 196616 | tf_op jit(solution)/shard_map/ppermute | solution.py:186
  37.7 6.4 %collective-permute-start.8 = (f32[32,512]{1,0:T(8,128)S(1)}, f32[32,512]{1,0:T(8,128)S(1)}, u32[]{:S(2)}, u32[]{:S(2)}) collective-permute-start(f32[32,512]{1,0:T(8,128)S(1)} %get-tuple-element.6), channel_id=1, source_target_pairs={{0,8},{4,12},{8,0},{12,4},{1,9},{5,13},{9,1},{13,5},{2,10},{6,14},... | collective-permute-start | bytes 196616 | tf_op jit(solution)/shard_map/ppermute | solution.py:186
  41.2 4.8 %collective-permute-start.9 = (f32[32,512]{1,0:T(8,128)S(1)}, f32[32,512]{1,0:T(8,128)S(1)}, u32[]{:S(2)}, u32[]{:S(2)}) collective-permute-start(f32[32,512]{1,0:T(8,128)S(1)} %get-tuple-element.5), channel_id=1, source_target_pairs={{0,12},{4,0},{8,4},{12,8},{1,13},{5,1},{9,5},{13,9},{2,14},{6,2},{... | collective-permute-start | bytes 196616 | tf_op jit(solution)/shard_map/ppermute | solution.py:186
  44.2 1.8 %copy-start.1 = (f32[1,32,2048]{2,1,0:T(8,128)}, f32[1,32,2048]{2,1,0:T(8,128)S(1)}, u32[]{:S(2)}) copy-start(f32[1,32,2048]{2,1,0:T(8,128)S(1)} %bitcast_dynamic-update-slice_fusion.1) | copy-start | bytes 786436

commit v11 on v8

--- a/solution.py
+++ b/solution.py
@@ -124,19 +124,36 @@
     filtered = jnp.where(past_end[None, :], jnp.zeros_like(filtered), filtered)
     per_block = corr_count // filt_count
     block = per_block * decimated
-    width = block // corr_count
+    halves = per_block // 2
+    width = halves * decimated
     span = width + 128
+    pairs = corr_count // 2
+    partner_of = [(i, i ^ 1) for i in range(corr_count)]
+    side = corr_place % 2
     received = []
-    for k in range(filt_count):
-        piece = (filt_place + k) % filt_count
-        part = lax.dynamic_slice_in_dim(filtered, piece * width, span, 1)
+    for k in range(pairs):
         route = []
         for c in range(corr_count):
             for f in range(filt_count):
-                dest = ((c % per_block) * filt_count + (f + k) % filt_count) * filt_count + c // per_block
+                number = (c % halves) * filt_count + f
+                h = (c % per_block) // halves
+                dest = (2 * ((number + k) % pairs) + h) * filt_count + c // per_block
                 route.append((c * filt_count + f, dest))
-        received.append(lax.ppermute(part, ("corr", "filt"), route))
-    rows = jnp.concatenate(received, axis=0)
+        received.append(lax.ppermute(filtered, ("corr", "filt"), route))
+    pair_place = corr_place // 2
+    if halves == 1:
+        rows = jnp.concatenate(received, axis=0)
+        arrival = (pair_place - lax.iota(jnp.int32, filt_count)) % filt_count
+    else:
+        order = (pair_place - lax.iota(jnp.int32, pairs)) % pairs
+        ordered = jnp.take(jnp.stack(received, axis=0), order, axis=0)
+        ordered = ordered.reshape(halves, filt_count, filtered.shape[0], decimated + 128)
+        heads = jnp.transpose(ordered[:, :, :, :decimated], (1, 2, 0, 3)).reshape(
+            filt_count, filtered.shape[0], width
+        )
+        tail = ordered[halves - 1, :, :, decimated:]
+        rows = jnp.concatenate([heads, tail], axis=2).reshape(filt_count * filtered.shape[0], span)
+        arrival = lax.iota(jnp.int32, filt_count)
     energy = window_energy(rows.astype(jnp.float32), width)
     inv = lax.rsqrt(jnp.maximum(energy, 1.0))
     tile = min(TT, width)
@@ -149,16 +166,16 @@
     wide = jnp.concatenate(
         [templates, jnp.zeros((local_count, lanes - template_width), templates.dtype)], axis=1
     )
-    copies = jnp.broadcast_to(wide[None], (corr_count,) + wide.shape)
-    templates = lax.all_to_all(copies, "corr", 0, 0, tiled=True).reshape(
-        corr_count * local_count, lanes
-    )[:, :template_width]
+    other = lax.ppermute(wide, "corr", partner_of)
+    first = jnp.where(side == 0, wide, other)
+    second = jnp.where(side == 0, other, wide)
+    templates = jnp.concatenate([first, second], axis=0)[:, :template_width]
     count = templates.shape[0]
     stations = masks.shape[2]
     shaped = templates.astype(jnp.float32).reshape(count, 3, L)
     norms = jnp.sqrt(jnp.sum(shaped * shaped, axis=2) + 1e-06)
     base = shaped / norms[:, :, None]
-    arrival = (corr_place - lax.iota(jnp.int32, filt_count)) % filt_count
+    masks = lax.dynamic_slice_in_dim(masks, pair_place * count, count, 0)
     chosen = jnp.take(masks.reshape(count, 3, filt_count, stations // filt_count), arrival, axis=2)
     chosen = chosen.reshape(count, 3, stations).astype(jnp.float32)
     full = jnp.transpose(base, (0, 2, 1))[:, :, None, :] * jnp.transpose(chosen, (0, 2, 1))[:, None, :, :]
@@ -173,16 +190,12 @@
         .reshape(count, chunks * JP * row_block)
     )
     stacked = correlate(windows, inv, weights, row_block)
-    pieces = [lax.dynamic_slice_in_dim(stacked, corr_place * local_count, local_count, 0)]
-    for d in range(1, corr_count):
-        target = (corr_place + d) % corr_count
-        part = lax.dynamic_slice_in_dim(stacked, target * local_count, local_count, 0)
-        route = [(i, (i + d) % corr_count) for i in range(corr_count)]
-        pieces.append(lax.ppermute(part, "corr", route))
-    stacked = jnp.zeros((local_count, corr_count * width), jnp.float32)
-    for d, part in enumerate(pieces):
-        place = ((corr_place - d) % corr_count) * width
-        stacked = lax.dynamic_update_slice_in_dim(stacked, part, place, 1)
+    mine = lax.dynamic_slice_in_dim(stacked, side * local_count, local_count, 0)
+    theirs = lax.dynamic_slice_in_dim(stacked, (1 - side) * local_count, local_count, 0)
+    back = lax.ppermute(theirs, "corr", partner_of)
+    stacked = jnp.where(
+        side == 0, jnp.concatenate([mine, back], axis=1), jnp.concatenate([back, mine], axis=1)
+    )
     return stacked[None]
 
 

time: 43.8 us -> 47.7 us (1.089)
  the two profiles are of different devices: /device:TPU:0 before, /device:TPU:2 now
where the time goes in v11:
time: 47.7 us; the launch traced here: 47.5 us
  starting transfers between devices  12.6 us (26%)
  waiting for transfers between devices  11.4 us (24%)
  local copies, waits for them, and re-layouts  9.98 us (21%)
  Pallas kernels  8.78 us (18%)
  other arithmetic  3.78 us (8%)
  between operations  0.48 us (1%)
    pallas_call x1, Pallas kernels, correlate(): pl.pallas_call(functools.partial(corr_kernel, row_block=row_block, tile=t...  8.78 us
    ppermute x2, waiting for transfers between devices, body(): received.append(lax.ppermute(filtered, ('corr', 'filt'), route))  6.79 us
    ppermute x2, starting transfers between devices, from_behind(): return lax.ppermute(block, axis, route)  4.77 us
    ppermute x2, starting transfers between devices, body(): received.append(lax.ppermute(filtered, ('corr', 'filt'), route))  4.56 us
    ppermute x1, waiting for transfers between devices, body(): back = lax.ppermute(theirs, 'corr', partner_of)  4.48 us
    unnamed x18, local copies, waits for them, and re-layouts  3.4 us
    ppermute x1, starting transfers between devices, body(): other = lax.ppermute(wide, 'corr', partner_of)  2.71 us
    another operation x1, local copies, waits for them, and re-layouts, body(): weights = full.reshape(count, JP, chunks, row_block).transpose(0, 2, 1, 3...  2.39 us
  transfers between devices with their start and end apart: 6, of which 3 were waited for; matrix products, arithmetic and copies ran while one was open for 19% of the time, Pallas kernels for 0%

profile of v11, /device:TPU:2, one launch (start us, length us, event | category | flops | bytes accessed | tf_op | source)
XLA Modules:
  0.0 47.5 jit_solution(12428804609791934854)
XLA Ops:
  0.0 1.4 %copy.12 = bf16[1,16,3,4096]{3,2,1,0:T(4,128)(2,1)S(1)} copy(bf16[1,16,3,4096]{3,1,2,0:T(8,128)(2,1)} %param.5) | data formatting | bytes 786432 | tf_op args[0]
  1.4 0.3 reshape_squeeze.3
  2.1 3.5 %collective-permute-start = (bf16[48,128]{1,0:T(8,128)(2,1)S(1)}, bf16[48,128]{1,0:T(8,128)(2,1)S(1)}, u32[]{:S(2)}, u32[]{:S(2)}) collective-permute-start(bf16[48,128]{1,0:T(8,128)(2,1)S(1)} %slice.128), channel_id=1, source_target_pairs={{0,4},{4,8},{8,12},{1,5},{5,9},{9,13},{2,6},{6,10},{10,14},{3,7},{... | collective-permute-start | bytes 36872 | tf_op jit(solution)/shard_map/ppermute | solution.py:21
  5.6 1.3 %collective-permute-start.1 = (bf16[48,512]{1,0:T(8,128)(2,1)S(1)}, bf16[48,512]{1,0:T(8,128)(2,1)S(1)}, u32[]{:S(2)}, u32[]{:S(2)}) collective-permute-start(bf16[48,512]{1,0:T(8,128)(2,1)S(1)} %slice.136), channel_id=1, source_target_pairs={{4,0},{8,4},{12,8},{5,1},{9,5},{13,9},{6,2},{10,6},{14,10},{7,3},{... | collective-permute-start | bytes 147464 | tf_op jit(solution)/shard_map/ppermute | solution.py:21
  6.9 2.7 %collective-permute-start.4 = (bf16[32,256]{1,0:T(8,128)(2,1)S(1)}, bf16[32,256]{1,0:T(8,128)(2,1)S(1)}, u32[]{:S(2)}, u32[]{:S(2)}) collective-permute-start(bf16[32,256]{1,0:T(8,128)(2,1)S(1)} %concatenate.50), channel_id=1, source_target_pairs={{0,4},{4,0},{8,12},{12,8},{1,5},{5,1},{9,13},{13,9},{2,6},{6,2},{1... | collective-permute-start | bytes 49160 | tf_op jit(solution)/shard_map/ppermute | solution.py:169
  9.9 0.6 %gather_fusion = s32[2,64,3,16]{1,3,2,0:T(8,128)S(1)} fusion(s32[64,3,2,16]{0,3,2,1:T(8,128)S(1)} %bitcast.70, s32[1024]{0:T(1024)S(1)} %pad_clamp_fusion), kind=kCustom, calls=%fused_computation | custom fusion | bytes 49160 | tf_op jit(solution)/shard_map/jit(_take)/gather | solution.py:179
  10.8 0.4 tile.10
  12.3 0.2 reshape.155
  12.5 0.3 convolution_convert_fusion
  13.0 4.5 %collective-permute-start.2 = (bf16[48,1152]{1,0:T(8,128)(2,1)S(1)}, bf16[48,1152]{1,0:T(8,128)(2,1)S(1)}, u32[]{:S(2)}, u32[]{:S(2)}) collective-permute-start(bf16[48,1152]{1,0:T(8,128)(2,1)S(1)} %broadcast_select_fusion), channel_id=1, source_target_pairs={{0,0},{2,8},{4,4},{6,12},{8,2},{10,10},{12,6},{14,14},{1,1},{3,9},... | collective-permute-start | bytes 331784 | tf_op jit(solution)/shard_map/ppermute | solution.py:142
  17.7 1.0 %fusion = bf16[64,75,96]{1,0,2:T(8,128)(2,1)S(1)} fusion(f32[64,96]{0,1:T(8,128)S(1)} %mul.42, f32[64,75,3]{1,0,2:T(8,128)S(1)} %copy.14), kind=kLoop, calls=%fused_computation.2 | loop fusion | flops 921600 | bytes 1003776 | tf_op jit(solution)/shard_map/convert_element_type | solution.py:182
  18.7 1.9 %copy.18 = bf16[64,75,96]{2,1,0:T(8,128)(2,1)S(1)} copy(bf16[64,75,96]{1,0,2:T(8,128)(2,1)S(1)} %fusion) | data formatting | bytes 1843200
  20.7 1.4 %concatenate.52.clone = bf16[64,76,96]{2,1,0:T(8,128)(2,1)} pad(bf16[64,75,96]{2,1,0:T(8,128)(2,1)S(1)} %copy.18, bf16[]{:T(256)} %constant.70.clone.1), padding=0_0x0_1x0_0 | pad | bytes 1855490 | tf_op jit(solution)/shard_map/concatenate | solution.py:183
  22.0 2.4 %reshape_transpose_reshape.3.w_ref = bf16[64,7296]{1,0:T(8,128)(2,1)S(1)} reshape(bf16[64,76,96]{2,1,0:T(8,128)(2,1)} %concatenate.52.clone) | data formatting | bytes 1867776 | tf_op jit(solution)/shard_map/reshape;transpose;reshape | solution.py:190
  24.5 6.8 %collective-permute-done.3 = bf16[48,1152]{1,0:T(8,128)(2,1)S(1)} collective-permute-done((bf16[48,1152]{1,0:T(8,128)(2,1)S(1)}, bf16[48,1152]{1,0:T(8,128)(2,1)S(1)}, u32[]{:S(2)}, u32[]{:S(2)}) %collective-permute-start.3) | collective-permute-done | bytes 110624 | tf_op jit(solution)/shard_map/ppermute | solution.py:142
  31.4 0.2 slice_add_fusion.4
  31.6 0.2 slice_add_fusion.3
  31.8 0.2 slice_add_fusion.2
  31.9 0.2 slice_add_fusion.1
  32.5 0.4 fusion.3.inv_ref
  32.9 8.8 %shard_map.55 = f32[64,1024]{1,0:T(8,128)S(1)} custom-call(bf16[2,96,640]{2,1,0:T(8,128)(2,1)S(1)} %pad_maximum_fusion.f_ref, f32[96,1024]{1,0:T(8,128)S(1)} %fusion.3.inv_ref, bf16[64,7296]{1,0:T(8,128)(2,1)S(1)} %reshape_transpose_reshape.3.w_ref), custom_call_target="tpu_custom_call" | custom-call | tf_op jit(solution)/shard_map/pallas_call | solution.py:72
  41.7 0.6 %collective-permute-start.5 = (f32[32,1024]{1,0:T(8,128)S(1)}, f32[32,1024]{1,0:T(8,128)S(1)}, u32[]{:S(2)}, u32[]{:S(2)}) collective-permute-start(f32[32,1024]{1,0:T(8,128)S(1)} %get-tuple-element.8), channel_id=1, source_target_pairs={{0,4},{4,0},{8,12},{12,8},{1,5},{5,1},{9,13},{13,9},{2,6},{6,2},{1... | collective-permute-start | bytes 393224 | tf_op jit(solution)/shard_map/ppermute | solution.py:195
  42.3 4.5 %collective-permute-done.5 = f32[32,1024]{1,0:T(8,128)S(1)} collective-permute-done((f32[32,1024]{1,0:T(8,128)S(1)}, f32[32,1024]{1,0:T(8,128)S(1)}, u32[]{:S(2)}, u32[]{:S(2)}) %collective-permute-start.5) | collective-permute-done | bytes 131104 | tf_op jit(solution)/shard_map/ppermute | solution.py:195
  46.8 0.7 %maximum_select_fusion = f32[1,32,2048]{2,1,0:T(8,128)} fusion(f32[1,32,1024]{2,1,0:T(8,128)S(1)} %bitcast.73, f32[1,32,1024]{2,1,0:T(8,128)S(1)} %get-tuple-element.7, pred[]{:T(512)S(6)} %eq.18), kind=kLoop, calls=%fused_computation.19 | loop fusion | flops 196608 | bytes 524289 | tf_op jit(solution)/shard_map/jit(_where)/select_n | solution.py:196
  (65 shorter events, 2.8 us)
Async XLA Ops:
  0.0 9.8 %copy-start = (s32[128,3,32]{0,2,1:T(8,128)S(1)}, s32[128,3,32]{0,2,1:T(8,128)}, u32[]{:S(2)}) copy-start(s32[128,3,32]{0,2,1:T(8,128)} %param.9) | copy-start | bytes 147460
  0.0 1.7 %copy-start.2 = (s32[1,16]{1,0:T(1,128)S(1)}, s32[1,16]{1,0:T(1,128)}, u32[]{:S(2)}) copy-start(s32[1,16]{1,0:T(1,128)} %param.6) | copy-start | bytes 196
  0.0 6.9 %copy-start.1 = (bf16[32,225]{1,0:T(8,128)(2,1)S(1)}, bf16[32,225]{1,0:T(8,128)(2,1)}, u32[]{:S(2)}) copy-start(bf16[32,225]{1,0:T(8,128)(2,1)} %param.8) | copy-start | bytes 43204
  0.0 9.6 %copy-start.3 = (bf16[64]{0:T(256)(128)(2,1)S(1)}, bf16[64]{0:T(256)(128)(2,1)}, u32[]{:S(2)}) copy-start(bf16[64]{0:T(256)(128)(2,1)} %param.7) | copy-start | bytes 388
  2.1 9.4 %collective-permute-start = (bf16[48,128]{1,0:T(8,128)(2,1)S(1)}, bf16[48,128]{1,0:T(8,128)(2,1)S(1)}, u32[]{:S(2)}, u32[]{:S(2)}) collective-permute-start(bf16[48,128]{1,0:T(8,128)(2,1)S(1)} %slice.128), channel_id=1, source_target_pairs={{0,4},{4,8},{8,12},{1,5},{5,9},{9,13},{2,6},{6,10},{10,14},{3,7},{... | collective-permute-start | bytes 36872 | tf_op jit(solution)/shard_map/ppermute | solution.py:21
  5.6 6.5 %collective-permute-start.1 = (bf16[48,512]{1,0:T(8,128)(2,1)S(1)}, bf16[48,512]{1,0:T(8,128)(2,1)S(1)}, u32[]{:S(2)}, u32[]{:S(2)}) collective-permute-start(bf16[48,512]{1,0:T(8,128)(2,1)S(1)} %slice.136), channel_id=1, source_target_pairs={{4,0},{8,4},{12,8},{5,1},{9,5},{13,9},{6,2},{10,6},{14,10},{7,3},{... | collective-permute-start | bytes 147464 | tf_op jit(solution)/shard_map/ppermute | solution.py:21
  6.9 4.8 %collective-permute-start.4 = (bf16[32,256]{1,0:T(8,128)(2,1)S(1)}, bf16[32,256]{1,0:T(8,128)(2,1)S(1)}, u32[]{:S(2)}, u32[]{:S(2)}) collective-permute-start(bf16[32,256]{1,0:T(8,128)(2,1)S(1)} %concatenate.50), channel_id=1, source_target_pairs={{0,4},{4,0},{8,12},{12,8},{1,5},{5,1},{9,13},{13,9},{2,6},{6,2},{1... | collective-permute-start | bytes 49160 | tf_op jit(solution)/shard_map/ppermute | solution.py:169
  13.0 11.4 %collective-permute-start.2 = (bf16[48,1152]{1,0:T(8,128)(2,1)S(1)}, bf16[48,1152]{1,0:T(8,128)(2,1)S(1)}, u32[]{:S(2)}, u32[]{:S(2)}) collective-permute-start(bf16[48,1152]{1,0:T(8,128)(2,1)S(1)} %broadcast_select_fusion), channel_id=1, source_target_pairs={{0,0},{2,8},{4,4},{6,12},{8,2},{10,10},{12,6},{14,14},{1,1},{3,9},... | collective-permute-start | bytes 331784 | tf_op jit(solution)/shard_map/ppermute | solution.py:142
  24.4 6.9 %collective-permute-start.3 = (bf16[48,1152]{1,0:T(8,128)(2,1)S(1)}, bf16[48,1152]{1,0:T(8,128)(2,1)S(1)}, u32[]{:S(2)}, u32[]{:S(2)}) collective-permute-start(bf16[48,1152]{1,0:T(8,128)(2,1)S(1)} %broadcast_select_fusion), channel_id=1, source_target_pairs={{0,8},{2,0},{4,12},{6,4},{8,10},{10,2},{12,14},{14,6},{1,9},{3,1},... | collective-permute-start | bytes 331784 | tf_op jit(solution)/shard_map/ppermute | solution.py:142
  41.7 5.0 %collective-permute-start.5 = (f32[32,1024]{1,0:T(8,128)S(1)}, f32[32,1024]{1,0:T(8,128)S(1)}, u32[]{:S(2)}, u32[]{:S(2)}) collective-permute-start(f32[32,1024]{1,0:T(8,128)S(1)} %get-tuple-element.8), channel_id=1, source_target_pairs={{0,4},{4,0},{8,12},{12,8},{1,5},{5,1},{9,13},{13,9},{2,6},{6,2},{1... | collective-permute-start | bytes 393224 | tf_op jit(solution)/shard_map/ppermute | solution.py:195

commit v12 on v8

--- a/solution.py
+++ b/solution.py
@@ -161,17 +161,38 @@
     arrival = (corr_place - lax.iota(jnp.int32, filt_count)) % filt_count
     chosen = jnp.take(masks.reshape(count, 3, filt_count, stations // filt_count), arrival, axis=2)
     chosen = chosen.reshape(count, 3, stations).astype(jnp.float32)
-    full = jnp.transpose(base, (0, 2, 1))[:, :, None, :] * jnp.transpose(chosen, (0, 2, 1))[:, None, :, :]
-    full = full.astype(jnp.bfloat16).reshape(count, L, stations * 3)
-    full = jnp.concatenate([full, jnp.zeros((count, JP - L, stations * 3), full.dtype)], axis=1)
     total_rows = stations * 3
     row_block = 96 if total_rows % 96 == 0 else total_rows
     chunks = total_rows // row_block
-    weights = (
-        full.reshape(count, JP, chunks, row_block)
-        .transpose(0, 2, 1, 3)
-        .reshape(count, chunks * JP * row_block)
-    )
+    if chunks == 1:
+        padded = jnp.concatenate([base, jnp.zeros((count, 3, JP - L), base.dtype)], axis=2)
+        padded = padded.astype(jnp.bfloat16).reshape(count, 3 * JP)
+        flat = jnp.transpose(chosen, (0, 1, 2)).reshape(count, total_rows).astype(jnp.bfloat16)
+        start_zero = lax.optimization_barrier(jnp.zeros((), jnp.int32))
+        column = lax.iota(jnp.int32, JP * total_rows) + start_zero
+        lag = column // total_rows
+        row = column % total_rows
+        source = lax.iota(jnp.int32, 3 * JP)
+        pick_base = (
+            (source[:, None] % JP == lag[None, :]) & (source[:, None] // JP == row[None, :] % 3)
+        ).astype(jnp.bfloat16)
+        slot = lax.iota(jnp.int32, total_rows)
+        pick_mask = (
+            (slot[:, None] // stations == row[None, :] % 3)
+            & (slot[:, None] % stations == row[None, :] // 3)
+        ).astype(jnp.bfloat16)
+        spread = jnp.dot(padded, pick_base, preferred_element_type=jnp.float32)
+        gate = jnp.dot(flat, pick_mask, preferred_element_type=jnp.float32)
+        weights = (spread * gate).astype(jnp.bfloat16)
+    else:
+        full = jnp.transpose(base, (0, 2, 1))[:, :, None, :] * jnp.transpose(chosen, (0, 2, 1))[:, None, :, :]
+        full = full.astype(jnp.bfloat16).reshape(count, L, stations * 3)
+        full = jnp.concatenate([full, jnp.zeros((count, JP - L, stations * 3), full.dtype)], axis=1)
+        weights = (
+            full.reshape(count, JP, chunks, row_block)
+            .transpose(0, 2, 1, 3)
+            .reshape(count, chunks * JP * row_block)
+        )
     stacked = correlate(windows, inv, weights, row_block)
     pieces = [lax.dynamic_slice_in_dim(stacked, corr_place * local_count, local_count, 0)]
     for d in range(1, corr_count):

time: 43.8 us -> 42.1 us (0.961)
  local copies, waits for them, and re-layouts: 10.9 us -> 6.2 us
  matrix products: 0.46 us -> 3.58 us
    dot_general x0 -> x2, matrix products: none -> 3.12 us  [the longest x1 1.91 us: body(): spread = jnp.dot(padded, pick_base, preferred_element_type=jnp.float32)]
    another operation x1 -> x0, local copies, waits for them, and re-layouts: 2.76 us -> none  [body(): weights = full.reshape(count, JP, chunks, row_block).transpose(0, 2, 1, 3...]
    concatenate x1, local copies, waits for them, and re-layouts: 1.41 us -> 0.01 us  [body(): jnp.concatenate([base, jnp.zeros((count, 3, JP - L), base.dtype)], axis=2)]
    unnamed x19 -> x18, local copies, waits for them, and re-layouts: 2.15 us -> 1.59 us
  transfers between devices with their start and end apart: 8 -> 8, of which waited for: 3 -> 3; matrix products, arithmetic and copies ran while one was open for 20% -> 16% of each run, Pallas kernels for 0% -> 0%
where the time goes in v12:
time: 42.1 us; the launch traced here: 41.8 us
  starting transfers between devices  23.9 us (57%)
  local copies, waits for them, and re-layouts  6.2 us (15%)
  Pallas kernels  3.97 us (9%)
  matrix products  3.58 us (9%)
  waiting for transfers between devices  2.09 us (5%)
  other arithmetic  1.45 us (3%)
  between operations  0.62 us (1%)
    ppermute x2, starting transfers between devices, from_behind(): return lax.ppermute(block, axis, route)  6.25 us
    ppermute x3, starting transfers between devices, body(): pieces.append(lax.ppermute(part, 'corr', route))  6.24 us
    all_to_all x1, starting transfers between devices, body(): lax.all_to_all(copies, 'corr', 0, 0, tiled=True)  5.94 us
    ppermute x2, starting transfers between devices, body(): received.append(lax.ppermute(part, ('corr', 'filt'), route))  5.45 us
    pallas_call x1, Pallas kernels, correlate(): pl.pallas_call(functools.partial(corr_kernel, row_block=row_block, tile=t...  3.97 us
    ppermute x3, waiting for transfers between devices, body(): pieces.append(lax.ppermute(part, 'corr', route))  2.08 us
    dot_general x1, matrix products, body(): spread = jnp.dot(padded, pick_base, preferred_element_type=jnp.float32)  1.91 us
    unnamed x18, local copies, waits for them, and re-layouts  1.59 us
  transfers between devices with their start and end apart: 8, of which 3 were waited for; matrix products, arithmetic and copies ran while one was open for 16% of the time, Pallas kernels for 0%

profile of v12, /device:TPU:0, one launch (start us, length us, event | category | flops | bytes accessed | tf_op | source)
XLA Modules:
  0.0 41.8 jit_solution(13012212539779451745)
XLA Ops:
  0.0 1.4 %copy.13 = bf16[1,16,3,4096]{3,2,1,0:T(4,128)(2,1)S(1)} copy(bf16[1,16,3,4096]{3,1,2,0:T(8,128)(2,1)} %param.5) | data formatting | bytes 786432 | tf_op args[0]
  1.4 0.3 reshape_squeeze.3
  1.7 0.7 %broadcast_in_dim.78 = s32[16,3]{1,0:T(8,128)S(1)} broadcast(s32[16]{0:T(128)} %bitcast.77), dimensions={0} | broadcast | bytes 256 | tf_op jit(solution)/shard_map/broadcast_in_dim | solution.py:100
  2.7 5.0 %collective-permute-start = (bf16[48,128]{1,0:T(8,128)(2,1)S(1)}, bf16[48,128]{1,0:T(8,128)(2,1)S(1)}, u32[]{:S(2)}, u32[]{:S(2)}) collective-permute-start(bf16[48,128]{1,0:T(8,128)(2,1)S(1)} %slice.120), channel_id=1, source_target_pairs={{0,4},{4,8},{8,12},{1,5},{5,9},{9,13},{2,6},{6,10},{10,14},{3,7},{... | collective-permute-start | bytes 36872 | tf_op jit(solution)/shard_map/ppermute | solution.py:21
  7.7 1.3 %collective-permute-start.1 = (bf16[48,512]{1,0:T(8,128)(2,1)S(1)}, bf16[48,512]{1,0:T(8,128)(2,1)S(1)}, u32[]{:S(2)}, u32[]{:S(2)}) collective-permute-start(bf16[48,512]{1,0:T(8,128)(2,1)S(1)} %slice.128), channel_id=1, source_target_pairs={{4,0},{8,4},{12,8},{5,1},{9,5},{13,9},{6,2},{10,6},{14,10},{7,3},{... | collective-permute-start | bytes 147464 | tf_op jit(solution)/shard_map/ppermute | solution.py:21
  9.0 0.6 %broadcast_in_dim.82 = bf16[4,32,256]{2,1,0:T(8,128)(2,1)} broadcast(bf16[32,256]{1,0:T(8,128)(2,1)S(1)} %concatenate.23), dimensions={1,2} | broadcast | bytes 81920 | tf_op jit(solution)/shard_map/broadcast_in_dim | solution.py:152
  9.7 5.9 %all-to-all-start = ((bf16[4,32,256]{2,1,0:T(8,128)(2,1)}), bf16[4,32,256]{2,1,0:T(8,128)(2,1)S(1)}, u32[]{:S(2)}, u32[]{:S(2)}) async-start(bf16[4,32,256]{2,1,0:T(8,128)(2,1)} %broadcast_in_dim.82), calls=%async_computation | async-start | bytes 131072 | tf_op jit(solution)/shard_map/all_to_all | solution.py:153
  15.9 0.5 %gather_fusion = s32[2,128,3,16]{1,3,2,0:T(8,128)S(1)} fusion(s32[128,3,2,16]{0,3,2,1:T(8,128)S(1)} %bitcast.73, s32[1024]{0:T(1024)S(1)} %pad_clamp_fusion), kind=kCustom, calls=%fused_computation | custom fusion | bytes 98312 | tf_op jit(solution)/shard_map/jit(_take)/gather | solution.py:162
  17.0 0.4 tile.10
  18.0 0.2 reshape.245
  18.2 0.3 convolution_convert_fusion
  18.8 0.7 %collective-permute-start.2 = (bf16[48,640]{1,0:T(8,128)(2,1)S(1)}, bf16[48,640]{1,0:T(8,128)(2,1)S(1)}, u32[]{:S(2)}, u32[]{:S(2)}) collective-permute-start(bf16[48,640]{1,0:T(8,128)(2,1)S(1)} %get-tuple-element.11), channel_id=1, source_target_pairs={{0,0},{2,4},{4,8},{6,12},{8,2},{10,6},{12,10},{14,14},{1,1},{3,5},... | collective-permute-start | bytes 184328 | tf_op jit(solution)/shard_map/ppermute | solution.py:138
  19.4 4.8 %collective-permute-start.3 = (bf16[48,640]{1,0:T(8,128)(2,1)S(1)}, bf16[48,640]{1,0:T(8,128)(2,1)S(1)}, u32[]{:S(2)}, u32[]{:S(2)}) collective-permute-start(bf16[48,640]{1,0:T(8,128)(2,1)S(1)} %get-tuple-element.10), channel_id=1, source_target_pairs={{0,4},{2,0},{4,12},{6,8},{8,6},{10,2},{12,14},{14,10},{1,5},{3,1},... | collective-permute-start | bytes 184328 | tf_op jit(solution)/shard_map/ppermute | solution.py:138
  24.5 1.9 %fusion.1 = f32[128,7296]{1,0:T(8,128)S(1)} fusion(bf16[128,228]{0,1:T(8,128)(2,1)S(1)} %reshape.251, s32[7296]{0:T(1024)S(1)} %get-tuple-element.17, s32[7296]{0:T(1024)S(1)} %add_select_fusion.3, s32[228]{0:T(256)S(1)} %get-tuple-element.14, s32[228]{0:T(256)S(1)} %get-tuple-element.15), kind=kOutput, calls=%fused_computation.3 | convolution fusion | flops 430843392 | bytes 3854112 | tf_op jit(solution)/shard_map/dot_general | solution.py:184
  26.4 1.2 %fusion.w_ref = bf16[128,7296]{1,0:T(8,128)(2,1)S(1)} fusion(f32[128,7296]{1,0:T(8,128)S(1)} %fusion.1, bf16[128,96]{0,1:T(8,128)(2,1)S(1)} %fusion.31, s32[7296]{0:T(1024)S(1)} %get-tuple-element.16, s32[7296]{0:T(1024)S(1)} %get-tuple-element.17, s32[96]{0:T(128)S(1)} %get-tuple-element.12, s32[96]{0:T(128)S(1)} %get-tuple-element.13), kind=kOutput, calls=%fused_computation.2 | convolution fusion | flops 183275520 | bytes 5687040 | tf_op jit(solution)/shard_map/dot_general | solution.py:185
  28.5 0.2 fusion.18.inv_ref
  28.7 4.0 %shard_map.55 = f32[128,512]{1,0:T(8,128)S(1)} custom-call(bf16[1,96,640]{2,1,0:T(8,128)(2,1)S(1)} %bitcast.74, f32[96,512]{1,0:T(8,128)S(1)} %fusion.18.inv_ref, bf16[128,7296]{1,0:T(8,128)(2,1)S(1)} %fusion.w_ref), custom_call_target="tpu_custom_call" | custom-call | tf_op jit(solution)/shard_map/pallas_call | solution.py:72
  32.8 2.4 %collective-permute-start.4 = (f32[32,512]{1,0:T(8,128)S(1)}, f32[32,512]{1,0:T(8,128)S(1)}, u32[]{:S(2)}, u32[]{:S(2)}) collective-permute-start(f32[32,512]{1,0:T(8,128)S(1)} %get-tuple-element.7), channel_id=1, source_target_pairs={{0,4},{4,8},{8,12},{12,0},{1,5},{5,9},{9,13},{13,1},{2,6},{6,10},{... | collective-permute-start | bytes 196616 | tf_op jit(solution)/shard_map/ppermute | solution.py:202
  35.2 1.7 %collective-permute-start.5 = (f32[32,512]{1,0:T(8,128)S(1)}, f32[32,512]{1,0:T(8,128)S(1)}, u32[]{:S(2)}, u32[]{:S(2)}) collective-permute-start(f32[32,512]{1,0:T(8,128)S(1)} %get-tuple-element.6), channel_id=1, source_target_pairs={{0,8},{4,12},{8,0},{12,4},{1,9},{5,13},{9,1},{13,5},{2,10},{6,14},... | collective-permute-start | bytes 196616 | tf_op jit(solution)/shard_map/ppermute | solution.py:202
  36.9 2.1 %collective-permute-start.6 = (f32[32,512]{1,0:T(8,128)S(1)}, f32[32,512]{1,0:T(8,128)S(1)}, u32[]{:S(2)}, u32[]{:S(2)}) collective-permute-start(f32[32,512]{1,0:T(8,128)S(1)} %get-tuple-element.5), channel_id=1, source_target_pairs={{0,12},{4,0},{8,4},{12,8},{1,13},{5,1},{9,5},{13,9},{2,14},{6,2},{... | collective-permute-start | bytes 196616 | tf_op jit(solution)/shard_map/ppermute | solution.py:202
  39.0 0.5 %collective-permute-done.4 = f32[32,512]{1,0:T(8,128)S(1)} collective-permute-done((f32[32,512]{1,0:T(8,128)S(1)}, f32[32,512]{1,0:T(8,128)S(1)}, u32[]{:S(2)}, u32[]{:S(2)}) %collective-permute-start.4) | collective-permute-done | bytes 65568 | tf_op jit(solution)/shard_map/ppermute | solution.py:202
  39.6 0.8 %collective-permute-done.5 = f32[32,512]{1,0:T(8,128)S(1)} collective-permute-done((f32[32,512]{1,0:T(8,128)S(1)}, f32[32,512]{1,0:T(8,128)S(1)}, u32[]{:S(2)}, u32[]{:S(2)}) %collective-permute-start.5) | collective-permute-done | bytes 65568 | tf_op jit(solution)/shard_map/ppermute | solution.py:202
  40.4 0.8 %collective-permute-done.6 = f32[32,512]{1,0:T(8,128)S(1)} collective-permute-done((f32[32,512]{1,0:T(8,128)S(1)}, f32[32,512]{1,0:T(8,128)S(1)}, u32[]{:S(2)}, u32[]{:S(2)}) %collective-permute-start.6) | collective-permute-done | bytes 65568 | tf_op jit(solution)/shard_map/ppermute | solution.py:202
  41.2 0.6 %bitcast_dynamic-update-slice_fusion = f32[1,32,2048]{2,1,0:T(8,128)} fusion(f32[1,32,2048]{2,1,0:T(8,128)} %copy-done.1, s32[]{:T(128)S(6)} %select_n.236, f32[32,512]{1,0:T(8,128)S(1)} %collective-permute-done.6), kind=kLoop, calls=%fused_computation.37 | loop fusion | bytes 131076 | tf_op jit(solution)/shard_map/dynamic_update_slice | solution.py:206
  (74 shorter events, 2.7 us)
Async XLA Ops:
  0.0 15.9 %copy-start = (s32[128,3,32]{0,2,1:T(8,128)S(1)}, s32[128,3,32]{0,2,1:T(8,128)}, u32[]{:S(2)}) copy-start(s32[128,3,32]{0,2,1:T(8,128)} %param.9) | copy-start | bytes 147460
  0.0 9.0 %copy-start.2 = (bf16[32,225]{1,0:T(8,128)(2,1)S(1)}, bf16[32,225]{1,0:T(8,128)(2,1)}, u32[]{:S(2)}) copy-start(bf16[32,225]{1,0:T(8,128)(2,1)} %param.8) | copy-start | bytes 43204
  0.0 15.7 %copy-start.3 = (bf16[64]{0:T(256)(128)(2,1)S(1)}, bf16[64]{0:T(256)(128)(2,1)}, u32[]{:S(2)}) copy-start(bf16[64]{0:T(256)(128)(2,1)} %param.7) | copy-start | bytes 388
  2.7 14.9 %collective-permute-start = (bf16[48,128]{1,0:T(8,128)(2,1)S(1)}, bf16[48,128]{1,0:T(8,128)(2,1)S(1)}, u32[]{:S(2)}, u32[]{:S(2)}) collective-permute-start(bf16[48,128]{1,0:T(8,128)(2,1)S(1)} %slice.120), channel_id=1, source_target_pairs={{0,4},{4,8},{8,12},{1,5},{5,9},{9,13},{2,6},{6,10},{10,14},{3,7},{... | collective-permute-start | bytes 36872 | tf_op jit(solution)/shard_map/ppermute | solution.py:21
  7.7 10.1 %collective-permute-start.1 = (bf16[48,512]{1,0:T(8,128)(2,1)S(1)}, bf16[48,512]{1,0:T(8,128)(2,1)S(1)}, u32[]{:S(2)}, u32[]{:S(2)}) collective-permute-start(bf16[48,512]{1,0:T(8,128)(2,1)S(1)} %slice.128), channel_id=1, source_target_pairs={{4,0},{8,4},{12,8},{5,1},{9,5},{13,9},{6,2},{10,6},{14,10},{7,3},{... | collective-permute-start | bytes 147464 | tf_op jit(solution)/shard_map/ppermute | solution.py:21
  9.7 14.6 %all-to-all-start = ((bf16[4,32,256]{2,1,0:T(8,128)(2,1)}), bf16[4,32,256]{2,1,0:T(8,128)(2,1)S(1)}, u32[]{:S(2)}, u32[]{:S(2)}) async-start(bf16[4,32,256]{2,1,0:T(8,128)(2,1)} %broadcast_in_dim.82), calls=%async_computation | async-start | bytes 131072 | tf_op jit(solution)/shard_map/all_to_all | solution.py:153
  18.8 8.9 %collective-permute-start.2 = (bf16[48,640]{1,0:T(8,128)(2,1)S(1)}, bf16[48,640]{1,0:T(8,128)(2,1)S(1)}, u32[]{:S(2)}, u32[]{:S(2)}) collective-permute-start(bf16[48,640]{1,0:T(8,128)(2,1)S(1)} %get-tuple-element.11), channel_id=1, source_target_pairs={{0,0},{2,4},{4,8},{6,12},{8,2},{10,6},{12,10},{14,14},{1,1},{3,5},... | collective-permute-start | bytes 184328 | tf_op jit(solution)/shard_map/ppermute | solution.py:138
  19.4 8.2 %collective-permute-start.3 = (bf16[48,640]{1,0:T(8,128)(2,1)S(1)}, bf16[48,640]{1,0:T(8,128)(2,1)S(1)}, u32[]{:S(2)}, u32[]{:S(2)}) collective-permute-start(bf16[48,640]{1,0:T(8,128)(2,1)S(1)} %get-tuple-element.10), channel_id=1, source_target_pairs={{0,4},{2,0},{4,12},{6,8},{8,6},{10,2},{12,14},{14,10},{1,5},{3,1},... | collective-permute-start | bytes 184328 | tf_op jit(solution)/shard_map/ppermute | solution.py:138
  32.8 6.8 %collective-permute-start.4 = (f32[32,512]{1,0:T(8,128)S(1)}, f32[32,512]{1,0:T(8,128)S(1)}, u32[]{:S(2)}, u32[]{:S(2)}) collective-permute-start(f32[32,512]{1,0:T(8,128)S(1)} %get-tuple-element.7), channel_id=1, source_target_pairs={{0,4},{4,8},{8,12},{12,0},{1,5},{5,9},{9,13},{13,1},{2,6},{6,10},{... | collective-permute-start | bytes 196616 | tf_op jit(solution)/shard_map/ppermute | solution.py:202
  35.2 5.2 %collective-permute-start.5 = (f32[32,512]{1,0:T(8,128)S(1)}, f32[32,512]{1,0:T(8,128)S(1)}, u32[]{:S(2)}, u32[]{:S(2)}) collective-permute-start(f32[32,512]{1,0:T(8,128)S(1)} %get-tuple-element.6), channel_id=1, source_target_pairs={{0,8},{4,12},{8,0},{12,4},{1,9},{5,13},{9,1},{13,5},{2,10},{6,14},... | collective-permute-start | bytes 196616 | tf_op jit(solution)/shard_map/ppermute | solution.py:202
  36.9 4.3 %collective-permute-start.6 = (f32[32,512]{1,0:T(8,128)S(1)}, f32[32,512]{1,0:T(8,128)S(1)}, u32[]{:S(2)}, u32[]{:S(2)}) collective-permute-start(f32[32,512]{1,0:T(8,128)S(1)} %get-tuple-element.5), channel_id=1, source_target_pairs={{0,12},{4,0},{8,4},{12,8},{1,13},{5,1},{9,5},{13,9},{2,14},{6,2},{... | collective-permute-start | bytes 196616 | tf_op jit(solution)/shard_map/ppermute | solution.py:202
  40.4 0.8 %copy-start.1 = (f32[1,32,2048]{2,1,0:T(8,128)}, f32[1,32,2048]{2,1,0:T(8,128)S(1)}, u32[]{:S(2)}) copy-start(f32[1,32,2048]{2,1,0:T(8,128)S(1)} %bitcast_dynamic-update-slice_fusion.1) | copy-start | bytes 786436

commit v13 on v12

--- a/solution.py
+++ b/solution.py
@@ -96,9 +96,8 @@
     filt_place = lax.axis_index("filt")
     filt_count = lax.axis_size("filt")
     sample_times = corr_place * raw_width + lax.iota(jnp.int32, raw_width)
-    dense = samples.reshape(local_stations * 3, raw_width)
-    row_counts = jnp.repeat(counts, 3)
-    live = jnp.where(sample_times[None, :] < row_counts[:, None], dense, jnp.zeros_like(dense))
+    keep = sample_times[None, None, :] < counts[:, None, None]
+    live = jnp.where(keep, samples, jnp.zeros_like(samples)).reshape(local_stations * 3, raw_width)
     history = from_behind(live[:, raw_width - 128 :], "corr", 1)
     corr_count = lax.axis_size("corr")
     ahead = from_behind(live[:, :512], "corr", -1)
@@ -159,7 +158,12 @@
     norms = jnp.sqrt(jnp.sum(shaped * shaped, axis=2) + 1e-06)
     base = shaped / norms[:, :, None]
     arrival = (corr_place - lax.iota(jnp.int32, filt_count)) % filt_count
-    chosen = jnp.take(masks.reshape(count, 3, filt_count, stations // filt_count), arrival, axis=2)
+    blocked = masks.reshape(count, 3, filt_count, stations // filt_count)
+    if filt_count == 2:
+        swapped = jnp.concatenate([blocked[:, :, 1:], blocked[:, :, :1]], axis=2)
+        chosen = jnp.where(arrival[0] == 0, blocked, swapped)
+    else:
+        chosen = jnp.take(blocked, arrival, axis=2)
     chosen = chosen.reshape(count, 3, stations).astype(jnp.float32)
     total_rows = stations * 3
     row_block = 96 if total_rows % 96 == 0 else total_rows

time: 42.1 us -> 41.7 us (level)
  local copies, waits for them, and re-layouts: 6.2 us -> 5.21 us
  other arithmetic: 1.45 us -> 2.02 us
    lt x0 -> x1, other arithmetic: none -> 0.78 us  [body(): keep = sample_times[None, None, :] < counts[:, None, None]]
    gather x2 -> x0, local copies, waits for them, and re-layouts: 0.55 us -> none  [body(): jnp.take(masks.reshape(count, 3, filt_count, stations // filt_count), arr...]
    broadcast_in_dim x5 -> x2, local copies, waits for them, and re-layouts: 0.98 us -> 0.65 us  [body(): jnp.where(keep, samples, jnp.zeros_like(samples))]
  transfers between devices with their start and end apart: 8 -> 8, of which waited for: 3 -> 3; matrix products, arithmetic and copies ran while one was open for 16% -> 14% of each run, Pallas kernels for 0% -> 0%
where the time goes in v13:
time: 41.7 us; the launch traced here: 41.4 us
  starting transfers between devices  23.9 us (57%)
  local copies, waits for them, and re-layouts  5.21 us (12%)
  Pallas kernels  3.97 us (10%)
  matrix products  3.56 us (9%)
  waiting for transfers between devices  2.11 us (5%)
  other arithmetic  2.02 us (5%)
  between operations  0.66 us (2%)
    ppermute x2, starting transfers between devices, from_behind(): return lax.ppermute(block, axis, route)  6.25 us
    ppermute x3, starting transfers between devices, body(): pieces.append(lax.ppermute(part, 'corr', route))  6.24 us
    all_to_all x1, starting transfers between devices, body(): lax.all_to_all(copies, 'corr', 0, 0, tiled=True)  5.94 us
    ppermute x2, starting transfers between devices, body(): received.append(lax.ppermute(part, ('corr', 'filt'), route))  5.45 us
    pallas_call x1, Pallas kernels, correlate(): pl.pallas_call(functools.partial(corr_kernel, row_block=row_block, tile=t...  3.97 us
    ppermute x3, waiting for transfers between devices, body(): pieces.append(lax.ppermute(part, 'corr', route))  2.09 us
    dot_general x1, matrix products, body(): spread = jnp.dot(padded, pick_base, preferred_element_type=jnp.float32)  1.9 us
    unnamed x18, local copies, waits for them, and re-layouts  1.57 us
  transfers between devices with their start and end apart: 8, of which 3 were waited for; matrix products, arithmetic and copies ran while one was open for 14% of the time, Pallas kernels for 0%

profile of v13, /device:TPU:0, one launch (start us, length us, event | category | flops | bytes accessed | tf_op | source)
XLA Modules:
  0.0 41.4 jit_solution(2711218587186377316)
XLA Ops:
  0.0 0.8 %broadcast_compare_fusion = pred[16,4096]{1,0:T(8,128)(4,1)S(1)} fusion(s32[4096]{0:T(1024)S(1)} %iota_add_fusion.1, s32[16]{0:T(128)} %bitcast.77), kind=kLoop, calls=%fused_computation.33 | loop fusion | flops 65536 | bytes 81984 | tf_op jit(solution)/shard_map/lt | solution.py:99
  0.8 0.3 broadcast_in_dim.67
  1.1 0.4 broadcast_in_dim.68
  1.5 1.3 %copy.12 = bf16[1,16,3,4096]{3,2,1,0:T(4,128)(2,1)S(1)} copy(bf16[1,16,3,4096]{3,1,2,0:T(8,128)(2,1)} %param.5) | data formatting | bytes 786432 | tf_op args[0]
  2.8 0.3 squeeze.2
  3.2 5.0 %collective-permute-start = (bf16[48,128]{1,0:T(8,128)(2,1)S(1)}, bf16[48,128]{1,0:T(8,128)(2,1)S(1)}, u32[]{:S(2)}, u32[]{:S(2)}) collective-permute-start(bf16[48,128]{1,0:T(8,128)(2,1)S(1)} %slice.130), channel_id=1, source_target_pairs={{0,4},{4,8},{8,12},{1,5},{5,9},{9,13},{2,6},{6,10},{10,14},{3,7},{... | collective-permute-start | bytes 36872 | tf_op jit(solution)/shard_map/ppermute | solution.py:21
  8.2 1.3 %collective-permute-start.1 = (bf16[48,512]{1,0:T(8,128)(2,1)S(1)}, bf16[48,512]{1,0:T(8,128)(2,1)S(1)}, u32[]{:S(2)}, u32[]{:S(2)}) collective-permute-start(bf16[48,512]{1,0:T(8,128)(2,1)S(1)} %slice.138), channel_id=1, source_target_pairs={{4,0},{8,4},{12,8},{5,1},{9,5},{13,9},{6,2},{10,6},{14,10},{7,3},{... | collective-permute-start | bytes 147464 | tf_op jit(solution)/shard_map/ppermute | solution.py:21
  9.5 0.6 %broadcast_in_dim.72 = bf16[4,32,256]{2,1,0:T(8,128)(2,1)} broadcast(bf16[32,256]{1,0:T(8,128)(2,1)S(1)} %concatenate.28), dimensions={1,2} | broadcast | bytes 81920 | tf_op jit(solution)/shard_map/broadcast_in_dim | solution.py:151
  10.1 5.9 %all-to-all-start = ((bf16[4,32,256]{2,1,0:T(8,128)(2,1)}), bf16[4,32,256]{2,1,0:T(8,128)(2,1)S(1)}, u32[]{:S(2)}, u32[]{:S(2)}) async-start(bf16[4,32,256]{2,1,0:T(8,128)(2,1)} %broadcast_in_dim.72), calls=%async_computation | async-start | bytes 131072 | tf_op jit(solution)/shard_map/all_to_all | solution.py:152
  16.6 0.4 tile.10
  17.6 0.2 reshape.225
  17.8 0.3 convolution_convert_fusion
  18.4 0.7 %collective-permute-start.2 = (bf16[48,640]{1,0:T(8,128)(2,1)S(1)}, bf16[48,640]{1,0:T(8,128)(2,1)S(1)}, u32[]{:S(2)}, u32[]{:S(2)}) collective-permute-start(bf16[48,640]{1,0:T(8,128)(2,1)S(1)} %get-tuple-element.11), channel_id=1, source_target_pairs={{0,0},{2,4},{4,8},{6,12},{8,2},{10,6},{12,10},{14,14},{1,1},{3,5},... | collective-permute-start | bytes 184328 | tf_op jit(solution)/shard_map/ppermute | solution.py:137
  19.1 4.8 %collective-permute-start.3 = (bf16[48,640]{1,0:T(8,128)(2,1)S(1)}, bf16[48,640]{1,0:T(8,128)(2,1)S(1)}, u32[]{:S(2)}, u32[]{:S(2)}) collective-permute-start(bf16[48,640]{1,0:T(8,128)(2,1)S(1)} %get-tuple-element.10), channel_id=1, source_target_pairs={{0,4},{2,0},{4,12},{6,8},{8,6},{10,2},{12,14},{14,10},{1,5},{3,1},... | collective-permute-start | bytes 184328 | tf_op jit(solution)/shard_map/ppermute | solution.py:137
  24.1 1.9 %fusion.1 = f32[128,7296]{1,0:T(8,128)S(1)} fusion(bf16[128,228]{0,1:T(8,128)(2,1)S(1)} %reshape.231, s32[7296]{0:T(1024)S(1)} %get-tuple-element.19, s32[7296]{0:T(1024)S(1)} %add_select_fusion.3, s32[228]{0:T(256)S(1)} %get-tuple-element.16, s32[228]{0:T(256)S(1)} %get-tuple-element.17), kind=kOutput, calls=%fused_computation.2 | convolution fusion | flops 430843392 | bytes 3854112 | tf_op jit(solution)/shard_map/dot_general | solution.py:188
  26.0 1.2 %fusion.w_ref = bf16[128,7296]{1,0:T(8,128)(2,1)S(1)} fusion(f32[128,7296]{1,0:T(8,128)S(1)} %fusion.1, bf16[128,96]{0,1:T(8,128)(2,1)S(1)} %bitcast.76, s32[7296]{0:T(1024)S(1)} %get-tuple-element.18, s32[7296]{0:T(1024)S(1)} %get-tuple-element.19, s32[96]{0:T(128)S(1)} %get-tuple-element.14, s32[96]{0:T(128)S(1)} %get-tuple-element.15), kind=kOutput, calls=%fused_computation.1 | convolution fusion | flops 183275520 | bytes 5687040 | tf_op jit(solution)/shard_map/dot_general | solution.py:189
  28.3 4.0 %shard_map.55 = f32[128,512]{1,0:T(8,128)S(1)} custom-call(bf16[1,96,640]{2,1,0:T(8,128)(2,1)S(1)} %bitcast.73, f32[96,512]{1,0:T(8,128)S(1)} %fusion.18.inv_ref, bf16[128,7296]{1,0:T(8,128)(2,1)S(1)} %fusion.w_ref), custom_call_target="tpu_custom_call" | custom-call | tf_op jit(solution)/shard_map/pallas_call | solution.py:72
  32.4 2.4 %collective-permute-start.4 = (f32[32,512]{1,0:T(8,128)S(1)}, f32[32,512]{1,0:T(8,128)S(1)}, u32[]{:S(2)}, u32[]{:S(2)}) collective-permute-start(f32[32,512]{1,0:T(8,128)S(1)} %get-tuple-element.7), channel_id=1, source_target_pairs={{0,4},{4,8},{8,12},{12,0},{1,5},{5,9},{9,13},{13,1},{2,6},{6,10},{... | collective-permute-start | bytes 196616 | tf_op jit(solution)/shard_map/ppermute | solution.py:206
  34.8 1.7 %collective-permute-start.5 = (f32[32,512]{1,0:T(8,128)S(1)}, f32[32,512]{1,0:T(8,128)S(1)}, u32[]{:S(2)}, u32[]{:S(2)}) collective-permute-start(f32[32,512]{1,0:T(8,128)S(1)} %get-tuple-element.6), channel_id=1, source_target_pairs={{0,8},{4,12},{8,0},{12,4},{1,9},{5,13},{9,1},{13,5},{2,10},{6,14},... | collective-permute-start | bytes 196616 | tf_op jit(solution)/shard_map/ppermute | solution.py:206
  36.5 2.1 %collective-permute-start.6 = (f32[32,512]{1,0:T(8,128)S(1)}, f32[32,512]{1,0:T(8,128)S(1)}, u32[]{:S(2)}, u32[]{:S(2)}) collective-permute-start(f32[32,512]{1,0:T(8,128)S(1)} %get-tuple-element.5), channel_id=1, source_target_pairs={{0,12},{4,0},{8,4},{12,8},{1,13},{5,1},{9,5},{13,9},{2,14},{6,2},{... | collective-permute-start | bytes 196616 | tf_op jit(solution)/shard_map/ppermute | solution.py:206
  38.6 0.5 %collective-permute-done.4 = f32[32,512]{1,0:T(8,128)S(1)} collective-permute-done((f32[32,512]{1,0:T(8,128)S(1)}, f32[32,512]{1,0:T(8,128)S(1)}, u32[]{:S(2)}, u32[]{:S(2)}) %collective-permute-start.4) | collective-permute-done | bytes 65568 | tf_op jit(solution)/shard_map/ppermute | solution.py:206
  39.2 0.8 %collective-permute-done.5 = f32[32,512]{1,0:T(8,128)S(1)} collective-permute-done((f32[32,512]{1,0:T(8,128)S(1)}, f32[32,512]{1,0:T(8,128)S(1)}, u32[]{:S(2)}, u32[]{:S(2)}) %collective-permute-start.5) | collective-permute-done | bytes 65568 | tf_op jit(solution)/shard_map/ppermute | solution.py:206
  40.0 0.8 %collective-permute-done.6 = f32[32,512]{1,0:T(8,128)S(1)} collective-permute-done((f32[32,512]{1,0:T(8,128)S(1)}, f32[32,512]{1,0:T(8,128)S(1)}, u32[]{:S(2)}, u32[]{:S(2)}) %collective-permute-start.6) | collective-permute-done | bytes 65568 | tf_op jit(solution)/shard_map/ppermute | solution.py:206
  40.8 0.6 %bitcast_dynamic-update-slice_fusion = f32[1,32,2048]{2,1,0:T(8,128)} fusion(f32[1,32,2048]{2,1,0:T(8,128)} %copy-done.1, s32[]{:T(128)S(6)} %select_n.211, f32[32,512]{1,0:T(8,128)S(1)} %collective-permute-done.6), kind=kLoop, calls=%fused_computation.37 | loop fusion | bytes 131076 | tf_op jit(solution)/shard_map/dynamic_update_slice | solution.py:210
  (69 shorter events, 2.4 us)
Async XLA Ops:
  0.0 16.2 %copy-start = (bf16[64]{0:T(256)(128)(2,1)S(1)}, bf16[64]{0:T(256)(128)(2,1)}, u32[]{:S(2)}) copy-start(bf16[64]{0:T(256)(128)(2,1)} %param.7) | copy-start | bytes 388
  0.0 9.5 %copy-start.3 = (bf16[32,225]{1,0:T(8,128)(2,1)S(1)}, bf16[32,225]{1,0:T(8,128)(2,1)}, u32[]{:S(2)}) copy-start(bf16[32,225]{1,0:T(8,128)(2,1)} %param.8) | copy-start | bytes 43204
  0.0 16.3 %copy-start.2 = (s32[128,3,32]{0,2,1:T(8,128)S(1)}, s32[128,3,32]{0,2,1:T(8,128)}, u32[]{:S(2)}) copy-start(s32[128,3,32]{0,2,1:T(8,128)} %param.9) | copy-start | bytes 147460
  3.2 14.0 %collective-permute-start = (bf16[48,128]{1,0:T(8,128)(2,1)S(1)}, bf16[48,128]{1,0:T(8,128)(2,1)S(1)}, u32[]{:S(2)}, u32[]{:S(2)}) collective-permute-start(bf16[48,128]{1,0:T(8,128)(2,1)S(1)} %slice.130), channel_id=1, source_target_pairs={{0,4},{4,8},{8,12},{1,5},{5,9},{9,13},{2,6},{6,10},{10,14},{3,7},{... | collective-permute-start | bytes 36872 | tf_op jit(solution)/shard_map/ppermute | solution.py:21
  8.2 9.2 %collective-permute-start.1 = (bf16[48,512]{1,0:T(8,128)(2,1)S(1)}, bf16[48,512]{1,0:T(8,128)(2,1)S(1)}, u32[]{:S(2)}, u32[]{:S(2)}) collective-permute-start(bf16[48,512]{1,0:T(8,128)(2,1)S(1)} %slice.138), channel_id=1, source_target_pairs={{4,0},{8,4},{12,8},{5,1},{9,5},{13,9},{6,2},{10,6},{14,10},{7,3},{... | collective-permute-start | bytes 147464 | tf_op jit(solution)/shard_map/ppermute | solution.py:21
  10.1 13.7 %all-to-all-start = ((bf16[4,32,256]{2,1,0:T(8,128)(2,1)}), bf16[4,32,256]{2,1,0:T(8,128)(2,1)S(1)}, u32[]{:S(2)}, u32[]{:S(2)}) async-start(bf16[4,32,256]{2,1,0:T(8,128)(2,1)} %broadcast_in_dim.72), calls=%async_computation | async-start | bytes 131072 | tf_op jit(solution)/shard_map/all_to_all | solution.py:152
  18.4 8.8 %collective-permute-start.2 = (bf16[48,640]{1,0:T(8,128)(2,1)S(1)}, bf16[48,640]{1,0:T(8,128)(2,1)S(1)}, u32[]{:S(2)}, u32[]{:S(2)}) collective-permute-start(bf16[48,640]{1,0:T(8,128)(2,1)S(1)} %get-tuple-element.11), channel_id=1, source_target_pairs={{0,0},{2,4},{4,8},{6,12},{8,2},{10,6},{12,10},{14,14},{1,1},{3,5},... | collective-permute-start | bytes 184328 | tf_op jit(solution)/shard_map/ppermute | solution.py:137
  19.1 8.2 %collective-permute-start.3 = (bf16[48,640]{1,0:T(8,128)(2,1)S(1)}, bf16[48,640]{1,0:T(8,128)(2,1)S(1)}, u32[]{:S(2)}, u32[]{:S(2)}) collective-permute-start(bf16[48,640]{1,0:T(8,128)(2,1)S(1)} %get-tuple-element.10), channel_id=1, source_target_pairs={{0,4},{2,0},{4,12},{6,8},{8,6},{10,2},{12,14},{14,10},{1,5},{3,1},... | collective-permute-start | bytes 184328 | tf_op jit(solution)/shard_map/ppermute | solution.py:137
  32.4 6.8 %collective-permute-start.4 = (f32[32,512]{1,0:T(8,128)S(1)}, f32[32,512]{1,0:T(8,128)S(1)}, u32[]{:S(2)}, u32[]{:S(2)}) collective-permute-start(f32[32,512]{1,0:T(8,128)S(1)} %get-tuple-element.7), channel_id=1, source_target_pairs={{0,4},{4,8},{8,12},{12,0},{1,5},{5,9},{9,13},{13,1},{2,6},{6,10},{... | collective-permute-start | bytes 196616 | tf_op jit(solution)/shard_map/ppermute | solution.py:206
  34.8 5.2 %collective-permute-start.5 = (f32[32,512]{1,0:T(8,128)S(1)}, f32[32,512]{1,0:T(8,128)S(1)}, u32[]{:S(2)}, u32[]{:S(2)}) collective-permute-start(f32[32,512]{1,0:T(8,128)S(1)} %get-tuple-element.6), channel_id=1, source_target_pairs={{0,8},{4,12},{8,0},{12,4},{1,9},{5,13},{9,1},{13,5},{2,10},{6,14},... | collective-permute-start | bytes 196616 | tf_op jit(solution)/shard_map/ppermute | solution.py:206
  36.5 4.3 %collective-permute-start.6 = (f32[32,512]{1,0:T(8,128)S(1)}, f32[32,512]{1,0:T(8,128)S(1)}, u32[]{:S(2)}, u32[]{:S(2)}) collective-permute-start(f32[32,512]{1,0:T(8,128)S(1)} %get-tuple-element.5), channel_id=1, source_target_pairs={{0,12},{4,0},{8,4},{12,8},{1,13},{5,1},{9,5},{13,9},{2,14},{6,2},{... | collective-permute-start | bytes 196616 | tf_op jit(solution)/shard_map/ppermute | solution.py:206
  40.0 0.8 %copy-start.1 = (f32[1,32,2048]{2,1,0:T(8,128)}, f32[1,32,2048]{2,1,0:T(8,128)S(1)}, u32[]{:S(2)}) copy-start(f32[1,32,2048]{2,1,0:T(8,128)S(1)} %bitcast_dynamic-update-slice_fusion.1) | copy-start | bytes 786436

commit v14 on v13

--- a/solution.py
+++ b/solution.py
@@ -98,9 +98,33 @@
     sample_times = corr_place * raw_width + lax.iota(jnp.int32, raw_width)
     keep = sample_times[None, None, :] < counts[:, None, None]
     live = jnp.where(keep, samples, jnp.zeros_like(samples)).reshape(local_stations * 3, raw_width)
-    history = from_behind(live[:, raw_width - 128 :], "corr", 1)
     corr_count = lax.axis_size("corr")
-    ahead = from_behind(live[:, :512], "corr", -1)
+    local_count = templates.shape[0]
+    template_width = templates.shape[1]
+    lanes = -(-template_width // 512) * 512
+    wide = jnp.concatenate(
+        [templates, jnp.zeros((local_count, lanes - template_width), templates.dtype)], axis=1
+    )
+    forward = [(i, (i + 1) % corr_count) for i in range(corr_count)]
+    backward = [(i, (i - 1) % corr_count) for i in range(corr_count)]
+    tail_rows = live.shape[0]
+    sent = jnp.concatenate([live[:, raw_width - 128 :], wide.reshape(-1, 128)], axis=0)
+    got = lax.ppermute(sent, "corr", forward)
+    history = jnp.where(corr_place > 0, got[:tail_rows], jnp.zeros_like(got[:tail_rows]))
+    from_previous = got[tail_rows:].reshape(local_count, lanes)
+    sent = jnp.concatenate([live[:, :512], wide.reshape(-1, 512)], axis=0)
+    got = lax.ppermute(sent, "corr", backward)
+    ahead = jnp.where(corr_place < corr_count - 1, got[:tail_rows], jnp.zeros_like(got[:tail_rows]))
+    from_next = got[tail_rows:].reshape(local_count, lanes)
+    blocks_by_offset = {0: wide, 1: from_previous, corr_count - 1: from_next}
+    for d in range(2, corr_count - 1):
+        route = [(i, (i + d) % corr_count) for i in range(corr_count)]
+        blocks_by_offset[d] = lax.ppermute(wide, "corr", route)
+    by_offset = jnp.stack([blocks_by_offset[d] for d in range(corr_count)], axis=0)
+    offsets = (corr_place - lax.iota(jnp.int32, corr_count)) % corr_count
+    gathered_templates = jnp.take(by_offset, offsets, axis=0).reshape(
+        corr_count * local_count, lanes
+    )[:, :template_width]
     extended = jnp.concatenate([history, live, ahead], axis=1)
     decimated = raw_width // DEC
     blocks = decimated // 128 + 1
@@ -142,16 +166,7 @@
     tiles = width // tile
     windows = jnp.stack([rows[:, i * tile : i * tile + tile + 128] for i in range(tiles)], axis=0)
 
-    local_count = templates.shape[0]
-    template_width = templates.shape[1]
-    lanes = -(-template_width // 128) * 128
-    wide = jnp.concatenate(
-        [templates, jnp.zeros((local_count, lanes - template_width), templates.dtype)], axis=1
-    )
-    copies = jnp.broadcast_to(wide[None], (corr_count,) + wide.shape)
-    templates = lax.all_to_all(copies, "corr", 0, 0, tiled=True).reshape(
-        corr_count * local_count, lanes
-    )[:, :template_width]
+    templates = gathered_templates
     count = templates.shape[0]
     stations = masks.shape[2]
     shaped = templates.astype(jnp.float32).reshape(count, 3, L)

time: 41.7 us -> 39.1 us (0.938)
  starting transfers between devices: 23.9 us -> 19.4 us
  local copies, waits for them, and re-layouts: 5.21 us -> 6.1 us
  waiting for transfers between devices: 2.11 us -> 2.91 us
    all_to_all x1 -> x0, starting transfers between devices: 5.94 us -> none  [body(): lax.all_to_all(copies, 'corr', 0, 0, tiled=True)]
    ppermute x2, starting transfers between devices: 5.45 us -> 3.24 us  [body(): received.append(lax.ppermute(part, ('corr', 'filt'), route))]
    ppermute x3, starting transfers between devices: 6.24 us -> 8.2 us  [body(): pieces.append(lax.ppermute(part, 'corr', route))]
    ppermute x2 -> x3, starting transfers between devices: 6.25 us -> 7.99 us  [the longest x1 4.06 us: body(): blocks_by_offset[d] = lax.ppermute(wide, 'corr', route)]
    ppermute x2 -> x3, waiting for transfers between devices: 0.01 us -> 1.11 us  [the longest x1 0.69 us: body(): got = lax.ppermute(sent, 'corr', forward)]
    another operation x0 -> x3, local copies, waits for them, and re-layouts: none -> 0.78 us  [body(): jnp.stack([blocks_by_offset[d] for d in range(corr_count)], axis=0)]
    gather x0 -> x1, local copies, waits for them, and re-layouts: none -> 0.56 us  [body(): jnp.take(by_offset, offsets, axis=0)]
    broadcast_in_dim x1 -> x2, local copies, waits for them, and re-layouts: 0.63 us -> 0.16 us  [body(): jnp.take(by_offset, offsets, axis=0)]
  transfers between devices with their start and end apart: 8 -> 8, of which waited for: 3 -> 3; matrix products, arithmetic and copies ran while one was open for 14% -> 24% of each run, Pallas kernels for 0% -> 0%
where the time goes in v14:
time: 39.1 us; the launch traced here: 38.8 us
  starting transfers between devices  19.4 us (50%)
  local copies, waits for them, and re-layouts  6.1 us (16%)
  Pallas kernels  3.97 us (10%)
  matrix products  3.57 us (9%)
  waiting for transfers between devices  2.91 us (7%)
  other arithmetic  2.1 us (5%)
  between operations  0.72 us (2%)
    ppermute x3, starting transfers between devices, body(): pieces.append(lax.ppermute(part, 'corr', route))  8.2 us
    ppermute x1, starting transfers between devices, body(): blocks_by_offset[d] = lax.ppermute(wide, 'corr', route)  4.06 us
    pallas_call x1, Pallas kernels, correlate(): pl.pallas_call(functools.partial(corr_kernel, row_block=row_block, tile=t...  3.97 us
    ppermute x2, starting transfers between devices, body(): received.append(lax.ppermute(part, ('corr', 'filt'), route))  3.24 us
    ppermute x1, starting transfers between devices, body(): got = lax.ppermute(sent, 'corr', backward)  2.3 us
    dot_general x1, matrix products, body(): spread = jnp.dot(padded, pick_base, preferred_element_type=jnp.float32)  1.91 us
    ppermute x3, waiting for transfers between devices, body(): pieces.append(lax.ppermute(part, 'corr', route))  1.79 us
    ppermute x1, starting transfers between devices, body(): got = lax.ppermute(sent, 'corr', forward)  1.63 us
  transfers between devices with their start and end apart: 8, of which 3 were waited for; matrix products, arithmetic and copies ran while one was open for 24% of the time, Pallas kernels for 0%

profile of v14, /device:TPU:0, one launch (start us, length us, event | category | flops | bytes accessed | tf_op | source)
XLA Modules:
  0.0 38.8 jit_solution(9195835854963332829)
XLA Ops:
  0.0 0.7 %pad_bitcast_fusion = (bf16[1,32,512]{2,1,0:T(8,128)(2,1)S(1)}, bf16[32,512]{1,0:T(8,128)(2,1)S(1)}) fusion(bf16[32,225]{1,0:T(8,128)(2,1)} %param.8), kind=kLoop, calls=%fused_computation.97 | loop fusion | bytes 79936 | tf_op jit(solution)/shard_map/stack | solution.py:123
  0.7 4.1 %collective-permute-start.4 = (bf16[32,512]{1,0:T(8,128)(2,1)S(1)}, bf16[32,512]{1,0:T(8,128)(2,1)S(1)}, u32[]{:S(2)}, u32[]{:S(2)}) collective-permute-start(bf16[32,512]{1,0:T(8,128)(2,1)S(1)} %get-tuple-element.15), channel_id=1, source_target_pairs={{0,8},{4,12},{8,0},{12,4},{1,9},{5,13},{9,1},{13,5},{2,10},{6,14},... | collective-permute-start | bytes 98312 | tf_op jit(solution)/shard_map/ppermute | solution.py:122
  4.9 0.8 %broadcast_compare_fusion = pred[16,4096]{1,0:T(8,128)(4,1)S(1)} fusion(s32[4096]{0:T(1024)S(1)} %iota_add_fusion.1, s32[16]{0:T(128)} %bitcast.84), kind=kLoop, calls=%fused_computation.35 | loop fusion | flops 65536 | bytes 81984 | tf_op jit(solution)/shard_map/lt | solution.py:99
  5.6 0.3 broadcast_in_dim.81
  5.9 0.4 broadcast_in_dim.82
  6.3 1.3 %copy.7 = bf16[1,16,3,4096]{3,2,1,0:T(4,128)(2,1)S(1)} copy(bf16[1,16,3,4096]{3,1,2,0:T(8,128)(2,1)} %param.5) | data formatting | bytes 786432 | tf_op args[0]
  7.6 0.3 squeeze.2
  8.0 1.6 %collective-permute-start = (bf16[176,128]{1,0:T(8,128)(2,1)S(1)}, bf16[176,128]{1,0:T(8,128)(2,1)S(1)}, u32[]{:S(2)}, u32[]{:S(2)}) collective-permute-start(bf16[176,128]{1,0:T(8,128)(2,1)S(1)} %pad_maximum_fusion.4), channel_id=1, source_target_pairs={{0,4},{4,8},{8,12},{12,0},{1,5},{5,9},{9,13},{13,1},{2,6},{6,10},{... | collective-permute-start | bytes 135176 | tf_op jit(solution)/shard_map/ppermute | solution.py:112
  9.7 2.3 %collective-permute-start.1 = (bf16[80,512]{1,0:T(8,128)(2,1)S(1)}, bf16[80,512]{1,0:T(8,128)(2,1)S(1)}, u32[]{:S(2)}, u32[]{:S(2)}) collective-permute-start(bf16[80,512]{1,0:T(8,128)(2,1)S(1)} %pad_maximum_fusion.1), channel_id=1, source_target_pairs={{0,12},{4,0},{8,4},{12,8},{1,13},{5,1},{9,5},{13,9},{2,14},{6,2},{... | collective-permute-start | bytes 245768 | tf_op jit(solution)/shard_map/ppermute | solution.py:116
  12.7 0.4 tile.10
  13.4 0.7 %collective-permute-done = bf16[176,128]{1,0:T(8,128)(2,1)S(1)} collective-permute-done((bf16[176,128]{1,0:T(8,128)(2,1)S(1)}, bf16[176,128]{1,0:T(8,128)(2,1)S(1)}, u32[]{:S(2)}, u32[]{:S(2)}) %collective-permute-start) | collective-permute-done | bytes 45088 | tf_op jit(solution)/shard_map/ppermute | solution.py:112
  14.2 0.4 %collective-permute-done.1 = bf16[80,512]{1,0:T(8,128)(2,1)S(1)} collective-permute-done((bf16[80,512]{1,0:T(8,128)(2,1)S(1)}, bf16[80,512]{1,0:T(8,128)(2,1)S(1)}, u32[]{:S(2)}, u32[]{:S(2)}) %collective-permute-start.1) | collective-permute-done | bytes 81952 | tf_op jit(solution)/shard_map/ppermute | solution.py:116
  15.1 0.3 convolution_convert_fusion
  15.7 0.7 %collective-permute-start.2 = (bf16[48,640]{1,0:T(8,128)(2,1)S(1)}, bf16[48,640]{1,0:T(8,128)(2,1)S(1)}, u32[]{:S(2)}, u32[]{:S(2)}) collective-permute-start(bf16[48,640]{1,0:T(8,128)(2,1)S(1)} %get-tuple-element.11), channel_id=1, source_target_pairs={{0,0},{2,4},{4,8},{6,12},{8,2},{10,6},{12,10},{14,14},{1,1},{3,5},... | collective-permute-start | bytes 184328 | tf_op jit(solution)/shard_map/ppermute | solution.py:161
  16.3 2.6 %collective-permute-start.3 = (bf16[48,640]{1,0:T(8,128)(2,1)S(1)}, bf16[48,640]{1,0:T(8,128)(2,1)S(1)}, u32[]{:S(2)}, u32[]{:S(2)}) collective-permute-start(bf16[48,640]{1,0:T(8,128)(2,1)S(1)} %get-tuple-element.10), channel_id=1, source_target_pairs={{0,4},{2,0},{4,12},{6,8},{8,6},{10,2},{12,14},{14,10},{1,5},{3,1},... | collective-permute-start | bytes 184328 | tf_op jit(solution)/shard_map/ppermute | solution.py:161
  19.0 0.6 %gather_fusion = bf16[4,32,512]{2,1,0:T(8,128)(2,1)S(1)} fusion(bf16[4,32,512]{2,1,0:T(8,128)(2,1)S(1)} %pad_maximum_fusion, s32[1024]{0:T(1024)S(1)} %pad_clamp_fusion), kind=kCustom, calls=%fused_computation | custom fusion | bytes 262160 | tf_op jit(solution)/shard_map/jit(_take)/gather | solution.py:125
  19.8 1.9 %fusion.1 = f32[128,7296]{1,0:T(8,128)S(1)} fusion(bf16[128,228]{0,1:T(8,128)(2,1)S(1)} %reshape.287, s32[7296]{0:T(1024)S(1)} %get-tuple-element.21, s32[7296]{0:T(1024)S(1)} %add_select_fusion.3, s32[228]{0:T(256)S(1)} %get-tuple-element.18, s32[228]{0:T(256)S(1)} %get-tuple-element.19), kind=kOutput, calls=%fused_computation.3 | convolution fusion | flops 430843392 | bytes 3854112 | tf_op jit(solution)/shard_map/dot_general | solution.py:203
  21.7 1.2 %fusion.w_ref = bf16[128,7296]{1,0:T(8,128)(2,1)S(1)} fusion(f32[128,7296]{1,0:T(8,128)S(1)} %fusion.1, bf16[128,96]{0,1:T(8,128)(2,1)S(1)} %bitcast.82, s32[7296]{0:T(1024)S(1)} %get-tuple-element.20, s32[7296]{0:T(1024)S(1)} %get-tuple-element.21, s32[96]{0:T(128)S(1)} %get-tuple-element.16, s32[96]{0:T(128)S(1)} %get-tuple-element.17), kind=kOutput, calls=%fused_computation.2 | convolution fusion | flops 183275520 | bytes 5687040 | tf_op jit(solution)/shard_map/dot_general | solution.py:204
  24.0 4.0 %shard_map.55 = f32[128,512]{1,0:T(8,128)S(1)} custom-call(bf16[1,96,640]{2,1,0:T(8,128)(2,1)S(1)} %bitcast.79, f32[96,512]{1,0:T(8,128)S(1)} %fusion.18.inv_ref, bf16[128,7296]{1,0:T(8,128)(2,1)S(1)} %fusion.w_ref), custom_call_target="tpu_custom_call" | custom-call | tf_op jit(solution)/shard_map/pallas_call | solution.py:72
  28.1 2.9 %collective-permute-start.5 = (f32[32,512]{1,0:T(8,128)S(1)}, f32[32,512]{1,0:T(8,128)S(1)}, u32[]{:S(2)}, u32[]{:S(2)}) collective-permute-start(f32[32,512]{1,0:T(8,128)S(1)} %get-tuple-element.7), channel_id=1, source_target_pairs={{0,4},{4,8},{8,12},{12,0},{1,5},{5,9},{9,13},{13,1},{2,6},{6,10},{... | collective-permute-start | bytes 196616 | tf_op jit(solution)/shard_map/ppermute | solution.py:221
  31.0 2.4 %collective-permute-start.6 = (f32[32,512]{1,0:T(8,128)S(1)}, f32[32,512]{1,0:T(8,128)S(1)}, u32[]{:S(2)}, u32[]{:S(2)}) collective-permute-start(f32[32,512]{1,0:T(8,128)S(1)} %get-tuple-element.6), channel_id=1, source_target_pairs={{0,8},{4,12},{8,0},{12,4},{1,9},{5,13},{9,1},{13,5},{2,10},{6,14},... | collective-permute-start | bytes 196616 | tf_op jit(solution)/shard_map/ppermute | solution.py:221
  33.4 2.8 %collective-permute-start.7 = (f32[32,512]{1,0:T(8,128)S(1)}, f32[32,512]{1,0:T(8,128)S(1)}, u32[]{:S(2)}, u32[]{:S(2)}) collective-permute-start(f32[32,512]{1,0:T(8,128)S(1)} %get-tuple-element.5), channel_id=1, source_target_pairs={{0,12},{4,0},{8,4},{12,8},{1,13},{5,1},{9,5},{13,9},{2,14},{6,2},{... | collective-permute-start | bytes 196616 | tf_op jit(solution)/shard_map/ppermute | solution.py:221
  36.4 1.8 %collective-permute-done.7 = f32[32,512]{1,0:T(8,128)S(1)} collective-permute-done((f32[32,512]{1,0:T(8,128)S(1)}, f32[32,512]{1,0:T(8,128)S(1)}, u32[]{:S(2)}, u32[]{:S(2)}) %collective-permute-start.7) | collective-permute-done | bytes 65568 | tf_op jit(solution)/shard_map/ppermute | solution.py:221
  38.2 0.6 %bitcast_dynamic-update-slice_fusion = f32[1,32,2048]{2,1,0:T(8,128)} fusion(f32[1,32,2048]{2,1,0:T(8,128)} %copy-done.1, s32[]{:T(128)S(6)} %select_n.274, f32[32,512]{1,0:T(8,128)S(1)} %collective-permute-done.7), kind=kLoop, calls=%fused_computation.40 | loop fusion | bytes 131076 | tf_op jit(solution)/shard_map/dynamic_update_slice | solution.py:225
  (83 shorter events, 3.0 us)
Async XLA Ops:
  0.0 12.1 %copy-start = (bf16[64]{0:T(256)(128)(2,1)S(1)}, bf16[64]{0:T(256)(128)(2,1)}, u32[]{:S(2)}) copy-start(bf16[64]{0:T(256)(128)(2,1)} %param.7) | copy-start | bytes 388
  0.0 12.3 %copy-start.2 = (s32[128,3,32]{0,2,1:T(8,128)S(1)}, s32[128,3,32]{0,2,1:T(8,128)}, u32[]{:S(2)}) copy-start(s32[128,3,32]{0,2,1:T(8,128)} %param.9) | copy-start | bytes 147460
  0.7 18.2 %collective-permute-start.4 = (bf16[32,512]{1,0:T(8,128)(2,1)S(1)}, bf16[32,512]{1,0:T(8,128)(2,1)S(1)}, u32[]{:S(2)}, u32[]{:S(2)}) collective-permute-start(bf16[32,512]{1,0:T(8,128)(2,1)S(1)} %get-tuple-element.15), channel_id=1, source_target_pairs={{0,8},{4,12},{8,0},{12,4},{1,9},{5,13},{9,1},{13,5},{2,10},{6,14},... | collective-permute-start | bytes 98312 | tf_op jit(solution)/shard_map/ppermute | solution.py:122
  8.0 6.0 %collective-permute-start = (bf16[176,128]{1,0:T(8,128)(2,1)S(1)}, bf16[176,128]{1,0:T(8,128)(2,1)S(1)}, u32[]{:S(2)}, u32[]{:S(2)}) collective-permute-start(bf16[176,128]{1,0:T(8,128)(2,1)S(1)} %pad_maximum_fusion.4), channel_id=1, source_target_pairs={{0,4},{4,8},{8,12},{12,0},{1,5},{5,9},{9,13},{13,1},{2,6},{6,10},{... | collective-permute-start | bytes 135176 | tf_op jit(solution)/shard_map/ppermute | solution.py:112
  9.7 5.0 %collective-permute-start.1 = (bf16[80,512]{1,0:T(8,128)(2,1)S(1)}, bf16[80,512]{1,0:T(8,128)(2,1)S(1)}, u32[]{:S(2)}, u32[]{:S(2)}) collective-permute-start(bf16[80,512]{1,0:T(8,128)(2,1)S(1)} %pad_maximum_fusion.1), channel_id=1, source_target_pairs={{0,12},{4,0},{8,4},{12,8},{1,13},{5,1},{9,5},{13,9},{2,14},{6,2},{... | collective-permute-start | bytes 245768 | tf_op jit(solution)/shard_map/ppermute | solution.py:116
  15.7 7.2 %collective-permute-start.2 = (bf16[48,640]{1,0:T(8,128)(2,1)S(1)}, bf16[48,640]{1,0:T(8,128)(2,1)S(1)}, u32[]{:S(2)}, u32[]{:S(2)}) collective-permute-start(bf16[48,640]{1,0:T(8,128)(2,1)S(1)} %get-tuple-element.11), channel_id=1, source_target_pairs={{0,0},{2,4},{4,8},{6,12},{8,2},{10,6},{12,10},{14,14},{1,1},{3,5},... | collective-permute-start | bytes 184328 | tf_op jit(solution)/shard_map/ppermute | solution.py:161
  16.3 6.6 %collective-permute-start.3 = (bf16[48,640]{1,0:T(8,128)(2,1)S(1)}, bf16[48,640]{1,0:T(8,128)(2,1)S(1)}, u32[]{:S(2)}, u32[]{:S(2)}) collective-permute-start(bf16[48,640]{1,0:T(8,128)(2,1)S(1)} %get-tuple-element.10), channel_id=1, source_target_pairs={{0,4},{2,0},{4,12},{6,8},{8,6},{10,2},{12,14},{14,10},{1,5},{3,1},... | collective-permute-start | bytes 184328 | tf_op jit(solution)/shard_map/ppermute | solution.py:161
  28.1 8.2 %collective-permute-start.5 = (f32[32,512]{1,0:T(8,128)S(1)}, f32[32,512]{1,0:T(8,128)S(1)}, u32[]{:S(2)}, u32[]{:S(2)}) collective-permute-start(f32[32,512]{1,0:T(8,128)S(1)} %get-tuple-element.7), channel_id=1, source_target_pairs={{0,4},{4,8},{8,12},{12,0},{1,5},{5,9},{9,13},{13,1},{2,6},{6,10},{... | collective-permute-start | bytes 196616 | tf_op jit(solution)/shard_map/ppermute | solution.py:221
  31.0 5.4 %collective-permute-start.6 = (f32[32,512]{1,0:T(8,128)S(1)}, f32[32,512]{1,0:T(8,128)S(1)}, u32[]{:S(2)}, u32[]{:S(2)}) collective-permute-start(f32[32,512]{1,0:T(8,128)S(1)} %get-tuple-element.6), channel_id=1, source_target_pairs={{0,8},{4,12},{8,0},{12,4},{1,9},{5,13},{9,1},{13,5},{2,10},{6,14},... | collective-permute-start | bytes 196616 | tf_op jit(solution)/shard_map/ppermute | solution.py:221
  33.4 4.8 %collective-permute-start.7 = (f32[32,512]{1,0:T(8,128)S(1)}, f32[32,512]{1,0:T(8,128)S(1)}, u32[]{:S(2)}, u32[]{:S(2)}) collective-permute-start(f32[32,512]{1,0:T(8,128)S(1)} %get-tuple-element.5), channel_id=1, source_target_pairs={{0,12},{4,0},{8,4},{12,8},{1,13},{5,1},{9,5},{13,9},{2,14},{6,2},{... | collective-permute-start | bytes 196616 | tf_op jit(solution)/shard_map/ppermute | solution.py:221
  36.4 1.8 %copy-start.1 = (f32[1,32,2048]{2,1,0:T(8,128)}, f32[1,32,2048]{2,1,0:T(8,128)S(1)}, u32[]{:S(2)}) copy-start(f32[1,32,2048]{2,1,0:T(8,128)S(1)} %bitcast_dynamic-update-slice_fusion.1) | copy-start | bytes 786436

commit v15 on v14

--- a/solution.py
+++ b/solution.py
@@ -101,7 +101,7 @@
     corr_count = lax.axis_size("corr")
     local_count = templates.shape[0]
     template_width = templates.shape[1]
-    lanes = -(-template_width // 512) * 512
+    lanes = -(-template_width // 256) * 256
     wide = jnp.concatenate(
         [templates, jnp.zeros((local_count, lanes - template_width), templates.dtype)], axis=1
     )
@@ -121,9 +121,12 @@
         route = [(i, (i + d) % corr_count) for i in range(corr_count)]
         blocks_by_offset[d] = lax.ppermute(wide, "corr", route)
     by_offset = jnp.stack([blocks_by_offset[d] for d in range(corr_count)], axis=0)
-    offsets = (corr_place - lax.iota(jnp.int32, corr_count)) % corr_count
-    gathered_templates = jnp.take(by_offset, offsets, axis=0).reshape(
-        corr_count * local_count, lanes
+    gathered_templates = jnp.concatenate(
+        [
+            lax.dynamic_index_in_dim(by_offset, (corr_place - b) % corr_count, 0, keepdims=False)
+            for b in range(corr_count)
+        ],
+        axis=0,
     )[:, :template_width]
     extended = jnp.concatenate([history, live, ahead], axis=1)
     decimated = raw_width // DEC

time: 39.1 us -> 39.1 us (level)
  waiting for transfers between devices: 2.91 us -> 5.68 us
  starting transfers between devices: 19.4 us -> 16.9 us
    ppermute x1, waiting for transfers between devices: 0.69 us -> 3.78 us  [body(): got = lax.ppermute(sent, 'corr', forward)]
    ppermute x1, starting transfers between devices: 1.63 us -> 0.73 us  [body(): got = lax.ppermute(sent, 'corr', forward)]
    ppermute x1, starting transfers between devices: 2.3 us -> 1.4 us  [body(): got = lax.ppermute(sent, 'corr', backward)]
    ppermute x2, starting transfers between devices: 3.24 us -> 2.42 us  [body(): received.append(lax.ppermute(part, ('corr', 'filt'), route))]
    gather x1 -> x0, local copies, waits for them, and re-layouts: 0.56 us -> none  [body(): jnp.take(by_offset, offsets, axis=0)]
    squeeze x0 -> x5, local copies, waits for them, and re-layouts: none -> 0.49 us  [body(): lax.dynamic_index_in_dim(by_offset, (corr_place - b) % corr_count, 0, kee...]
    ppermute x1, waiting for transfers between devices: 0.42 us -> 0.01 us  [body(): got = lax.ppermute(sent, 'corr', backward)]
    unnamed x16 -> x15, local copies, waits for them, and re-layouts: 1.56 us -> 1.45 us
  transfers between devices with their start and end apart: 8 -> 8, of which waited for: 3 -> 3; matrix products, arithmetic and copies ran while one was open for 24% -> 19% of each run, Pallas kernels for 0% -> 0%
where the time goes in v15:
time: 39.1 us; the launch traced here: 38.8 us
  starting transfers between devices  16.9 us (43%)
  local copies, waits for them, and re-layouts  5.74 us (15%)
  waiting for transfers between devices  5.68 us (15%)
  Pallas kernels  3.97 us (10%)
  matrix products  3.56 us (9%)
  other arithmetic  2.17 us (6%)
  between operations  0.79 us (2%)
    ppermute x3, starting transfers between devices, body(): pieces.append(lax.ppermute(part, 'corr', route))  8.25 us
    ppermute x1, starting transfers between devices, body(): blocks_by_offset[d] = lax.ppermute(wide, 'corr', route)  4.06 us
    pallas_call x1, Pallas kernels, correlate(): pl.pallas_call(functools.partial(corr_kernel, row_block=row_block, tile=t...  3.97 us
    ppermute x1, waiting for transfers between devices, body(): got = lax.ppermute(sent, 'corr', forward)  3.78 us
    ppermute x2, starting transfers between devices, body(): received.append(lax.ppermute(part, ('corr', 'filt'), route))  2.42 us
    dot_general x1, matrix products, body(): spread = jnp.dot(padded, pick_base, preferred_element_type=jnp.float32)  1.9 us
    ppermute x3, waiting for transfers between devices, body(): pieces.append(lax.ppermute(part, 'corr', route))  1.79 us
    unnamed x15, local copies, waits for them, and re-layouts  1.45 us
  transfers between devices with their start and end apart: 8, of which 3 were waited for; matrix products, arithmetic and copies ran while one was open for 19% of the time, Pallas kernels for 0%

profile of v15, /device:TPU:0, one launch (start us, length us, event | category | flops | bytes accessed | tf_op | source)
XLA Modules:
  0.0 38.8 jit_solution(11238050409809754296)
XLA Ops:
  0.0 0.7 %pad_bitcast_fusion = (bf16[1,32,256]{2,1,0:T(8,128)(2,1)S(1)}, bf16[32,256]{1,0:T(8,128)(2,1)S(1)}) fusion(bf16[32,225]{1,0:T(8,128)(2,1)} %param.8), kind=kLoop, calls=%fused_computation.126 | loop fusion | bytes 47168 | tf_op jit(solution)/shard_map/stack | solution.py:123
  0.8 4.1 %collective-permute-start.4 = (bf16[32,256]{1,0:T(8,128)(2,1)S(1)}, bf16[32,256]{1,0:T(8,128)(2,1)S(1)}, u32[]{:S(2)}, u32[]{:S(2)}) collective-permute-start(bf16[32,256]{1,0:T(8,128)(2,1)S(1)} %get-tuple-element.19), channel_id=1, source_target_pairs={{0,8},{4,12},{8,0},{12,4},{1,9},{5,13},{9,1},{13,5},{2,10},{6,14},... | collective-permute-start | bytes 49160 | tf_op jit(solution)/shard_map/ppermute | solution.py:122
  4.9 0.8 %broadcast_compare_fusion = pred[16,4096]{1,0:T(8,128)(4,1)S(1)} fusion(s32[4096]{0:T(1024)S(1)} %iota_add_fusion.1, s32[16]{0:T(128)} %bitcast.86), kind=kLoop, calls=%fused_computation.33 | loop fusion | flops 65536 | bytes 81984 | tf_op jit(solution)/shard_map/lt | solution.py:99
  5.6 0.3 broadcast_in_dim.67
  5.9 0.4 broadcast_in_dim.68
  6.3 1.3 %copy.11 = bf16[1,16,3,4096]{3,2,1,0:T(4,128)(2,1)S(1)} copy(bf16[1,16,3,4096]{3,1,2,0:T(8,128)(2,1)} %param.5) | data formatting | bytes 786432 | tf_op args[0]
  7.6 0.3 squeeze.18
  8.0 1.4 %collective-permute-start.1 = (bf16[64,512]{1,0:T(8,128)(2,1)S(1)}, bf16[64,512]{1,0:T(8,128)(2,1)S(1)}, u32[]{:S(2)}, u32[]{:S(2)}) collective-permute-start(bf16[64,512]{1,0:T(8,128)(2,1)S(1)} %pad_maximum_fusion), channel_id=1, source_target_pairs={{0,12},{4,0},{8,4},{12,8},{1,13},{5,1},{9,5},{13,9},{2,14},{6,2},{... | collective-permute-start | bytes 196616 | tf_op jit(solution)/shard_map/ppermute | solution.py:116
  9.5 0.7 %collective-permute-start = (bf16[112,128]{1,0:T(8,128)(2,1)S(1)}, bf16[112,128]{1,0:T(8,128)(2,1)S(1)}, u32[]{:S(2)}, u32[]{:S(2)}) collective-permute-start(bf16[112,128]{1,0:T(8,128)(2,1)S(1)} %pad_maximum_fusion.7), channel_id=1, source_target_pairs={{0,4},{4,8},{8,12},{12,0},{1,5},{5,9},{9,13},{13,1},{2,6},{6,10},{... | collective-permute-start | bytes 86024 | tf_op jit(solution)/shard_map/ppermute | solution.py:112
  10.8 0.4 tile.10
  11.4 3.8 %collective-permute-done = bf16[112,128]{1,0:T(8,128)(2,1)S(1)} collective-permute-done((bf16[112,128]{1,0:T(8,128)(2,1)S(1)}, bf16[112,128]{1,0:T(8,128)(2,1)S(1)}, u32[]{:S(2)}, u32[]{:S(2)}) %collective-permute-start) | collective-permute-done | bytes 28704 | tf_op jit(solution)/shard_map/ppermute | solution.py:112
  16.4 0.2 reshape.229
  16.7 0.3 convolution_convert_fusion
  17.2 0.7 %collective-permute-start.2 = (bf16[48,640]{1,0:T(8,128)(2,1)S(1)}, bf16[48,640]{1,0:T(8,128)(2,1)S(1)}, u32[]{:S(2)}, u32[]{:S(2)}) collective-permute-start(bf16[48,640]{1,0:T(8,128)(2,1)S(1)} %get-tuple-element.11), channel_id=1, source_target_pairs={{0,0},{2,4},{4,8},{6,12},{8,2},{10,6},{12,10},{14,14},{1,1},{3,5},... | collective-permute-start | bytes 184328 | tf_op jit(solution)/shard_map/ppermute | solution.py:164
  17.9 1.8 %collective-permute-start.3 = (bf16[48,640]{1,0:T(8,128)(2,1)S(1)}, bf16[48,640]{1,0:T(8,128)(2,1)S(1)}, u32[]{:S(2)}, u32[]{:S(2)}) collective-permute-start(bf16[48,640]{1,0:T(8,128)(2,1)S(1)} %get-tuple-element.10), channel_id=1, source_target_pairs={{0,4},{2,0},{4,12},{6,8},{8,6},{10,2},{12,14},{14,10},{1,5},{3,1},... | collective-permute-start | bytes 184328 | tf_op jit(solution)/shard_map/ppermute | solution.py:164
  19.6 1.9 %fusion.1 = f32[128,7296]{1,0:T(8,128)S(1)} fusion(bf16[128,228]{0,1:T(8,128)(2,1)S(1)} %reshape.234, s32[7296]{0:T(1024)S(1)} %get-tuple-element.25, s32[7296]{0:T(1024)S(1)} %add_select_fusion.3, s32[228]{0:T(256)S(1)} %get-tuple-element.22, s32[228]{0:T(256)S(1)} %get-tuple-element.23), kind=kOutput, calls=%fused_computation.2 | convolution fusion | flops 430843392 | bytes 3854112 | tf_op jit(solution)/shard_map/dot_general | solution.py:206
  21.6 1.2 %fusion.w_ref = bf16[128,7296]{1,0:T(8,128)(2,1)S(1)} fusion(f32[128,7296]{1,0:T(8,128)S(1)} %fusion.1, bf16[128,96]{0,1:T(8,128)(2,1)S(1)} %bitcast.84, s32[7296]{0:T(1024)S(1)} %get-tuple-element.24, s32[7296]{0:T(1024)S(1)} %get-tuple-element.25, s32[96]{0:T(128)S(1)} %get-tuple-element.20, s32[96]{0:T(128)S(1)} %get-tuple-element.21), kind=kOutput, calls=%fused_computation.1 | convolution fusion | flops 183275520 | bytes 5687040 | tf_op jit(solution)/shard_map/dot_general | solution.py:207
  23.7 0.2 fusion.18.inv_ref
  24.0 4.0 %shard_map.55 = f32[128,512]{1,0:T(8,128)S(1)} custom-call(bf16[1,96,640]{2,1,0:T(8,128)(2,1)S(1)} %bitcast.82, f32[96,512]{1,0:T(8,128)S(1)} %fusion.18.inv_ref, bf16[128,7296]{1,0:T(8,128)(2,1)S(1)} %fusion.w_ref), custom_call_target="tpu_custom_call" | custom-call | tf_op jit(solution)/shard_map/pallas_call | solution.py:72
  28.0 2.4 %collective-permute-start.5 = (f32[32,512]{1,0:T(8,128)S(1)}, f32[32,512]{1,0:T(8,128)S(1)}, u32[]{:S(2)}, u32[]{:S(2)}) collective-permute-start(f32[32,512]{1,0:T(8,128)S(1)} %get-tuple-element.7), channel_id=1, source_target_pairs={{0,4},{4,8},{8,12},{12,0},{1,5},{5,9},{9,13},{13,1},{2,6},{6,10},{... | collective-permute-start | bytes 196616 | tf_op jit(solution)/shard_map/ppermute | solution.py:224
  30.4 3.0 %collective-permute-start.6 = (f32[32,512]{1,0:T(8,128)S(1)}, f32[32,512]{1,0:T(8,128)S(1)}, u32[]{:S(2)}, u32[]{:S(2)}) collective-permute-start(f32[32,512]{1,0:T(8,128)S(1)} %get-tuple-element.6), channel_id=1, source_target_pairs={{0,8},{4,12},{8,0},{12,4},{1,9},{5,13},{9,1},{13,5},{2,10},{6,14},... | collective-permute-start | bytes 196616 | tf_op jit(solution)/shard_map/ppermute | solution.py:224
  33.4 2.8 %collective-permute-start.7 = (f32[32,512]{1,0:T(8,128)S(1)}, f32[32,512]{1,0:T(8,128)S(1)}, u32[]{:S(2)}, u32[]{:S(2)}) collective-permute-start(f32[32,512]{1,0:T(8,128)S(1)} %get-tuple-element.5), channel_id=1, source_target_pairs={{0,12},{4,0},{8,4},{12,8},{1,13},{5,1},{9,5},{13,9},{2,14},{6,2},{... | collective-permute-start | bytes 196616 | tf_op jit(solution)/shard_map/ppermute | solution.py:224
  36.4 1.8 %collective-permute-done.7 = f32[32,512]{1,0:T(8,128)S(1)} collective-permute-done((f32[32,512]{1,0:T(8,128)S(1)}, f32[32,512]{1,0:T(8,128)S(1)}, u32[]{:S(2)}, u32[]{:S(2)}) %collective-permute-start.7) | collective-permute-done | bytes 65568 | tf_op jit(solution)/shard_map/ppermute | solution.py:224
  38.2 0.6 %bitcast_dynamic-update-slice_fusion = f32[1,32,2048]{2,1,0:T(8,128)} fusion(f32[1,32,2048]{2,1,0:T(8,128)} %copy-done.1, s32[]{:T(128)S(6)} %select_n.256, f32[32,512]{1,0:T(8,128)S(1)} %collective-permute-done.7), kind=kLoop, calls=%fused_computation.39 | loop fusion | bytes 131076 | tf_op jit(solution)/shard_map/dynamic_update_slice | solution.py:228
  (82 shorter events, 2.9 us)
Async XLA Ops:
  0.0 10.4 %copy-start = (bf16[64]{0:T(256)(128)(2,1)S(1)}, bf16[64]{0:T(256)(128)(2,1)}, u32[]{:S(2)}) copy-start(bf16[64]{0:T(256)(128)(2,1)} %param.7) | copy-start | bytes 388
  0.0 10.3 %copy-start.2 = (s32[128,3,32]{0,2,1:T(8,128)S(1)}, s32[128,3,32]{0,2,1:T(8,128)}, u32[]{:S(2)}) copy-start(s32[128,3,32]{0,2,1:T(8,128)} %param.9) | copy-start | bytes 147460
  0.8 14.7 %collective-permute-start.4 = (bf16[32,256]{1,0:T(8,128)(2,1)S(1)}, bf16[32,256]{1,0:T(8,128)(2,1)S(1)}, u32[]{:S(2)}, u32[]{:S(2)}) collective-permute-start(bf16[32,256]{1,0:T(8,128)(2,1)S(1)} %get-tuple-element.19), channel_id=1, source_target_pairs={{0,8},{4,12},{8,0},{12,4},{1,9},{5,13},{9,1},{13,5},{2,10},{6,14},... | collective-permute-start | bytes 49160 | tf_op jit(solution)/shard_map/ppermute | solution.py:122
  8.0 7.3 %collective-permute-start.1 = (bf16[64,512]{1,0:T(8,128)(2,1)S(1)}, bf16[64,512]{1,0:T(8,128)(2,1)S(1)}, u32[]{:S(2)}, u32[]{:S(2)}) collective-permute-start(bf16[64,512]{1,0:T(8,128)(2,1)S(1)} %pad_maximum_fusion), channel_id=1, source_target_pairs={{0,12},{4,0},{8,4},{12,8},{1,13},{5,1},{9,5},{13,9},{2,14},{6,2},{... | collective-permute-start | bytes 196616 | tf_op jit(solution)/shard_map/ppermute | solution.py:116
  9.5 5.7 %collective-permute-start = (bf16[112,128]{1,0:T(8,128)(2,1)S(1)}, bf16[112,128]{1,0:T(8,128)(2,1)S(1)}, u32[]{:S(2)}, u32[]{:S(2)}) collective-permute-start(bf16[112,128]{1,0:T(8,128)(2,1)S(1)} %pad_maximum_fusion.7), channel_id=1, source_target_pairs={{0,4},{4,8},{8,12},{12,0},{1,5},{5,9},{9,13},{13,1},{2,6},{6,10},{... | collective-permute-start | bytes 86024 | tf_op jit(solution)/shard_map/ppermute | solution.py:112
  17.2 5.5 %collective-permute-start.2 = (bf16[48,640]{1,0:T(8,128)(2,1)S(1)}, bf16[48,640]{1,0:T(8,128)(2,1)S(1)}, u32[]{:S(2)}, u32[]{:S(2)}) collective-permute-start(bf16[48,640]{1,0:T(8,128)(2,1)S(1)} %get-tuple-element.11), channel_id=1, source_target_pairs={{0,0},{2,4},{4,8},{6,12},{8,2},{10,6},{12,10},{14,14},{1,1},{3,5},... | collective-permute-start | bytes 184328 | tf_op jit(solution)/shard_map/ppermute | solution.py:164
  17.9 5.0 %collective-permute-start.3 = (bf16[48,640]{1,0:T(8,128)(2,1)S(1)}, bf16[48,640]{1,0:T(8,128)(2,1)S(1)}, u32[]{:S(2)}, u32[]{:S(2)}) collective-permute-start(bf16[48,640]{1,0:T(8,128)(2,1)S(1)} %get-tuple-element.10), channel_id=1, source_target_pairs={{0,4},{2,0},{4,12},{6,8},{8,6},{10,2},{12,14},{14,10},{1,5},{3,1},... | collective-permute-start | bytes 184328 | tf_op jit(solution)/shard_map/ppermute | solution.py:164
  28.0 8.3 %collective-permute-start.5 = (f32[32,512]{1,0:T(8,128)S(1)}, f32[32,512]{1,0:T(8,128)S(1)}, u32[]{:S(2)}, u32[]{:S(2)}) collective-permute-start(f32[32,512]{1,0:T(8,128)S(1)} %get-tuple-element.7), channel_id=1, source_target_pairs={{0,4},{4,8},{8,12},{12,0},{1,5},{5,9},{9,13},{13,1},{2,6},{6,10},{... | collective-permute-start | bytes 196616 | tf_op jit(solution)/shard_map/ppermute | solution.py:224
  30.4 6.0 %collective-permute-start.6 = (f32[32,512]{1,0:T(8,128)S(1)}, f32[32,512]{1,0:T(8,128)S(1)}, u32[]{:S(2)}, u32[]{:S(2)}) collective-permute-start(f32[32,512]{1,0:T(8,128)S(1)} %get-tuple-element.6), channel_id=1, source_target_pairs={{0,8},{4,12},{8,0},{12,4},{1,9},{5,13},{9,1},{13,5},{2,10},{6,14},... | collective-permute-start | bytes 196616 | tf_op jit(solution)/shard_map/ppermute | solution.py:224
  33.4 4.8 %collective-permute-start.7 = (f32[32,512]{1,0:T(8,128)S(1)}, f32[32,512]{1,0:T(8,128)S(1)}, u32[]{:S(2)}, u32[]{:S(2)}) collective-permute-start(f32[32,512]{1,0:T(8,128)S(1)} %get-tuple-element.5), channel_id=1, source_target_pairs={{0,12},{4,0},{8,4},{12,8},{1,13},{5,1},{9,5},{13,9},{2,14},{6,2},{... | collective-permute-start | bytes 196616 | tf_op jit(solution)/shard_map/ppermute | solution.py:224
  36.4 1.8 %copy-start.1 = (f32[1,32,2048]{2,1,0:T(8,128)}, f32[1,32,2048]{2,1,0:T(8,128)S(1)}, u32[]{:S(2)}) copy-start(f32[1,32,2048]{2,1,0:T(8,128)S(1)} %bitcast_dynamic-update-slice_fusion.1) | copy-start | bytes 786436

commit v16 on v15

--- a/solution.py
+++ b/solution.py
@@ -216,16 +216,16 @@
             .reshape(count, chunks * JP * row_block)
         )
     stacked = correlate(windows, inv, weights, row_block)
-    pieces = [lax.dynamic_slice_in_dim(stacked, corr_place * local_count, local_count, 0)]
+    mine = lax.dynamic_slice_in_dim(stacked, corr_place * local_count, local_count, 0)
+    result = jnp.zeros((local_count, corr_count * width), jnp.float32)
+    result = lax.dynamic_update_slice_in_dim(result, mine, corr_place * width, 1)
     for d in range(1, corr_count):
-        target = (corr_place + d) % corr_count
-        part = lax.dynamic_slice_in_dim(stacked, target * local_count, local_count, 0)
-        route = [(i, (i + d) % corr_count) for i in range(corr_count)]
-        pieces.append(lax.ppermute(part, "corr", route))
-    stacked = jnp.zeros((local_count, corr_count * width), jnp.float32)
-    for d, part in enumerate(pieces):
-        place = ((corr_place - d) % corr_count) * width
-        stacked = lax.dynamic_update_slice_in_dim(stacked, part, place, 1)
+        partner = corr_place ^ d
+        part = lax.dynamic_slice_in_dim(stacked, partner * local_count, local_count, 0)
+        route = [(i, i ^ d) for i in range(corr_count)]
+        part = lax.ppermute(part, "corr", route)
+        result = lax.dynamic_update_slice_in_dim(result, part, partner * width, 1)
+    stacked = result
     return stacked[None]
 
 

time: 39.1 us -> 40.5 us (1.036)
  waiting for transfers between devices: 5.68 us -> 8.61 us
  starting transfers between devices: 16.9 us -> 15.4 us
    ppermute x3, waiting for transfers between devices: 1.79 us -> 4.68 us  [body(): part = lax.ppermute(part, 'corr', route)]
    ppermute x3, starting transfers between devices: 8.25 us -> 6.8 us  [body(): part = lax.ppermute(part, 'corr', route)]
  transfers between devices with their start and end apart: 8 -> 8, of which waited for: 3 -> 4; matrix products, arithmetic and copies ran while one was open for 19% -> 18% of each run, Pallas kernels for 0% -> 0%
where the time goes in v16:
time: 40.5 us; the launch traced here: 40.2 us
  starting transfers between devices  15.4 us (38%)
  waiting for transfers between devices  8.61 us (21%)
  local copies, waits for them, and re-layouts  5.74 us (14%)
  Pallas kernels  3.97 us (10%)
  matrix products  3.56 us (9%)
  other arithmetic  2.17 us (5%)
  between operations  0.74 us (2%)
    ppermute x3, starting transfers between devices, body(): part = lax.ppermute(part, 'corr', route)  6.8 us
    ppermute x3, waiting for transfers between devices, body(): part = lax.ppermute(part, 'corr', route)  4.68 us
    ppermute x1, starting transfers between devices, body(): blocks_by_offset[d] = lax.ppermute(wide, 'corr', route)  4.06 us
    pallas_call x1, Pallas kernels, correlate(): pl.pallas_call(functools.partial(corr_kernel, row_block=row_block, tile=t...  3.97 us
    ppermute x1, waiting for transfers between devices, body(): got = lax.ppermute(sent, 'corr', forward)  3.82 us
    ppermute x2, starting transfers between devices, body(): received.append(lax.ppermute(part, ('corr', 'filt'), route))  2.42 us
    dot_general x1, matrix products, body(): spread = jnp.dot(padded, pick_base, preferred_element_type=jnp.float32)  1.9 us
    unnamed x15, local copies, waits for them, and re-layouts  1.45 us
  transfers between devices with their start and end apart: 8, of which 4 were waited for; matrix products, arithmetic and copies ran while one was open for 18% of the time, Pallas kernels for 0%

profile of v16, /device:TPU:0, one launch (start us, length us, event | category | flops | bytes accessed | tf_op | source)
XLA Modules:
  0.0 40.2 jit_solution(13799243765297053435)
XLA Ops:
  0.0 0.7 %pad_bitcast_fusion = (bf16[1,32,256]{2,1,0:T(8,128)(2,1)S(1)}, bf16[32,256]{1,0:T(8,128)(2,1)S(1)}) fusion(bf16[32,225]{1,0:T(8,128)(2,1)} %param.8), kind=kLoop, calls=%fused_computation.126 | loop fusion | bytes 47168 | tf_op jit(solution)/shard_map/stack | solution.py:123
  0.8 4.1 %collective-permute-start.4 = (bf16[32,256]{1,0:T(8,128)(2,1)S(1)}, bf16[32,256]{1,0:T(8,128)(2,1)S(1)}, u32[]{:S(2)}, u32[]{:S(2)}) collective-permute-start(bf16[32,256]{1,0:T(8,128)(2,1)S(1)} %get-tuple-element.19), channel_id=1, source_target_pairs={{0,8},{4,12},{8,0},{12,4},{1,9},{5,13},{9,1},{13,5},{2,10},{6,14},... | collective-permute-start | bytes 49160 | tf_op jit(solution)/shard_map/ppermute | solution.py:122
  4.9 0.8 %broadcast_compare_fusion = pred[16,4096]{1,0:T(8,128)(4,1)S(1)} fusion(s32[4096]{0:T(1024)S(1)} %iota_add_fusion.1, s32[16]{0:T(128)} %bitcast.86), kind=kLoop, calls=%fused_computation.33 | loop fusion | flops 65536 | bytes 81984 | tf_op jit(solution)/shard_map/lt | solution.py:99
  5.6 0.3 broadcast_in_dim.67
  5.9 0.4 broadcast_in_dim.68
  6.3 1.3 %copy.11 = bf16[1,16,3,4096]{3,2,1,0:T(4,128)(2,1)S(1)} copy(bf16[1,16,3,4096]{3,1,2,0:T(8,128)(2,1)} %param.5) | data formatting | bytes 786432 | tf_op args[0]
  7.6 0.3 squeeze.18
  8.0 1.4 %collective-permute-start.1 = (bf16[64,512]{1,0:T(8,128)(2,1)S(1)}, bf16[64,512]{1,0:T(8,128)(2,1)S(1)}, u32[]{:S(2)}, u32[]{:S(2)}) collective-permute-start(bf16[64,512]{1,0:T(8,128)(2,1)S(1)} %pad_maximum_fusion), channel_id=1, source_target_pairs={{0,12},{4,0},{8,4},{12,8},{1,13},{5,1},{9,5},{13,9},{2,14},{6,2},{... | collective-permute-start | bytes 196616 | tf_op jit(solution)/shard_map/ppermute | solution.py:116
  9.5 0.7 %collective-permute-start = (bf16[112,128]{1,0:T(8,128)(2,1)S(1)}, bf16[112,128]{1,0:T(8,128)(2,1)S(1)}, u32[]{:S(2)}, u32[]{:S(2)}) collective-permute-start(bf16[112,128]{1,0:T(8,128)(2,1)S(1)} %pad_maximum_fusion.7), channel_id=1, source_target_pairs={{0,4},{4,8},{8,12},{12,0},{1,5},{5,9},{9,13},{13,1},{2,6},{6,10},{... | collective-permute-start | bytes 86024 | tf_op jit(solution)/shard_map/ppermute | solution.py:112
  10.8 0.4 tile.10
  11.4 3.8 %collective-permute-done = bf16[112,128]{1,0:T(8,128)(2,1)S(1)} collective-permute-done((bf16[112,128]{1,0:T(8,128)(2,1)S(1)}, bf16[112,128]{1,0:T(8,128)(2,1)S(1)}, u32[]{:S(2)}, u32[]{:S(2)}) %collective-permute-start) | collective-permute-done | bytes 28704 | tf_op jit(solution)/shard_map/ppermute | solution.py:112
  16.4 0.2 reshape.229
  16.7 0.3 convolution_convert_fusion
  17.2 0.7 %collective-permute-start.2 = (bf16[48,640]{1,0:T(8,128)(2,1)S(1)}, bf16[48,640]{1,0:T(8,128)(2,1)S(1)}, u32[]{:S(2)}, u32[]{:S(2)}) collective-permute-start(bf16[48,640]{1,0:T(8,128)(2,1)S(1)} %get-tuple-element.11), channel_id=1, source_target_pairs={{0,0},{2,4},{4,8},{6,12},{8,2},{10,6},{12,10},{14,14},{1,1},{3,5},... | collective-permute-start | bytes 184328 | tf_op jit(solution)/shard_map/ppermute | solution.py:164
  17.9 1.8 %collective-permute-start.3 = (bf16[48,640]{1,0:T(8,128)(2,1)S(1)}, bf16[48,640]{1,0:T(8,128)(2,1)S(1)}, u32[]{:S(2)}, u32[]{:S(2)}) collective-permute-start(bf16[48,640]{1,0:T(8,128)(2,1)S(1)} %get-tuple-element.10), channel_id=1, source_target_pairs={{0,4},{2,0},{4,12},{6,8},{8,6},{10,2},{12,14},{14,10},{1,5},{3,1},... | collective-permute-start | bytes 184328 | tf_op jit(solution)/shard_map/ppermute | solution.py:164
  19.6 1.9 %fusion.1 = f32[128,7296]{1,0:T(8,128)S(1)} fusion(bf16[128,228]{0,1:T(8,128)(2,1)S(1)} %reshape.234, s32[7296]{0:T(1024)S(1)} %get-tuple-element.25, s32[7296]{0:T(1024)S(1)} %add_select_fusion.3, s32[228]{0:T(256)S(1)} %get-tuple-element.22, s32[228]{0:T(256)S(1)} %get-tuple-element.23), kind=kOutput, calls=%fused_computation.2 | convolution fusion | flops 430843392 | bytes 3854112 | tf_op jit(solution)/shard_map/dot_general | solution.py:206
  21.6 1.2 %fusion.w_ref = bf16[128,7296]{1,0:T(8,128)(2,1)S(1)} fusion(f32[128,7296]{1,0:T(8,128)S(1)} %fusion.1, bf16[128,96]{0,1:T(8,128)(2,1)S(1)} %bitcast.84, s32[7296]{0:T(1024)S(1)} %get-tuple-element.24, s32[7296]{0:T(1024)S(1)} %get-tuple-element.25, s32[96]{0:T(128)S(1)} %get-tuple-element.20, s32[96]{0:T(128)S(1)} %get-tuple-element.21), kind=kOutput, calls=%fused_computation.1 | convolution fusion | flops 183275520 | bytes 5687040 | tf_op jit(solution)/shard_map/dot_general | solution.py:207
  24.0 4.0 %shard_map.55 = f32[128,512]{1,0:T(8,128)S(1)} custom-call(bf16[1,96,640]{2,1,0:T(8,128)(2,1)S(1)} %bitcast.82, f32[96,512]{1,0:T(8,128)S(1)} %fusion.18.inv_ref, bf16[128,7296]{1,0:T(8,128)(2,1)S(1)} %fusion.w_ref), custom_call_target="tpu_custom_call" | custom-call | tf_op jit(solution)/shard_map/pallas_call | solution.py:72
  28.0 2.4 %collective-permute-start.5 = (f32[32,512]{1,0:T(8,128)S(1)}, f32[32,512]{1,0:T(8,128)S(1)}, u32[]{:S(2)}, u32[]{:S(2)}) collective-permute-start(f32[32,512]{1,0:T(8,128)S(1)} %get-tuple-element.7), channel_id=1, source_target_pairs={{0,4},{4,0},{8,12},{12,8},{1,5},{5,1},{9,13},{13,9},{2,6},{6,2},{1... | collective-permute-start | bytes 196616 | tf_op jit(solution)/shard_map/ppermute | solution.py:226
  30.4 3.0 %collective-permute-start.6 = (f32[32,512]{1,0:T(8,128)S(1)}, f32[32,512]{1,0:T(8,128)S(1)}, u32[]{:S(2)}, u32[]{:S(2)}) collective-permute-start(f32[32,512]{1,0:T(8,128)S(1)} %get-tuple-element.6), channel_id=1, source_target_pairs={{0,8},{4,12},{8,0},{12,4},{1,9},{5,13},{9,1},{13,5},{2,10},{6,14},... | collective-permute-start | bytes 196616 | tf_op jit(solution)/shard_map/ppermute | solution.py:226
  33.4 1.4 %collective-permute-start.7 = (f32[32,512]{1,0:T(8,128)S(1)}, f32[32,512]{1,0:T(8,128)S(1)}, u32[]{:S(2)}, u32[]{:S(2)}) collective-permute-start(f32[32,512]{1,0:T(8,128)S(1)} %get-tuple-element.5), channel_id=1, source_target_pairs={{0,12},{4,8},{8,4},{12,0},{1,13},{5,9},{9,5},{13,1},{2,14},{6,10},... | collective-permute-start | bytes 196616 | tf_op jit(solution)/shard_map/ppermute | solution.py:226
  34.9 0.9 %collective-permute-done.6 = f32[32,512]{1,0:T(8,128)S(1)} collective-permute-done((f32[32,512]{1,0:T(8,128)S(1)}, f32[32,512]{1,0:T(8,128)S(1)}, u32[]{:S(2)}, u32[]{:S(2)}) %collective-permute-start.6) | collective-permute-done | bytes 65568 | tf_op jit(solution)/shard_map/ppermute | solution.py:226
  35.8 3.8 %collective-permute-done.7 = f32[32,512]{1,0:T(8,128)S(1)} collective-permute-done((f32[32,512]{1,0:T(8,128)S(1)}, f32[32,512]{1,0:T(8,128)S(1)}, u32[]{:S(2)}, u32[]{:S(2)}) %collective-permute-start.7) | collective-permute-done | bytes 65568 | tf_op jit(solution)/shard_map/ppermute | solution.py:226
  39.6 0.6 %bitcast_dynamic-update-slice_fusion = f32[1,32,2048]{2,1,0:T(8,128)} fusion(f32[1,32,2048]{2,1,0:T(8,128)} %copy-done.1, s32[]{:T(128)S(6)} %select_n.233, f32[32,512]{1,0:T(8,128)S(1)} %collective-permute-done.7), kind=kLoop, calls=%fused_computation.39 | loop fusion | bytes 131076 | tf_op jit(solution)/shard_map/dynamic_update_slice | solution.py:227
  (82 shorter events, 3.1 us)
Async XLA Ops:
  0.0 10.4 %copy-start = (bf16[64]{0:T(256)(128)(2,1)S(1)}, bf16[64]{0:T(256)(128)(2,1)}, u32[]{:S(2)}) copy-start(bf16[64]{0:T(256)(128)(2,1)} %param.7) | copy-start | bytes 388
  0.0 10.3 %copy-start.2 = (s32[128,3,32]{0,2,1:T(8,128)S(1)}, s32[128,3,32]{0,2,1:T(8,128)}, u32[]{:S(2)}) copy-start(s32[128,3,32]{0,2,1:T(8,128)} %param.9) | copy-start | bytes 147460
  0.8 14.7 %collective-permute-start.4 = (bf16[32,256]{1,0:T(8,128)(2,1)S(1)}, bf16[32,256]{1,0:T(8,128)(2,1)S(1)}, u32[]{:S(2)}, u32[]{:S(2)}) collective-permute-start(bf16[32,256]{1,0:T(8,128)(2,1)S(1)} %get-tuple-element.19), channel_id=1, source_target_pairs={{0,8},{4,12},{8,0},{12,4},{1,9},{5,13},{9,1},{13,5},{2,10},{6,14},... | collective-permute-start | bytes 49160 | tf_op jit(solution)/shard_map/ppermute | solution.py:122
  8.0 7.3 %collective-permute-start.1 = (bf16[64,512]{1,0:T(8,128)(2,1)S(1)}, bf16[64,512]{1,0:T(8,128)(2,1)S(1)}, u32[]{:S(2)}, u32[]{:S(2)}) collective-permute-start(bf16[64,512]{1,0:T(8,128)(2,1)S(1)} %pad_maximum_fusion), channel_id=1, source_target_pairs={{0,12},{4,0},{8,4},{12,8},{1,13},{5,1},{9,5},{13,9},{2,14},{6,2},{... | collective-permute-start | bytes 196616 | tf_op jit(solution)/shard_map/ppermute | solution.py:116
  9.5 5.7 %collective-permute-start = (bf16[112,128]{1,0:T(8,128)(2,1)S(1)}, bf16[112,128]{1,0:T(8,128)(2,1)S(1)}, u32[]{:S(2)}, u32[]{:S(2)}) collective-permute-start(bf16[112,128]{1,0:T(8,128)(2,1)S(1)} %pad_maximum_fusion.7), channel_id=1, source_target_pairs={{0,4},{4,8},{8,12},{12,0},{1,5},{5,9},{9,13},{13,1},{2,6},{6,10},{... | collective-permute-start | bytes 86024 | tf_op jit(solution)/shard_map/ppermute | solution.py:112
  17.2 5.5 %collective-permute-start.2 = (bf16[48,640]{1,0:T(8,128)(2,1)S(1)}, bf16[48,640]{1,0:T(8,128)(2,1)S(1)}, u32[]{:S(2)}, u32[]{:S(2)}) collective-permute-start(bf16[48,640]{1,0:T(8,128)(2,1)S(1)} %get-tuple-element.11), channel_id=1, source_target_pairs={{0,0},{2,4},{4,8},{6,12},{8,2},{10,6},{12,10},{14,14},{1,1},{3,5},... | collective-permute-start | bytes 184328 | tf_op jit(solution)/shard_map/ppermute | solution.py:164
  17.9 5.0 %collective-permute-start.3 = (bf16[48,640]{1,0:T(8,128)(2,1)S(1)}, bf16[48,640]{1,0:T(8,128)(2,1)S(1)}, u32[]{:S(2)}, u32[]{:S(2)}) collective-permute-start(bf16[48,640]{1,0:T(8,128)(2,1)S(1)} %get-tuple-element.10), channel_id=1, source_target_pairs={{0,4},{2,0},{4,12},{6,8},{8,6},{10,2},{12,14},{14,10},{1,5},{3,1},... | collective-permute-start | bytes 184328 | tf_op jit(solution)/shard_map/ppermute | solution.py:164
  28.0 6.9 %collective-permute-start.5 = (f32[32,512]{1,0:T(8,128)S(1)}, f32[32,512]{1,0:T(8,128)S(1)}, u32[]{:S(2)}, u32[]{:S(2)}) collective-permute-start(f32[32,512]{1,0:T(8,128)S(1)} %get-tuple-element.7), channel_id=1, source_target_pairs={{0,4},{4,0},{8,12},{12,8},{1,5},{5,1},{9,13},{13,9},{2,6},{6,2},{1... | collective-permute-start | bytes 196616 | tf_op jit(solution)/shard_map/ppermute | solution.py:226
  30.4 5.4 %collective-permute-start.6 = (f32[32,512]{1,0:T(8,128)S(1)}, f32[32,512]{1,0:T(8,128)S(1)}, u32[]{:S(2)}, u32[]{:S(2)}) collective-permute-start(f32[32,512]{1,0:T(8,128)S(1)} %get-tuple-element.6), channel_id=1, source_target_pairs={{0,8},{4,12},{8,0},{12,4},{1,9},{5,13},{9,1},{13,5},{2,10},{6,14},... | collective-permute-start | bytes 196616 | tf_op jit(solution)/shard_map/ppermute | solution.py:226
  33.4 6.2 %collective-permute-start.7 = (f32[32,512]{1,0:T(8,128)S(1)}, f32[32,512]{1,0:T(8,128)S(1)}, u32[]{:S(2)}, u32[]{:S(2)}) collective-permute-start(f32[32,512]{1,0:T(8,128)S(1)} %get-tuple-element.5), channel_id=1, source_target_pairs={{0,12},{4,8},{8,4},{12,0},{1,13},{5,9},{9,5},{13,1},{2,14},{6,10},... | collective-permute-start | bytes 196616 | tf_op jit(solution)/shard_map/ppermute | solution.py:226
  35.7 3.8 %copy-start.1 = (f32[1,32,2048]{2,1,0:T(8,128)}, f32[1,32,2048]{2,1,0:T(8,128)S(1)}, u32[]{:S(2)}) copy-start(f32[1,32,2048]{2,1,0:T(8,128)S(1)} %bitcast_dynamic-update-slice_fusion.1) | copy-start | bytes 786436

commit v17 on v15

--- a/solution.py
+++ b/solution.py
@@ -11,6 +11,7 @@
 TAPS = 64
 DEC = 4
 JP = 76
+JPI = 80
 TT = 512
 RSUB = 16
 
@@ -63,23 +64,46 @@
         o_ref[...] += part
 
 
-def correlate(windows, inv, weights, row_block):
+def corr_kernel_interleaved(f_ref, inv_ref, w_ref, o_ref, s_ref, *, row_block, tile):
+    span = tile + 128
+    depth = JPI * RSUB
+    part = None
+    for sub in range(row_block // RSUB):
+        r0 = sub * RSUB
+        seg = f_ref[0, r0 : r0 + RSUB, :].astype(jnp.float32)
+        inv = inv_ref[r0 : r0 + RSUB, :]
+        for j in range(JPI):
+            moved = seg if j == 0 else pltpu.roll(seg, span - j, 1)
+            piece = (moved[:, :tile] * inv).astype(jnp.bfloat16)
+            s_ref[sub * depth + j * RSUB : sub * depth + (j + 1) * RSUB, :] = piece
+        step = jnp.dot(
+            w_ref[:, sub * depth : (sub + 1) * depth],
+            s_ref[sub * depth : (sub + 1) * depth, :],
+            preferred_element_type=jnp.float32,
+        )
+        part = step if part is None else part + step
+    o_ref[...] = part
+
+
+def correlate(windows, inv, weights, row_block, interleaved=False):
     tiles, rows, span = windows.shape
     count = weights.shape[0]
     width = inv.shape[1]
     tile = width // tiles
     chunks = rows // row_block
+    lags = JPI if interleaved else JP
+    body_fn = corr_kernel_interleaved if interleaved else corr_kernel
     return pl.pallas_call(
-        functools.partial(corr_kernel, row_block=row_block, tile=tile),
+        functools.partial(body_fn, row_block=row_block, tile=tile),
         grid=(tiles, chunks),
         in_specs=[
             pl.BlockSpec((1, row_block, span), lambda i, q: (i, q, 0)),
             pl.BlockSpec((row_block, tile), lambda i, q: (q, i)),
-            pl.BlockSpec((count, JP * row_block), lambda i, q: (0, q)),
+            pl.BlockSpec((count, lags * row_block), lambda i, q: (0, q)),
         ],
         out_specs=pl.BlockSpec((count, tile), lambda i, q: (0, i)),
         out_shape=jax.ShapeDtypeStruct((count, width), jnp.float32),
-        scratch_shapes=[pltpu.VMEM((JP * row_block, tile), jnp.bfloat16)],
+        scratch_shapes=[pltpu.VMEM((lags * row_block, tile), jnp.bfloat16)],
         compiler_params=pltpu.CompilerParams(
             dimension_semantics=("parallel", "arbitrary"),
             vmem_limit_bytes=48 * 1024 * 1024,
@@ -187,16 +211,17 @@
     row_block = 96 if total_rows % 96 == 0 else total_rows
     chunks = total_rows // row_block
     if chunks == 1:
-        padded = jnp.concatenate([base, jnp.zeros((count, 3, JP - L), base.dtype)], axis=2)
-        padded = padded.astype(jnp.bfloat16).reshape(count, 3 * JP)
+        padded = jnp.concatenate([base, jnp.zeros((count, 3, JPI - L), base.dtype)], axis=2)
+        padded = padded.astype(jnp.bfloat16).reshape(count, 3 * JPI)
         flat = jnp.transpose(chosen, (0, 1, 2)).reshape(count, total_rows).astype(jnp.bfloat16)
         start_zero = lax.optimization_barrier(jnp.zeros((), jnp.int32))
-        column = lax.iota(jnp.int32, JP * total_rows) + start_zero
-        lag = column // total_rows
-        row = column % total_rows
-        source = lax.iota(jnp.int32, 3 * JP)
+        column = lax.iota(jnp.int32, JPI * total_rows) + start_zero
+        group = column // (JPI * RSUB)
+        lag = (column % (JPI * RSUB)) // RSUB
+        row = group * RSUB + column % RSUB
+        source = lax.iota(jnp.int32, 3 * JPI)
         pick_base = (
-            (source[:, None] % JP == lag[None, :]) & (source[:, None] // JP == row[None, :] % 3)
+            (source[:, None] % JPI == lag[None, :]) & (source[:, None] // JPI == row[None, :] % 3)
         ).astype(jnp.bfloat16)
         slot = lax.iota(jnp.int32, total_rows)
         pick_mask = (
@@ -215,7 +240,7 @@
             .transpose(0, 2, 1, 3)
             .reshape(count, chunks * JP * row_block)
         )
-    stacked = correlate(windows, inv, weights, row_block)
+    stacked = correlate(windows, inv, weights, row_block, interleaved=chunks == 1)
     pieces = [lax.dynamic_slice_in_dim(stacked, corr_place * local_count, local_count, 0)]
     for d in range(1, corr_count):
         target = (corr_place + d) % corr_count

time: 39.1 us -> 38.3 us (0.980)
  Pallas kernels: 3.97 us -> 3.2 us
    pallas_call x1, Pallas kernels: 3.97 us -> 3.2 us  [correlate(): pl.pallas_call(functools.partial(body_fn, row_block=row_block, tile=tile)...]
  transfers between devices with their start and end apart: 8 -> 8, of which waited for: 3 -> 2; matrix products, arithmetic and copies ran while one was open for 19% -> 20% of each run, Pallas kernels for 0% -> 0%
where the time goes in v17:
time: 38.3 us; the launch traced here: 38 us
  starting transfers between devices  16.8 us (44%)
  local copies, waits for them, and re-layouts  5.73 us (15%)
  waiting for transfers between devices  5.55 us (14%)
  matrix products  3.76 us (10%)
  Pallas kernels  3.2 us (8%)
  other arithmetic  2.2 us (6%)
  between operations  0.8 us (2%)
    ppermute x3, starting transfers between devices, body(): pieces.append(lax.ppermute(part, 'corr', route))  8.15 us
    ppermute x1, starting transfers between devices, body(): blocks_by_offset[d] = lax.ppermute(wide, 'corr', route)  4.06 us
    ppermute x1, waiting for transfers between devices, body(): got = lax.ppermute(sent, 'corr', forward)  3.75 us
    pallas_call x1, Pallas kernels, correlate(): pl.pallas_call(functools.partial(body_fn, row_block=row_block, tile=tile)...  3.2 us
    ppermute x2, starting transfers between devices, body(): received.append(lax.ppermute(part, ('corr', 'filt'), route))  2.42 us
    dot_general x1, matrix products, body(): spread = jnp.dot(padded, pick_base, preferred_element_type=jnp.float32)  2.03 us
    ppermute x3, waiting for transfers between devices, body(): pieces.append(lax.ppermute(part, 'corr', route))  1.79 us
    unnamed x15, local copies, waits for them, and re-layouts  1.45 us
  transfers between devices with their start and end apart: 8, of which 2 were waited for; matrix products, arithmetic and copies ran while one was open for 20% of the time, Pallas kernels for 0%

profile of v17, /device:TPU:0, one launch (start us, length us, event | category | flops | bytes accessed | tf_op | source)
XLA Modules:
  0.0 38.0 jit_solution(1089488882214126073)
XLA Ops:
  0.0 0.7 %pad_bitcast_fusion = (bf16[1,32,256]{2,1,0:T(8,128)(2,1)S(1)}, bf16[32,256]{1,0:T(8,128)(2,1)S(1)}) fusion(bf16[32,225]{1,0:T(8,128)(2,1)} %param.8), kind=kLoop, calls=%fused_computation.140 | loop fusion | bytes 47168 | tf_op jit(solution)/shard_map/stack | solution.py:147
  0.8 4.1 %collective-permute-start.4 = (bf16[32,256]{1,0:T(8,128)(2,1)S(1)}, bf16[32,256]{1,0:T(8,128)(2,1)S(1)}, u32[]{:S(2)}, u32[]{:S(2)}) collective-permute-start(bf16[32,256]{1,0:T(8,128)(2,1)S(1)} %get-tuple-element.19), channel_id=1, source_target_pairs={{0,8},{4,12},{8,0},{12,4},{1,9},{5,13},{9,1},{13,5},{2,10},{6,14},... | collective-permute-start | bytes 49160 | tf_op jit(solution)/shard_map/ppermute | solution.py:146
  4.9 0.8 %broadcast_compare_fusion = pred[16,4096]{1,0:T(8,128)(4,1)S(1)} fusion(s32[4096]{0:T(1024)S(1)} %iota_add_fusion.1, s32[16]{0:T(128)} %bitcast.86), kind=kLoop, calls=%fused_computation.33 | loop fusion | flops 65536 | bytes 81984 | tf_op jit(solution)/shard_map/lt | solution.py:123
  5.6 0.3 broadcast_in_dim.67
  5.9 0.4 broadcast_in_dim.68
  6.3 1.3 %copy.11 = bf16[1,16,3,4096]{3,2,1,0:T(4,128)(2,1)S(1)} copy(bf16[1,16,3,4096]{3,1,2,0:T(8,128)(2,1)} %param.5) | data formatting | bytes 786432 | tf_op args[0]
  7.6 0.3 squeeze.18
  8.0 1.4 %collective-permute-start.1 = (bf16[64,512]{1,0:T(8,128)(2,1)S(1)}, bf16[64,512]{1,0:T(8,128)(2,1)S(1)}, u32[]{:S(2)}, u32[]{:S(2)}) collective-permute-start(bf16[64,512]{1,0:T(8,128)(2,1)S(1)} %pad_maximum_fusion), channel_id=1, source_target_pairs={{0,12},{4,0},{8,4},{12,8},{1,13},{5,1},{9,5},{13,9},{2,14},{6,2},{... | collective-permute-start | bytes 196616 | tf_op jit(solution)/shard_map/ppermute | solution.py:140
  9.5 0.7 %collective-permute-start = (bf16[112,128]{1,0:T(8,128)(2,1)S(1)}, bf16[112,128]{1,0:T(8,128)(2,1)S(1)}, u32[]{:S(2)}, u32[]{:S(2)}) collective-permute-start(bf16[112,128]{1,0:T(8,128)(2,1)S(1)} %pad_maximum_fusion.7), channel_id=1, source_target_pairs={{0,4},{4,8},{8,12},{12,0},{1,5},{5,9},{9,13},{13,1},{2,6},{6,10},{... | collective-permute-start | bytes 86024 | tf_op jit(solution)/shard_map/ppermute | solution.py:136
  10.8 0.4 tile.10
  11.4 3.7 %collective-permute-done = bf16[112,128]{1,0:T(8,128)(2,1)S(1)} collective-permute-done((bf16[112,128]{1,0:T(8,128)(2,1)S(1)}, bf16[112,128]{1,0:T(8,128)(2,1)S(1)}, u32[]{:S(2)}, u32[]{:S(2)}) %collective-permute-start) | collective-permute-done | bytes 28704 | tf_op jit(solution)/shard_map/ppermute | solution.py:136
  16.4 0.2 reshape.257
  16.6 0.3 convolution_convert_fusion
  17.2 0.7 %collective-permute-start.2 = (bf16[48,640]{1,0:T(8,128)(2,1)S(1)}, bf16[48,640]{1,0:T(8,128)(2,1)S(1)}, u32[]{:S(2)}, u32[]{:S(2)}) collective-permute-start(bf16[48,640]{1,0:T(8,128)(2,1)S(1)} %get-tuple-element.11), channel_id=1, source_target_pairs={{0,0},{2,4},{4,8},{6,12},{8,2},{10,6},{12,10},{14,14},{1,1},{3,5},... | collective-permute-start | bytes 184328 | tf_op jit(solution)/shard_map/ppermute | solution.py:188
  17.9 1.8 %collective-permute-start.3 = (bf16[48,640]{1,0:T(8,128)(2,1)S(1)}, bf16[48,640]{1,0:T(8,128)(2,1)S(1)}, u32[]{:S(2)}, u32[]{:S(2)}) collective-permute-start(bf16[48,640]{1,0:T(8,128)(2,1)S(1)} %get-tuple-element.10), channel_id=1, source_target_pairs={{0,4},{2,0},{4,12},{6,8},{8,6},{10,2},{12,14},{14,10},{1,5},{3,1},... | collective-permute-start | bytes 184328 | tf_op jit(solution)/shard_map/ppermute | solution.py:188
  19.6 2.0 %fusion.1 = f32[128,7680]{1,0:T(8,128)S(1)} fusion(bf16[128,240]{0,1:T(8,128)(2,1)S(1)} %bitcast.84, s32[7680]{0:T(1024)S(1)} %get-tuple-element.25, s32[7680]{0:T(1024)S(1)} %add_select_fusion.4, s32[240]{0:T(256)S(1)} %get-tuple-element.22, s32[240]{0:T(256)S(1)} %get-tuple-element.23), kind=kOutput, calls=%fused_computation.2 | convolution fusion | flops 477388800 | bytes 4056960 | tf_op jit(solution)/shard_map/dot_general | solution.py:231
  21.7 1.3 %fusion.w_ref = bf16[128,7680]{1,0:T(8,128)(2,1)S(1)} fusion(f32[128,7680]{1,0:T(8,128)S(1)} %fusion.1, bf16[128,96]{0,1:T(8,128)(2,1)S(1)} %bitcast.83, s32[7680]{0:T(1024)S(1)} %get-tuple-element.24, s32[7680]{0:T(1024)S(1)} %get-tuple-element.25, s32[96]{0:T(128)S(1)} %get-tuple-element.20, s32[96]{0:T(128)S(1)} %get-tuple-element.21), kind=kOutput, calls=%fused_computation.1 | convolution fusion | flops 192921600 | bytes 5985024 | tf_op jit(solution)/shard_map/dot_general | solution.py:232
  23.8 0.2 fusion.18.inv_ref
  24.1 3.2 %shard_map.55 = f32[128,512]{1,0:T(8,128)S(1)} custom-call(bf16[1,96,640]{2,1,0:T(8,128)(2,1)S(1)} %bitcast.81, f32[96,512]{1,0:T(8,128)S(1)} %fusion.18.inv_ref, bf16[128,7680]{1,0:T(8,128)(2,1)S(1)} %fusion.w_ref), custom_call_target="tpu_custom_call" | custom-call | tf_op jit(solution)/shard_map/pallas_call | solution.py:96
  27.3 2.4 %collective-permute-start.5 = (f32[32,512]{1,0:T(8,128)S(1)}, f32[32,512]{1,0:T(8,128)S(1)}, u32[]{:S(2)}, u32[]{:S(2)}) collective-permute-start(f32[32,512]{1,0:T(8,128)S(1)} %get-tuple-element.7), channel_id=1, source_target_pairs={{0,4},{4,8},{8,12},{12,0},{1,5},{5,9},{9,13},{13,1},{2,6},{6,10},{... | collective-permute-start | bytes 196616 | tf_op jit(solution)/shard_map/ppermute | solution.py:249
  29.8 2.9 %collective-permute-start.6 = (f32[32,512]{1,0:T(8,128)S(1)}, f32[32,512]{1,0:T(8,128)S(1)}, u32[]{:S(2)}, u32[]{:S(2)}) collective-permute-start(f32[32,512]{1,0:T(8,128)S(1)} %get-tuple-element.6), channel_id=1, source_target_pairs={{0,8},{4,12},{8,0},{12,4},{1,9},{5,13},{9,1},{13,5},{2,10},{6,14},... | collective-permute-start | bytes 196616 | tf_op jit(solution)/shard_map/ppermute | solution.py:249
  32.6 2.8 %collective-permute-start.7 = (f32[32,512]{1,0:T(8,128)S(1)}, f32[32,512]{1,0:T(8,128)S(1)}, u32[]{:S(2)}, u32[]{:S(2)}) collective-permute-start(f32[32,512]{1,0:T(8,128)S(1)} %get-tuple-element.5), channel_id=1, source_target_pairs={{0,12},{4,0},{8,4},{12,8},{1,13},{5,1},{9,5},{13,9},{2,14},{6,2},{... | collective-permute-start | bytes 196616 | tf_op jit(solution)/shard_map/ppermute | solution.py:249
  35.6 1.8 %collective-permute-done.7 = f32[32,512]{1,0:T(8,128)S(1)} collective-permute-done((f32[32,512]{1,0:T(8,128)S(1)}, f32[32,512]{1,0:T(8,128)S(1)}, u32[]{:S(2)}, u32[]{:S(2)}) %collective-permute-start.7) | collective-permute-done | bytes 65568 | tf_op jit(solution)/shard_map/ppermute | solution.py:249
  37.4 0.6 %bitcast_dynamic-update-slice_fusion = f32[1,32,2048]{2,1,0:T(8,128)} fusion(f32[1,32,2048]{2,1,0:T(8,128)} %copy-done.1, s32[]{:T(128)S(6)} %select_n.276, f32[32,512]{1,0:T(8,128)S(1)} %collective-permute-done.7), kind=kLoop, calls=%fused_computation.39 | loop fusion | bytes 131076 | tf_op jit(solution)/shard_map/dynamic_update_slice | solution.py:253
  (81 shorter events, 2.8 us)
Async XLA Ops:
  0.0 10.4 %copy-start = (bf16[64]{0:T(256)(128)(2,1)S(1)}, bf16[64]{0:T(256)(128)(2,1)}, u32[]{:S(2)}) copy-start(bf16[64]{0:T(256)(128)(2,1)} %param.7) | copy-start | bytes 388
  0.0 10.4 %copy-start.2 = (s32[128,3,32]{0,2,1:T(8,128)S(1)}, s32[128,3,32]{0,2,1:T(8,128)}, u32[]{:S(2)}) copy-start(s32[128,3,32]{0,2,1:T(8,128)} %param.9) | copy-start | bytes 147460
  0.8 14.7 %collective-permute-start.4 = (bf16[32,256]{1,0:T(8,128)(2,1)S(1)}, bf16[32,256]{1,0:T(8,128)(2,1)S(1)}, u32[]{:S(2)}, u32[]{:S(2)}) collective-permute-start(bf16[32,256]{1,0:T(8,128)(2,1)S(1)} %get-tuple-element.19), channel_id=1, source_target_pairs={{0,8},{4,12},{8,0},{12,4},{1,9},{5,13},{9,1},{13,5},{2,10},{6,14},... | collective-permute-start | bytes 49160 | tf_op jit(solution)/shard_map/ppermute | solution.py:146
  8.0 7.3 %collective-permute-start.1 = (bf16[64,512]{1,0:T(8,128)(2,1)S(1)}, bf16[64,512]{1,0:T(8,128)(2,1)S(1)}, u32[]{:S(2)}, u32[]{:S(2)}) collective-permute-start(bf16[64,512]{1,0:T(8,128)(2,1)S(1)} %pad_maximum_fusion), channel_id=1, source_target_pairs={{0,12},{4,0},{8,4},{12,8},{1,13},{5,1},{9,5},{13,9},{2,14},{6,2},{... | collective-permute-start | bytes 196616 | tf_op jit(solution)/shard_map/ppermute | solution.py:140
  9.5 5.7 %collective-permute-start = (bf16[112,128]{1,0:T(8,128)(2,1)S(1)}, bf16[112,128]{1,0:T(8,128)(2,1)S(1)}, u32[]{:S(2)}, u32[]{:S(2)}) collective-permute-start(bf16[112,128]{1,0:T(8,128)(2,1)S(1)} %pad_maximum_fusion.7), channel_id=1, source_target_pairs={{0,4},{4,8},{8,12},{12,0},{1,5},{5,9},{9,13},{13,1},{2,6},{6,10},{... | collective-permute-start | bytes 86024 | tf_op jit(solution)/shard_map/ppermute | solution.py:136
  17.2 5.7 %collective-permute-start.2 = (bf16[48,640]{1,0:T(8,128)(2,1)S(1)}, bf16[48,640]{1,0:T(8,128)(2,1)S(1)}, u32[]{:S(2)}, u32[]{:S(2)}) collective-permute-start(bf16[48,640]{1,0:T(8,128)(2,1)S(1)} %get-tuple-element.11), channel_id=1, source_target_pairs={{0,0},{2,4},{4,8},{6,12},{8,2},{10,6},{12,10},{14,14},{1,1},{3,5},... | collective-permute-start | bytes 184328 | tf_op jit(solution)/shard_map/ppermute | solution.py:188
  17.9 5.1 %collective-permute-start.3 = (bf16[48,640]{1,0:T(8,128)(2,1)S(1)}, bf16[48,640]{1,0:T(8,128)(2,1)S(1)}, u32[]{:S(2)}, u32[]{:S(2)}) collective-permute-start(bf16[48,640]{1,0:T(8,128)(2,1)S(1)} %get-tuple-element.10), channel_id=1, source_target_pairs={{0,4},{2,0},{4,12},{6,8},{8,6},{10,2},{12,14},{14,10},{1,5},{3,1},... | collective-permute-start | bytes 184328 | tf_op jit(solution)/shard_map/ppermute | solution.py:188
  27.3 8.2 %collective-permute-start.5 = (f32[32,512]{1,0:T(8,128)S(1)}, f32[32,512]{1,0:T(8,128)S(1)}, u32[]{:S(2)}, u32[]{:S(2)}) collective-permute-start(f32[32,512]{1,0:T(8,128)S(1)} %get-tuple-element.7), channel_id=1, source_target_pairs={{0,4},{4,8},{8,12},{12,0},{1,5},{5,9},{9,13},{13,1},{2,6},{6,10},{... | collective-permute-start | bytes 196616 | tf_op jit(solution)/shard_map/ppermute | solution.py:249
  29.8 5.8 %collective-permute-start.6 = (f32[32,512]{1,0:T(8,128)S(1)}, f32[32,512]{1,0:T(8,128)S(1)}, u32[]{:S(2)}, u32[]{:S(2)}) collective-permute-start(f32[32,512]{1,0:T(8,128)S(1)} %get-tuple-element.6), channel_id=1, source_target_pairs={{0,8},{4,12},{8,0},{12,4},{1,9},{5,13},{9,1},{13,5},{2,10},{6,14},... | collective-permute-start | bytes 196616 | tf_op jit(solution)/shard_map/ppermute | solution.py:249
  32.6 4.8 %collective-permute-start.7 = (f32[32,512]{1,0:T(8,128)S(1)}, f32[32,512]{1,0:T(8,128)S(1)}, u32[]{:S(2)}, u32[]{:S(2)}) collective-permute-start(f32[32,512]{1,0:T(8,128)S(1)} %get-tuple-element.5), channel_id=1, source_target_pairs={{0,12},{4,0},{8,4},{12,8},{1,13},{5,1},{9,5},{13,9},{2,14},{6,2},{... | collective-permute-start | bytes 196616 | tf_op jit(solution)/shard_map/ppermute | solution.py:249
  35.6 1.8 %copy-start.1 = (f32[1,32,2048]{2,1,0:T(8,128)}, f32[1,32,2048]{2,1,0:T(8,128)S(1)}, u32[]{:S(2)}) copy-start(f32[1,32,2048]{2,1,0:T(8,128)S(1)} %bitcast_dynamic-update-slice_fusion.1) | copy-start | bytes 786436

commit v18 on v17

--- a/solution.py
+++ b/solution.py
@@ -241,16 +241,10 @@
             .reshape(count, chunks * JP * row_block)
         )
     stacked = correlate(windows, inv, weights, row_block, interleaved=chunks == 1)
-    pieces = [lax.dynamic_slice_in_dim(stacked, corr_place * local_count, local_count, 0)]
-    for d in range(1, corr_count):
-        target = (corr_place + d) % corr_count
-        part = lax.dynamic_slice_in_dim(stacked, target * local_count, local_count, 0)
-        route = [(i, (i + d) % corr_count) for i in range(corr_count)]
-        pieces.append(lax.ppermute(part, "corr", route))
-    stacked = jnp.zeros((local_count, corr_count * width), jnp.float32)
-    for d, part in enumerate(pieces):
-        place = ((corr_place - d) % corr_count) * width
-        stacked = lax.dynamic_update_slice_in_dim(stacked, part, place, 1)
+    stacked = lax.all_to_all(
+        stacked.reshape(corr_count, local_count, width), "corr", 0, 0, tiled=True
+    )
+    stacked = jnp.transpose(stacked, (1, 0, 2)).reshape(local_count, corr_count * width)
     return stacked[None]
 
 

time: 38.3 us -> 43.2 us (1.13)
  blocking collectives: 0 us -> 17.1 us
  starting transfers between devices: 16.8 us -> 8.72 us
  waiting for transfers between devices: 5.55 us -> 1.23 us
    all_to_all x0 -> x1, blocking collectives: none -> 17.1 us  [body(): lax.all_to_all(stacked.reshape(corr_count, local_count, width), 'corr', 0...]
    ppermute x3 -> x0, starting transfers between devices: 8.15 us -> none  [body(): pieces.append(lax.ppermute(part, 'corr', route))]
    ppermute x1, waiting for transfers between devices: 3.75 us -> 0.73 us  [body(): got = lax.ppermute(sent, 'corr', forward)]
    ppermute x3 -> x0, waiting for transfers between devices: 1.79 us -> none  [body(): pieces.append(lax.ppermute(part, 'corr', route))]
    ppermute x2, starting transfers between devices: 2.42 us -> 0.72 us  [body(): received.append(lax.ppermute(part, ('corr', 'filt'), route))]
    ppermute x1, starting transfers between devices: 0.73 us -> 1.63 us  [body(): got = lax.ppermute(sent, 'corr', forward)]
    ppermute x1, starting transfers between devices: 1.4 us -> 2.3 us  [body(): got = lax.ppermute(sent, 'corr', backward)]
    another operation x0 -> x1, local copies, waits for them, and re-layouts: none -> 0.88 us  [body(): return stacked[None]]
  transfers between devices with their start and end apart: 8 -> 5, of which waited for: 2 -> 3; matrix products, arithmetic and copies ran while one was open for 20% -> 18% of each run, Pallas kernels for 0% -> 0%
where the time goes in v18:
time: 43.2 us; the launch traced here: 42.9 us
  blocking collectives  17.1 us (40%)
  starting transfers between devices  8.72 us (20%)
  local copies, waits for them, and re-layouts  6.05 us (14%)
  matrix products  3.76 us (9%)
  Pallas kernels  3.21 us (7%)
  other arithmetic  2.2 us (5%)
  waiting for transfers between devices  1.23 us (3%)
  between operations  0.6 us (1%)
    all_to_all x1, blocking collectives, body(): lax.all_to_all(stacked.reshape(corr_count, local_count, width), 'corr', 0...  17.1 us
    ppermute x1, starting transfers between devices, body(): blocks_by_offset[d] = lax.ppermute(wide, 'corr', route)  4.06 us
    pallas_call x1, Pallas kernels, correlate(): pl.pallas_call(functools.partial(body_fn, row_block=row_block, tile=tile)...  3.21 us
    ppermute x1, starting transfers between devices, body(): got = lax.ppermute(sent, 'corr', backward)  2.3 us
    dot_general x1, matrix products, body(): spread = jnp.dot(padded, pick_base, preferred_element_type=jnp.float32)  2.03 us
    ppermute x1, starting transfers between devices, body(): got = lax.ppermute(sent, 'corr', forward)  1.63 us
    unnamed x13, local copies, waits for them, and re-layouts  1.45 us
    dot_general x1, matrix products, body(): gate = jnp.dot(flat, pick_mask, preferred_element_type=jnp.float32)  1.26 us
  transfers between devices with their start and end apart: 5, of which 3 were waited for; matrix products, arithmetic and copies ran while one was open for 18% of the time, Pallas kernels for 0%

profile of v18, /device:TPU:0, one launch (start us, length us, event | category | flops | bytes accessed | tf_op | source)
XLA Modules:
  0.0 42.9 jit_solution(1389834846052383872)
XLA Ops:
  0.0 0.7 %pad_bitcast_fusion = (bf16[1,32,256]{2,1,0:T(8,128)(2,1)S(1)}, bf16[32,256]{1,0:T(8,128)(2,1)S(1)}) fusion(bf16[32,225]{1,0:T(8,128)(2,1)} %param.8), kind=kLoop, calls=%fused_computation.133 | loop fusion | bytes 47168 | tf_op jit(solution)/shard_map/stack | solution.py:147
  0.7 4.1 %collective-permute-start.4 = (bf16[32,256]{1,0:T(8,128)(2,1)S(1)}, bf16[32,256]{1,0:T(8,128)(2,1)S(1)}, u32[]{:S(2)}, u32[]{:S(2)}) collective-permute-start(bf16[32,256]{1,0:T(8,128)(2,1)S(1)} %get-tuple-element.16), channel_id=1, source_target_pairs={{0,8},{4,12},{8,0},{12,4},{1,9},{5,13},{9,1},{13,5},{2,10},{6,14},... | collective-permute-start | bytes 49160 | tf_op jit(solution)/shard_map/ppermute | solution.py:146
  4.8 0.8 %broadcast_compare_fusion = pred[16,4096]{1,0:T(8,128)(4,1)S(1)} fusion(s32[4096]{0:T(1024)S(1)} %iota_add_fusion.1, s32[16]{0:T(128)} %bitcast.82), kind=kLoop, calls=%fused_computation.33 | loop fusion | flops 65536 | bytes 81984 | tf_op jit(solution)/shard_map/lt | solution.py:123
  5.6 0.3 broadcast_in_dim.32
  5.9 0.4 broadcast_in_dim.33
  6.3 1.3 %copy.14 = bf16[1,16,3,4096]{3,2,1,0:T(4,128)(2,1)S(1)} copy(bf16[1,16,3,4096]{3,1,2,0:T(8,128)(2,1)} %param.5) | data formatting | bytes 786432 | tf_op args[0]
  7.6 0.3 squeeze.18
  8.0 1.6 %collective-permute-start = (bf16[112,128]{1,0:T(8,128)(2,1)S(1)}, bf16[112,128]{1,0:T(8,128)(2,1)S(1)}, u32[]{:S(2)}, u32[]{:S(2)}) collective-permute-start(bf16[112,128]{1,0:T(8,128)(2,1)S(1)} %pad_maximum_fusion.7), channel_id=1, source_target_pairs={{0,4},{4,8},{8,12},{12,0},{1,5},{5,9},{9,13},{13,1},{2,6},{6,10},{... | collective-permute-start | bytes 86024 | tf_op jit(solution)/shard_map/ppermute | solution.py:136
  9.7 2.3 %collective-permute-start.1 = (bf16[64,512]{1,0:T(8,128)(2,1)S(1)}, bf16[64,512]{1,0:T(8,128)(2,1)S(1)}, u32[]{:S(2)}, u32[]{:S(2)}) collective-permute-start(bf16[64,512]{1,0:T(8,128)(2,1)S(1)} %pad_maximum_fusion), channel_id=1, source_target_pairs={{0,12},{4,0},{8,4},{12,8},{1,13},{5,1},{9,5},{13,9},{2,14},{6,2},{... | collective-permute-start | bytes 196616 | tf_op jit(solution)/shard_map/ppermute | solution.py:140
  12.6 0.4 tile.10
  13.1 0.7 %collective-permute-done = bf16[112,128]{1,0:T(8,128)(2,1)S(1)} collective-permute-done((bf16[112,128]{1,0:T(8,128)(2,1)S(1)}, bf16[112,128]{1,0:T(8,128)(2,1)S(1)}, u32[]{:S(2)}, u32[]{:S(2)}) %collective-permute-start) | collective-permute-done | bytes 28704 | tf_op jit(solution)/shard_map/ppermute | solution.py:136
  14.0 0.3 collective-permute-done.1
  15.2 0.2 copy.15
  15.3 0.2 reshape.252
  15.6 0.3 convolution_convert_fusion
  16.2 0.7 %collective-permute-start.2 = (bf16[48,640]{1,0:T(8,128)(2,1)S(1)}, bf16[48,640]{1,0:T(8,128)(2,1)S(1)}, u32[]{:S(2)}, u32[]{:S(2)}) collective-permute-start(bf16[48,640]{1,0:T(8,128)(2,1)S(1)} %get-tuple-element.8), channel_id=1, source_target_pairs={{0,0},{2,4},{4,8},{6,12},{8,2},{10,6},{12,10},{14,14},{1,1},{3,5},... | collective-permute-start | bytes 184328 | tf_op jit(solution)/shard_map/ppermute | solution.py:188
  16.9 2.0 %fusion.1 = f32[128,7680]{1,0:T(8,128)S(1)} fusion(bf16[128,240]{0,1:T(8,128)(2,1)S(1)} %bitcast.80, s32[7680]{0:T(1024)S(1)} %get-tuple-element.22, s32[7680]{0:T(1024)S(1)} %add_select_fusion.4, s32[240]{0:T(256)S(1)} %get-tuple-element.19, s32[240]{0:T(256)S(1)} %get-tuple-element.20), kind=kOutput, calls=%fused_computation.2 | convolution fusion | flops 477388800 | bytes 4056960 | tf_op jit(solution)/shard_map/dot_general | solution.py:231
  18.9 1.3 %fusion.w_ref = bf16[128,7680]{1,0:T(8,128)(2,1)S(1)} fusion(f32[128,7680]{1,0:T(8,128)S(1)} %fusion.1, bf16[128,96]{0,1:T(8,128)(2,1)S(1)} %bitcast.79, s32[7680]{0:T(1024)S(1)} %get-tuple-element.21, s32[7680]{0:T(1024)S(1)} %get-tuple-element.22, s32[96]{0:T(128)S(1)} %get-tuple-element.17, s32[96]{0:T(128)S(1)} %get-tuple-element.18), kind=kOutput, calls=%fused_computation.1 | convolution fusion | flops 192921600 | bytes 5985024 | tf_op jit(solution)/shard_map/dot_general | solution.py:232
  20.2 0.2 collective-permute-done.3
  21.3 0.2 fusion.18.inv_ref
  21.5 3.2 %shard_map.55 = f32[128,512]{1,0:T(8,128)S(1)} custom-call(bf16[1,96,640]{2,1,0:T(8,128)(2,1)S(1)} %bitcast.76, f32[96,512]{1,0:T(8,128)S(1)} %fusion.18.inv_ref, bf16[128,7680]{1,0:T(8,128)(2,1)S(1)} %fusion.w_ref), custom_call_target="tpu_custom_call" | custom-call | tf_op jit(solution)/shard_map/pallas_call | solution.py:96
  24.7 17.1 %all_to_all.5 = f32[4,32,512]{2,1,0:T(8,128)S(1)} all-to-all(f32[4,32,512]{2,1,0:T(8,128)S(1)} %bitcast.75), channel_id=1, replica_groups=mesh['groups'=2,'corr'=4,'filt'=2,'pair'=2] {'corr'}, dimensions={0} | all-to-all | bytes 524288 | tf_op jit(solution)/shard_map/all_to_all | solution.py:244
  41.8 0.2 copy.20
  42.0 0.9 %broadcast_in_dim_reshape.3 = f32[1,32,2048]{2,1,0:T(8,128)} reshape(f32[32,4,512]{2,1,0:T(4,128)S(1)} %copy.20) | data formatting | bytes 524288 | tf_op jit(solution)/shard_map/broadcast_in_dim;reshape | solution.py:248
  (70 shorter events, 2.6 us)
Async XLA Ops:
  0.0 12.2 %copy-start = (bf16[64]{0:T(256)(128)(2,1)S(1)}, bf16[64]{0:T(256)(128)(2,1)}, u32[]{:S(2)}) copy-start(bf16[64]{0:T(256)(128)(2,1)} %param.7) | copy-start | bytes 388
  0.0 12.3 %copy-start.1 = (s32[128,3,32]{0,2,1:T(8,128)S(1)}, s32[128,3,32]{0,2,1:T(8,128)}, u32[]{:S(2)}) copy-start(s32[128,3,32]{0,2,1:T(8,128)} %param.9) | copy-start | bytes 147460
  0.7 13.6 %collective-permute-start.4 = (bf16[32,256]{1,0:T(8,128)(2,1)S(1)}, bf16[32,256]{1,0:T(8,128)(2,1)S(1)}, u32[]{:S(2)}, u32[]{:S(2)}) collective-permute-start(bf16[32,256]{1,0:T(8,128)(2,1)S(1)} %get-tuple-element.16), channel_id=1, source_target_pairs={{0,8},{4,12},{8,0},{12,4},{1,9},{5,13},{9,1},{13,5},{2,10},{6,14},... | collective-permute-start | bytes 49160 | tf_op jit(solution)/shard_map/ppermute | solution.py:146
  8.0 5.8 %collective-permute-start = (bf16[112,128]{1,0:T(8,128)(2,1)S(1)}, bf16[112,128]{1,0:T(8,128)(2,1)S(1)}, u32[]{:S(2)}, u32[]{:S(2)}) collective-permute-start(bf16[112,128]{1,0:T(8,128)(2,1)S(1)} %pad_maximum_fusion.7), channel_id=1, source_target_pairs={{0,4},{4,8},{8,12},{12,0},{1,5},{5,9},{9,13},{13,1},{2,6},{6,10},{... | collective-permute-start | bytes 86024 | tf_op jit(solution)/shard_map/ppermute | solution.py:136
  9.7 4.6 %collective-permute-start.1 = (bf16[64,512]{1,0:T(8,128)(2,1)S(1)}, bf16[64,512]{1,0:T(8,128)(2,1)S(1)}, u32[]{:S(2)}, u32[]{:S(2)}) collective-permute-start(bf16[64,512]{1,0:T(8,128)(2,1)S(1)} %pad_maximum_fusion), channel_id=1, source_target_pairs={{0,12},{4,0},{8,4},{12,8},{1,13},{5,1},{9,5},{13,9},{2,14},{6,2},{... | collective-permute-start | bytes 196616 | tf_op jit(solution)/shard_map/ppermute | solution.py:140
  16.1 4.3 %collective-permute-start.3 = (bf16[48,640]{1,0:T(8,128)(2,1)S(1)}, bf16[48,640]{1,0:T(8,128)(2,1)S(1)}, u32[]{:S(2)}, u32[]{:S(2)}) collective-permute-start(bf16[48,640]{1,0:T(8,128)(2,1)S(1)} %get-tuple-element.7), channel_id=1, source_target_pairs={{0,4},{2,0},{4,12},{6,8},{8,6},{10,2},{12,14},{14,10},{1,5},{3,1},... | collective-permute-start | bytes 184328 | tf_op jit(solution)/shard_map/ppermute | solution.py:188
  16.2 4.0 %collective-permute-start.2 = (bf16[48,640]{1,0:T(8,128)(2,1)S(1)}, bf16[48,640]{1,0:T(8,128)(2,1)S(1)}, u32[]{:S(2)}, u32[]{:S(2)}) collective-permute-start(bf16[48,640]{1,0:T(8,128)(2,1)S(1)} %get-tuple-element.8), channel_id=1, source_target_pairs={{0,0},{2,4},{4,8},{6,12},{8,2},{10,6},{12,10},{14,14},{1,1},{3,5},... | collective-permute-start | bytes 184328 | tf_op jit(solution)/shard_map/ppermute | solution.py:188

commit v19 on v17

--- a/solution.py
+++ b/solution.py
@@ -152,12 +152,9 @@
         ],
         axis=0,
     )[:, :template_width]
-    extended = jnp.concatenate([history, live, ahead], axis=1)
     decimated = raw_width // DEC
     blocks = decimated // 128 + 1
-    frames = jnp.stack(
-        [extended[:, 512 * a : 512 * a + 640] for a in range(blocks)], axis=1
-    ).reshape(local_stations * 3 * blocks, 640)
+    rows_in = live.shape[0]
     flip = (lax.iota(jnp.int32, TAPS)[:, None] + lax.iota(jnp.int32, TAPS)[None, :] == TAPS - 1)
     reversed_taps = jnp.dot(
         taps[None, :], flip.astype(taps.dtype), preferred_element_type=jnp.float32
@@ -166,9 +163,19 @@
         [jnp.zeros((65,), taps.dtype), reversed_taps, jnp.zeros((644 - 129,), taps.dtype)]
     )
     bank = jnp.tile(ring, 128)[: 128 * 640].reshape(128, 640)
-    filtered = lax.dot_general(
-        frames, bank, (((1,), (1,)), ((), ())), preferred_element_type=jnp.float32
-    )
+
+    def apply_bank(frames):
+        return lax.dot_general(
+            frames, bank, (((1,), (1,)), ((), ())), preferred_element_type=jnp.float32
+        )
+
+    inner = jnp.stack(
+        [live[:, 512 * a - 128 : 512 * a + 512] for a in range(1, blocks - 1)], axis=1
+    ).reshape(rows_in * (blocks - 2), 640)
+    inner = apply_bank(inner).reshape(rows_in, (blocks - 2) * 128)
+    first = apply_bank(jnp.concatenate([history, live[:, :512]], axis=1))
+    last = apply_bank(jnp.concatenate([live[:, raw_width - 128 :], ahead], axis=1))
+    filtered = jnp.concatenate([first, inner, last], axis=1)
     filtered = filtered.astype(jnp.bfloat16).reshape(local_stations * 3, decimated + 128)
     past_end = (corr_place == corr_count - 1) & (lax.iota(jnp.int32, decimated + 128) >= decimated)
     filtered = jnp.where(past_end[None, :], jnp.zeros_like(filtered), filtered)

time: 38.3 us -> 37.6 us (0.982)
  waiting for transfers between devices: 5.55 us -> 4.7 us
    ppermute x1, waiting for transfers between devices: 3.75 us -> 2.89 us  [body(): got = lax.ppermute(sent, 'corr', forward)]
    unnamed x15 -> x14, local copies, waits for them, and re-layouts: 1.45 us -> 1.44 us
  transfers between devices with their start and end apart: 8 -> 8, of which waited for: 2 -> 2; matrix products, arithmetic and copies ran while one was open for 20% -> 23% of each run, Pallas kernels for 0% -> 0%
where the time goes in v19:
time: 37.6 us; the launch traced here: 37.3 us
  starting transfers between devices  16.8 us (45%)
  local copies, waits for them, and re-layouts  5.54 us (15%)
  waiting for transfers between devices  4.7 us (12%)
  matrix products  4.04 us (11%)
  Pallas kernels  3.21 us (9%)
  other arithmetic  2.22 us (6%)
  between operations  0.86 us (2%)
    ppermute x3, starting transfers between devices, body(): pieces.append(lax.ppermute(part, 'corr', route))  8.14 us
    ppermute x1, starting transfers between devices, body(): blocks_by_offset[d] = lax.ppermute(wide, 'corr', route)  4.06 us
    pallas_call x1, Pallas kernels, correlate(): pl.pallas_call(functools.partial(body_fn, row_block=row_block, tile=tile)...  3.21 us
    ppermute x1, waiting for transfers between devices, body(): got = lax.ppermute(sent, 'corr', forward)  2.89 us
    ppermute x2, starting transfers between devices, body(): received.append(lax.ppermute(part, ('corr', 'filt'), route))  2.42 us
    dot_general x1, matrix products, body(): spread = jnp.dot(padded, pick_base, preferred_element_type=jnp.float32)  2.03 us
    ppermute x3, waiting for transfers between devices, body(): pieces.append(lax.ppermute(part, 'corr', route))  1.79 us
    unnamed x14, local copies, waits for them, and re-layouts  1.44 us
  transfers between devices with their start and end apart: 8, of which 2 were waited for; matrix products, arithmetic and copies ran while one was open for 23% of the time, Pallas kernels for 0%

profile of v19, /device:TPU:0, one launch (start us, length us, event | category | flops | bytes accessed | tf_op | source)
XLA Modules:
  0.0 37.3 jit_solution(1047094003100647220)
XLA Ops:
  0.0 0.7 %pad_bitcast_fusion = (bf16[1,32,256]{2,1,0:T(8,128)(2,1)S(1)}, bf16[32,256]{1,0:T(8,128)(2,1)S(1)}) fusion(bf16[32,225]{1,0:T(8,128)(2,1)} %param.8), kind=kLoop, calls=%fused_computation.144 | loop fusion | bytes 47168 | tf_op jit(solution)/shard_map/stack | solution.py:147
  0.8 4.1 %collective-permute-start.4 = (bf16[32,256]{1,0:T(8,128)(2,1)S(1)}, bf16[32,256]{1,0:T(8,128)(2,1)S(1)}, u32[]{:S(2)}, u32[]{:S(2)}) collective-permute-start(bf16[32,256]{1,0:T(8,128)(2,1)S(1)} %get-tuple-element.19), channel_id=1, source_target_pairs={{0,8},{4,12},{8,0},{12,4},{1,9},{5,13},{9,1},{13,5},{2,10},{6,14},... | collective-permute-start | bytes 49160 | tf_op jit(solution)/shard_map/ppermute | solution.py:146
  4.9 0.8 %broadcast_compare_fusion = pred[16,4096]{1,0:T(8,128)(4,1)S(1)} fusion(s32[4096]{0:T(1024)S(1)} %iota_add_fusion.1, s32[16]{0:T(128)} %bitcast.80), kind=kLoop, calls=%fused_computation.35 | loop fusion | flops 65536 | bytes 81984 | tf_op jit(solution)/shard_map/lt | solution.py:123
  5.6 0.3 broadcast_in_dim.67
  5.9 0.4 broadcast_in_dim.68
  6.3 1.3 %copy.11 = bf16[1,16,3,4096]{3,2,1,0:T(4,128)(2,1)S(1)} copy(bf16[1,16,3,4096]{3,1,2,0:T(8,128)(2,1)} %param.5) | data formatting | bytes 786432 | tf_op args[0]
  7.6 0.3 squeeze.18
  8.0 1.4 %collective-permute-start.1 = (bf16[64,512]{1,0:T(8,128)(2,1)S(1)}, bf16[64,512]{1,0:T(8,128)(2,1)S(1)}, u32[]{:S(2)}, u32[]{:S(2)}) collective-permute-start(bf16[64,512]{1,0:T(8,128)(2,1)S(1)} %pad_maximum_fusion), channel_id=1, source_target_pairs={{0,12},{4,0},{8,4},{12,8},{1,13},{5,1},{9,5},{13,9},{2,14},{6,2},{... | collective-permute-start | bytes 196616 | tf_op jit(solution)/shard_map/ppermute | solution.py:140
  9.5 0.7 %collective-permute-start = (bf16[112,128]{1,0:T(8,128)(2,1)S(1)}, bf16[112,128]{1,0:T(8,128)(2,1)S(1)}, u32[]{:S(2)}, u32[]{:S(2)}) collective-permute-start(bf16[112,128]{1,0:T(8,128)(2,1)S(1)} %pad_maximum_fusion.5), channel_id=1, source_target_pairs={{0,4},{4,8},{8,12},{12,0},{1,5},{5,9},{9,13},{13,1},{2,6},{6,10},{... | collective-permute-start | bytes 86024 | tf_op jit(solution)/shard_map/ppermute | solution.py:136
  11.0 0.4 tile.10
  11.6 0.3 convolution_convert_fusion
  12.3 2.9 %collective-permute-done = bf16[112,128]{1,0:T(8,128)(2,1)S(1)} collective-permute-done((bf16[112,128]{1,0:T(8,128)(2,1)S(1)}, bf16[112,128]{1,0:T(8,128)(2,1)S(1)}, u32[]{:S(2)}, u32[]{:S(2)}) %collective-permute-start) | collective-permute-done | bytes 28704 | tf_op jit(solution)/shard_map/ppermute | solution.py:136
  15.2 0.2 convolution_convert_fusion.2
  16.5 0.7 %collective-permute-start.2 = (bf16[48,640]{1,0:T(8,128)(2,1)S(1)}, bf16[48,640]{1,0:T(8,128)(2,1)S(1)}, u32[]{:S(2)}, u32[]{:S(2)}) collective-permute-start(bf16[48,640]{1,0:T(8,128)(2,1)S(1)} %get-tuple-element.11), channel_id=1, source_target_pairs={{0,0},{2,4},{4,8},{6,12},{8,2},{10,6},{12,10},{14,14},{1,1},{3,5},... | collective-permute-start | bytes 184328 | tf_op jit(solution)/shard_map/ppermute | solution.py:195
  17.2 1.8 %collective-permute-start.3 = (bf16[48,640]{1,0:T(8,128)(2,1)S(1)}, bf16[48,640]{1,0:T(8,128)(2,1)S(1)}, u32[]{:S(2)}, u32[]{:S(2)}) collective-permute-start(bf16[48,640]{1,0:T(8,128)(2,1)S(1)} %get-tuple-element.10), channel_id=1, source_target_pairs={{0,4},{2,0},{4,12},{6,8},{8,6},{10,2},{12,14},{14,10},{1,5},{3,1},... | collective-permute-start | bytes 184328 | tf_op jit(solution)/shard_map/ppermute | solution.py:195
  18.9 2.0 %fusion.1 = f32[128,7680]{1,0:T(8,128)S(1)} fusion(bf16[128,240]{0,1:T(8,128)(2,1)S(1)} %bitcast.78, s32[7680]{0:T(1024)S(1)} %get-tuple-element.25, s32[7680]{0:T(1024)S(1)} %add_select_fusion.4, s32[240]{0:T(256)S(1)} %get-tuple-element.22, s32[240]{0:T(256)S(1)} %get-tuple-element.23), kind=kOutput, calls=%fused_computation.2 | convolution fusion | flops 477388800 | bytes 4056960 | tf_op jit(solution)/shard_map/dot_general | solution.py:238
  21.0 1.3 %fusion.w_ref = bf16[128,7680]{1,0:T(8,128)(2,1)S(1)} fusion(f32[128,7680]{1,0:T(8,128)S(1)} %fusion.1, bf16[128,96]{0,1:T(8,128)(2,1)S(1)} %bitcast.77, s32[7680]{0:T(1024)S(1)} %get-tuple-element.24, s32[7680]{0:T(1024)S(1)} %get-tuple-element.25, s32[96]{0:T(128)S(1)} %get-tuple-element.20, s32[96]{0:T(128)S(1)} %get-tuple-element.21), kind=kOutput, calls=%fused_computation.1 | convolution fusion | flops 192921600 | bytes 5985024 | tf_op jit(solution)/shard_map/dot_general | solution.py:239
  23.1 0.2 fusion.18.inv_ref
  23.4 3.2 %shard_map.55 = f32[128,512]{1,0:T(8,128)S(1)} custom-call(bf16[1,96,640]{2,1,0:T(8,128)(2,1)S(1)} %bitcast.75, f32[96,512]{1,0:T(8,128)S(1)} %fusion.18.inv_ref, bf16[128,7680]{1,0:T(8,128)(2,1)S(1)} %fusion.w_ref), custom_call_target="tpu_custom_call" | custom-call | tf_op jit(solution)/shard_map/pallas_call | solution.py:96
  26.6 2.4 %collective-permute-start.5 = (f32[32,512]{1,0:T(8,128)S(1)}, f32[32,512]{1,0:T(8,128)S(1)}, u32[]{:S(2)}, u32[]{:S(2)}) collective-permute-start(f32[32,512]{1,0:T(8,128)S(1)} %get-tuple-element.7), channel_id=1, source_target_pairs={{0,4},{4,8},{8,12},{12,0},{1,5},{5,9},{9,13},{13,1},{2,6},{6,10},{... | collective-permute-start | bytes 196616 | tf_op jit(solution)/shard_map/ppermute | solution.py:256
  29.1 2.9 %collective-permute-start.6 = (f32[32,512]{1,0:T(8,128)S(1)}, f32[32,512]{1,0:T(8,128)S(1)}, u32[]{:S(2)}, u32[]{:S(2)}) collective-permute-start(f32[32,512]{1,0:T(8,128)S(1)} %get-tuple-element.6), channel_id=1, source_target_pairs={{0,8},{4,12},{8,0},{12,4},{1,9},{5,13},{9,1},{13,5},{2,10},{6,14},... | collective-permute-start | bytes 196616 | tf_op jit(solution)/shard_map/ppermute | solution.py:256
  31.9 2.8 %collective-permute-start.7 = (f32[32,512]{1,0:T(8,128)S(1)}, f32[32,512]{1,0:T(8,128)S(1)}, u32[]{:S(2)}, u32[]{:S(2)}) collective-permute-start(f32[32,512]{1,0:T(8,128)S(1)} %get-tuple-element.5), channel_id=1, source_target_pairs={{0,12},{4,0},{8,4},{12,8},{1,13},{5,1},{9,5},{13,9},{2,14},{6,2},{... | collective-permute-start | bytes 196616 | tf_op jit(solution)/shard_map/ppermute | solution.py:256
  34.9 1.8 %collective-permute-done.7 = f32[32,512]{1,0:T(8,128)S(1)} collective-permute-done((f32[32,512]{1,0:T(8,128)S(1)}, f32[32,512]{1,0:T(8,128)S(1)}, u32[]{:S(2)}, u32[]{:S(2)}) %collective-permute-start.7) | collective-permute-done | bytes 65568 | tf_op jit(solution)/shard_map/ppermute | solution.py:256
  36.7 0.6 %bitcast_dynamic-update-slice_fusion = f32[1,32,2048]{2,1,0:T(8,128)} fusion(f32[1,32,2048]{2,1,0:T(8,128)} %copy-done.1, s32[]{:T(128)S(6)} %select_n.276, f32[32,512]{1,0:T(8,128)S(1)} %collective-permute-done.7), kind=kLoop, calls=%fused_computation.41 | loop fusion | bytes 131076 | tf_op jit(solution)/shard_map/dynamic_update_slice | solution.py:260
  (81 shorter events, 3.0 us)
Async XLA Ops:
  0.0 10.8 %copy-start = (bf16[64]{0:T(256)(128)(2,1)S(1)}, bf16[64]{0:T(256)(128)(2,1)}, u32[]{:S(2)}) copy-start(bf16[64]{0:T(256)(128)(2,1)} %param.7) | copy-start | bytes 388
  0.0 10.4 %copy-start.2 = (s32[128,3,32]{0,2,1:T(8,128)S(1)}, s32[128,3,32]{0,2,1:T(8,128)}, u32[]{:S(2)}) copy-start(s32[128,3,32]{0,2,1:T(8,128)} %param.9) | copy-start | bytes 147460
  0.8 14.7 %collective-permute-start.4 = (bf16[32,256]{1,0:T(8,128)(2,1)S(1)}, bf16[32,256]{1,0:T(8,128)(2,1)S(1)}, u32[]{:S(2)}, u32[]{:S(2)}) collective-permute-start(bf16[32,256]{1,0:T(8,128)(2,1)S(1)} %get-tuple-element.19), channel_id=1, source_target_pairs={{0,8},{4,12},{8,0},{12,4},{1,9},{5,13},{9,1},{13,5},{2,10},{6,14},... | collective-permute-start | bytes 49160 | tf_op jit(solution)/shard_map/ppermute | solution.py:146
  8.0 7.4 %collective-permute-start.1 = (bf16[64,512]{1,0:T(8,128)(2,1)S(1)}, bf16[64,512]{1,0:T(8,128)(2,1)S(1)}, u32[]{:S(2)}, u32[]{:S(2)}) collective-permute-start(bf16[64,512]{1,0:T(8,128)(2,1)S(1)} %pad_maximum_fusion), channel_id=1, source_target_pairs={{0,12},{4,0},{8,4},{12,8},{1,13},{5,1},{9,5},{13,9},{2,14},{6,2},{... | collective-permute-start | bytes 196616 | tf_op jit(solution)/shard_map/ppermute | solution.py:140
  9.5 5.7 %collective-permute-start = (bf16[112,128]{1,0:T(8,128)(2,1)S(1)}, bf16[112,128]{1,0:T(8,128)(2,1)S(1)}, u32[]{:S(2)}, u32[]{:S(2)}) collective-permute-start(bf16[112,128]{1,0:T(8,128)(2,1)S(1)} %pad_maximum_fusion.5), channel_id=1, source_target_pairs={{0,4},{4,8},{8,12},{12,0},{1,5},{5,9},{9,13},{13,1},{2,6},{6,10},{... | collective-permute-start | bytes 86024 | tf_op jit(solution)/shard_map/ppermute | solution.py:136
  16.5 5.7 %collective-permute-start.2 = (bf16[48,640]{1,0:T(8,128)(2,1)S(1)}, bf16[48,640]{1,0:T(8,128)(2,1)S(1)}, u32[]{:S(2)}, u32[]{:S(2)}) collective-permute-start(bf16[48,640]{1,0:T(8,128)(2,1)S(1)} %get-tuple-element.11), channel_id=1, source_target_pairs={{0,0},{2,4},{4,8},{6,12},{8,2},{10,6},{12,10},{14,14},{1,1},{3,5},... | collective-permute-start | bytes 184328 | tf_op jit(solution)/shard_map/ppermute | solution.py:195
  17.2 5.1 %collective-permute-start.3 = (bf16[48,640]{1,0:T(8,128)(2,1)S(1)}, bf16[48,640]{1,0:T(8,128)(2,1)S(1)}, u32[]{:S(2)}, u32[]{:S(2)}) collective-permute-start(bf16[48,640]{1,0:T(8,128)(2,1)S(1)} %get-tuple-element.10), channel_id=1, source_target_pairs={{0,4},{2,0},{4,12},{6,8},{8,6},{10,2},{12,14},{14,10},{1,5},{3,1},... | collective-permute-start | bytes 184328 | tf_op jit(solution)/shard_map/ppermute | solution.py:195
  26.6 8.2 %collective-permute-start.5 = (f32[32,512]{1,0:T(8,128)S(1)}, f32[32,512]{1,0:T(8,128)S(1)}, u32[]{:S(2)}, u32[]{:S(2)}) collective-permute-start(f32[32,512]{1,0:T(8,128)S(1)} %get-tuple-element.7), channel_id=1, source_target_pairs={{0,4},{4,8},{8,12},{12,0},{1,5},{5,9},{9,13},{13,1},{2,6},{6,10},{... | collective-permute-start | bytes 196616 | tf_op jit(solution)/shard_map/ppermute | solution.py:256
  29.1 5.8 %collective-permute-start.6 = (f32[32,512]{1,0:T(8,128)S(1)}, f32[32,512]{1,0:T(8,128)S(1)}, u32[]{:S(2)}, u32[]{:S(2)}) collective-permute-start(f32[32,512]{1,0:T(8,128)S(1)} %get-tuple-element.6), channel_id=1, source_target_pairs={{0,8},{4,12},{8,0},{12,4},{1,9},{5,13},{9,1},{13,5},{2,10},{6,14},... | collective-permute-start | bytes 196616 | tf_op jit(solution)/shard_map/ppermute | solution.py:256
  31.9 4.8 %collective-permute-start.7 = (f32[32,512]{1,0:T(8,128)S(1)}, f32[32,512]{1,0:T(8,128)S(1)}, u32[]{:S(2)}, u32[]{:S(2)}) collective-permute-start(f32[32,512]{1,0:T(8,128)S(1)} %get-tuple-element.5), channel_id=1, source_target_pairs={{0,12},{4,0},{8,4},{12,8},{1,13},{5,1},{9,5},{13,9},{2,14},{6,2},{... | collective-permute-start | bytes 196616 | tf_op jit(solution)/shard_map/ppermute | solution.py:256
  34.9 1.8 %copy-start.1 = (f32[1,32,2048]{2,1,0:T(8,128)}, f32[1,32,2048]{2,1,0:T(8,128)S(1)}, u32[]{:S(2)}) copy-start(f32[1,32,2048]{2,1,0:T(8,128)S(1)} %bitcast_dynamic-update-slice_fusion.1) | copy-start | bytes 786436

commit v20 on v19

--- a/solution.py
+++ b/solution.py
@@ -120,8 +120,11 @@
     filt_place = lax.axis_index("filt")
     filt_count = lax.axis_size("filt")
     sample_times = corr_place * raw_width + lax.iota(jnp.int32, raw_width)
-    keep = sample_times[None, None, :] < counts[:, None, None]
-    live = jnp.where(keep, samples, jnp.zeros_like(samples)).reshape(local_stations * 3, raw_width)
+    dense = samples.reshape(local_stations * 3, raw_width)
+    limit = jnp.repeat(counts - corr_place * raw_width, 3)
+    live = jnp.where(
+        lax.iota(jnp.int32, raw_width)[None, :] < limit[:, None], dense, jnp.zeros_like(dense)
+    )
     corr_count = lax.axis_size("corr")
     local_count = templates.shape[0]
     template_width = templates.shape[1]

time: 37.6 us -> 37.1 us (0.987)
  local copies, waits for them, and re-layouts: 5.54 us -> 5.05 us
    lt x1 -> x0, other arithmetic: 0.76 us -> none  [body(): keep = sample_times[None, None, :] < counts[:, None, None]]
    sub x0 -> x1, other arithmetic: none -> 0.66 us  [body(): limit = jnp.repeat(counts - corr_place * raw_width, 3)]
    broadcast_in_dim x2 -> x1, local copies, waits for them, and re-layouts: 0.65 us -> 0.07 us  [body(): limit = jnp.repeat(counts - corr_place * raw_width, 3)]
  transfers between devices with their start and end apart: 8 -> 8, of which waited for: 2 -> 2; matrix products, arithmetic and copies ran while one was open for 23% -> 22% of each run, Pallas kernels for 0% -> 0%
where the time goes in v20:
time: 37.1 us; the launch traced here: 36.8 us
  starting transfers between devices  16.7 us (45%)
  local copies, waits for them, and re-layouts  5.05 us (14%)
  waiting for transfers between devices  4.7 us (13%)
  matrix products  4.05 us (11%)
  Pallas kernels  3.21 us (9%)
  other arithmetic  2.25 us (6%)
  between operations  0.84 us (2%)
    ppermute x3, starting transfers between devices, body(): pieces.append(lax.ppermute(part, 'corr', route))  8.13 us
    ppermute x1, starting transfers between devices, body(): blocks_by_offset[d] = lax.ppermute(wide, 'corr', route)  4.06 us
    pallas_call x1, Pallas kernels, correlate(): pl.pallas_call(functools.partial(body_fn, row_block=row_block, tile=tile)...  3.21 us
    ppermute x1, waiting for transfers between devices, body(): got = lax.ppermute(sent, 'corr', forward)  2.9 us
    ppermute x2, starting transfers between devices, body(): received.append(lax.ppermute(part, ('corr', 'filt'), route))  2.42 us
    dot_general x1, matrix products, body(): spread = jnp.dot(padded, pick_base, preferred_element_type=jnp.float32)  2.03 us
    ppermute x3, waiting for transfers between devices, body(): pieces.append(lax.ppermute(part, 'corr', route))  1.79 us
    unnamed x14, local copies, waits for them, and re-layouts  1.44 us
  transfers between devices with their start and end apart: 8, of which 2 were waited for; matrix products, arithmetic and copies ran while one was open for 22% of the time, Pallas kernels for 0%

profile of v20, /device:TPU:0, one launch (start us, length us, event | category | flops | bytes accessed | tf_op | source)
XLA Modules:
  0.0 36.8 jit_solution(699728378221647993)
XLA Ops:
  0.0 0.7 %pad_bitcast_fusion = (bf16[1,32,256]{2,1,0:T(8,128)(2,1)S(1)}, bf16[32,256]{1,0:T(8,128)(2,1)S(1)}) fusion(bf16[32,225]{1,0:T(8,128)(2,1)} %param.8), kind=kLoop, calls=%fused_computation.144 | loop fusion | bytes 47168 | tf_op jit(solution)/shard_map/stack | solution.py:150
  0.8 4.1 %collective-permute-start.4 = (bf16[32,256]{1,0:T(8,128)(2,1)S(1)}, bf16[32,256]{1,0:T(8,128)(2,1)S(1)}, u32[]{:S(2)}, u32[]{:S(2)}) collective-permute-start(bf16[32,256]{1,0:T(8,128)(2,1)S(1)} %get-tuple-element.19), channel_id=1, source_target_pairs={{0,8},{4,12},{8,0},{12,4},{1,9},{5,13},{9,1},{13,5},{2,10},{6,14},... | collective-permute-start | bytes 49160 | tf_op jit(solution)/shard_map/ppermute | solution.py:149
  4.8 0.7 %subtract_bitcast_fusion = s32[16]{0:T(128)S(1)} fusion(s32[1,16]{1,0:T(1,128)} %param.6, s32[]{:T(128)S(6)} %mul.53), kind=kLoop, calls=%fused_computation.139 | loop fusion | flops 16 | bytes 132 | tf_op jit(solution)/shard_map/sub | solution.py:124
  5.7 1.3 %copy.11 = bf16[1,16,3,4096]{3,2,1,0:T(4,128)(2,1)S(1)} copy(bf16[1,16,3,4096]{3,1,2,0:T(8,128)(2,1)} %param.5) | data formatting | bytes 786432 | tf_op args[0]
  7.0 0.3 reshape_squeeze.3
  7.3 0.2 fusion.17
  7.6 1.4 %collective-permute-start.1 = (bf16[64,512]{1,0:T(8,128)(2,1)S(1)}, bf16[64,512]{1,0:T(8,128)(2,1)S(1)}, u32[]{:S(2)}, u32[]{:S(2)}) collective-permute-start(bf16[64,512]{1,0:T(8,128)(2,1)S(1)} %pad_maximum_fusion), channel_id=1, source_target_pairs={{0,12},{4,0},{8,4},{12,8},{1,13},{5,1},{9,5},{13,9},{2,14},{6,2},{... | collective-permute-start | bytes 196616 | tf_op jit(solution)/shard_map/ppermute | solution.py:143
  9.0 0.7 %collective-permute-start = (bf16[112,128]{1,0:T(8,128)(2,1)S(1)}, bf16[112,128]{1,0:T(8,128)(2,1)S(1)}, u32[]{:S(2)}, u32[]{:S(2)}) collective-permute-start(bf16[112,128]{1,0:T(8,128)(2,1)S(1)} %pad_maximum_fusion.5), channel_id=1, source_target_pairs={{0,4},{4,8},{8,12},{12,0},{1,5},{5,9},{9,13},{13,1},{2,6},{6,10},{... | collective-permute-start | bytes 86024 | tf_op jit(solution)/shard_map/ppermute | solution.py:139
  10.5 0.4 tile.10
  11.1 0.3 convolution_convert_fusion
  11.8 2.9 %collective-permute-done = bf16[112,128]{1,0:T(8,128)(2,1)S(1)} collective-permute-done((bf16[112,128]{1,0:T(8,128)(2,1)S(1)}, bf16[112,128]{1,0:T(8,128)(2,1)S(1)}, u32[]{:S(2)}, u32[]{:S(2)}) %collective-permute-start) | collective-permute-done | bytes 28704 | tf_op jit(solution)/shard_map/ppermute | solution.py:139
  14.7 0.2 convolution_convert_fusion.2
  15.8 0.2 convolution_convert_fusion.1
  16.0 0.7 %collective-permute-start.2 = (bf16[48,640]{1,0:T(8,128)(2,1)S(1)}, bf16[48,640]{1,0:T(8,128)(2,1)S(1)}, u32[]{:S(2)}, u32[]{:S(2)}) collective-permute-start(bf16[48,640]{1,0:T(8,128)(2,1)S(1)} %get-tuple-element.11), channel_id=1, source_target_pairs={{0,0},{2,4},{4,8},{6,12},{8,2},{10,6},{12,10},{14,14},{1,1},{3,5},... | collective-permute-start | bytes 184328 | tf_op jit(solution)/shard_map/ppermute | solution.py:198
  16.7 1.8 %collective-permute-start.3 = (bf16[48,640]{1,0:T(8,128)(2,1)S(1)}, bf16[48,640]{1,0:T(8,128)(2,1)S(1)}, u32[]{:S(2)}, u32[]{:S(2)}) collective-permute-start(bf16[48,640]{1,0:T(8,128)(2,1)S(1)} %get-tuple-element.10), channel_id=1, source_target_pairs={{0,4},{2,0},{4,12},{6,8},{8,6},{10,2},{12,14},{14,10},{1,5},{3,1},... | collective-permute-start | bytes 184328 | tf_op jit(solution)/shard_map/ppermute | solution.py:198
  18.5 2.0 %fusion.1 = f32[128,7680]{1,0:T(8,128)S(1)} fusion(bf16[128,240]{0,1:T(8,128)(2,1)S(1)} %bitcast.79, s32[7680]{0:T(1024)S(1)} %get-tuple-element.25, s32[7680]{0:T(1024)S(1)} %add_select_fusion.4, s32[240]{0:T(256)S(1)} %get-tuple-element.22, s32[240]{0:T(256)S(1)} %get-tuple-element.23), kind=kOutput, calls=%fused_computation.2 | convolution fusion | flops 477388800 | bytes 4056960 | tf_op jit(solution)/shard_map/dot_general | solution.py:241
  20.5 1.3 %fusion.w_ref = bf16[128,7680]{1,0:T(8,128)(2,1)S(1)} fusion(f32[128,7680]{1,0:T(8,128)S(1)} %fusion.1, bf16[128,96]{0,1:T(8,128)(2,1)S(1)} %bitcast.78, s32[7680]{0:T(1024)S(1)} %get-tuple-element.24, s32[7680]{0:T(1024)S(1)} %get-tuple-element.25, s32[96]{0:T(128)S(1)} %get-tuple-element.20, s32[96]{0:T(128)S(1)} %get-tuple-element.21), kind=kOutput, calls=%fused_computation.1 | convolution fusion | flops 192921600 | bytes 5985024 | tf_op jit(solution)/shard_map/dot_general | solution.py:242
  22.7 0.2 fusion.19.inv_ref
  22.9 3.2 %shard_map.55 = f32[128,512]{1,0:T(8,128)S(1)} custom-call(bf16[1,96,640]{2,1,0:T(8,128)(2,1)S(1)} %bitcast.76, f32[96,512]{1,0:T(8,128)S(1)} %fusion.19.inv_ref, bf16[128,7680]{1,0:T(8,128)(2,1)S(1)} %fusion.w_ref), custom_call_target="tpu_custom_call" | custom-call | tf_op jit(solution)/shard_map/pallas_call | solution.py:96
  26.2 2.4 %collective-permute-start.5 = (f32[32,512]{1,0:T(8,128)S(1)}, f32[32,512]{1,0:T(8,128)S(1)}, u32[]{:S(2)}, u32[]{:S(2)}) collective-permute-start(f32[32,512]{1,0:T(8,128)S(1)} %get-tuple-element.7), channel_id=1, source_target_pairs={{0,4},{4,8},{8,12},{12,0},{1,5},{5,9},{9,13},{13,1},{2,6},{6,10},{... | collective-permute-start | bytes 196616 | tf_op jit(solution)/shard_map/ppermute | solution.py:259
  28.6 2.8 %collective-permute-start.6 = (f32[32,512]{1,0:T(8,128)S(1)}, f32[32,512]{1,0:T(8,128)S(1)}, u32[]{:S(2)}, u32[]{:S(2)}) collective-permute-start(f32[32,512]{1,0:T(8,128)S(1)} %get-tuple-element.6), channel_id=1, source_target_pairs={{0,8},{4,12},{8,0},{12,4},{1,9},{5,13},{9,1},{13,5},{2,10},{6,14},... | collective-permute-start | bytes 196616 | tf_op jit(solution)/shard_map/ppermute | solution.py:259
  31.5 2.8 %collective-permute-start.7 = (f32[32,512]{1,0:T(8,128)S(1)}, f32[32,512]{1,0:T(8,128)S(1)}, u32[]{:S(2)}, u32[]{:S(2)}) collective-permute-start(f32[32,512]{1,0:T(8,128)S(1)} %get-tuple-element.5), channel_id=1, source_target_pairs={{0,12},{4,0},{8,4},{12,8},{1,13},{5,1},{9,5},{13,9},{2,14},{6,2},{... | collective-permute-start | bytes 196616 | tf_op jit(solution)/shard_map/ppermute | solution.py:259
  34.4 1.8 %collective-permute-done.7 = f32[32,512]{1,0:T(8,128)S(1)} collective-permute-done((f32[32,512]{1,0:T(8,128)S(1)}, f32[32,512]{1,0:T(8,128)S(1)}, u32[]{:S(2)}, u32[]{:S(2)}) %collective-permute-start.7) | collective-permute-done | bytes 65568 | tf_op jit(solution)/shard_map/ppermute | solution.py:259
  36.2 0.6 %bitcast_dynamic-update-slice_fusion = f32[1,32,2048]{2,1,0:T(8,128)} fusion(f32[1,32,2048]{2,1,0:T(8,128)} %copy-done.1, s32[]{:T(128)S(6)} %select_n.275, f32[32,512]{1,0:T(8,128)S(1)} %collective-permute-done.7), kind=kLoop, calls=%fused_computation.41 | loop fusion | bytes 131076 | tf_op jit(solution)/shard_map/dynamic_update_slice | solution.py:263
  (80 shorter events, 3.0 us)
Async XLA Ops:
  0.0 10.3 %copy-start = (bf16[64]{0:T(256)(128)(2,1)S(1)}, bf16[64]{0:T(256)(128)(2,1)}, u32[]{:S(2)}) copy-start(bf16[64]{0:T(256)(128)(2,1)} %param.7) | copy-start | bytes 388
  0.0 9.9 %copy-start.2 = (s32[128,3,32]{0,2,1:T(8,128)S(1)}, s32[128,3,32]{0,2,1:T(8,128)}, u32[]{:S(2)}) copy-start(s32[128,3,32]{0,2,1:T(8,128)} %param.9) | copy-start | bytes 147460
  0.8 14.2 %collective-permute-start.4 = (bf16[32,256]{1,0:T(8,128)(2,1)S(1)}, bf16[32,256]{1,0:T(8,128)(2,1)S(1)}, u32[]{:S(2)}, u32[]{:S(2)}) collective-permute-start(bf16[32,256]{1,0:T(8,128)(2,1)S(1)} %get-tuple-element.19), channel_id=1, source_target_pairs={{0,8},{4,12},{8,0},{12,4},{1,9},{5,13},{9,1},{13,5},{2,10},{6,14},... | collective-permute-start | bytes 49160 | tf_op jit(solution)/shard_map/ppermute | solution.py:149
  7.6 7.4 %collective-permute-start.1 = (bf16[64,512]{1,0:T(8,128)(2,1)S(1)}, bf16[64,512]{1,0:T(8,128)(2,1)S(1)}, u32[]{:S(2)}, u32[]{:S(2)}) collective-permute-start(bf16[64,512]{1,0:T(8,128)(2,1)S(1)} %pad_maximum_fusion), channel_id=1, source_target_pairs={{0,12},{4,0},{8,4},{12,8},{1,13},{5,1},{9,5},{13,9},{2,14},{6,2},{... | collective-permute-start | bytes 196616 | tf_op jit(solution)/shard_map/ppermute | solution.py:143
  9.0 5.7 %collective-permute-start = (bf16[112,128]{1,0:T(8,128)(2,1)S(1)}, bf16[112,128]{1,0:T(8,128)(2,1)S(1)}, u32[]{:S(2)}, u32[]{:S(2)}) collective-permute-start(bf16[112,128]{1,0:T(8,128)(2,1)S(1)} %pad_maximum_fusion.5), channel_id=1, source_target_pairs={{0,4},{4,8},{8,12},{12,0},{1,5},{5,9},{9,13},{13,1},{2,6},{6,10},{... | collective-permute-start | bytes 86024 | tf_op jit(solution)/shard_map/ppermute | solution.py:139
  16.0 5.7 %collective-permute-start.2 = (bf16[48,640]{1,0:T(8,128)(2,1)S(1)}, bf16[48,640]{1,0:T(8,128)(2,1)S(1)}, u32[]{:S(2)}, u32[]{:S(2)}) collective-permute-start(bf16[48,640]{1,0:T(8,128)(2,1)S(1)} %get-tuple-element.11), channel_id=1, source_target_pairs={{0,0},{2,4},{4,8},{6,12},{8,2},{10,6},{12,10},{14,14},{1,1},{3,5},... | collective-permute-start | bytes 184328 | tf_op jit(solution)/shard_map/ppermute | solution.py:198
  16.7 5.1 %collective-permute-start.3 = (bf16[48,640]{1,0:T(8,128)(2,1)S(1)}, bf16[48,640]{1,0:T(8,128)(2,1)S(1)}, u32[]{:S(2)}, u32[]{:S(2)}) collective-permute-start(bf16[48,640]{1,0:T(8,128)(2,1)S(1)} %get-tuple-element.10), channel_id=1, source_target_pairs={{0,4},{2,0},{4,12},{6,8},{8,6},{10,2},{12,14},{14,10},{1,5},{3,1},... | collective-permute-start | bytes 184328 | tf_op jit(solution)/shard_map/ppermute | solution.py:198
  26.2 8.2 %collective-permute-start.5 = (f32[32,512]{1,0:T(8,128)S(1)}, f32[32,512]{1,0:T(8,128)S(1)}, u32[]{:S(2)}, u32[]{:S(2)}) collective-permute-start(f32[32,512]{1,0:T(8,128)S(1)} %get-tuple-element.7), channel_id=1, source_target_pairs={{0,4},{4,8},{8,12},{12,0},{1,5},{5,9},{9,13},{13,1},{2,6},{6,10},{... | collective-permute-start | bytes 196616 | tf_op jit(solution)/shard_map/ppermute | solution.py:259
  28.6 5.8 %collective-permute-start.6 = (f32[32,512]{1,0:T(8,128)S(1)}, f32[32,512]{1,0:T(8,128)S(1)}, u32[]{:S(2)}, u32[]{:S(2)}) collective-permute-start(f32[32,512]{1,0:T(8,128)S(1)} %get-tuple-element.6), channel_id=1, source_target_pairs={{0,8},{4,12},{8,0},{12,4},{1,9},{5,13},{9,1},{13,5},{2,10},{6,14},... | collective-permute-start | bytes 196616 | tf_op jit(solution)/shard_map/ppermute | solution.py:259
  31.5 4.8 %collective-permute-start.7 = (f32[32,512]{1,0:T(8,128)S(1)}, f32[32,512]{1,0:T(8,128)S(1)}, u32[]{:S(2)}, u32[]{:S(2)}) collective-permute-start(f32[32,512]{1,0:T(8,128)S(1)} %get-tuple-element.5), channel_id=1, source_target_pairs={{0,12},{4,0},{8,4},{12,8},{1,13},{5,1},{9,5},{13,9},{2,14},{6,2},{... | collective-permute-start | bytes 196616 | tf_op jit(solution)/shard_map/ppermute | solution.py:259
  34.4 1.8 %copy-start.1 = (f32[1,32,2048]{2,1,0:T(8,128)}, f32[1,32,2048]{2,1,0:T(8,128)S(1)}, u32[]{:S(2)}) copy-start(f32[1,32,2048]{2,1,0:T(8,128)S(1)} %bitcast_dynamic-update-slice_fusion.1) | copy-start | bytes 786436

commit v21 on v20

--- a/solution.py
+++ b/solution.py
@@ -64,14 +64,26 @@
         o_ref[...] += part
 
 
-def corr_kernel_interleaved(f_ref, inv_ref, w_ref, o_ref, s_ref, *, row_block, tile):
+def corr_kernel_interleaved(f_ref, w_ref, o_ref, s_ref, *, row_block, tile):
     span = tile + 128
     depth = JPI * RSUB
     part = None
     for sub in range(row_block // RSUB):
         r0 = sub * RSUB
         seg = f_ref[0, r0 : r0 + RSUB, :].astype(jnp.float32)
-        inv = inv_ref[r0 : r0 + RSUB, :]
+
+        def ahead(x, k):
+            return pltpu.roll(x, span - k, 1)
+
+        p1 = seg * seg
+        p2 = p1 + ahead(p1, 1)
+        p4 = p2 + ahead(p2, 2)
+        p8 = p4 + ahead(p4, 4)
+        p16 = p8 + ahead(p8, 8)
+        p32 = p16 + ahead(p16, 16)
+        p64 = p32 + ahead(p32, 32)
+        energy = ((p64 + ahead(p8, 64)) + ahead(p2, 72)) + ahead(p1, 74)
+        inv = lax.rsqrt(jnp.maximum(energy[:, :tile], 1.0))
         for j in range(JPI):
             moved = seg if j == 0 else pltpu.roll(seg, span - j, 1)
             piece = (moved[:, :tile] * inv).astype(jnp.bfloat16)
@@ -96,11 +108,9 @@
     return pl.pallas_call(
         functools.partial(body_fn, row_block=row_block, tile=tile),
         grid=(tiles, chunks),
-        in_specs=[
-            pl.BlockSpec((1, row_block, span), lambda i, q: (i, q, 0)),
-            pl.BlockSpec((row_block, tile), lambda i, q: (q, i)),
-            pl.BlockSpec((count, lags * row_block), lambda i, q: (0, q)),
-        ],
+        in_specs=[pl.BlockSpec((1, row_block, span), lambda i, q: (i, q, 0))]
+        + ([] if interleaved else [pl.BlockSpec((row_block, tile), lambda i, q: (q, i))])
+        + [pl.BlockSpec((count, lags * row_block), lambda i, q: (0, q))],
         out_specs=pl.BlockSpec((count, tile), lambda i, q: (0, i)),
         out_shape=jax.ShapeDtypeStruct((count, width), jnp.float32),
         scratch_shapes=[pltpu.VMEM((lags * row_block, tile), jnp.bfloat16)],
@@ -108,7 +118,7 @@
             dimension_semantics=("parallel", "arbitrary"),
             vmem_limit_bytes=48 * 1024 * 1024,
         ),
-    )(windows, inv, weights)
+    )(*((windows, weights) if interleaved else (windows, inv, weights)))
 
 
 def body(raw_rows, valid_counts, taps, templates, masks):

time: 37.1 us -> 37.9 us (1.022)
  Pallas kernels: 3.21 us -> 5.35 us
  starting transfers between devices: 16.7 us -> 15.5 us
  waiting for transfers between devices: 4.7 us -> 5.67 us
  other arithmetic: 2.25 us -> 1.38 us
    pallas_call x1, Pallas kernels: 3.21 us -> 5.35 us  [correlate(): pl.pallas_call(functools.partial(body_fn, row_block=row_block, tile=tile)...]
    ppermute x2, starting transfers between devices: 2.42 us -> 0.72 us  [body(): received.append(lax.ppermute(part, ('corr', 'filt'), route))]
    ppermute x3, waiting for transfers between devices: 1.79 us -> 2.75 us  [body(): pieces.append(lax.ppermute(part, 'corr', route))]
    add x5 -> x0, other arithmetic: 0.63 us -> none  [the longest x1 0.13 us: window_energy(): p2 = p1[:, :-1] + p1[:, 1:]]
    ppermute x3, starting transfers between devices: 8.13 us -> 8.58 us  [body(): pieces.append(lax.ppermute(part, 'corr', route))]
    unnamed x14 -> x13, local copies, waits for them, and re-layouts: 1.44 us -> 1.43 us
  transfers between devices with their start and end apart: 8 -> 8, of which waited for: 2 -> 4; matrix products, arithmetic and copies ran while one was open for 22% -> 24% of each run, Pallas kernels for 0% -> 0%
where the time goes in v21:
time: 37.9 us; the launch traced here: 37.6 us
  starting transfers between devices  15.5 us (41%)
  waiting for transfers between devices  5.67 us (15%)
  Pallas kernels  5.35 us (14%)
  local copies, waits for them, and re-layouts  4.89 us (13%)
  matrix products  4.05 us (11%)
  other arithmetic  1.38 us (4%)
  between operations  0.75 us (2%)
    ppermute x3, starting transfers between devices, body(): pieces.append(lax.ppermute(part, 'corr', route))  8.58 us
    pallas_call x1, Pallas kernels, correlate(): pl.pallas_call(functools.partial(body_fn, row_block=row_block, tile=tile)...  5.35 us
    ppermute x1, starting transfers between devices, body(): blocks_by_offset[d] = lax.ppermute(wide, 'corr', route)  4.06 us
    ppermute x1, waiting for transfers between devices, body(): got = lax.ppermute(sent, 'corr', forward)  2.91 us
    ppermute x3, waiting for transfers between devices, body(): pieces.append(lax.ppermute(part, 'corr', route))  2.75 us
    dot_general x1, matrix products, body(): spread = jnp.dot(padded, pick_base, preferred_element_type=jnp.float32)  2.04 us
    unnamed x13, local copies, waits for them, and re-layouts  1.43 us
    ppermute x1, starting transfers between devices, body(): got = lax.ppermute(sent, 'corr', backward)  1.4 us
  transfers between devices with their start and end apart: 8, of which 4 were waited for; matrix products, arithmetic and copies ran while one was open for 24% of the time, Pallas kernels for 0%

profile of v21, /device:TPU:0, one launch (start us, length us, event | category | flops | bytes accessed | tf_op | source)
XLA Modules:
  0.0 37.6 jit_solution(14909895357631513554)
XLA Ops:
  0.0 0.7 %pad_bitcast_fusion = (bf16[1,32,256]{2,1,0:T(8,128)(2,1)S(1)}, bf16[32,256]{1,0:T(8,128)(2,1)S(1)}) fusion(bf16[32,225]{1,0:T(8,128)(2,1)} %param.8), kind=kLoop, calls=%fused_computation.131 | loop fusion | bytes 47168 | tf_op jit(solution)/shard_map/stack | solution.py:160
  0.7 4.1 %collective-permute-start.4 = (bf16[32,256]{1,0:T(8,128)(2,1)S(1)}, bf16[32,256]{1,0:T(8,128)(2,1)S(1)}, u32[]{:S(2)}, u32[]{:S(2)}) collective-permute-start(bf16[32,256]{1,0:T(8,128)(2,1)S(1)} %get-tuple-element.17), channel_id=1, source_target_pairs={{0,8},{4,12},{8,0},{12,4},{1,9},{5,13},{9,1},{13,5},{2,10},{6,14},... | collective-permute-start | bytes 49160 | tf_op jit(solution)/shard_map/ppermute | solution.py:159
  4.8 1.3 %copy.11 = bf16[1,16,3,4096]{3,2,1,0:T(4,128)(2,1)S(1)} copy(bf16[1,16,3,4096]{3,1,2,0:T(8,128)(2,1)} %param.5) | data formatting | bytes 786432 | tf_op args[0]
  6.2 0.3 reshape_squeeze.3
  6.5 0.7 %subtract_bitcast_fusion = s32[16]{0:T(128)S(1)} fusion(s32[1,16]{1,0:T(1,128)} %param.6, s32[]{:T(128)S(6)} %mul.50), kind=kLoop, calls=%fused_computation.126 | loop fusion | flops 16 | bytes 132 | tf_op jit(solution)/shard_map/sub | solution.py:134
  7.3 0.2 fusion.17
  7.6 1.4 %collective-permute-start.1 = (bf16[64,512]{1,0:T(8,128)(2,1)S(1)}, bf16[64,512]{1,0:T(8,128)(2,1)S(1)}, u32[]{:S(2)}, u32[]{:S(2)}) collective-permute-start(bf16[64,512]{1,0:T(8,128)(2,1)S(1)} %pad_maximum_fusion), channel_id=1, source_target_pairs={{0,12},{4,0},{8,4},{12,8},{1,13},{5,1},{9,5},{13,9},{2,14},{6,2},{... | collective-permute-start | bytes 196616 | tf_op jit(solution)/shard_map/ppermute | solution.py:153
  9.0 0.7 %collective-permute-start = (bf16[112,128]{1,0:T(8,128)(2,1)S(1)}, bf16[112,128]{1,0:T(8,128)(2,1)S(1)}, u32[]{:S(2)}, u32[]{:S(2)}) collective-permute-start(bf16[112,128]{1,0:T(8,128)(2,1)S(1)} %pad_maximum_fusion.5), channel_id=1, source_target_pairs={{0,4},{4,8},{8,12},{12,0},{1,5},{5,9},{9,13},{13,1},{2,6},{6,10},{... | collective-permute-start | bytes 86024 | tf_op jit(solution)/shard_map/ppermute | solution.py:149
  10.1 0.4 tile.10
  11.1 0.3 convolution_convert_fusion
  11.8 2.9 %collective-permute-done = bf16[112,128]{1,0:T(8,128)(2,1)S(1)} collective-permute-done((bf16[112,128]{1,0:T(8,128)(2,1)S(1)}, bf16[112,128]{1,0:T(8,128)(2,1)S(1)}, u32[]{:S(2)}, u32[]{:S(2)}) %collective-permute-start) | collective-permute-done | bytes 28704 | tf_op jit(solution)/shard_map/ppermute | solution.py:149
  14.7 0.2 convolution_convert_fusion.2
  15.0 0.2 convolution_convert_fusion.1
  15.3 0.7 %collective-permute-start.2 = (bf16[48,640]{1,0:T(8,128)(2,1)S(1)}, bf16[48,640]{1,0:T(8,128)(2,1)S(1)}, u32[]{:S(2)}, u32[]{:S(2)}) collective-permute-start(bf16[48,640]{1,0:T(8,128)(2,1)S(1)} %get-tuple-element.8), channel_id=1, source_target_pairs={{0,0},{2,4},{4,8},{6,12},{8,2},{10,6},{12,10},{14,14},{1,1},{3,5},... | collective-permute-start | bytes 184328 | tf_op jit(solution)/shard_map/ppermute | solution.py:208
  16.8 2.0 %fusion.1 = f32[128,7680]{1,0:T(8,128)S(1)} fusion(bf16[128,240]{0,1:T(8,128)(2,1)S(1)} %bitcast.79, s32[7680]{0:T(1024)S(1)} %get-tuple-element.23, s32[7680]{0:T(1024)S(1)} %add_select_fusion.4, s32[240]{0:T(256)S(1)} %get-tuple-element.20, s32[240]{0:T(256)S(1)} %get-tuple-element.21), kind=kOutput, calls=%fused_computation.2 | convolution fusion | flops 477388800 | bytes 4056960 | tf_op jit(solution)/shard_map/dot_general | solution.py:251
  18.8 1.3 %fusion.w_ref = bf16[128,7680]{1,0:T(8,128)(2,1)S(1)} fusion(f32[128,7680]{1,0:T(8,128)S(1)} %fusion.1, bf16[128,96]{0,1:T(8,128)(2,1)S(1)} %bitcast.78, s32[7680]{0:T(1024)S(1)} %get-tuple-element.22, s32[7680]{0:T(1024)S(1)} %get-tuple-element.23, s32[96]{0:T(128)S(1)} %get-tuple-element.18, s32[96]{0:T(128)S(1)} %get-tuple-element.19), kind=kOutput, calls=%fused_computation.1 | convolution fusion | flops 192921600 | bytes 5985024 | tf_op jit(solution)/shard_map/dot_general | solution.py:252
  20.1 5.4 %shard_map.55 = f32[128,512]{1,0:T(8,128)S(1)} custom-call(bf16[1,96,640]{2,1,0:T(8,128)(2,1)S(1)} %maximum_bitcast_fusion.f_ref, bf16[128,7680]{1,0:T(8,128)(2,1)S(1)} %fusion.w_ref), custom_call_target="tpu_custom_call" | custom-call | tf_op jit(solution)/shard_map/pallas_call | solution.py:108
  25.5 3.1 %collective-permute-start.5 = (f32[32,512]{1,0:T(8,128)S(1)}, f32[32,512]{1,0:T(8,128)S(1)}, u32[]{:S(2)}, u32[]{:S(2)}) collective-permute-start(f32[32,512]{1,0:T(8,128)S(1)} %get-tuple-element.7), channel_id=1, source_target_pairs={{0,4},{4,8},{8,12},{12,0},{1,5},{5,9},{9,13},{13,1},{2,6},{6,10},{... | collective-permute-start | bytes 196616 | tf_op jit(solution)/shard_map/ppermute | solution.py:269
  28.6 4.0 %collective-permute-start.6 = (f32[32,512]{1,0:T(8,128)S(1)}, f32[32,512]{1,0:T(8,128)S(1)}, u32[]{:S(2)}, u32[]{:S(2)}) collective-permute-start(f32[32,512]{1,0:T(8,128)S(1)} %get-tuple-element.6), channel_id=1, source_target_pairs={{0,8},{4,12},{8,0},{12,4},{1,9},{5,13},{9,1},{13,5},{2,10},{6,14},... | collective-permute-start | bytes 196616 | tf_op jit(solution)/shard_map/ppermute | solution.py:269
  32.7 1.4 %collective-permute-start.7 = (f32[32,512]{1,0:T(8,128)S(1)}, f32[32,512]{1,0:T(8,128)S(1)}, u32[]{:S(2)}, u32[]{:S(2)}) collective-permute-start(f32[32,512]{1,0:T(8,128)S(1)} %get-tuple-element.5), channel_id=1, source_target_pairs={{0,12},{4,0},{8,4},{12,8},{1,13},{5,1},{9,5},{13,9},{2,14},{6,2},{... | collective-permute-start | bytes 196616 | tf_op jit(solution)/shard_map/ppermute | solution.py:269
  34.2 0.2 collective-permute-done.5
  34.4 0.7 %collective-permute-done.6 = f32[32,512]{1,0:T(8,128)S(1)} collective-permute-done((f32[32,512]{1,0:T(8,128)S(1)}, f32[32,512]{1,0:T(8,128)S(1)}, u32[]{:S(2)}, u32[]{:S(2)}) %collective-permute-start.6) | collective-permute-done | bytes 65568 | tf_op jit(solution)/shard_map/ppermute | solution.py:269
  35.1 1.9 %collective-permute-done.7 = f32[32,512]{1,0:T(8,128)S(1)} collective-permute-done((f32[32,512]{1,0:T(8,128)S(1)}, f32[32,512]{1,0:T(8,128)S(1)}, u32[]{:S(2)}, u32[]{:S(2)}) %collective-permute-start.7) | collective-permute-done | bytes 65568 | tf_op jit(solution)/shard_map/ppermute | solution.py:269
  37.0 0.6 %bitcast_dynamic-update-slice_fusion = f32[1,32,2048]{2,1,0:T(8,128)} fusion(f32[1,32,2048]{2,1,0:T(8,128)} %copy-done.1, s32[]{:T(128)S(6)} %select_n.275, f32[32,512]{1,0:T(8,128)S(1)} %collective-permute-done.7), kind=kLoop, calls=%fused_computation.30 | loop fusion | bytes 131076 | tf_op jit(solution)/shard_map/dynamic_update_slice | solution.py:273
  (71 shorter events, 2.2 us)
Async XLA Ops:
  0.0 9.9 %copy-start = (bf16[64]{0:T(256)(128)(2,1)S(1)}, bf16[64]{0:T(256)(128)(2,1)}, u32[]{:S(2)}) copy-start(bf16[64]{0:T(256)(128)(2,1)} %param.7) | copy-start | bytes 388
  0.7 15.3 %collective-permute-start.4 = (bf16[32,256]{1,0:T(8,128)(2,1)S(1)}, bf16[32,256]{1,0:T(8,128)(2,1)S(1)}, u32[]{:S(2)}, u32[]{:S(2)}) collective-permute-start(bf16[32,256]{1,0:T(8,128)(2,1)S(1)} %get-tuple-element.17), channel_id=1, source_target_pairs={{0,8},{4,12},{8,0},{12,4},{1,9},{5,13},{9,1},{13,5},{2,10},{6,14},... | collective-permute-start | bytes 49160 | tf_op jit(solution)/shard_map/ppermute | solution.py:159
  6.2 4.9 %copy-start.2 = (s32[128,3,32]{0,2,1:T(8,128)S(1)}, s32[128,3,32]{0,2,1:T(8,128)}, u32[]{:S(2)}) copy-start(s32[128,3,32]{0,2,1:T(8,128)} %param.9) | copy-start | bytes 147460
  7.6 7.4 %collective-permute-start.1 = (bf16[64,512]{1,0:T(8,128)(2,1)S(1)}, bf16[64,512]{1,0:T(8,128)(2,1)S(1)}, u32[]{:S(2)}, u32[]{:S(2)}) collective-permute-start(bf16[64,512]{1,0:T(8,128)(2,1)S(1)} %pad_maximum_fusion), channel_id=1, source_target_pairs={{0,12},{4,0},{8,4},{12,8},{1,13},{5,1},{9,5},{13,9},{2,14},{6,2},{... | collective-permute-start | bytes 196616 | tf_op jit(solution)/shard_map/ppermute | solution.py:153
  9.0 5.7 %collective-permute-start = (bf16[112,128]{1,0:T(8,128)(2,1)S(1)}, bf16[112,128]{1,0:T(8,128)(2,1)S(1)}, u32[]{:S(2)}, u32[]{:S(2)}) collective-permute-start(bf16[112,128]{1,0:T(8,128)(2,1)S(1)} %pad_maximum_fusion.5), channel_id=1, source_target_pairs={{0,4},{4,8},{8,12},{12,0},{1,5},{5,9},{9,13},{13,1},{2,6},{6,10},{... | collective-permute-start | bytes 86024 | tf_op jit(solution)/shard_map/ppermute | solution.py:149
  15.2 4.9 %collective-permute-start.3 = (bf16[48,640]{1,0:T(8,128)(2,1)S(1)}, bf16[48,640]{1,0:T(8,128)(2,1)S(1)}, u32[]{:S(2)}, u32[]{:S(2)}) collective-permute-start(bf16[48,640]{1,0:T(8,128)(2,1)S(1)} %get-tuple-element.9), channel_id=1, source_target_pairs={{0,4},{2,0},{4,12},{6,8},{8,6},{10,2},{12,14},{14,10},{1,5},{3,1},... | collective-permute-start | bytes 184328 | tf_op jit(solution)/shard_map/ppermute | solution.py:208
  15.3 4.8 %collective-permute-start.2 = (bf16[48,640]{1,0:T(8,128)(2,1)S(1)}, bf16[48,640]{1,0:T(8,128)(2,1)S(1)}, u32[]{:S(2)}, u32[]{:S(2)}) collective-permute-start(bf16[48,640]{1,0:T(8,128)(2,1)S(1)} %get-tuple-element.8), channel_id=1, source_target_pairs={{0,0},{2,4},{4,8},{6,12},{8,2},{10,6},{12,10},{14,14},{1,1},{3,5},... | collective-permute-start | bytes 184328 | tf_op jit(solution)/shard_map/ppermute | solution.py:208
  25.5 8.8 %collective-permute-start.5 = (f32[32,512]{1,0:T(8,128)S(1)}, f32[32,512]{1,0:T(8,128)S(1)}, u32[]{:S(2)}, u32[]{:S(2)}) collective-permute-start(f32[32,512]{1,0:T(8,128)S(1)} %get-tuple-element.7), channel_id=1, source_target_pairs={{0,4},{4,8},{8,12},{12,0},{1,5},{5,9},{9,13},{13,1},{2,6},{6,10},{... | collective-permute-start | bytes 196616 | tf_op jit(solution)/shard_map/ppermute | solution.py:269
  28.6 6.4 %collective-permute-start.6 = (f32[32,512]{1,0:T(8,128)S(1)}, f32[32,512]{1,0:T(8,128)S(1)}, u32[]{:S(2)}, u32[]{:S(2)}) collective-permute-start(f32[32,512]{1,0:T(8,128)S(1)} %get-tuple-element.6), channel_id=1, source_target_pairs={{0,8},{4,12},{8,0},{12,4},{1,9},{5,13},{9,1},{13,5},{2,10},{6,14},... | collective-permute-start | bytes 196616 | tf_op jit(solution)/shard_map/ppermute | solution.py:269
  32.7 4.3 %collective-permute-start.7 = (f32[32,512]{1,0:T(8,128)S(1)}, f32[32,512]{1,0:T(8,128)S(1)}, u32[]{:S(2)}, u32[]{:S(2)}) collective-permute-start(f32[32,512]{1,0:T(8,128)S(1)} %get-tuple-element.5), channel_id=1, source_target_pairs={{0,12},{4,0},{8,4},{12,8},{1,13},{5,1},{9,5},{13,9},{2,14},{6,2},{... | collective-permute-start | bytes 196616 | tf_op jit(solution)/shard_map/ppermute | solution.py:269
  35.1 1.9 %copy-start.1 = (f32[1,32,2048]{2,1,0:T(8,128)}, f32[1,32,2048]{2,1,0:T(8,128)S(1)}, u32[]{:S(2)}) copy-start(f32[1,32,2048]{2,1,0:T(8,128)S(1)} %bitcast_dynamic-update-slice_fusion.1) | copy-start | bytes 786436

commit v22 on v20

--- a/solution.py
+++ b/solution.py
@@ -11,9 +11,9 @@
 TAPS = 64
 DEC = 4
 JP = 76
-JPI = 80
+JPI = 76
 TT = 512
-RSUB = 16
+RSUB = 32
 
 
 def from_behind(block, axis, distance):

time: 37.1 us -> 37 us (level)
  transfers between devices with their start and end apart: 8 -> 8, of which waited for: 2 -> 3; matrix products, arithmetic and copies ran while one was open for 22% -> 21% of each run, Pallas kernels for 0% -> 0%
where the time goes in v22:
time: 37 us; the launch traced here: 36.8 us
  starting transfers between devices  16.9 us (46%)
  local copies, waits for them, and re-layouts  5.06 us (14%)
  waiting for transfers between devices  4.78 us (13%)
  matrix products  3.85 us (10%)
  Pallas kernels  3.1 us (8%)
  other arithmetic  2.26 us (6%)
  between operations  0.84 us (2%)
    ppermute x3, starting transfers between devices, body(): pieces.append(lax.ppermute(part, 'corr', route))  8.24 us
    ppermute x1, starting transfers between devices, body(): blocks_by_offset[d] = lax.ppermute(wide, 'corr', route)  4.06 us
    pallas_call x1, Pallas kernels, correlate(): pl.pallas_call(functools.partial(body_fn, row_block=row_block, tile=tile)...  3.1 us
    ppermute x1, waiting for transfers between devices, body(): got = lax.ppermute(sent, 'corr', forward)  2.89 us
    ppermute x2, starting transfers between devices, body(): received.append(lax.ppermute(part, ('corr', 'filt'), route))  2.42 us
    dot_general x1, matrix products, body(): spread = jnp.dot(padded, pick_base, preferred_element_type=jnp.float32)  1.91 us
    ppermute x3, waiting for transfers between devices, body(): pieces.append(lax.ppermute(part, 'corr', route))  1.79 us
    unnamed x14, local copies, waits for them, and re-layouts  1.44 us
  transfers between devices with their start and end apart: 8, of which 3 were waited for; matrix products, arithmetic and copies ran while one was open for 21% of the time, Pallas kernels for 0%

profile of v22, /device:TPU:0, one launch (start us, length us, event | category | flops | bytes accessed | tf_op | source)
XLA Modules:
  0.0 36.8 jit_solution(11194488032378144951)
XLA Ops:
  0.0 0.7 %pad_bitcast_fusion = (bf16[1,32,256]{2,1,0:T(8,128)(2,1)S(1)}, bf16[32,256]{1,0:T(8,128)(2,1)S(1)}) fusion(bf16[32,225]{1,0:T(8,128)(2,1)} %param.8), kind=kLoop, calls=%fused_computation.144 | loop fusion | bytes 47168 | tf_op jit(solution)/shard_map/stack | solution.py:150
  0.8 4.1 %collective-permute-start.4 = (bf16[32,256]{1,0:T(8,128)(2,1)S(1)}, bf16[32,256]{1,0:T(8,128)(2,1)S(1)}, u32[]{:S(2)}, u32[]{:S(2)}) collective-permute-start(bf16[32,256]{1,0:T(8,128)(2,1)S(1)} %get-tuple-element.19), channel_id=1, source_target_pairs={{0,8},{4,12},{8,0},{12,4},{1,9},{5,13},{9,1},{13,5},{2,10},{6,14},... | collective-permute-start | bytes 49160 | tf_op jit(solution)/shard_map/ppermute | solution.py:149
  4.8 0.7 %subtract_bitcast_fusion = s32[16]{0:T(128)S(1)} fusion(s32[1,16]{1,0:T(1,128)} %param.6, s32[]{:T(128)S(6)} %mul.53), kind=kLoop, calls=%fused_computation.139 | loop fusion | flops 16 | bytes 132 | tf_op jit(solution)/shard_map/sub | solution.py:124
  5.7 1.3 %copy.11 = bf16[1,16,3,4096]{3,2,1,0:T(4,128)(2,1)S(1)} copy(bf16[1,16,3,4096]{3,1,2,0:T(8,128)(2,1)} %param.5) | data formatting | bytes 786432 | tf_op args[0]
  7.0 0.3 reshape_squeeze.3
  7.3 0.2 fusion.17
  7.6 1.4 %collective-permute-start.1 = (bf16[64,512]{1,0:T(8,128)(2,1)S(1)}, bf16[64,512]{1,0:T(8,128)(2,1)S(1)}, u32[]{:S(2)}, u32[]{:S(2)}) collective-permute-start(bf16[64,512]{1,0:T(8,128)(2,1)S(1)} %pad_maximum_fusion), channel_id=1, source_target_pairs={{0,12},{4,0},{8,4},{12,8},{1,13},{5,1},{9,5},{13,9},{2,14},{6,2},{... | collective-permute-start | bytes 196616 | tf_op jit(solution)/shard_map/ppermute | solution.py:143
  9.0 0.7 %collective-permute-start = (bf16[112,128]{1,0:T(8,128)(2,1)S(1)}, bf16[112,128]{1,0:T(8,128)(2,1)S(1)}, u32[]{:S(2)}, u32[]{:S(2)}) collective-permute-start(bf16[112,128]{1,0:T(8,128)(2,1)S(1)} %pad_maximum_fusion.5), channel_id=1, source_target_pairs={{0,4},{4,8},{8,12},{12,0},{1,5},{5,9},{9,13},{13,1},{2,6},{6,10},{... | collective-permute-start | bytes 86024 | tf_op jit(solution)/shard_map/ppermute | solution.py:139
  10.5 0.4 tile.10
  11.2 0.3 convolution_convert_fusion
  11.8 2.9 %collective-permute-done = bf16[112,128]{1,0:T(8,128)(2,1)S(1)} collective-permute-done((bf16[112,128]{1,0:T(8,128)(2,1)S(1)}, bf16[112,128]{1,0:T(8,128)(2,1)S(1)}, u32[]{:S(2)}, u32[]{:S(2)}) %collective-permute-start) | collective-permute-done | bytes 28704 | tf_op jit(solution)/shard_map/ppermute | solution.py:139
  14.7 0.2 convolution_convert_fusion.2
  15.8 0.2 convolution_convert_fusion.1
  16.1 0.7 %collective-permute-start.2 = (bf16[48,640]{1,0:T(8,128)(2,1)S(1)}, bf16[48,640]{1,0:T(8,128)(2,1)S(1)}, u32[]{:S(2)}, u32[]{:S(2)}) collective-permute-start(bf16[48,640]{1,0:T(8,128)(2,1)S(1)} %get-tuple-element.11), channel_id=1, source_target_pairs={{0,0},{2,4},{4,8},{6,12},{8,2},{10,6},{12,10},{14,14},{1,1},{3,5},... | collective-permute-start | bytes 184328 | tf_op jit(solution)/shard_map/ppermute | solution.py:198
  16.7 1.8 %collective-permute-start.3 = (bf16[48,640]{1,0:T(8,128)(2,1)S(1)}, bf16[48,640]{1,0:T(8,128)(2,1)S(1)}, u32[]{:S(2)}, u32[]{:S(2)}) collective-permute-start(bf16[48,640]{1,0:T(8,128)(2,1)S(1)} %get-tuple-element.10), channel_id=1, source_target_pairs={{0,4},{2,0},{4,12},{6,8},{8,6},{10,2},{12,14},{14,10},{1,5},{3,1},... | collective-permute-start | bytes 184328 | tf_op jit(solution)/shard_map/ppermute | solution.py:198
  18.5 1.9 %fusion.1 = f32[128,7296]{1,0:T(8,128)S(1)} fusion(bf16[128,228]{0,1:T(8,128)(2,1)S(1)} %reshape.227, s32[7296]{0:T(1024)S(1)} %get-tuple-element.25, s32[7296]{0:T(1024)S(1)} %add_select_fusion.4, s32[228]{0:T(256)S(1)} %get-tuple-element.22, s32[228]{0:T(256)S(1)} %get-tuple-element.23), kind=kOutput, calls=%fused_computation.2 | convolution fusion | flops 430843392 | bytes 3854112 | tf_op jit(solution)/shard_map/dot_general | solution.py:241
  20.4 1.2 %fusion.w_ref = bf16[128,7296]{1,0:T(8,128)(2,1)S(1)} fusion(f32[128,7296]{1,0:T(8,128)S(1)} %fusion.1, bf16[128,96]{0,1:T(8,128)(2,1)S(1)} %bitcast.79, s32[7296]{0:T(1024)S(1)} %get-tuple-element.24, s32[7296]{0:T(1024)S(1)} %get-tuple-element.25, s32[96]{0:T(128)S(1)} %get-tuple-element.20, s32[96]{0:T(128)S(1)} %get-tuple-element.21), kind=kOutput, calls=%fused_computation.1 | convolution fusion | flops 183275520 | bytes 5687040 | tf_op jit(solution)/shard_map/dot_general | solution.py:242
  22.6 0.2 fusion.19.inv_ref
  22.8 3.1 %shard_map.55 = f32[128,512]{1,0:T(8,128)S(1)} custom-call(bf16[1,96,640]{2,1,0:T(8,128)(2,1)S(1)} %bitcast.77, f32[96,512]{1,0:T(8,128)S(1)} %fusion.19.inv_ref, bf16[128,7296]{1,0:T(8,128)(2,1)S(1)} %fusion.w_ref), custom_call_target="tpu_custom_call" | custom-call | tf_op jit(solution)/shard_map/pallas_call | solution.py:96
  26.0 2.4 %collective-permute-start.5 = (f32[32,512]{1,0:T(8,128)S(1)}, f32[32,512]{1,0:T(8,128)S(1)}, u32[]{:S(2)}, u32[]{:S(2)}) collective-permute-start(f32[32,512]{1,0:T(8,128)S(1)} %get-tuple-element.7), channel_id=1, source_target_pairs={{0,4},{4,8},{8,12},{12,0},{1,5},{5,9},{9,13},{13,1},{2,6},{6,10},{... | collective-permute-start | bytes 196616 | tf_op jit(solution)/shard_map/ppermute | solution.py:259
  28.3 3.0 %collective-permute-start.6 = (f32[32,512]{1,0:T(8,128)S(1)}, f32[32,512]{1,0:T(8,128)S(1)}, u32[]{:S(2)}, u32[]{:S(2)}) collective-permute-start(f32[32,512]{1,0:T(8,128)S(1)} %get-tuple-element.6), channel_id=1, source_target_pairs={{0,8},{4,12},{8,0},{12,4},{1,9},{5,13},{9,1},{13,5},{2,10},{6,14},... | collective-permute-start | bytes 196616 | tf_op jit(solution)/shard_map/ppermute | solution.py:259
  31.4 2.8 %collective-permute-start.7 = (f32[32,512]{1,0:T(8,128)S(1)}, f32[32,512]{1,0:T(8,128)S(1)}, u32[]{:S(2)}, u32[]{:S(2)}) collective-permute-start(f32[32,512]{1,0:T(8,128)S(1)} %get-tuple-element.5), channel_id=1, source_target_pairs={{0,12},{4,0},{8,4},{12,8},{1,13},{5,1},{9,5},{13,9},{2,14},{6,2},{... | collective-permute-start | bytes 196616 | tf_op jit(solution)/shard_map/ppermute | solution.py:259
  34.3 1.8 %collective-permute-done.7 = f32[32,512]{1,0:T(8,128)S(1)} collective-permute-done((f32[32,512]{1,0:T(8,128)S(1)}, f32[32,512]{1,0:T(8,128)S(1)}, u32[]{:S(2)}, u32[]{:S(2)}) %collective-permute-start.7) | collective-permute-done | bytes 65568 | tf_op jit(solution)/shard_map/ppermute | solution.py:259
  36.1 0.6 %bitcast_dynamic-update-slice_fusion = f32[1,32,2048]{2,1,0:T(8,128)} fusion(f32[1,32,2048]{2,1,0:T(8,128)} %copy-done.1, s32[]{:T(128)S(6)} %select_n.275, f32[32,512]{1,0:T(8,128)S(1)} %collective-permute-done.7), kind=kLoop, calls=%fused_computation.41 | loop fusion | bytes 131076 | tf_op jit(solution)/shard_map/dynamic_update_slice | solution.py:263
  (81 shorter events, 3.1 us)
Async XLA Ops:
  0.0 10.3 %copy-start = (bf16[64]{0:T(256)(128)(2,1)S(1)}, bf16[64]{0:T(256)(128)(2,1)}, u32[]{:S(2)}) copy-start(bf16[64]{0:T(256)(128)(2,1)} %param.7) | copy-start | bytes 388
  0.0 9.9 %copy-start.2 = (s32[128,3,32]{0,2,1:T(8,128)S(1)}, s32[128,3,32]{0,2,1:T(8,128)}, u32[]{:S(2)}) copy-start(s32[128,3,32]{0,2,1:T(8,128)} %param.9) | copy-start | bytes 147460
  0.8 14.2 %collective-permute-start.4 = (bf16[32,256]{1,0:T(8,128)(2,1)S(1)}, bf16[32,256]{1,0:T(8,128)(2,1)S(1)}, u32[]{:S(2)}, u32[]{:S(2)}) collective-permute-start(bf16[32,256]{1,0:T(8,128)(2,1)S(1)} %get-tuple-element.19), channel_id=1, source_target_pairs={{0,8},{4,12},{8,0},{12,4},{1,9},{5,13},{9,1},{13,5},{2,10},{6,14},... | collective-permute-start | bytes 49160 | tf_op jit(solution)/shard_map/ppermute | solution.py:149
  7.6 7.4 %collective-permute-start.1 = (bf16[64,512]{1,0:T(8,128)(2,1)S(1)}, bf16[64,512]{1,0:T(8,128)(2,1)S(1)}, u32[]{:S(2)}, u32[]{:S(2)}) collective-permute-start(bf16[64,512]{1,0:T(8,128)(2,1)S(1)} %pad_maximum_fusion), channel_id=1, source_target_pairs={{0,12},{4,0},{8,4},{12,8},{1,13},{5,1},{9,5},{13,9},{2,14},{6,2},{... | collective-permute-start | bytes 196616 | tf_op jit(solution)/shard_map/ppermute | solution.py:143
  9.0 5.7 %collective-permute-start = (bf16[112,128]{1,0:T(8,128)(2,1)S(1)}, bf16[112,128]{1,0:T(8,128)(2,1)S(1)}, u32[]{:S(2)}, u32[]{:S(2)}) collective-permute-start(bf16[112,128]{1,0:T(8,128)(2,1)S(1)} %pad_maximum_fusion.5), channel_id=1, source_target_pairs={{0,4},{4,8},{8,12},{12,0},{1,5},{5,9},{9,13},{13,1},{2,6},{6,10},{... | collective-permute-start | bytes 86024 | tf_op jit(solution)/shard_map/ppermute | solution.py:139
  16.1 5.6 %collective-permute-start.2 = (bf16[48,640]{1,0:T(8,128)(2,1)S(1)}, bf16[48,640]{1,0:T(8,128)(2,1)S(1)}, u32[]{:S(2)}, u32[]{:S(2)}) collective-permute-start(bf16[48,640]{1,0:T(8,128)(2,1)S(1)} %get-tuple-element.11), channel_id=1, source_target_pairs={{0,0},{2,4},{4,8},{6,12},{8,2},{10,6},{12,10},{14,14},{1,1},{3,5},... | collective-permute-start | bytes 184328 | tf_op jit(solution)/shard_map/ppermute | solution.py:198
  16.7 5.0 %collective-permute-start.3 = (bf16[48,640]{1,0:T(8,128)(2,1)S(1)}, bf16[48,640]{1,0:T(8,128)(2,1)S(1)}, u32[]{:S(2)}, u32[]{:S(2)}) collective-permute-start(bf16[48,640]{1,0:T(8,128)(2,1)S(1)} %get-tuple-element.10), channel_id=1, source_target_pairs={{0,4},{2,0},{4,12},{6,8},{8,6},{10,2},{12,14},{14,10},{1,5},{3,1},... | collective-permute-start | bytes 184328 | tf_op jit(solution)/shard_map/ppermute | solution.py:198
  26.0 8.3 %collective-permute-start.5 = (f32[32,512]{1,0:T(8,128)S(1)}, f32[32,512]{1,0:T(8,128)S(1)}, u32[]{:S(2)}, u32[]{:S(2)}) collective-permute-start(f32[32,512]{1,0:T(8,128)S(1)} %get-tuple-element.7), channel_id=1, source_target_pairs={{0,4},{4,8},{8,12},{12,0},{1,5},{5,9},{9,13},{13,1},{2,6},{6,10},{... | collective-permute-start | bytes 196616 | tf_op jit(solution)/shard_map/ppermute | solution.py:259
  28.3 6.0 %collective-permute-start.6 = (f32[32,512]{1,0:T(8,128)S(1)}, f32[32,512]{1,0:T(8,128)S(1)}, u32[]{:S(2)}, u32[]{:S(2)}) collective-permute-start(f32[32,512]{1,0:T(8,128)S(1)} %get-tuple-element.6), channel_id=1, source_target_pairs={{0,8},{4,12},{8,0},{12,4},{1,9},{5,13},{9,1},{13,5},{2,10},{6,14},... | collective-permute-start | bytes 196616 | tf_op jit(solution)/shard_map/ppermute | solution.py:259
  31.4 4.8 %collective-permute-start.7 = (f32[32,512]{1,0:T(8,128)S(1)}, f32[32,512]{1,0:T(8,128)S(1)}, u32[]{:S(2)}, u32[]{:S(2)}) collective-permute-start(f32[32,512]{1,0:T(8,128)S(1)} %get-tuple-element.5), channel_id=1, source_target_pairs={{0,12},{4,0},{8,4},{12,8},{1,13},{5,1},{9,5},{13,9},{2,14},{6,2},{... | collective-permute-start | bytes 196616 | tf_op jit(solution)/shard_map/ppermute | solution.py:259
  34.3 1.8 %copy-start.1 = (f32[1,32,2048]{2,1,0:T(8,128)}, f32[1,32,2048]{2,1,0:T(8,128)S(1)}, u32[]{:S(2)}) copy-start(f32[1,32,2048]{2,1,0:T(8,128)S(1)} %bitcast_dynamic-update-slice_fusion.1) | copy-start | bytes 786436
